TPU v7x, 32 devices: a whole 2x2x4 slice. The times are simulated.
32 devices in a mesh: tm: 2 (over x), space: 16 (over z, y, core).
Axes of the slice: x: 2, y: 2, z: 4, core: 2. Of those that a mesh axis runs over, the one named last changes fastest.
Arguments:
- initial: float32 [2, 64, 128, 256], P(None, None, 'space'), may hold values from -12 to 12
- x_velocity: float32 [64, 128, 256], P(None, 'space'), may hold values from -4 to 4
- y_velocity: float32 [64, 128, 256], P(None, 'space'), may hold values from -1 to 1
- h_diffusion: float32 [64, 128, 256], P(None, 'space'), may hold values from 0.1 to 0.5
- v_diffusion: float32 [64, 128, 256], P(None, 'space'), may hold values from 0.05 to 0.5
- coupling: float32 [2, 2], replicated, may hold values from -0.5 to 0.5
Outputs:
- slab_end: float32 [2, 2, 64, 128, 256], P('tm', None, None, 'space')
All inputs are finite; a program needn't handle non-finite values.
Results may differ from a plain program's by a relative error of at most 0.00002.
Values sent between devices are 32-bit elements; how exact they have to be, the bound alone decides.
No kernel may reach another device: no remote copies, remote signals or barrier semaphores. Data moves between devices by JAX's collectives and lax.ppermute only.
A program may use at most 64 MiB of HBM per device.

v0:
```python
import jax
import jax.numpy as jnp
from jax import lax
from jax.sharding import PartitionSpec as P

ITERS = 2


slab_step = 0.5
half_step = 0.25


def shift_pairs(count, steps):
    return [(i, i + steps) for i in range(max(0, -steps), min(count, count - steps))]


def exchange(to_right, to_left):
    count = lax.axis_size("space")
    before = lax.ppermute(to_right, "space", shift_pairs(count, 1))
    after = lax.ppermute(to_left, "space", shift_pairs(count, -1))
    return before, after


def lo(field, width=1):
    return field[..., :width, :]


def hi(field, width=1):
    return field[..., field.shape[-2] - width:, :]


def halo_of(field):
    return exchange(hi(field), lo(field))


def tendency(field, halo, x_speed, y_speed, h_spread, v_spread, coupling, x_spacing, z_spacing):
    reach = int(x_spacing)
    padded = jnp.concatenate([halo[0]] * reach + [field] + [halo[1]] * reach, axis=-2)
    width = field.shape[-2]
    middle = field
    eastward = padded[..., 2 * reach:, :]
    westward = padded[..., :width, :]
    y_widths = [(0, 0)] * (middle.ndim - 1) + [(1, 1)]
    y_padded = jnp.pad(middle, y_widths)
    northward = y_padded[..., 2:]
    southward = y_padded[..., :-2]
    z_widths = [(0, 0)] * (middle.ndim - 3) + [(1, 1), (0, 0), (0, 0)]
    z_padded = jnp.pad(middle, z_widths)
    upward = z_padded[..., 2:, :, :]
    downward = z_padded[..., :-2, :, :]
    advection = (
        x_speed * (eastward - westward) / (2.0 * x_spacing)
        + y_speed * (northward - southward) * 0.5
    )
    diffusion = h_spread * (
        (eastward - 2.0 * middle + westward) / (x_spacing * x_spacing)
        + (northward - 2.0 * middle + southward)
    )
    vertical = v_spread * (upward - 2.0 * middle + downward) / (z_spacing * z_spacing)
    reaction = coupling[:, 0].reshape(-1, 1, 1, 1) * middle[..., 0:1, :, :, :]
    reaction = reaction + coupling[:, 1].reshape(-1, 1, 1, 1) * middle[..., 1:2, :, :, :]
    return diffusion + vertical - advection + reaction


def pair_sum(field):
    row = lax.broadcasted_iota(jnp.int32, field.shape, field.ndim - 2)
    partner = jnp.where(
        row % 2 == 0, jnp.roll(field, -1, axis=-2), jnp.roll(field, 1, axis=-2)
    )
    return field + partner


def shrink(field):
    levels = field[..., 0::2, :, :] + field[..., 1::2, :, :]
    return pair_sum(levels) * 0.25


def expand(field):
    return jnp.repeat(field, 2, axis=-3)


def expand_z(field):
    return jnp.repeat(field, 2, axis=-3)


def pick(items, index):
    out = items[0]
    for k in range(1, len(items)):
        out = jax.tree.map(lambda new, old: jnp.where(index == k, new, old), items[k], out)
    return out


def pair_map(fn, *pairs):
    return tuple(fn(*parts) for parts in zip(*pairs))


def body(initial, x_velocity, y_velocity, h_diffusion, v_diffusion, coupling):
    coarse_x = shrink(x_velocity)
    coarse_y = shrink(y_velocity)
    coarse_h = shrink(h_diffusion)
    coarse_v = shrink(v_diffusion)
    slabs = lax.axis_size("tm")
    columns = lax.axis_size("space")
    slab = lax.axis_index("tm")
    first = slab == 0

    def fine_rate(field, halo):
        return tendency(
            field, halo, x_velocity, y_velocity, h_diffusion, v_diffusion, coupling, 1.0, 1.0
        )

    def coarse_rate(field, halo):
        return tendency(field, halo, coarse_x, coarse_y, coarse_h, coarse_v, coupling, 2.0, 2.0)

    def first_node(node_zero, rate_zero, s0, s1, s2):
        return (
            node_zero
            + half_step * (rate_zero - s0)
            + slab_step * (s0 * (5.0 / 24.0) + s1 * (1.0 / 3.0) - s2 * (1.0 / 24.0))
        )

    def second_node(node_one, rate_one, s0, s1, s2):
        return (
            node_one
            + half_step * (rate_one - s1)
            + slab_step * (s0 * (-1.0 / 24.0) + s1 * (1.0 / 3.0) + s2 * (5.0 / 24.0))
        )

    coarse_first = shrink(initial)
    (init_b, first_b), (init_a, first_a) = exchange(
        (hi(initial), hi(coarse_first)), (lo(initial), lo(coarse_first))
    )
    halo_zero = (init_b, init_a)
    halo_first = (first_b, first_a)
    first_rate = fine_rate(initial, halo_zero)
    coarse_first_rate = coarse_rate(coarse_first, halo_first)

    node_zero = initial
    rate_zero = first_rate
    node_one = first_node(node_zero, rate_zero, first_rate, first_rate, first_rate)
    halo_one = halo_of(node_one)
    rate_one = fine_rate(node_one, halo_one)
    node_two = second_node(node_one, rate_one, first_rate, first_rate, first_rate)
    two_b, two_a = exchange(hi(node_two, 2), lo(node_two, 2))
    halo_two = (hi(two_b), lo(two_a))
    coarse_end = shrink(node_two)
    halo_end = (hi(shrink(two_b)), lo(shrink(two_a)))
    rate_two = fine_rate(node_two, halo_two)
    source = shrink(slab_step * (rate_zero + 4.0 * rate_one + rate_two) / 6.0)
    offset = source - slab_step * coarse_first_rate

    chain = [coarse_first]
    chain_halo = [halo_first]
    rate = coarse_first_rate
    for count in range(slabs):
        after = chain[-1] + slab_step * rate + offset
        after_halo = halo_of(after)
        chain.append(after)
        chain_halo.append(after_halo)
        if count + 1 < slabs:
            rate = coarse_rate(after, after_halo)
    begins = pick(chain, slab)
    finals = pick(chain, slab + 1)
    begins_halo = pick(chain_halo, slab)
    finals_halo = pick(chain_halo, slab + 1)

    delta_zero = begins - coarse_first
    delta_one = finals - coarse_end
    fixed_zero = node_zero + expand(delta_zero)
    fixed_one = node_one + expand((delta_zero + delta_one) * 0.5)
    fixed_two = node_two + expand(delta_one)
    halo_dz = pair_map(lambda y, v: y - v, begins_halo, halo_first)
    halo_d1 = pair_map(lambda y, v: y - v, finals_halo, halo_end)
    halo_f0 = pair_map(lambda w, d: w + expand_z(d), halo_zero, halo_dz)
    halo_f1 = pair_map(
        lambda w, d0, d1: w + expand_z((d0 + d1) * 0.5), halo_one, halo_dz, halo_d1
    )
    halo_f2 = pair_map(lambda w, d: w + expand_z(d), halo_two, halo_d1)

    earlier_delta = begins - coarse_end
    earlier_end = node_two + expand(earlier_delta)
    halo_earlier_delta = pair_map(lambda y, v: y - v, begins_halo, halo_end)
    halo_earlier = pair_map(lambda w, d: w + expand_z(d), halo_two, halo_earlier_delta)
    wide_earlier = (
        two_b + expand(halo_earlier_delta[0]),
        two_a + expand(halo_earlier_delta[1]),
    )
    start = jnp.where(first, initial, earlier_end)
    halo_start = pair_map(lambda a, b: jnp.where(first, a, b), halo_zero, halo_earlier)
    halo_start_coarse = pair_map(
        lambda a, w: jnp.where(first, a, lo(shrink(w))), halo_first, wide_earlier
    )

    slope_zero = fine_rate(fixed_zero, halo_f0)
    slope_one = fine_rate(fixed_one, halo_f1)
    slope_two = fine_rate(fixed_two, halo_f2)
    node_zero = start
    rate_zero = fine_rate(node_zero, halo_start)
    node_one = first_node(node_zero, rate_zero, slope_zero, slope_one, slope_two)
    rate_one = fine_rate(node_one, halo_of(node_one))
    node_two = second_node(node_one, rate_one, slope_zero, slope_one, slope_two)
    rate_two = fine_rate(node_two, halo_of(node_two))
    coarse_zero = shrink(node_zero)
    coarse_end = shrink(node_two)
    source = shrink(slab_step * (rate_zero + 4.0 * rate_one + rate_two) / 6.0)
    offset = source - slab_step * coarse_rate(coarse_zero, halo_start_coarse)

    down = shift_pairs(slabs, 1)
    to_east = [
        (t * columns + c, (t + 1) * columns + c + 1)
        for t in range(slabs - 1)
        for c in range(columns - 1)
    ]
    to_west = [
        (t * columns + c, (t + 1) * columns + c - 1)
        for t in range(slabs - 1)
        for c in range(1, columns)
    ]
    carried = coarse_first
    carried_halo = halo_first
    rate = coarse_first_rate
    for count in range(slabs - 1):
        after = carried + slab_step * rate + offset
        passed = lax.ppermute(after, "tm", down)
        passed_b = lax.ppermute(hi(after), ("tm", "space"), to_east)
        passed_a = lax.ppermute(lo(after), ("tm", "space"), to_west)
        carried = jnp.where(first, coarse_first, passed)
        carried_halo = pair_map(
            lambda a, b: jnp.where(first, a, b), halo_first, (passed_b, passed_a)
        )
        rate = coarse_rate(carried, carried_halo)
    finals = carried + slab_step * rate + offset
    result = node_two + expand(finals - coarse_end)
    return result[None]


def solution(mesh):
    return jax.shard_map(
        body,
        mesh=mesh,
        in_specs=(
            P(None, None, "space", None),
            P(None, "space", None),
            P(None, "space", None),
            P(None, "space", None),
            P(None, "space", None),
            P(),
        ),
        out_specs=P("tm", None, None, "space", None),
        check_vma=False,
    )
```

profile of v0, /device:TPU:11, one launch (start us, length us, event | category | flops | bytes accessed | tf_op | source)
XLA Modules:
  0.0 158.2 jit_solution(16683598211363608552)
XLA Ops:
  0.0 2.5 %fusion.95 = (f32[2,64,1,256]{3,2,1,0:T(1,128)}, f32[2,64,1,256]{3,2,1,0:T(1,128)}) fusion(f32[2,64,8,256]{3,2,1,0:T(8,128)} %param.6), kind=kLoop, calls=%fused_computation.263 | loop fusion | bytes 524288 | tf_op jit(solution)/shard_map/slice | solution.py:25
  2.5 2.6 %collective-permute-start = (f32[2,64,1,256]{3,2,1,0:T(1,128)}, f32[2,64,1,256]{3,2,1,0:T(1,128)}, u32[]{:S(2)}, u32[]{:S(2)}) collective-permute-start(f32[2,64,1,256]{3,2,1,0:T(1,128)} %get-tuple-element.65), channel_id=1, source_target_pairs={{1,0},{2,1},{3,2},{4,3},{5,4},{6,5},{7,6},{8,7},{9,8},{10,9},{11,1... | collective-permute-start | bytes 393224 | tf_op jit(solution)/shard_map/ppermute | solution.py:20
  5.1 3.0 %collective-permute-start.1 = (f32[2,64,1,256]{3,2,1,0:T(1,128)}, f32[2,64,1,256]{3,2,1,0:T(1,128)}, u32[]{:S(2)}, u32[]{:S(2)}) collective-permute-start(f32[2,64,1,256]{3,2,1,0:T(1,128)} %get-tuple-element.66), channel_id=1, source_target_pairs={{0,1},{1,2},{2,3},{3,4},{4,5},{5,6},{6,7},{7,8},{8,9},{9,10},{10,1... | collective-permute-start | bytes 393224 | tf_op jit(solution)/shard_map/ppermute | solution.py:19
  14.5 3.8 %collective-permute-start.5 = (f32[2,32,1,256]{3,2,1,0:T(1,128)}, f32[2,32,1,256]{3,2,1,0:T(1,128)S(1)}, u32[]{:S(2)}, u32[]{:S(2)}) collective-permute-start(f32[2,32,1,256]{3,2,1,0:T(1,128)} %get-tuple-element.98), channel_id=1, source_target_pairs={{0,1},{1,2},{2,3},{3,4},{4,5},{5,6},{6,7},{7,8},{8,9},{9,10},{10,1... | collective-permute-start | bytes 196616 | tf_op jit(solution)/shard_map/ppermute | solution.py:19
  24.8 2.8 %multiply_add_fusion.3 = (f32[2,64,8,256]{3,2,1,0:T(8,128)S(1)}, f32[2,64,8,256]{3,2,1,0:T(8,128)S(1)}) fusion(f32[2,64,8,256]{3,2,1,0:T(8,128)S(1)} %copy-done.2, f32[64,8,256]{2,1,0:T(8,128)} %get-tuple-element.68, f32[2]{0:T(128)S(1)} %get-tuple-element.6, f32[64,8,256]{2,1,0:T(8,128)} %get-tuple-element.67, f32[2]{0:T(128)S(1)} %get-tuple-element.5, ...), kind=kLoop, calls=%fused_computation.49 | loop fusion | flops 8912896 | bytes 6553616 | tf_op jit(solution)/shard_map/add | solution.py:117
  27.7 2.5 %collective-permute-start.2 = (f32[2,64,1,256]{3,2,1,0:T(1,128)S(1)}, f32[2,64,1,256]{3,2,1,0:T(1,128)S(1)}, u32[]{:S(2)}, u32[]{:S(2)}) collective-permute-start(f32[2,64,1,256]{3,2,1,0:T(1,128)S(1)} %get-tuple-element.61), channel_id=1, source_target_pairs={{1,0},{2,1},{3,2},{4,3},{5,4},{6,5},{7,6},{8,7},{9,8},{10,9},{11,1... | collective-permute-start | bytes 393224 | tf_op jit(solution)/shard_map/ppermute | solution.py:20
  30.2 3.0 %collective-permute-start.3 = (f32[2,64,1,256]{3,2,1,0:T(1,128)S(1)}, f32[2,64,1,256]{3,2,1,0:T(1,128)S(1)}, u32[]{:S(2)}, u32[]{:S(2)}) collective-permute-start(f32[2,64,1,256]{3,2,1,0:T(1,128)S(1)} %get-tuple-element.62), channel_id=1, source_target_pairs={{0,1},{1,2},{2,3},{3,4},{4,5},{5,6},{6,7},{7,8},{8,9},{9,10},{10,1... | collective-permute-start | bytes 393224 | tf_op jit(solution)/shard_map/ppermute | solution.py:19
  34.0 2.6 %collective-permute-done.3 = f32[2,64,1,256]{3,2,1,0:T(1,128)S(1)} collective-permute-done((f32[2,64,1,256]{3,2,1,0:T(1,128)S(1)}, f32[2,64,1,256]{3,2,1,0:T(1,128)S(1)}, u32[]{:S(2)}, u32[]{:S(2)}) %collective-permute-start.3) | collective-permute-done | bytes 131104 | tf_op jit(solution)/shard_map/ppermute | solution.py:19
  38.6 5.4 %collective-permute-start.6 = (f32[2,64,2,256]{3,2,1,0:T(2,128)S(1)}, f32[2,64,2,256]{3,2,1,0:T(2,128)S(1)}, u32[]{:S(2)}, u32[]{:S(2)}) collective-permute-start(f32[2,64,2,256]{3,2,1,0:T(2,128)S(1)} %get-tuple-element.59), channel_id=1, source_target_pairs={{1,0},{2,1},{3,2},{4,3},{5,4},{6,5},{7,6},{8,7},{9,8},{10,9},{11,1... | collective-permute-start | bytes 786440 | tf_op jit(solution)/shard_map/ppermute | solution.py:20
  47.1 4.2 %collective-permute-done.7 = f32[2,64,2,256]{3,2,1,0:T(2,128)S(1)} collective-permute-done((f32[2,64,2,256]{3,2,1,0:T(2,128)S(1)}, f32[2,64,2,256]{3,2,1,0:T(2,128)S(1)}, u32[]{:S(2)}, u32[]{:S(2)}) %collective-permute-start.7) | collective-permute-done | bytes 262176 | tf_op jit(solution)/shard_map/ppermute | solution.py:19
  56.9 3.2 %collective-permute-start.8 = (f32[2,32,1,256]{3,2,1,0:T(1,128)S(1)}, f32[2,32,1,256]{3,2,1,0:T(1,128)S(1)}, u32[]{:S(2)}, u32[]{:S(2)}) collective-permute-start(f32[2,32,1,256]{3,2,1,0:T(1,128)S(1)} %get-tuple-element.93), channel_id=1, source_target_pairs={{1,0},{2,1},{3,2},{4,3},{5,4},{6,5},{7,6},{8,7},{9,8},{10,9},{11,1... | collective-permute-start | bytes 196616 | tf_op jit(solution)/shard_map/ppermute | solution.py:20
  60.1 3.1 %collective-permute-start.9 = (f32[2,32,1,256]{3,2,1,0:T(1,128)S(1)}, f32[2,32,1,256]{3,2,1,0:T(1,128)S(1)}, u32[]{:S(2)}, u32[]{:S(2)}) collective-permute-start(f32[2,32,1,256]{3,2,1,0:T(1,128)S(1)} %get-tuple-element.94), channel_id=1, source_target_pairs={{0,1},{1,2},{2,3},{3,4},{4,5},{5,6},{6,7},{7,8},{8,9},{9,10},{10,1... | collective-permute-start | bytes 196616 | tf_op jit(solution)/shard_map/ppermute | solution.py:19
  68.8 4.0 %collective-permute-start.10 = (f32[2,32,1,256]{3,2,1,0:T(1,128)S(1)}, f32[2,32,1,256]{3,2,1,0:T(1,128)S(1)}, u32[]{:S(2)}, u32[]{:S(2)}) collective-permute-start(f32[2,32,1,256]{3,2,1,0:T(1,128)S(1)} %get-tuple-element.87), channel_id=1, source_target_pairs={{1,0},{2,1},{3,2},{4,3},{5,4},{6,5},{7,6},{8,7},{9,8},{10,9},{11,1... | collective-permute-start | bytes 196616 | tf_op jit(solution)/shard_map/ppermute | solution.py:20
  72.8 2.4 %collective-permute-start.11 = (f32[2,32,1,256]{3,2,1,0:T(1,128)}, f32[2,32,1,256]{3,2,1,0:T(1,128)S(1)}, u32[]{:S(2)}, u32[]{:S(2)}) collective-permute-start(f32[2,32,1,256]{3,2,1,0:T(1,128)} %get-tuple-element.88), channel_id=1, source_target_pairs={{0,1},{1,2},{2,3},{3,4},{4,5},{5,6},{6,7},{7,8},{8,9},{9,10},{10,1... | collective-permute-start | bytes 196616 | tf_op jit(solution)/shard_map/ppermute | solution.py:19
  88.7 2.3 %slice_add_fusion.15 = (f32[2,64,1,256]{3,2,1,0:T(1,128)S(1)}, f32[2,64,1,256]{3,2,1,0:T(1,128)S(1)}, f32[2,64,1,256]{3,2,1,0:T(1,128)}) fusion(f32[2,64,1,256]{3,2,1,0:T(1,128)} %broadcast_in_dim.61, f32[2,64,2,256]{3,2,1,0:T(2,128)} %copy-done.31, f32[2,64,1,256]{3,2,1,0:T(1,128)} %collective-permute-done, f32[2,64,1,256]{3,2,1,0:T(1,128)} %broadcast_in_dim.46, ...), kind=kLoop, calls=%fused_computation.254 | loop fusion | flops 131072 | bytes 1048577 | tf_op jit(solution)/shard_map/add | solution.py:178
  91.0 2.4 %slice_add_fusion.14 = (f32[2,64,1,256]{3,2,1,0:T(1,128)}, f32[2,64,1,256]{3,2,1,0:T(1,128)}, f32[2,64,1,256]{3,2,1,0:T(1,128)}) fusion(f32[2,64,1,256]{3,2,1,0:T(1,128)} %broadcast_in_dim.63, f32[2,64,2,256]{3,2,1,0:T(2,128)S(1)} %copy-done.30, f32[2,64,1,256]{3,2,1,0:T(1,128)} %collective-permute-done.1, f32[2,64,1,256]{3,2,1,0:T(1,128)} %broadcast_in_dim.48, ...), kind=kLoop, calls=%fused_computation.253 | loop fusion | flops 131072 | bytes 1048577 | tf_op jit(solution)/shard_map/add | solution.py:178
  93.4 11.8 %multiply_add_fusion.1 = (f32[2,64,8,256]{3,2,1,0:T(8,128)S(1)}, f32[2,64,8,256]{3,2,1,0:T(8,128)}, f32[2,64,8,256]{3,2,1,0:T(8,128)}, f32[2,64,8,256]{3,2,1,0:T(8,128)}, f32[2,64,8,256]{3,2,1,0:T(8,128)}) fusion(f32[2,64,8,256]{3,2,1,0:T(8,128)S(1)} %get-tuple-element.49, f32[64,8,256]{2,1,0:T(8,128)} %get-tuple-element.56, f32[2]{0:T(128)S(1)} %get-tuple-element.6, ...), kind=kLoop, calls=%fused_computation.40 | loop fusion | flops 27787264 | bytes 16777232 | tf_op jit(solution)/shard_map/add | solution.py:117
  109.2 2.1 %collective-permute-start.12 = (f32[2,64,1,256]{3,2,1,0:T(1,128)}, f32[2,64,1,256]{3,2,1,0:T(1,128)S(1)}, u32[]{:S(2)}, u32[]{:S(2)}) collective-permute-start(f32[2,64,1,256]{3,2,1,0:T(1,128)} %get-tuple-element.42), channel_id=1, source_target_pairs={{1,0},{2,1},{3,2},{4,3},{5,4},{6,5},{7,6},{8,7},{9,8},{10,9},{11,1... | collective-permute-start | bytes 393224 | tf_op jit(solution)/shard_map/ppermute | solution.py:20
  111.3 3.4 %collective-permute-start.13 = (f32[2,64,1,256]{3,2,1,0:T(1,128)}, f32[2,64,1,256]{3,2,1,0:T(1,128)S(1)}, u32[]{:S(2)}, u32[]{:S(2)}) collective-permute-start(f32[2,64,1,256]{3,2,1,0:T(1,128)} %get-tuple-element.43), channel_id=1, source_target_pairs={{0,1},{1,2},{2,3},{3,4},{4,5},{5,6},{6,7},{7,8},{8,9},{9,10},{10,1... | collective-permute-start | bytes 393224 | tf_op jit(solution)/shard_map/ppermute | solution.py:19
  118.3 2.8 %multiply_add_fusion = (f32[2,64,8,256]{3,2,1,0:T(8,128)S(1)}, f32[2,64,8,256]{3,2,1,0:T(8,128)S(1)}) fusion(f32[2,64,8,256]{3,2,1,0:T(8,128)S(1)} %copy-done.27, f32[2,64,8,256]{3,2,1,0:T(8,128)S(1)} %copy-done.26, f32[2,64,8,256]{3,2,1,0:T(8,128)S(1)} %copy-done.10, f32[2,64,8,256]{3,2,1,0:T(8,128)S(1)} %copy-done.25, f32[64,8,256]{2,1,0:T(8,128)} %get-tuple-element.45, ...), kind=kLoop, calls=%fused_computation.38 | loop fusion | flops 8912896 | bytes 9699344 | tf_op jit(solution)/shard_map/add | solution.py:124
  121.4 4.5 %collective-permute-start.14 = (f32[2,64,1,256]{3,2,1,0:T(1,128)S(1)}, f32[2,64,1,256]{3,2,1,0:T(1,128)S(1)}, u32[]{:S(2)}, u32[]{:S(2)}) collective-permute-start(f32[2,64,1,256]{3,2,1,0:T(1,128)S(1)} %get-tuple-element.40), channel_id=1, source_target_pairs={{1,0},{2,1},{3,2},{4,3},{5,4},{6,5},{7,6},{8,7},{9,8},{10,9},{11,1... | collective-permute-start | bytes 393224 | tf_op jit(solution)/shard_map/ppermute | solution.py:20
  125.9 2.3 %collective-permute-start.15 = (f32[2,64,1,256]{3,2,1,0:T(1,128)S(1)}, f32[2,64,1,256]{3,2,1,0:T(1,128)S(1)}, u32[]{:S(2)}, u32[]{:S(2)}) collective-permute-start(f32[2,64,1,256]{3,2,1,0:T(1,128)S(1)} %get-tuple-element.41), channel_id=1, source_target_pairs={{0,1},{1,2},{2,3},{3,4},{4,5},{5,6},{6,7},{7,8},{8,9},{9,10},{10,1... | collective-permute-start | bytes 393224 | tf_op jit(solution)/shard_map/ppermute | solution.py:19
  128.3 2.5 %collective-permute-done.15 = f32[2,64,1,256]{3,2,1,0:T(1,128)S(1)} collective-permute-done((f32[2,64,1,256]{3,2,1,0:T(1,128)S(1)}, f32[2,64,1,256]{3,2,1,0:T(1,128)S(1)}, u32[]{:S(2)}, u32[]{:S(2)}) %collective-permute-start.15) | collective-permute-done | bytes 131104 | tf_op jit(solution)/shard_map/ppermute | solution.py:19
  139.6 14.4 %collective-permute-done.18 = f32[2,32,1,256]{3,2,1,0:T(1,128)S(1)} collective-permute-done((f32[2,32,1,256]{3,2,1,0:T(1,128)S(1)}, f32[2,32,1,256]{3,2,1,0:T(1,128)S(1)}, u32[]{:S(2)}, u32[]{:S(2)}) %collective-permute-start.18) | collective-permute-done | bytes 65568 | tf_op jit(solution)/shard_map/ppermute | solution.py:225
  (253 shorter events, 63.3 us)
Async XLA Ops:
  2.5 22.2 %collective-permute-start = (f32[2,64,1,256]{3,2,1,0:T(1,128)}, f32[2,64,1,256]{3,2,1,0:T(1,128)}, u32[]{:S(2)}, u32[]{:S(2)}) collective-permute-start(f32[2,64,1,256]{3,2,1,0:T(1,128)} %get-tuple-element.65), channel_id=1, source_target_pairs={{1,0},{2,1},{3,2},{4,3},{5,4},{6,5},{7,6},{8,7},{9,8},{10,9},{11,1... | collective-permute-start | bytes 393224 | tf_op jit(solution)/shard_map/ppermute | solution.py:20
  5.1 19.7 %collective-permute-start.1 = (f32[2,64,1,256]{3,2,1,0:T(1,128)}, f32[2,64,1,256]{3,2,1,0:T(1,128)}, u32[]{:S(2)}, u32[]{:S(2)}) collective-permute-start(f32[2,64,1,256]{3,2,1,0:T(1,128)} %get-tuple-element.66), channel_id=1, source_target_pairs={{0,1},{1,2},{2,3},{3,4},{4,5},{5,6},{6,7},{7,8},{8,9},{9,10},{10,1... | collective-permute-start | bytes 393224 | tf_op jit(solution)/shard_map/ppermute | solution.py:19
  8.2 14.7 %copy-start.53 = (s32[8]{0:T(128)}, s32[8]{0:T(128)S(1)}, u32[]{:S(2)}) copy-start(s32[8]{0:T(128)S(1)} %iota_and_fusion) | copy-start | bytes 100
  12.6 40.8 %collective-permute-start.4 = (f32[2,32,1,256]{3,2,1,0:T(1,128)}, f32[2,32,1,256]{3,2,1,0:T(1,128)S(1)}, u32[]{:S(2)}, u32[]{:S(2)}) collective-permute-start(f32[2,32,1,256]{3,2,1,0:T(1,128)} %get-tuple-element.97), channel_id=1, source_target_pairs={{1,0},{2,1},{3,2},{4,3},{5,4},{6,5},{7,6},{8,7},{9,8},{10,9},{11,1... | collective-permute-start | bytes 196616 | tf_op jit(solution)/shard_map/ppermute | solution.py:20
  14.5 38.8 %collective-permute-start.5 = (f32[2,32,1,256]{3,2,1,0:T(1,128)}, f32[2,32,1,256]{3,2,1,0:T(1,128)S(1)}, u32[]{:S(2)}, u32[]{:S(2)}) collective-permute-start(f32[2,32,1,256]{3,2,1,0:T(1,128)} %get-tuple-element.98), channel_id=1, source_target_pairs={{0,1},{1,2},{2,3},{3,4},{4,5},{5,6},{6,7},{7,8},{8,9},{9,10},{10,1... | collective-permute-start | bytes 196616 | tf_op jit(solution)/shard_map/ppermute | solution.py:19
  27.7 6.3 %collective-permute-start.2 = (f32[2,64,1,256]{3,2,1,0:T(1,128)S(1)}, f32[2,64,1,256]{3,2,1,0:T(1,128)S(1)}, u32[]{:S(2)}, u32[]{:S(2)}) collective-permute-start(f32[2,64,1,256]{3,2,1,0:T(1,128)S(1)} %get-tuple-element.61), channel_id=1, source_target_pairs={{1,0},{2,1},{3,2},{4,3},{5,4},{6,5},{7,6},{8,7},{9,8},{10,9},{11,1... | collective-permute-start | bytes 393224 | tf_op jit(solution)/shard_map/ppermute | solution.py:20
  30.2 6.3 %collective-permute-start.3 = (f32[2,64,1,256]{3,2,1,0:T(1,128)S(1)}, f32[2,64,1,256]{3,2,1,0:T(1,128)S(1)}, u32[]{:S(2)}, u32[]{:S(2)}) collective-permute-start(f32[2,64,1,256]{3,2,1,0:T(1,128)S(1)} %get-tuple-element.62), channel_id=1, source_target_pairs={{0,1},{1,2},{2,3},{3,4},{4,5},{5,6},{6,7},{7,8},{8,9},{9,10},{10,1... | collective-permute-start | bytes 393224 | tf_op jit(solution)/shard_map/ppermute | solution.py:19
  38.6 8.4 %collective-permute-start.6 = (f32[2,64,2,256]{3,2,1,0:T(2,128)S(1)}, f32[2,64,2,256]{3,2,1,0:T(2,128)S(1)}, u32[]{:S(2)}, u32[]{:S(2)}) collective-permute-start(f32[2,64,2,256]{3,2,1,0:T(2,128)S(1)} %get-tuple-element.59), channel_id=1, source_target_pairs={{1,0},{2,1},{3,2},{4,3},{5,4},{6,5},{7,6},{8,7},{9,8},{10,9},{11,1... | collective-permute-start | bytes 786440 | tf_op jit(solution)/shard_map/ppermute | solution.py:20
  44.0 7.3 %collective-permute-start.7 = (f32[2,64,2,256]{3,2,1,0:T(2,128)S(1)}, f32[2,64,2,256]{3,2,1,0:T(2,128)S(1)}, u32[]{:S(2)}, u32[]{:S(2)}) collective-permute-start(f32[2,64,2,256]{3,2,1,0:T(2,128)S(1)} %get-tuple-element.60), channel_id=1, source_target_pairs={{0,1},{1,2},{2,3},{3,4},{4,5},{5,6},{6,7},{7,8},{8,9},{9,10},{10,1... | collective-permute-start | bytes 786440 | tf_op jit(solution)/shard_map/ppermute | solution.py:19
  47.0 16.2 %copy-start.31 = (f32[2,64,2,256]{3,2,1,0:T(2,128)}, f32[2,64,2,256]{3,2,1,0:T(2,128)S(1)}, u32[]{:S(2)}) copy-start(f32[2,64,2,256]{3,2,1,0:T(2,128)S(1)} %collective-permute-done.6) | copy-start | bytes 786436
  53.4 28.3 %copy-start.36 = (f32[2,32,1,256]{3,2,1,0:T(1,128)}, f32[2,32,1,256]{3,2,1,0:T(1,128)S(1)}, u32[]{:S(2)}) copy-start(f32[2,32,1,256]{3,2,1,0:T(1,128)S(1)} %collective-permute-done.4) | copy-start | bytes 196612
  56.9 7.4 %collective-permute-start.8 = (f32[2,32,1,256]{3,2,1,0:T(1,128)S(1)}, f32[2,32,1,256]{3,2,1,0:T(1,128)S(1)}, u32[]{:S(2)}, u32[]{:S(2)}) collective-permute-start(f32[2,32,1,256]{3,2,1,0:T(1,128)S(1)} %get-tuple-element.93), channel_id=1, source_target_pairs={{1,0},{2,1},{3,2},{4,3},{5,4},{6,5},{7,6},{8,7},{9,8},{10,9},{11,1... | collective-permute-start | bytes 196616 | tf_op jit(solution)/shard_map/ppermute | solution.py:20
  60.1 4.4 %collective-permute-start.9 = (f32[2,32,1,256]{3,2,1,0:T(1,128)S(1)}, f32[2,32,1,256]{3,2,1,0:T(1,128)S(1)}, u32[]{:S(2)}, u32[]{:S(2)}) collective-permute-start(f32[2,32,1,256]{3,2,1,0:T(1,128)S(1)} %get-tuple-element.94), channel_id=1, source_target_pairs={{0,1},{1,2},{2,3},{3,4},{4,5},{5,6},{6,7},{7,8},{8,9},{9,10},{10,1... | collective-permute-start | bytes 196616 | tf_op jit(solution)/shard_map/ppermute | solution.py:19
  68.8 12.9 %collective-permute-start.10 = (f32[2,32,1,256]{3,2,1,0:T(1,128)S(1)}, f32[2,32,1,256]{3,2,1,0:T(1,128)S(1)}, u32[]{:S(2)}, u32[]{:S(2)}) collective-permute-start(f32[2,32,1,256]{3,2,1,0:T(1,128)S(1)} %get-tuple-element.87), channel_id=1, source_target_pairs={{1,0},{2,1},{3,2},{4,3},{5,4},{6,5},{7,6},{8,7},{9,8},{10,9},{11,1... | collective-permute-start | bytes 196616 | tf_op jit(solution)/shard_map/ppermute | solution.py:20
  72.8 12.0 %collective-permute-start.11 = (f32[2,32,1,256]{3,2,1,0:T(1,128)}, f32[2,32,1,256]{3,2,1,0:T(1,128)S(1)}, u32[]{:S(2)}, u32[]{:S(2)}) collective-permute-start(f32[2,32,1,256]{3,2,1,0:T(1,128)} %get-tuple-element.88), channel_id=1, source_target_pairs={{0,1},{1,2},{2,3},{3,4},{4,5},{5,6},{6,7},{7,8},{8,9},{9,10},{10,1... | collective-permute-start | bytes 196616 | tf_op jit(solution)/shard_map/ppermute | solution.py:19
  109.2 8.8 %collective-permute-start.12 = (f32[2,64,1,256]{3,2,1,0:T(1,128)}, f32[2,64,1,256]{3,2,1,0:T(1,128)S(1)}, u32[]{:S(2)}, u32[]{:S(2)}) collective-permute-start(f32[2,64,1,256]{3,2,1,0:T(1,128)} %get-tuple-element.42), channel_id=1, source_target_pairs={{1,0},{2,1},{3,2},{4,3},{5,4},{6,5},{7,6},{8,7},{9,8},{10,9},{11,1... | collective-permute-start | bytes 393224 | tf_op jit(solution)/shard_map/ppermute | solution.py:20
  111.3 7.0 %collective-permute-start.13 = (f32[2,64,1,256]{3,2,1,0:T(1,128)}, f32[2,64,1,256]{3,2,1,0:T(1,128)S(1)}, u32[]{:S(2)}, u32[]{:S(2)}) collective-permute-start(f32[2,64,1,256]{3,2,1,0:T(1,128)} %get-tuple-element.43), channel_id=1, source_target_pairs={{0,1},{1,2},{2,3},{3,4},{4,5},{5,6},{6,7},{7,8},{8,9},{9,10},{10,1... | collective-permute-start | bytes 393224 | tf_op jit(solution)/shard_map/ppermute | solution.py:19
  121.4 6.9 %collective-permute-start.14 = (f32[2,64,1,256]{3,2,1,0:T(1,128)S(1)}, f32[2,64,1,256]{3,2,1,0:T(1,128)S(1)}, u32[]{:S(2)}, u32[]{:S(2)}) collective-permute-start(f32[2,64,1,256]{3,2,1,0:T(1,128)S(1)} %get-tuple-element.40), channel_id=1, source_target_pairs={{1,0},{2,1},{3,2},{4,3},{5,4},{6,5},{7,6},{8,7},{9,8},{10,9},{11,1... | collective-permute-start | bytes 393224 | tf_op jit(solution)/shard_map/ppermute | solution.py:20
  125.9 4.9 %collective-permute-start.15 = (f32[2,64,1,256]{3,2,1,0:T(1,128)S(1)}, f32[2,64,1,256]{3,2,1,0:T(1,128)S(1)}, u32[]{:S(2)}, u32[]{:S(2)}) collective-permute-start(f32[2,64,1,256]{3,2,1,0:T(1,128)S(1)} %get-tuple-element.41), channel_id=1, source_target_pairs={{0,1},{1,2},{2,3},{3,4},{4,5},{5,6},{6,7},{7,8},{8,9},{9,10},{10,1... | collective-permute-start | bytes 393224 | tf_op jit(solution)/shard_map/ppermute | solution.py:19
  134.3 19.7 %copy-start.40 = (f32[2,32,1,256]{3,2,1,0:T(1,128)S(1)}, f32[2,32,1,256]{3,2,1,0:T(1,128)}, u32[]{:S(2)}) copy-start(f32[2,32,1,256]{3,2,1,0:T(1,128)} %copy-done.38) | copy-start | bytes 196612
  134.3 21.2 %copy-start.37 = (f32[2,32,1,256]{3,2,1,0:T(1,128)S(1)}, f32[2,32,1,256]{3,2,1,0:T(1,128)}, u32[]{:S(2)}) copy-start(f32[2,32,1,256]{3,2,1,0:T(1,128)} %copy-done.36) | copy-start | bytes 196612
  135.6 19.9 %collective-permute-start.16 = (f32[2,32,8,256]{3,2,1,0:T(8,128)S(1)}, f32[2,32,8,256]{3,2,1,0:T(8,128)S(1)}, u32[]{:S(2)}, u32[]{:S(2)}) collective-permute-start(f32[2,32,8,256]{3,2,1,0:T(8,128)S(1)} %get-tuple-element.7), channel_id=1, source_target_pairs={{0,16},{1,17},{2,18},{3,19},{4,20},{5,21},{6,22},{7,23},{8,24},{9,... | collective-permute-start | bytes 1572872 | tf_op jit(solution)/shard_map/ppermute | solution.py:224
  136.9 17.1 %collective-permute-start.18 = (f32[2,32,1,256]{3,2,1,0:T(1,128)S(1)}, f32[2,32,1,256]{3,2,1,0:T(1,128)S(1)}, u32[]{:S(2)}, u32[]{:S(2)}) collective-permute-start(f32[2,32,1,256]{3,2,1,0:T(1,128)S(1)} %get-tuple-element.71), channel_id=1, source_target_pairs={{0,17},{1,18},{2,19},{3,20},{4,21},{5,22},{6,23},{7,24},{8,25},{9,... | collective-permute-start | bytes 196616 | tf_op jit(solution)/shard_map/ppermute | solution.py:225
  138.3 17.2 %collective-permute-start.17 = (f32[2,32,1,256]{3,2,1,0:T(1,128)S(1)}, f32[2,32,1,256]{3,2,1,0:T(1,128)S(1)}, u32[]{:S(2)}, u32[]{:S(2)}) collective-permute-start(f32[2,32,1,256]{3,2,1,0:T(1,128)S(1)} %get-tuple-element.72), channel_id=1, source_target_pairs={{1,16},{2,17},{3,18},{4,19},{5,20},{6,21},{7,22},{8,23},{9,24},{10... | collective-permute-start | bytes 196616 | tf_op jit(solution)/shard_map/ppermute | solution.py:226
  (51 other events, 155.0 us)
where the time goes:
time: 159 us; the launch traced here: 158 us
  starting transfers between devices  53.1 us (33%)
  other arithmetic  44.5 us (28%)
  local copies, waits for them, and re-layouts  31.9 us (20%)
  waiting for transfers between devices  27.3 us (17%)
    ppermute x8, starting transfers between devices, exchange(): after = lax.ppermute(to_left, 'space', shift_pairs(count, -1))  26.2 us
    ppermute x8, starting transfers between devices, exchange(): before = lax.ppermute(to_right, 'space', shift_pairs(count, 1))  23 us
    add x2, other arithmetic, first_node(): node_zero + half_step * (rate_zero - s0)  14.6 us
    ppermute x1, waiting for transfers between devices, body(): passed_b = lax.ppermute(hi(after), ('tm', 'space'), to_east)  14.4 us
    ppermute x8, waiting for transfers between devices, exchange(): before = lax.ppermute(to_right, 'space', shift_pairs(count, 1))  9.79 us
    mul x13, local copies, waits for them, and re-layouts, tendency(): reaction = coupling[:, 0].reshape(-1, 1, 1, 1) * middle[..., 0:1, :, :, :]  8.53 us
    unnamed x120, local copies, waits for them, and re-layouts  6.36 us
    broadcast_in_dim x16, local copies, waits for them, and re-layouts, expand_z(): return jnp.repeat(field, 2, axis=-3)  5.83 us
  transfers between devices with their start and end apart: 19, of which 9 were waited for; matrix products, arithmetic and copies ran while one was open for 18% of the time, Pallas kernels for 0%

commit v1 on v0

--- a/solution.py
+++ b/solution.py
@@ -1,6 +1,10 @@
+import functools
+
 import jax
 import jax.numpy as jnp
 from jax import lax
+from jax.experimental import pallas as pl
+from jax.experimental.pallas import tpu as pltpu
 from jax.sharding import PartitionSpec as P
 
 ITERS = 2
@@ -62,6 +66,57 @@
     return diffusion + vertical - advection + reaction
 
 
+def _tendency_kernel(k_ref, f_ref, hb_ref, ha_ref, a_ref, b_ref, kh_ref, kv_ref, o_ref, *, reach, spacing):
+    levels, width, lanes = f_ref.shape[1], f_ref.shape[2], f_ref.shape[3]
+    row = lax.broadcasted_iota(jnp.int32, (width, lanes), 0)
+    col = lax.broadcasted_iota(jnp.int32, (width, lanes), 1)
+    east_edge = row >= width - reach
+    west_edge = row < reach
+    north_edge = col == lanes - 1
+    south_edge = col == 0
+    half_inv = 1.0 / (2.0 * spacing)
+    square_inv = 1.0 / (spacing * spacing)
+    rates = [[k_ref[t, d] for d in range(2)] for t in range(2)]
+
+    def level(z, carry):
+        above = jnp.minimum(z + 1, levels - 1)
+        below = jnp.maximum(z - 1, 0)
+        has_above = z + 1 < levels
+        has_below = z > 0
+        a = a_ref[z]
+        b = b_ref[z]
+        kh = kh_ref[z]
+        kv = kv_ref[z]
+        cs = [f_ref[t, z] for t in range(2)]
+        for t in range(2):
+            c = cs[t]
+            up = jnp.where(has_above, f_ref[t, above], 0.0)
+            down = jnp.where(has_below, f_ref[t, below], 0.0)
+            east = jnp.where(east_edge, ha_ref[t, z], pltpu.roll(c, width - reach, 0))
+            west = jnp.where(west_edge, hb_ref[t, z], pltpu.roll(c, reach, 0))
+            north = jnp.where(north_edge, 0.0, pltpu.roll(c, lanes - 1, 1))
+            south = jnp.where(south_edge, 0.0, pltpu.roll(c, 1, 1))
+            advection = a * (east - west) * half_inv + b * (north - south) * 0.5
+            diffusion = kh * ((east - 2.0 * c + west) * square_inv + (north - 2.0 * c + south))
+            vertical = kv * (up - 2.0 * c + down) * square_inv
+            reaction = rates[t][0] * cs[0] + rates[t][1] * cs[1]
+            o_ref[t, z] = diffusion + vertical - advection + reaction
+        return carry
+
+    lax.fori_loop(0, levels, level, 0)
+
+
+def tendency_kernel(field, halo, a, b, kh, kv, coupling, spacing):
+    reach = int(spacing)
+    vmem = pl.BlockSpec(memory_space=pltpu.VMEM)
+    return pl.pallas_call(
+        functools.partial(_tendency_kernel, reach=reach, spacing=float(spacing)),
+        out_shape=jax.ShapeDtypeStruct(field.shape, field.dtype),
+        in_specs=[pl.BlockSpec(memory_space=pltpu.SMEM)] + [vmem] * 7,
+        out_specs=vmem,
+    )(coupling, field, halo[0], halo[1], a, b, kh, kv)
+
+
 def pair_sum(field):
     row = lax.broadcasted_iota(jnp.int32, field.shape, field.ndim - 2)
     partner = jnp.where(
@@ -105,12 +160,12 @@
     first = slab == 0
 
     def fine_rate(field, halo):
-        return tendency(
-            field, halo, x_velocity, y_velocity, h_diffusion, v_diffusion, coupling, 1.0, 1.0
+        return tendency_kernel(
+            field, halo, x_velocity, y_velocity, h_diffusion, v_diffusion, coupling, 1.0
         )
 
     def coarse_rate(field, halo):
-        return tendency(field, halo, coarse_x, coarse_y, coarse_h, coarse_v, coupling, 2.0, 2.0)
+        return tendency_kernel(field, halo, coarse_x, coarse_y, coarse_h, coarse_v, coupling, 2.0)
 
     def first_node(node_zero, rate_zero, s0, s1, s2):
         return (

time: 159 us -> 238 us (1.50)
  Pallas kernels: 0 us -> 95.2 us
  other arithmetic: 44.5 us -> 37 us
  waiting for transfers between devices: 27.3 us -> 23.2 us
  local copies, waits for them, and re-layouts: 31.9 us -> 27.9 us
    pallas_call x0 -> x13, Pallas kernels: none -> 95.2 us  [tendency_kernel(): pl.pallas_call(functools.partial(_tendency_kernel, reach=reach, spacing=f...]
    ppermute x1, waiting for transfers between devices: 1.56 us -> 16.2 us  [body(): passed_a = lax.ppermute(lo(after), ('tm', 'space'), to_west)]
    ppermute x1, waiting for transfers between devices: 14.4 us -> 0.01 us  [body(): passed_b = lax.ppermute(hi(after), ('tm', 'space'), to_east)]
    add x2, other arithmetic: 14.6 us -> 4.12 us  [first_node(): node_zero + half_step * (rate_zero - s0)]
    unnamed x120, local copies, waits for them, and re-layouts: 6.36 us -> 15.5 us
    mul x13 -> x0, local copies, waits for them, and re-layouts: 8.53 us -> none  [tendency(): reaction = coupling[:, 0].reshape(-1, 1, 1, 1) * middle[..., 0:1, :, :, :]]
    add x3 -> x0, other arithmetic: 5.02 us -> none  [the longest x2 4.68 us: body(): halo_f2 = pair_map(lambda w, d: w + expand_z(d), halo_two, halo_d1)]
    broadcast_in_dim x16, local copies, waits for them, and re-layouts: 5.83 us -> 1.95 us  [expand_z(): return jnp.repeat(field, 2, axis=-3)]
  transfers between devices with their start and end apart: 19 -> 19, of which waited for: 9 -> 5; matrix products, arithmetic and copies ran while one was open for 18% -> 7% of each run, Pallas kernels for 0% -> 8%
where the time goes in v1:
time: 238 us; the launch traced here: 236 us
  Pallas kernels  95.2 us (40%)
  starting transfers between devices  51.7 us (22%)
  other arithmetic  37 us (16%)
  local copies, waits for them, and re-layouts  27.9 us (12%)
  waiting for transfers between devices  23.2 us (10%)
    pallas_call x13, Pallas kernels, tendency_kernel(): pl.pallas_call(functools.partial(_tendency_kernel, reach=reach, spacing=f...  95.2 us
    ppermute x8, starting transfers between devices, exchange(): after = lax.ppermute(to_left, 'space', shift_pairs(count, -1))  26.5 us
    ppermute x8, starting transfers between devices, exchange(): before = lax.ppermute(to_right, 'space', shift_pairs(count, 1))  21.3 us
    ppermute x1, waiting for transfers between devices, body(): passed_a = lax.ppermute(lo(after), ('tm', 'space'), to_west)  16.2 us
    unnamed x120, local copies, waits for them, and re-layouts  15.5 us
    ppermute x8, waiting for transfers between devices, exchange(): before = lax.ppermute(to_right, 'space', shift_pairs(count, 1))  5.96 us
  transfers between devices with their start and end apart: 19, of which 5 were waited for; matrix products, arithmetic and copies ran while one was open for 7% of the time, Pallas kernels for 8%

profile of v1, /device:TPU:11, one launch (start us, length us, event | category | flops | bytes accessed | tf_op | source)
XLA Modules:
  0.0 236.2 jit_solution(5552465123848962562)
XLA Ops:
  4.3 3.0 %collective-permute-start = (f32[2,64,1,256]{3,2,1,0:T(1,128)S(1)}, f32[2,64,1,256]{3,2,1,0:T(1,128)S(1)}, u32[]{:S(2)}, u32[]{:S(2)}) collective-permute-start(f32[2,64,1,256]{3,2,1,0:T(1,128)S(1)} %get-tuple-element.32), channel_id=1, source_target_pairs={{0,1},{1,2},{2,3},{3,4},{4,5},{5,6},{6,7},{7,8},{8,9},{9,10},{10,1... | collective-permute-start | bytes 393224 | tf_op jit(solution)/shard_map/ppermute | solution.py:23
  12.3 3.6 %collective-permute-start.4 = (f32[2,32,1,256]{3,2,1,0:T(1,128)S(1)}, f32[2,32,1,256]{3,2,1,0:T(1,128)S(1)}, u32[]{:S(2)}, u32[]{:S(2)}) collective-permute-start(f32[2,32,1,256]{3,2,1,0:T(1,128)S(1)} %get-tuple-element.60), channel_id=1, source_target_pairs={{0,1},{1,2},{2,3},{3,4},{4,5},{5,6},{6,7},{7,8},{8,9},{9,10},{10,1... | collective-permute-start | bytes 196616 | tf_op jit(solution)/shard_map/ppermute | solution.py:23
  21.2 8.3 %shard_map.64 = f32[2,64,8,256]{3,2,1,0:T(8,128)} custom-call(f32[2,2]{1,0:T(2,128)} %k_ref.25, f32[2,64,8,256]{3,2,1,0:T(8,128)} %f_ref.1, f32[2,64,1,256]{3,2,1,0:T(1,128)} %copy-done.46, f32[2,64,1,256]{3,2,1,0:T(1,128)} %copy-done.44, f32[64,8,256]{2,1,0:T(8,128)} %a_ref.17, f32[64,8,256]{2,1,0:T(8,128)} %b_ref.17, f32[64,8,256]{2,1,0:T(8,128)} %kh_ref.17, ...), custom_call_target="tpu_custom_call" | custom-call | tf_op jit(solution)/shard_map/pallas_call | solution.py:112
  34.0 3.0 %collective-permute-start.2 = (f32[2,64,1,256]{3,2,1,0:T(1,128)S(1)}, f32[2,64,1,256]{3,2,1,0:T(1,128)S(1)}, u32[]{:S(2)}, u32[]{:S(2)}) collective-permute-start(f32[2,64,1,256]{3,2,1,0:T(1,128)S(1)} %get-tuple-element.30), channel_id=1, source_target_pairs={{0,1},{1,2},{2,3},{3,4},{4,5},{5,6},{6,7},{7,8},{8,9},{9,10},{10,1... | collective-permute-start | bytes 393224 | tf_op jit(solution)/shard_map/ppermute | solution.py:23
  38.5 4.9 %shard_map.66 = f32[2,32,8,256]{3,2,1,0:T(8,128)} custom-call(f32[2,2]{1,0:T(2,128)} %k_ref.25, f32[2,32,8,256]{3,2,1,0:T(8,128)} %copy-done.11, f32[2,32,1,256]{3,2,1,0:T(1,128)} %copy-done.36, f32[2,32,1,256]{3,2,1,0:T(1,128)} %copy-done.38, f32[32,8,256]{2,1,0:T(8,128)} %get-tuple-element.98.a_ref, f32[32,8,256]{2,1,0:T(8,128)} %fusion.18.b_ref, ...), custom_call_target="tpu_custom_call" | custom-call | tf_op jit(solution)/shard_map/pallas_call | solution.py:112
  44.8 8.4 %shard_map.65 = f32[2,64,8,256]{3,2,1,0:T(8,128)} custom-call(f32[2,2]{1,0:T(2,128)} %k_ref.25, f32[2,64,8,256]{3,2,1,0:T(8,128)} %copy-done.15, f32[2,64,1,256]{3,2,1,0:T(1,128)} %copy-done.42, f32[2,64,1,256]{3,2,1,0:T(1,128)} %copy-done.40, f32[64,8,256]{2,1,0:T(8,128)} %a_ref.17, f32[64,8,256]{2,1,0:T(8,128)} %b_ref.17, f32[64,8,256]{2,1,0:T(8,128)} %kh_ref.17, ...), custom_call_target="tpu_custom_call" | custom-call | tf_op jit(solution)/shard_map/pallas_call | solution.py:112
  56.1 3.4 %collective-permute-start.7 = (f32[2,64,2,256]{3,2,1,0:T(2,128)S(1)}, f32[2,64,2,256]{3,2,1,0:T(2,128)S(1)}, u32[]{:S(2)}, u32[]{:S(2)}) collective-permute-start(f32[2,64,2,256]{3,2,1,0:T(2,128)S(1)} %get-tuple-element.27), channel_id=1, source_target_pairs={{1,0},{2,1},{3,2},{4,3},{5,4},{6,5},{7,6},{8,7},{9,8},{10,9},{11,1... | collective-permute-start | bytes 786440 | tf_op jit(solution)/shard_map/ppermute | solution.py:24
  64.5 3.3 %collective-permute-done.6 = f32[2,64,2,256]{3,2,1,0:T(2,128)S(1)} collective-permute-done((f32[2,64,2,256]{3,2,1,0:T(2,128)S(1)}, f32[2,64,2,256]{3,2,1,0:T(2,128)S(1)}, u32[]{:S(2)}, u32[]{:S(2)}) %collective-permute-start.6) | collective-permute-done | bytes 262176 | tf_op jit(solution)/shard_map/ppermute | solution.py:23
  69.3 8.4 %shard_map.67 = f32[2,64,8,256]{3,2,1,0:T(8,128)} custom-call(f32[2,2]{1,0:T(2,128)} %k_ref.25, f32[2,64,8,256]{3,2,1,0:T(8,128)} %copy-done.5, f32[2,64,1,256]{3,2,1,0:T(1,128)} %slice.445.hb_ref, f32[2,64,1,256]{3,2,1,0:T(1,128)} %slice.447.ha_ref, f32[64,8,256]{2,1,0:T(8,128)} %a_ref.17, f32[64,8,256]{2,1,0:T(8,128)} %b_ref.17, f32[64,8,256]{2,1,0:T(8,128)} %kh_ref.17, ...), custom_call_target="tpu_custom_call" | custom-call | tf_op jit(solution)/shard_map/pallas_call | solution.py:112
  82.2 5.0 %collective-permute-start.9 = (f32[2,32,1,256]{3,2,1,0:T(1,128)S(1)}, f32[2,32,1,256]{3,2,1,0:T(1,128)}, u32[]{:S(2)}, u32[]{:S(2)}) collective-permute-start(f32[2,32,1,256]{3,2,1,0:T(1,128)S(1)} %get-tuple-element.53), channel_id=1, source_target_pairs={{1,0},{2,1},{3,2},{4,3},{5,4},{6,5},{7,6},{8,7},{9,8},{10,9},{11,1... | collective-permute-start | bytes 196616 | tf_op jit(solution)/shard_map/ppermute | solution.py:24
  90.5 4.9 %shard_map.68 = f32[2,32,8,256]{3,2,1,0:T(8,128)} custom-call(f32[2,2]{1,0:T(2,128)} %k_ref.25, f32[2,32,8,256]{3,2,1,0:T(8,128)} %copy-done.21, f32[2,32,1,256]{3,2,1,0:T(1,128)} %collective-permute-done.8.hb_ref, f32[2,32,1,256]{3,2,1,0:T(1,128)} %collective-permute-done.9.ha_ref, f32[32,8,256]{2,1,0:T(8,128)} %get-tuple-element.98.a_ref, ...), custom_call_target="tpu_custom_call" | custom-call | tf_op jit(solution)/shard_map/pallas_call | solution.py:112
  100.6 5.2 %collective-permute-start.11 = (f32[2,32,1,256]{3,2,1,0:T(1,128)}, f32[2,32,1,256]{3,2,1,0:T(1,128)S(1)}, u32[]{:S(2)}, u32[]{:S(2)}) collective-permute-start(f32[2,32,1,256]{3,2,1,0:T(1,128)} %get-tuple-element.47), channel_id=1, source_target_pairs={{1,0},{2,1},{3,2},{4,3},{5,4},{6,5},{7,6},{8,7},{9,8},{10,9},{11,1... | collective-permute-start | bytes 196616 | tf_op jit(solution)/shard_map/ppermute | solution.py:24
  121.3 8.4 %shard_map.69 = f32[2,64,8,256]{3,2,1,0:T(8,128)} custom-call(f32[2,2]{1,0:T(2,128)} %k_ref.25, f32[2,64,8,256]{3,2,1,0:T(8,128)} %copy-done.13, f32[2,64,1,256]{3,2,1,0:T(1,128)} %get-tuple-element.69.hb_ref, f32[2,64,1,256]{3,2,1,0:T(1,128)} %get-tuple-element.67.ha_ref, f32[64,8,256]{2,1,0:T(8,128)} %a_ref.17, f32[64,8,256]{2,1,0:T(8,128)} %b_ref.17, ...), custom_call_target="tpu_custom_call" | custom-call | tf_op jit(solution)/shard_map/pallas_call | solution.py:112
  131.4 8.4 %shard_map.71 = f32[2,64,8,256]{3,2,1,0:T(8,128)} custom-call(f32[2,2]{1,0:T(2,128)} %k_ref.25, f32[2,64,8,256]{3,2,1,0:T(8,128)} %add.330.f_ref, f32[2,64,1,256]{3,2,1,0:T(1,128)} %add.332.hb_ref, f32[2,64,1,256]{3,2,1,0:T(1,128)} %add.334.ha_ref, f32[64,8,256]{2,1,0:T(8,128)} %a_ref.17, f32[64,8,256]{2,1,0:T(8,128)} %b_ref.17, f32[64,8,256]{2,1,0:T(8,128)} %kh_ref.17, ...), custom_call_target="tpu_custom_call" | custom-call | tf_op jit(solution)/shard_map/pallas_call | solution.py:112
  139.7 8.4 %shard_map.72 = f32[2,64,8,256]{3,2,1,0:T(8,128)} custom-call(f32[2,2]{1,0:T(2,128)} %k_ref.25, f32[2,64,8,256]{3,2,1,0:T(8,128)} %get-tuple-element.25.f_ref, f32[2,64,1,256]{3,2,1,0:T(1,128)} %get-tuple-element.70.hb_ref, f32[2,64,1,256]{3,2,1,0:T(1,128)} %get-tuple-element.68.ha_ref, f32[64,8,256]{2,1,0:T(8,128)} %a_ref.17, f32[64,8,256]{2,1,0:T(8,128)} %b_ref.17, ...), custom_call_target="tpu_custom_call" | custom-call | tf_op jit(solution)/shard_map/pallas_call | solution.py:112
  148.1 8.4 %shard_map.70 = f32[2,64,8,256]{3,2,1,0:T(8,128)} custom-call(f32[2,2]{1,0:T(2,128)} %k_ref.25, f32[2,64,8,256]{3,2,1,0:T(8,128)} %get-tuple-element.26.f_ref, f32[2,64,1,256]{3,2,1,0:T(1,128)} %get-tuple-element.92.hb_ref, f32[2,64,1,256]{3,2,1,0:T(1,128)} %get-tuple-element.91.ha_ref, f32[64,8,256]{2,1,0:T(8,128)} %a_ref.17, f32[64,8,256]{2,1,0:T(8,128)} %b_ref.17, ...), custom_call_target="tpu_custom_call" | custom-call | tf_op jit(solution)/shard_map/pallas_call | solution.py:112
  159.2 2.8 %collective-permute-start.13 = (f32[2,64,1,256]{3,2,1,0:T(1,128)S(1)}, f32[2,64,1,256]{3,2,1,0:T(1,128)S(1)}, u32[]{:S(2)}, u32[]{:S(2)}) collective-permute-start(f32[2,64,1,256]{3,2,1,0:T(1,128)S(1)} %get-tuple-element.22), channel_id=1, source_target_pairs={{1,0},{2,1},{3,2},{4,3},{5,4},{6,5},{7,6},{8,7},{9,8},{10,9},{11,1... | collective-permute-start | bytes 393224 | tf_op jit(solution)/shard_map/ppermute | solution.py:24
  166.4 5.0 %shard_map.75 = f32[2,32,8,256]{3,2,1,0:T(8,128)} custom-call(f32[2,2]{1,0:T(2,128)} %k_ref.25, f32[2,32,8,256]{3,2,1,0:T(8,128)} %fusion.11.f_ref, f32[2,32,1,256]{3,2,1,0:T(1,128)} %broadcast_select_fusion.6.hb_ref, f32[2,32,1,256]{3,2,1,0:T(1,128)} %broadcast_select_fusion.5.ha_ref, f32[32,8,256]{2,1,0:T(8,128)} %get-tuple-element.98.a_ref, ...), custom_call_target="tpu_custom_call" | custom-call | tf_op jit(solution)/shard_map/pallas_call | solution.py:112
  172.6 8.3 %shard_map.73 = f32[2,64,8,256]{3,2,1,0:T(8,128)} custom-call(f32[2,2]{1,0:T(2,128)} %k_ref.25, f32[2,64,8,256]{3,2,1,0:T(8,128)} %copy-done.19, f32[2,64,1,256]{3,2,1,0:T(1,128)} %copy-done.53, f32[2,64,1,256]{3,2,1,0:T(1,128)} %copy-done.52, f32[64,8,256]{2,1,0:T(8,128)} %a_ref.17, f32[64,8,256]{2,1,0:T(8,128)} %b_ref.17, f32[64,8,256]{2,1,0:T(8,128)} %kh_ref.17, ...), custom_call_target="tpu_custom_call" | custom-call | tf_op jit(solution)/shard_map/pallas_call | solution.py:112
  184.2 2.8 %collective-permute-start.15 = (f32[2,64,1,256]{3,2,1,0:T(1,128)S(1)}, f32[2,64,1,256]{3,2,1,0:T(1,128)S(1)}, u32[]{:S(2)}, u32[]{:S(2)}) collective-permute-start(f32[2,64,1,256]{3,2,1,0:T(1,128)S(1)} %get-tuple-element.20), channel_id=1, source_target_pairs={{1,0},{2,1},{3,2},{4,3},{5,4},{6,5},{7,6},{8,7},{9,8},{10,9},{11,1... | collective-permute-start | bytes 393224 | tf_op jit(solution)/shard_map/ppermute | solution.py:24
  187.0 2.7 %collective-permute-start.14 = (f32[2,64,1,256]{3,2,1,0:T(1,128)S(1)}, f32[2,64,1,256]{3,2,1,0:T(1,128)S(1)}, u32[]{:S(2)}, u32[]{:S(2)}) collective-permute-start(f32[2,64,1,256]{3,2,1,0:T(1,128)S(1)} %get-tuple-element.21), channel_id=1, source_target_pairs={{0,1},{1,2},{2,3},{3,4},{4,5},{5,6},{6,7},{7,8},{8,9},{9,10},{10,1... | collective-permute-start | bytes 393224 | tf_op jit(solution)/shard_map/ppermute | solution.py:23
  193.7 8.4 %shard_map.74 = f32[2,64,8,256]{3,2,1,0:T(8,128)} custom-call(f32[2,2]{1,0:T(2,128)} %k_ref.25, f32[2,64,8,256]{3,2,1,0:T(8,128)} %copy-done.9, f32[2,64,1,256]{3,2,1,0:T(1,128)} %copy-done.55, f32[2,64,1,256]{3,2,1,0:T(1,128)} %copy-done.54, f32[64,8,256]{2,1,0:T(8,128)} %a_ref.17, f32[64,8,256]{2,1,0:T(8,128)} %b_ref.17, f32[64,8,256]{2,1,0:T(8,128)} %kh_ref.17, ...), custom_call_target="tpu_custom_call" | custom-call | tf_op jit(solution)/shard_map/pallas_call | solution.py:112
  210.2 16.2 %collective-permute-done.18 = f32[2,32,1,256]{3,2,1,0:T(1,128)S(1)} collective-permute-done((f32[2,32,1,256]{3,2,1,0:T(1,128)S(1)}, f32[2,32,1,256]{3,2,1,0:T(1,128)S(1)}, u32[]{:S(2)}, u32[]{:S(2)}) %collective-permute-start.18) | collective-permute-done | bytes 65568 | tf_op jit(solution)/shard_map/ppermute | solution.py:281
  228.5 5.1 %shard_map.76 = f32[2,32,8,256]{3,2,1,0:T(8,128)} custom-call(f32[2,2]{1,0:T(2,128)} %k_ref.25, f32[2,32,8,256]{3,2,1,0:T(8,128)} %broadcast_select_fusion.f_ref, f32[2,32,1,256]{3,2,1,0:T(1,128)} %bitcast.45, f32[2,32,1,256]{3,2,1,0:T(1,128)} %bitcast.44, f32[32,8,256]{2,1,0:T(8,128)} %get-tuple-element.98.a_ref, f32[32,8,256]{2,1,0:T(8,128)} %fusion.18.b_ref, ...), custom_call_target="tpu_custom_call" | custom-call | tf_op jit(solution)/shard_map/pallas_call | solution.py:112
  (252 shorter events, 88.6 us)
Async XLA Ops:
  1.7 18.2 %collective-permute-start.1 = (f32[2,64,1,256]{3,2,1,0:T(1,128)S(1)}, f32[2,64,1,256]{3,2,1,0:T(1,128)S(1)}, u32[]{:S(2)}, u32[]{:S(2)}) collective-permute-start(f32[2,64,1,256]{3,2,1,0:T(1,128)S(1)} %get-tuple-element.31), channel_id=1, source_target_pairs={{1,0},{2,1},{3,2},{4,3},{5,4},{6,5},{7,6},{8,7},{9,8},{10,9},{11,1... | collective-permute-start | bytes 393224 | tf_op jit(solution)/shard_map/ppermute | solution.py:24
  4.3 15.6 %collective-permute-start = (f32[2,64,1,256]{3,2,1,0:T(1,128)S(1)}, f32[2,64,1,256]{3,2,1,0:T(1,128)S(1)}, u32[]{:S(2)}, u32[]{:S(2)}) collective-permute-start(f32[2,64,1,256]{3,2,1,0:T(1,128)S(1)} %get-tuple-element.32), channel_id=1, source_target_pairs={{0,1},{1,2},{2,3},{3,4},{4,5},{5,6},{6,7},{7,8},{8,9},{9,10},{10,1... | collective-permute-start | bytes 393224 | tf_op jit(solution)/shard_map/ppermute | solution.py:23
  10.4 27.5 %collective-permute-start.5 = (f32[2,32,1,256]{3,2,1,0:T(1,128)S(1)}, f32[2,32,1,256]{3,2,1,0:T(1,128)S(1)}, u32[]{:S(2)}, u32[]{:S(2)}) collective-permute-start(f32[2,32,1,256]{3,2,1,0:T(1,128)S(1)} %get-tuple-element.59), channel_id=1, source_target_pairs={{1,0},{2,1},{3,2},{4,3},{5,4},{6,5},{7,6},{8,7},{9,8},{10,9},{11,1... | collective-permute-start | bytes 196616 | tf_op jit(solution)/shard_map/ppermute | solution.py:24
  12.3 25.6 %collective-permute-start.4 = (f32[2,32,1,256]{3,2,1,0:T(1,128)S(1)}, f32[2,32,1,256]{3,2,1,0:T(1,128)S(1)}, u32[]{:S(2)}, u32[]{:S(2)}) collective-permute-start(f32[2,32,1,256]{3,2,1,0:T(1,128)S(1)} %get-tuple-element.60), channel_id=1, source_target_pairs={{0,1},{1,2},{2,3},{3,4},{4,5},{5,6},{6,7},{7,8},{8,9},{9,10},{10,1... | collective-permute-start | bytes 196616 | tf_op jit(solution)/shard_map/ppermute | solution.py:23
  19.9 9.7 %copy-start.8 = (f32[2,64,8,256]{3,2,1,0:T(8,128)S(1)}, f32[2,64,8,256]{3,2,1,0:T(8,128)}, u32[]{:S(2)}) copy-start(f32[2,64,8,256]{3,2,1,0:T(8,128)} %f_ref.1) | copy-start | bytes 3145732
  31.1 12.3 %copy-start.15 = (f32[2,64,8,256]{3,2,1,0:T(8,128)}, f32[2,64,8,256]{3,2,1,0:T(8,128)S(1)}, u32[]{:S(2)}) copy-start(f32[2,64,8,256]{3,2,1,0:T(8,128)S(1)} %multiply_add_fusion.3.f_ref) | copy-start | bytes 3145732
  31.3 12.1 %collective-permute-start.3 = (f32[2,64,1,256]{3,2,1,0:T(1,128)S(1)}, f32[2,64,1,256]{3,2,1,0:T(1,128)S(1)}, u32[]{:S(2)}, u32[]{:S(2)}) collective-permute-start(f32[2,64,1,256]{3,2,1,0:T(1,128)S(1)} %get-tuple-element.29), channel_id=1, source_target_pairs={{1,0},{2,1},{3,2},{4,3},{5,4},{6,5},{7,6},{8,7},{9,8},{10,9},{11,1... | collective-permute-start | bytes 393224 | tf_op jit(solution)/shard_map/ppermute | solution.py:24
  34.0 9.5 %collective-permute-start.2 = (f32[2,64,1,256]{3,2,1,0:T(1,128)S(1)}, f32[2,64,1,256]{3,2,1,0:T(1,128)S(1)}, u32[]{:S(2)}, u32[]{:S(2)}) collective-permute-start(f32[2,64,1,256]{3,2,1,0:T(1,128)S(1)} %get-tuple-element.30), channel_id=1, source_target_pairs={{0,1},{1,2},{2,3},{3,4},{4,5},{5,6},{6,7},{7,8},{8,9},{9,10},{10,1... | collective-permute-start | bytes 393224 | tf_op jit(solution)/shard_map/ppermute | solution.py:23
  56.1 7.7 %collective-permute-start.7 = (f32[2,64,2,256]{3,2,1,0:T(2,128)S(1)}, f32[2,64,2,256]{3,2,1,0:T(2,128)S(1)}, u32[]{:S(2)}, u32[]{:S(2)}) collective-permute-start(f32[2,64,2,256]{3,2,1,0:T(2,128)S(1)} %get-tuple-element.27), channel_id=1, source_target_pairs={{1,0},{2,1},{3,2},{4,3},{5,4},{6,5},{7,6},{8,7},{9,8},{10,9},{11,1... | collective-permute-start | bytes 786440 | tf_op jit(solution)/shard_map/ppermute | solution.py:24
  59.5 8.2 %collective-permute-start.6 = (f32[2,64,2,256]{3,2,1,0:T(2,128)S(1)}, f32[2,64,2,256]{3,2,1,0:T(2,128)S(1)}, u32[]{:S(2)}, u32[]{:S(2)}) collective-permute-start(f32[2,64,2,256]{3,2,1,0:T(2,128)S(1)} %get-tuple-element.28), channel_id=1, source_target_pairs={{0,1},{1,2},{2,3},{3,4},{4,5},{5,6},{6,7},{7,8},{8,9},{9,10},{10,1... | collective-permute-start | bytes 786440 | tf_op jit(solution)/shard_map/ppermute | solution.py:23
  82.2 7.8 %collective-permute-start.9 = (f32[2,32,1,256]{3,2,1,0:T(1,128)S(1)}, f32[2,32,1,256]{3,2,1,0:T(1,128)}, u32[]{:S(2)}, u32[]{:S(2)}) collective-permute-start(f32[2,32,1,256]{3,2,1,0:T(1,128)S(1)} %get-tuple-element.53), channel_id=1, source_target_pairs={{1,0},{2,1},{3,2},{4,3},{5,4},{6,5},{7,6},{8,7},{9,8},{10,9},{11,1... | collective-permute-start | bytes 196616 | tf_op jit(solution)/shard_map/ppermute | solution.py:24
  87.2 3.3 %collective-permute-start.8 = (f32[2,32,1,256]{3,2,1,0:T(1,128)S(1)}, f32[2,32,1,256]{3,2,1,0:T(1,128)}, u32[]{:S(2)}, u32[]{:S(2)}) collective-permute-start(f32[2,32,1,256]{3,2,1,0:T(1,128)S(1)} %get-tuple-element.54), channel_id=1, source_target_pairs={{0,1},{1,2},{2,3},{3,4},{4,5},{5,6},{6,7},{7,8},{8,9},{9,10},{10,1... | collective-permute-start | bytes 196616 | tf_op jit(solution)/shard_map/ppermute | solution.py:23
  100.6 12.4 %collective-permute-start.11 = (f32[2,32,1,256]{3,2,1,0:T(1,128)}, f32[2,32,1,256]{3,2,1,0:T(1,128)S(1)}, u32[]{:S(2)}, u32[]{:S(2)}) collective-permute-start(f32[2,32,1,256]{3,2,1,0:T(1,128)} %get-tuple-element.47), channel_id=1, source_target_pairs={{1,0},{2,1},{3,2},{4,3},{5,4},{6,5},{7,6},{8,7},{9,8},{10,9},{11,1... | collective-permute-start | bytes 196616 | tf_op jit(solution)/shard_map/ppermute | solution.py:24
  105.9 5.6 %collective-permute-start.10 = (f32[2,32,1,256]{3,2,1,0:T(1,128)S(1)}, f32[2,32,1,256]{3,2,1,0:T(1,128)S(1)}, u32[]{:S(2)}, u32[]{:S(2)}) collective-permute-start(f32[2,32,1,256]{3,2,1,0:T(1,128)S(1)} %get-tuple-element.48), channel_id=1, source_target_pairs={{0,1},{1,2},{2,3},{3,4},{4,5},{5,6},{6,7},{7,8},{8,9},{9,10},{10,1... | collective-permute-start | bytes 196616 | tf_op jit(solution)/shard_map/ppermute | solution.py:23
  159.1 12.3 %copy-start.19 = (f32[2,64,8,256]{3,2,1,0:T(8,128)}, f32[2,64,8,256]{3,2,1,0:T(8,128)S(1)}, u32[]{:S(2)}) copy-start(f32[2,64,8,256]{3,2,1,0:T(8,128)S(1)} %multiply_add_fusion.1.f_ref) | copy-start | bytes 3145732
  159.2 12.1 %collective-permute-start.13 = (f32[2,64,1,256]{3,2,1,0:T(1,128)S(1)}, f32[2,64,1,256]{3,2,1,0:T(1,128)S(1)}, u32[]{:S(2)}, u32[]{:S(2)}) collective-permute-start(f32[2,64,1,256]{3,2,1,0:T(1,128)S(1)} %get-tuple-element.22), channel_id=1, source_target_pairs={{1,0},{2,1},{3,2},{4,3},{5,4},{6,5},{7,6},{8,7},{9,8},{10,9},{11,1... | collective-permute-start | bytes 393224 | tf_op jit(solution)/shard_map/ppermute | solution.py:24
  162.1 9.3 %collective-permute-start.12 = (f32[2,64,1,256]{3,2,1,0:T(1,128)S(1)}, f32[2,64,1,256]{3,2,1,0:T(1,128)S(1)}, u32[]{:S(2)}, u32[]{:S(2)}) collective-permute-start(f32[2,64,1,256]{3,2,1,0:T(1,128)S(1)} %get-tuple-element.23), channel_id=1, source_target_pairs={{0,1},{1,2},{2,3},{3,4},{4,5},{5,6},{6,7},{7,8},{8,9},{9,10},{10,1... | collective-permute-start | bytes 393224 | tf_op jit(solution)/shard_map/ppermute | solution.py:23
  184.2 6.7 %collective-permute-start.15 = (f32[2,64,1,256]{3,2,1,0:T(1,128)S(1)}, f32[2,64,1,256]{3,2,1,0:T(1,128)S(1)}, u32[]{:S(2)}, u32[]{:S(2)}) collective-permute-start(f32[2,64,1,256]{3,2,1,0:T(1,128)S(1)} %get-tuple-element.20), channel_id=1, source_target_pairs={{1,0},{2,1},{3,2},{4,3},{5,4},{6,5},{7,6},{8,7},{9,8},{10,9},{11,1... | collective-permute-start | bytes 393224 | tf_op jit(solution)/shard_map/ppermute | solution.py:24
  187.0 6.0 %collective-permute-start.14 = (f32[2,64,1,256]{3,2,1,0:T(1,128)S(1)}, f32[2,64,1,256]{3,2,1,0:T(1,128)S(1)}, u32[]{:S(2)}, u32[]{:S(2)}) collective-permute-start(f32[2,64,1,256]{3,2,1,0:T(1,128)S(1)} %get-tuple-element.21), channel_id=1, source_target_pairs={{0,1},{1,2},{2,3},{3,4},{4,5},{5,6},{6,7},{7,8},{8,9},{9,10},{10,1... | collective-permute-start | bytes 393224 | tf_op jit(solution)/shard_map/ppermute | solution.py:23
  190.8 11.2 %copy-start.23 = (f32[2,64,8,256]{3,2,1,0:T(8,128)S(1)}, f32[2,64,8,256]{3,2,1,0:T(8,128)}, u32[]{:S(2)}) copy-start(f32[2,64,8,256]{3,2,1,0:T(8,128)} %shard_map.69) | copy-start | bytes 3145732
  190.9 11.2 %copy-start.25 = (f32[2,64,8,256]{3,2,1,0:T(8,128)S(1)}, f32[2,64,8,256]{3,2,1,0:T(8,128)}, u32[]{:S(2)}) copy-start(f32[2,64,8,256]{3,2,1,0:T(8,128)} %shard_map.73) | copy-start | bytes 3145732
  206.2 21.4 %collective-permute-start.16 = (f32[2,32,8,256]{3,2,1,0:T(8,128)S(1)}, f32[2,32,8,256]{3,2,1,0:T(8,128)S(1)}, u32[]{:S(2)}, u32[]{:S(2)}) collective-permute-start(f32[2,32,8,256]{3,2,1,0:T(8,128)S(1)} %get-tuple-element.5), channel_id=1, source_target_pairs={{0,16},{1,17},{2,18},{3,19},{4,20},{5,21},{6,22},{7,23},{8,24},{9,... | collective-permute-start | bytes 1572872 | tf_op jit(solution)/shard_map/ppermute | solution.py:279
  207.5 18.9 %collective-permute-start.18 = (f32[2,32,1,256]{3,2,1,0:T(1,128)S(1)}, f32[2,32,1,256]{3,2,1,0:T(1,128)S(1)}, u32[]{:S(2)}, u32[]{:S(2)}) collective-permute-start(f32[2,32,1,256]{3,2,1,0:T(1,128)S(1)} %get-tuple-element.33), channel_id=1, source_target_pairs={{1,16},{2,17},{3,18},{4,19},{5,20},{6,21},{7,22},{8,23},{9,24},{10... | collective-permute-start | bytes 196616 | tf_op jit(solution)/shard_map/ppermute | solution.py:281
  208.9 18.1 %collective-permute-start.17 = (f32[2,32,1,256]{3,2,1,0:T(1,128)S(1)}, f32[2,32,1,256]{3,2,1,0:T(1,128)S(1)}, u32[]{:S(2)}, u32[]{:S(2)}) collective-permute-start(f32[2,32,1,256]{3,2,1,0:T(1,128)S(1)} %get-tuple-element.34), channel_id=1, source_target_pairs={{0,17},{1,18},{2,19},{3,20},{4,21},{5,22},{6,23},{7,24},{8,25},{9,... | collective-permute-start | bytes 196616 | tf_op jit(solution)/shard_map/ppermute | solution.py:280
  (51 other events, 161.0 us)

commit v2 on v1

--- a/solution.py
+++ b/solution.py
@@ -66,8 +66,14 @@
     return diffusion + vertical - advection + reaction
 
 
-def _tendency_kernel(k_ref, f_ref, hb_ref, ha_ref, a_ref, b_ref, kh_ref, kv_ref, o_ref, *, reach, spacing):
-    levels, width, lanes = f_ref.shape[1], f_ref.shape[2], f_ref.shape[3]
+def _tendency_kernel(
+    k_ref, f_ref, below_ref, above_ref, hb_ref, ha_ref, a_ref, b_ref, kh_ref, kv_ref, o_ref,
+    *, reach, spacing
+):
+    block, width, lanes = f_ref.shape[1], f_ref.shape[2], f_ref.shape[3]
+    step = pl.program_id(0)
+    has_below = step > 0
+    has_above = step < pl.num_programs(0) - 1
     row = lax.broadcasted_iota(jnp.int32, (width, lanes), 0)
     col = lax.broadcasted_iota(jnp.int32, (width, lanes), 1)
     east_edge = row >= width - reach
@@ -77,12 +83,7 @@
     half_inv = 1.0 / (2.0 * spacing)
     square_inv = 1.0 / (spacing * spacing)
     rates = [[k_ref[t, d] for d in range(2)] for t in range(2)]
-
-    def level(z, carry):
-        above = jnp.minimum(z + 1, levels - 1)
-        below = jnp.maximum(z - 1, 0)
-        has_above = z + 1 < levels
-        has_below = z > 0
+    for z in range(block):
         a = a_ref[z]
         b = b_ref[z]
         kh = kh_ref[z]
@@ -90,8 +91,14 @@
         cs = [f_ref[t, z] for t in range(2)]
         for t in range(2):
             c = cs[t]
-            up = jnp.where(has_above, f_ref[t, above], 0.0)
-            down = jnp.where(has_below, f_ref[t, below], 0.0)
+            if z + 1 < block:
+                up = f_ref[t, z + 1]
+            else:
+                up = jnp.where(has_above, above_ref[t, 0], 0.0)
+            if z > 0:
+                down = f_ref[t, z - 1]
+            else:
+                down = jnp.where(has_below, below_ref[t, 0], 0.0)
             east = jnp.where(east_edge, ha_ref[t, z], pltpu.roll(c, width - reach, 0))
             west = jnp.where(west_edge, hb_ref[t, z], pltpu.roll(c, reach, 0))
             north = jnp.where(north_edge, 0.0, pltpu.roll(c, lanes - 1, 1))
@@ -101,20 +108,30 @@
             vertical = kv * (up - 2.0 * c + down) * square_inv
             reaction = rates[t][0] * cs[0] + rates[t][1] * cs[1]
             o_ref[t, z] = diffusion + vertical - advection + reaction
-        return carry
-
-    lax.fori_loop(0, levels, level, 0)
 
 
 def tendency_kernel(field, halo, a, b, kh, kv, coupling, spacing):
-    reach = int(spacing)
-    vmem = pl.BlockSpec(memory_space=pltpu.VMEM)
+    tracers, levels, width, lanes = field.shape
+    block = min(16, levels)
+    steps = levels // block
+    whole = pl.BlockSpec((tracers, block, width, lanes), lambda i: (0, i, 0, 0))
+    below = pl.BlockSpec(
+        (tracers, 1, width, lanes), lambda i: (0, jnp.maximum(i * block - 1, 0), 0, 0)
+    )
+    above = pl.BlockSpec(
+        (tracers, 1, width, lanes),
+        lambda i: (0, jnp.minimum((i + 1) * block, levels - 1), 0, 0),
+    )
+    side = pl.BlockSpec((tracers, block, 1, lanes), lambda i: (0, i, 0, 0))
+    grid_of = pl.BlockSpec((block, width, lanes), lambda i: (i, 0, 0))
     return pl.pallas_call(
-        functools.partial(_tendency_kernel, reach=reach, spacing=float(spacing)),
+        functools.partial(_tendency_kernel, reach=int(spacing), spacing=float(spacing)),
         out_shape=jax.ShapeDtypeStruct(field.shape, field.dtype),
-        in_specs=[pl.BlockSpec(memory_space=pltpu.SMEM)] + [vmem] * 7,
-        out_specs=vmem,
-    )(coupling, field, halo[0], halo[1], a, b, kh, kv)
+        grid=(steps,),
+        in_specs=[pl.BlockSpec(memory_space=pltpu.SMEM), whole, below, above, side, side]
+        + [grid_of] * 4,
+        out_specs=whole,
+    )(coupling, field, field, field, halo[0], halo[1], a, b, kh, kv)
 
 
 def pair_sum(field):

time: 238 us -> 194 us (0.82)
  Pallas kernels: 95.2 us -> 51.4 us
    pallas_call x13, Pallas kernels: 95.2 us -> 51.4 us  [tendency_kernel(): pl.pallas_call(functools.partial(_tendency_kernel, reach=int(spacing), sp...]
    unnamed x120 -> x124, local copies, waits for them, and re-layouts: 15.5 us -> 13.8 us
  transfers between devices with their start and end apart: 19 -> 19, of which waited for: 5 -> 5; matrix products, arithmetic and copies ran while one was open for 7% -> 9% of each run, Pallas kernels for 8% -> 5%
where the time goes in v2:
time: 194 us; the launch traced here: 192 us
  starting transfers between devices  51.8 us (27%)
  Pallas kernels  51.4 us (26%)
  other arithmetic  35.3 us (18%)
  local copies, waits for them, and re-layouts  29.5 us (15%)
  waiting for transfers between devices  23.2 us (12%)
    pallas_call x13, Pallas kernels, tendency_kernel(): pl.pallas_call(functools.partial(_tendency_kernel, reach=int(spacing), sp...  51.4 us
    ppermute x8, starting transfers between devices, exchange(): after = lax.ppermute(to_left, 'space', shift_pairs(count, -1))  27.6 us
    ppermute x8, starting transfers between devices, exchange(): before = lax.ppermute(to_right, 'space', shift_pairs(count, 1))  20.3 us
    ppermute x1, waiting for transfers between devices, body(): passed_a = lax.ppermute(lo(after), ('tm', 'space'), to_west)  15.9 us
    unnamed x124, local copies, waits for them, and re-layouts  13.8 us
    ppermute x8, waiting for transfers between devices, exchange(): before = lax.ppermute(to_right, 'space', shift_pairs(count, 1))  6.65 us
    slice x10, local copies, waits for them, and re-layouts, lo(): return field[..., :width, :]  6.26 us
    slice x10, local copies, waits for them, and re-layouts, pair_sum(): jnp.roll(field, -1, axis=-2)  4.44 us
  transfers between devices with their start and end apart: 19, of which 5 were waited for; matrix products, arithmetic and copies ran while one was open for 9% of the time, Pallas kernels for 5%

profile of v2, /device:TPU:11, one launch (start us, length us, event | category | flops | bytes accessed | tf_op | source)
XLA Modules:
  0.0 192.4 jit_solution(1255843860219097286)
XLA Ops:
  4.4 3.0 %collective-permute-start = (f32[2,64,1,256]{3,2,1,0:T(1,128)S(1)}, f32[2,64,1,256]{3,2,1,0:T(1,128)S(1)}, u32[]{:S(2)}, u32[]{:S(2)}) collective-permute-start(f32[2,64,1,256]{3,2,1,0:T(1,128)S(1)} %get-tuple-element.32), channel_id=1, source_target_pairs={{0,1},{1,2},{2,3},{3,4},{4,5},{5,6},{6,7},{7,8},{8,9},{9,10},{10,1... | collective-permute-start | bytes 393224 | tf_op jit(solution)/shard_map/ppermute | solution.py:23
  13.2 3.6 %collective-permute-start.4 = (f32[2,32,1,256]{3,2,1,0:T(1,128)}, f32[2,32,1,256]{3,2,1,0:T(1,128)S(1)}, u32[]{:S(2)}, u32[]{:S(2)}) collective-permute-start(f32[2,32,1,256]{3,2,1,0:T(1,128)} %get-tuple-element.60), channel_id=1, source_target_pairs={{0,1},{1,2},{2,3},{3,4},{4,5},{5,6},{6,7},{7,8},{8,9},{9,10},{10,1... | collective-permute-start | bytes 196616 | tf_op jit(solution)/shard_map/ppermute | solution.py:23
  22.1 4.5 %shard_map.64 = f32[2,64,8,256]{3,2,1,0:T(8,128)} custom-call(f32[2,2]{1,0:T(2,128)} %k_ref.25, f32[2,64,8,256]{3,2,1,0:T(8,128)} %above_ref.1, f32[2,64,8,256]{3,2,1,0:T(8,128)} %above_ref.1, f32[2,64,8,256]{3,2,1,0:T(8,128)} %above_ref.1, f32[2,64,1,256]{3,2,1,0:T(1,128)} %copy-done.46, f32[2,64,1,256]{3,2,1,0:T(1,128)} %copy-done.44, ...), custom_call_target="tpu_custom_call" | custom-call | tf_op jit(solution)/shard_map/pallas_call | solution.py:127
  31.5 3.0 %collective-permute-start.2 = (f32[2,64,1,256]{3,2,1,0:T(1,128)}, f32[2,64,1,256]{3,2,1,0:T(1,128)S(1)}, u32[]{:S(2)}, u32[]{:S(2)}) collective-permute-start(f32[2,64,1,256]{3,2,1,0:T(1,128)} %get-tuple-element.30), channel_id=1, source_target_pairs={{0,1},{1,2},{2,3},{3,4},{4,5},{5,6},{6,7},{7,8},{8,9},{9,10},{10,1... | collective-permute-start | bytes 393224 | tf_op jit(solution)/shard_map/ppermute | solution.py:23
  36.0 2.6 %shard_map.66 = f32[2,32,8,256]{3,2,1,0:T(8,128)} custom-call(f32[2,2]{1,0:T(2,128)} %k_ref.25, f32[2,32,8,256]{3,2,1,0:T(8,128)} %copy-done.13, f32[2,32,8,256]{3,2,1,0:T(8,128)} %copy-done.13, f32[2,32,8,256]{3,2,1,0:T(8,128)} %copy-done.13, f32[2,32,1,256]{3,2,1,0:T(1,128)} %copy-done.36, f32[2,32,1,256]{3,2,1,0:T(1,128)} %copy-done.38, ...), custom_call_target="tpu_custom_call" | custom-call | tf_op jit(solution)/shard_map/pallas_call | solution.py:127
  40.0 4.5 %shard_map.65 = f32[2,64,8,256]{3,2,1,0:T(8,128)} custom-call(f32[2,2]{1,0:T(2,128)} %k_ref.25, f32[2,64,8,256]{3,2,1,0:T(8,128)} %copy-done.16, f32[2,64,8,256]{3,2,1,0:T(8,128)} %copy-done.16, f32[2,64,8,256]{3,2,1,0:T(8,128)} %copy-done.16, f32[2,64,1,256]{3,2,1,0:T(1,128)} %copy-done.42, f32[2,64,1,256]{3,2,1,0:T(1,128)} %copy-done.40, ...), custom_call_target="tpu_custom_call" | custom-call | tf_op jit(solution)/shard_map/pallas_call | solution.py:127
  47.1 4.1 %collective-permute-start.7 = (f32[2,64,2,256]{3,2,1,0:T(2,128)S(1)}, f32[2,64,2,256]{3,2,1,0:T(2,128)S(1)}, u32[]{:S(2)}, u32[]{:S(2)}) collective-permute-start(f32[2,64,2,256]{3,2,1,0:T(2,128)S(1)} %get-tuple-element.27), channel_id=1, source_target_pairs={{1,0},{2,1},{3,2},{4,3},{5,4},{6,5},{7,6},{8,7},{9,8},{10,9},{11,1... | collective-permute-start | bytes 786440 | tf_op jit(solution)/shard_map/ppermute | solution.py:24
  55.5 3.7 %collective-permute-done.6 = f32[2,64,2,256]{3,2,1,0:T(2,128)S(1)} collective-permute-done((f32[2,64,2,256]{3,2,1,0:T(2,128)S(1)}, f32[2,64,2,256]{3,2,1,0:T(2,128)S(1)}, u32[]{:S(2)}, u32[]{:S(2)}) %collective-permute-start.6) | collective-permute-done | bytes 262176 | tf_op jit(solution)/shard_map/ppermute | solution.py:23
  60.7 4.6 %shard_map.67 = f32[2,64,8,256]{3,2,1,0:T(8,128)} custom-call(f32[2,2]{1,0:T(2,128)} %k_ref.25, f32[2,64,8,256]{3,2,1,0:T(8,128)} %copy-done.3, f32[2,64,8,256]{3,2,1,0:T(8,128)} %copy-done.3, f32[2,64,8,256]{3,2,1,0:T(8,128)} %copy-done.3, f32[2,64,1,256]{3,2,1,0:T(1,128)} %slice.445.hb_ref, f32[2,64,1,256]{3,2,1,0:T(1,128)} %slice.447.ha_ref, ...), custom_call_target="tpu_custom_call" | custom-call | tf_op jit(solution)/shard_map/pallas_call | solution.py:127
  69.4 4.5 %collective-permute-start.9 = (f32[2,32,1,256]{3,2,1,0:T(1,128)S(1)}, f32[2,32,1,256]{3,2,1,0:T(1,128)}, u32[]{:S(2)}, u32[]{:S(2)}) collective-permute-start(f32[2,32,1,256]{3,2,1,0:T(1,128)S(1)} %get-tuple-element.53), channel_id=1, source_target_pairs={{1,0},{2,1},{3,2},{4,3},{5,4},{6,5},{7,6},{8,7},{9,8},{10,9},{11,1... | collective-permute-start | bytes 196616 | tf_op jit(solution)/shard_map/ppermute | solution.py:24
  77.2 2.6 %shard_map.68 = f32[2,32,8,256]{3,2,1,0:T(8,128)} custom-call(f32[2,2]{1,0:T(2,128)} %k_ref.25, f32[2,32,8,256]{3,2,1,0:T(8,128)} %copy-done.21, f32[2,32,8,256]{3,2,1,0:T(8,128)} %copy-done.21, f32[2,32,8,256]{3,2,1,0:T(8,128)} %copy-done.21, f32[2,32,1,256]{3,2,1,0:T(1,128)} %collective-permute-done.8.hb_ref, ...), custom_call_target="tpu_custom_call" | custom-call | tf_op jit(solution)/shard_map/pallas_call | solution.py:127
  85.2 5.2 %collective-permute-start.11 = (f32[2,32,1,256]{3,2,1,0:T(1,128)}, f32[2,32,1,256]{3,2,1,0:T(1,128)S(1)}, u32[]{:S(2)}, u32[]{:S(2)}) collective-permute-start(f32[2,32,1,256]{3,2,1,0:T(1,128)} %get-tuple-element.47), channel_id=1, source_target_pairs={{1,0},{2,1},{3,2},{4,3},{5,4},{6,5},{7,6},{8,7},{9,8},{10,9},{11,1... | collective-permute-start | bytes 196616 | tf_op jit(solution)/shard_map/ppermute | solution.py:24
  106.5 4.5 %shard_map.69 = f32[2,64,8,256]{3,2,1,0:T(8,128)} custom-call(f32[2,2]{1,0:T(2,128)} %k_ref.25, f32[2,64,8,256]{3,2,1,0:T(8,128)} %copy-done.11, f32[2,64,8,256]{3,2,1,0:T(8,128)} %copy-done.11, f32[2,64,8,256]{3,2,1,0:T(8,128)} %copy-done.11, f32[2,64,1,256]{3,2,1,0:T(1,128)} %get-tuple-element.69.hb_ref, f32[2,64,1,256]{3,2,1,0:T(1,128)} %get-tuple-element.67.ha_ref, ...), custom_call_target="tpu_custom_call" | custom-call | tf_op jit(solution)/shard_map/pallas_call | solution.py:127
  112.7 4.4 %shard_map.71 = f32[2,64,8,256]{3,2,1,0:T(8,128)} custom-call(f32[2,2]{1,0:T(2,128)} %k_ref.25, f32[2,64,8,256]{3,2,1,0:T(8,128)} %add.330.f_ref.below_ref.above_ref, f32[2,64,8,256]{3,2,1,0:T(8,128)} %add.330.f_ref.below_ref.above_ref, f32[2,64,8,256]{3,2,1,0:T(8,128)} %add.330.f_ref.below_ref.above_ref, f32[2,64,1,256]{3,2,1,0:T(1,128)} %add.332.hb_ref, ...), custom_call_target="tpu_custom_call" | custom-call | tf_op jit(solution)/shard_map/pallas_call | solution.py:127
  117.2 4.5 %shard_map.72 = f32[2,64,8,256]{3,2,1,0:T(8,128)} custom-call(f32[2,2]{1,0:T(2,128)} %k_ref.25, f32[2,64,8,256]{3,2,1,0:T(8,128)} %get-tuple-element.25.f_ref.below_ref.above_ref, f32[2,64,8,256]{3,2,1,0:T(8,128)} %get-tuple-element.25.f_ref.below_ref.above_ref, f32[2,64,8,256]{3,2,1,0:T(8,128)} %get-tuple-element.25.f_ref.below_ref.above_ref, ...), custom_call_target="tpu_custom_call" | custom-call | tf_op jit(solution)/shard_map/pallas_call | solution.py:127
  121.7 4.6 %shard_map.70 = f32[2,64,8,256]{3,2,1,0:T(8,128)} custom-call(f32[2,2]{1,0:T(2,128)} %k_ref.25, f32[2,64,8,256]{3,2,1,0:T(8,128)} %get-tuple-element.26.f_ref.below_ref.above_ref, f32[2,64,8,256]{3,2,1,0:T(8,128)} %get-tuple-element.26.f_ref.below_ref.above_ref, f32[2,64,8,256]{3,2,1,0:T(8,128)} %get-tuple-element.26.f_ref.below_ref.above_ref, ...), custom_call_target="tpu_custom_call" | custom-call | tf_op jit(solution)/shard_map/pallas_call | solution.py:127
  129.5 2.8 %collective-permute-start.13 = (f32[2,64,1,256]{3,2,1,0:T(1,128)}, f32[2,64,1,256]{3,2,1,0:T(1,128)}, u32[]{:S(2)}, u32[]{:S(2)}) collective-permute-start(f32[2,64,1,256]{3,2,1,0:T(1,128)} %get-tuple-element.22), channel_id=1, source_target_pairs={{1,0},{2,1},{3,2},{4,3},{5,4},{6,5},{7,6},{8,7},{9,8},{10,9},{11,1... | collective-permute-start | bytes 393224 | tf_op jit(solution)/shard_map/ppermute | solution.py:24
  132.3 2.7 %collective-permute-start.12 = (f32[2,64,1,256]{3,2,1,0:T(1,128)}, f32[2,64,1,256]{3,2,1,0:T(1,128)}, u32[]{:S(2)}, u32[]{:S(2)}) collective-permute-start(f32[2,64,1,256]{3,2,1,0:T(1,128)} %get-tuple-element.23), channel_id=1, source_target_pairs={{0,1},{1,2},{2,3},{3,4},{4,5},{5,6},{6,7},{7,8},{8,9},{9,10},{10,1... | collective-permute-start | bytes 393224 | tf_op jit(solution)/shard_map/ppermute | solution.py:23
  136.7 2.6 %shard_map.75 = f32[2,32,8,256]{3,2,1,0:T(8,128)} custom-call(f32[2,2]{1,0:T(2,128)} %k_ref.25, f32[2,32,8,256]{3,2,1,0:T(8,128)} %fusion.11.f_ref.below_ref.above_ref, f32[2,32,8,256]{3,2,1,0:T(8,128)} %fusion.11.f_ref.below_ref.above_ref, f32[2,32,8,256]{3,2,1,0:T(8,128)} %fusion.11.f_ref.below_ref.above_ref, ...), custom_call_target="tpu_custom_call" | custom-call | tf_op jit(solution)/shard_map/pallas_call | solution.py:127
  139.4 4.6 %shard_map.73 = f32[2,64,8,256]{3,2,1,0:T(8,128)} custom-call(f32[2,2]{1,0:T(2,128)} %k_ref.25, f32[2,64,8,256]{3,2,1,0:T(8,128)} %copy-done.19, f32[2,64,8,256]{3,2,1,0:T(8,128)} %copy-done.19, f32[2,64,8,256]{3,2,1,0:T(8,128)} %copy-done.19, f32[2,64,1,256]{3,2,1,0:T(1,128)} %collective-permute-done.12.hb_ref, ...), custom_call_target="tpu_custom_call" | custom-call | tf_op jit(solution)/shard_map/pallas_call | solution.py:127
  147.2 3.9 %collective-permute-start.15 = (f32[2,64,1,256]{3,2,1,0:T(1,128)S(1)}, f32[2,64,1,256]{3,2,1,0:T(1,128)S(1)}, u32[]{:S(2)}, u32[]{:S(2)}) collective-permute-start(f32[2,64,1,256]{3,2,1,0:T(1,128)S(1)} %get-tuple-element.20), channel_id=1, source_target_pairs={{1,0},{2,1},{3,2},{4,3},{5,4},{6,5},{7,6},{8,7},{9,8},{10,9},{11,1... | collective-permute-start | bytes 393224 | tf_op jit(solution)/shard_map/ppermute | solution.py:24
  157.0 4.5 %shard_map.74 = f32[2,64,8,256]{3,2,1,0:T(8,128)} custom-call(f32[2,2]{1,0:T(2,128)} %k_ref.25, f32[2,64,8,256]{3,2,1,0:T(8,128)} %copy-done.7, f32[2,64,8,256]{3,2,1,0:T(8,128)} %copy-done.7, f32[2,64,8,256]{3,2,1,0:T(8,128)} %copy-done.7, f32[2,64,1,256]{3,2,1,0:T(1,128)} %copy-done.57, f32[2,64,1,256]{3,2,1,0:T(1,128)} %copy-done.56, ...), custom_call_target="tpu_custom_call" | custom-call | tf_op jit(solution)/shard_map/pallas_call | solution.py:127
  169.0 15.9 %collective-permute-done.18 = f32[2,32,1,256]{3,2,1,0:T(1,128)S(1)} collective-permute-done((f32[2,32,1,256]{3,2,1,0:T(1,128)S(1)}, f32[2,32,1,256]{3,2,1,0:T(1,128)S(1)}, u32[]{:S(2)}, u32[]{:S(2)}) %collective-permute-start.18) | collective-permute-done | bytes 65568 | tf_op jit(solution)/shard_map/ppermute | solution.py:298
  187.0 2.8 %shard_map.76 = f32[2,32,8,256]{3,2,1,0:T(8,128)} custom-call(f32[2,2]{1,0:T(2,128)} %k_ref.25, f32[2,32,8,256]{3,2,1,0:T(8,128)} %broadcast_select_fusion.f_ref.below_ref.above_ref, f32[2,32,8,256]{3,2,1,0:T(8,128)} %broadcast_select_fusion.f_ref.below_ref.above_ref, f32[2,32,8,256]{3,2,1,0:T(8,128)} %broadcast_select_fusion.f_ref.below_ref.above_ref, ...), custom_call_target="tpu_custom_call" | custom-call | tf_op jit(solution)/shard_map/pallas_call | solution.py:127
  (256 shorter events, 87.1 us)
Async XLA Ops:
  1.8 18.9 %collective-permute-start.1 = (f32[2,64,1,256]{3,2,1,0:T(1,128)S(1)}, f32[2,64,1,256]{3,2,1,0:T(1,128)S(1)}, u32[]{:S(2)}, u32[]{:S(2)}) collective-permute-start(f32[2,64,1,256]{3,2,1,0:T(1,128)S(1)} %get-tuple-element.31), channel_id=1, source_target_pairs={{1,0},{2,1},{3,2},{4,3},{5,4},{6,5},{7,6},{8,7},{9,8},{10,9},{11,1... | collective-permute-start | bytes 393224 | tf_op jit(solution)/shard_map/ppermute | solution.py:24
  4.4 16.4 %collective-permute-start = (f32[2,64,1,256]{3,2,1,0:T(1,128)S(1)}, f32[2,64,1,256]{3,2,1,0:T(1,128)S(1)}, u32[]{:S(2)}, u32[]{:S(2)}) collective-permute-start(f32[2,64,1,256]{3,2,1,0:T(1,128)S(1)} %get-tuple-element.32), channel_id=1, source_target_pairs={{0,1},{1,2},{2,3},{3,4},{4,5},{5,6},{6,7},{7,8},{8,9},{9,10},{10,1... | collective-permute-start | bytes 393224 | tf_op jit(solution)/shard_map/ppermute | solution.py:23
  11.2 24.1 %collective-permute-start.5 = (f32[2,32,1,256]{3,2,1,0:T(1,128)}, f32[2,32,1,256]{3,2,1,0:T(1,128)S(1)}, u32[]{:S(2)}, u32[]{:S(2)}) collective-permute-start(f32[2,32,1,256]{3,2,1,0:T(1,128)} %get-tuple-element.59), channel_id=1, source_target_pairs={{1,0},{2,1},{3,2},{4,3},{5,4},{6,5},{7,6},{8,7},{9,8},{10,9},{11,1... | collective-permute-start | bytes 196616 | tf_op jit(solution)/shard_map/ppermute | solution.py:24
  13.2 22.2 %collective-permute-start.4 = (f32[2,32,1,256]{3,2,1,0:T(1,128)}, f32[2,32,1,256]{3,2,1,0:T(1,128)S(1)}, u32[]{:S(2)}, u32[]{:S(2)}) collective-permute-start(f32[2,32,1,256]{3,2,1,0:T(1,128)} %get-tuple-element.60), channel_id=1, source_target_pairs={{0,1},{1,2},{2,3},{3,4},{4,5},{5,6},{6,7},{7,8},{8,9},{9,10},{10,1... | collective-permute-start | bytes 196616 | tf_op jit(solution)/shard_map/ppermute | solution.py:23
  28.1 10.6 %copy-start.16 = (f32[2,64,8,256]{3,2,1,0:T(8,128)}, f32[2,64,8,256]{3,2,1,0:T(8,128)S(1)}, u32[]{:S(2)}) copy-start(f32[2,64,8,256]{3,2,1,0:T(8,128)S(1)} %multiply_add_fusion.3.f_ref.below_ref.above_ref) | copy-start | bytes 3145732
  29.0 9.7 %collective-permute-start.3 = (f32[2,64,1,256]{3,2,1,0:T(1,128)}, f32[2,64,1,256]{3,2,1,0:T(1,128)S(1)}, u32[]{:S(2)}, u32[]{:S(2)}) collective-permute-start(f32[2,64,1,256]{3,2,1,0:T(1,128)} %get-tuple-element.29), channel_id=1, source_target_pairs={{1,0},{2,1},{3,2},{4,3},{5,4},{6,5},{7,6},{8,7},{9,8},{10,9},{11,1... | collective-permute-start | bytes 393224 | tf_op jit(solution)/shard_map/ppermute | solution.py:24
  31.5 7.2 %collective-permute-start.2 = (f32[2,64,1,256]{3,2,1,0:T(1,128)}, f32[2,64,1,256]{3,2,1,0:T(1,128)S(1)}, u32[]{:S(2)}, u32[]{:S(2)}) collective-permute-start(f32[2,64,1,256]{3,2,1,0:T(1,128)} %get-tuple-element.30), channel_id=1, source_target_pairs={{0,1},{1,2},{2,3},{3,4},{4,5},{5,6},{6,7},{7,8},{8,9},{9,10},{10,1... | collective-permute-start | bytes 393224 | tf_op jit(solution)/shard_map/ppermute | solution.py:23
  47.1 7.7 %collective-permute-start.7 = (f32[2,64,2,256]{3,2,1,0:T(2,128)S(1)}, f32[2,64,2,256]{3,2,1,0:T(2,128)S(1)}, u32[]{:S(2)}, u32[]{:S(2)}) collective-permute-start(f32[2,64,2,256]{3,2,1,0:T(2,128)S(1)} %get-tuple-element.27), channel_id=1, source_target_pairs={{1,0},{2,1},{3,2},{4,3},{5,4},{6,5},{7,6},{8,7},{9,8},{10,9},{11,1... | collective-permute-start | bytes 786440 | tf_op jit(solution)/shard_map/ppermute | solution.py:24
  51.2 8.0 %collective-permute-start.6 = (f32[2,64,2,256]{3,2,1,0:T(2,128)S(1)}, f32[2,64,2,256]{3,2,1,0:T(2,128)S(1)}, u32[]{:S(2)}, u32[]{:S(2)}) collective-permute-start(f32[2,64,2,256]{3,2,1,0:T(2,128)S(1)} %get-tuple-element.28), channel_id=1, source_target_pairs={{0,1},{1,2},{2,3},{3,4},{4,5},{5,6},{6,7},{7,8},{8,9},{9,10},{10,1... | collective-permute-start | bytes 786440 | tf_op jit(solution)/shard_map/ppermute | solution.py:23
  69.3 7.9 %copy-start.21 = (f32[2,32,8,256]{3,2,1,0:T(8,128)}, f32[2,32,8,256]{3,2,1,0:T(8,128)S(1)}, u32[]{:S(2)}) copy-start(f32[2,32,8,256]{3,2,1,0:T(8,128)S(1)} %get-tuple-element.18.f_ref.below_ref.above_ref) | copy-start | bytes 1572868
  69.4 7.3 %collective-permute-start.9 = (f32[2,32,1,256]{3,2,1,0:T(1,128)S(1)}, f32[2,32,1,256]{3,2,1,0:T(1,128)}, u32[]{:S(2)}, u32[]{:S(2)}) collective-permute-start(f32[2,32,1,256]{3,2,1,0:T(1,128)S(1)} %get-tuple-element.53), channel_id=1, source_target_pairs={{1,0},{2,1},{3,2},{4,3},{5,4},{6,5},{7,6},{8,7},{9,8},{10,9},{11,1... | collective-permute-start | bytes 196616 | tf_op jit(solution)/shard_map/ppermute | solution.py:24
  74.0 3.3 %collective-permute-start.8 = (f32[2,32,1,256]{3,2,1,0:T(1,128)S(1)}, f32[2,32,1,256]{3,2,1,0:T(1,128)}, u32[]{:S(2)}, u32[]{:S(2)}) collective-permute-start(f32[2,32,1,256]{3,2,1,0:T(1,128)S(1)} %get-tuple-element.54), channel_id=1, source_target_pairs={{0,1},{1,2},{2,3},{3,4},{4,5},{5,6},{6,7},{7,8},{8,9},{9,10},{10,1... | collective-permute-start | bytes 196616 | tf_op jit(solution)/shard_map/ppermute | solution.py:23
  84.9 7.6 %copy-start.11 = (f32[2,64,8,256]{3,2,1,0:T(8,128)}, f32[2,64,8,256]{3,2,1,0:T(8,128)S(1)}, u32[]{:S(2)}) copy-start(f32[2,64,8,256]{3,2,1,0:T(8,128)S(1)} %get-tuple-element.24.f_ref.below_ref.above_ref) | copy-start | bytes 3145732
  85.2 12.4 %collective-permute-start.11 = (f32[2,32,1,256]{3,2,1,0:T(1,128)}, f32[2,32,1,256]{3,2,1,0:T(1,128)S(1)}, u32[]{:S(2)}, u32[]{:S(2)}) collective-permute-start(f32[2,32,1,256]{3,2,1,0:T(1,128)} %get-tuple-element.47), channel_id=1, source_target_pairs={{1,0},{2,1},{3,2},{4,3},{5,4},{6,5},{7,6},{8,7},{9,8},{10,9},{11,1... | collective-permute-start | bytes 196616 | tf_op jit(solution)/shard_map/ppermute | solution.py:24
  90.4 5.6 %collective-permute-start.10 = (f32[2,32,1,256]{3,2,1,0:T(1,128)S(1)}, f32[2,32,1,256]{3,2,1,0:T(1,128)S(1)}, u32[]{:S(2)}, u32[]{:S(2)}) collective-permute-start(f32[2,32,1,256]{3,2,1,0:T(1,128)S(1)} %get-tuple-element.48), channel_id=1, source_target_pairs={{0,1},{1,2},{2,3},{3,4},{4,5},{5,6},{6,7},{7,8},{8,9},{9,10},{10,1... | collective-permute-start | bytes 196616 | tf_op jit(solution)/shard_map/ppermute | solution.py:23
  128.6 10.8 %copy-start.19 = (f32[2,64,8,256]{3,2,1,0:T(8,128)}, f32[2,64,8,256]{3,2,1,0:T(8,128)S(1)}, u32[]{:S(2)}) copy-start(f32[2,64,8,256]{3,2,1,0:T(8,128)S(1)} %multiply_add_fusion.1.f_ref.below_ref.above_ref) | copy-start | bytes 3145732
  129.5 9.9 %collective-permute-start.13 = (f32[2,64,1,256]{3,2,1,0:T(1,128)}, f32[2,64,1,256]{3,2,1,0:T(1,128)}, u32[]{:S(2)}, u32[]{:S(2)}) collective-permute-start(f32[2,64,1,256]{3,2,1,0:T(1,128)} %get-tuple-element.22), channel_id=1, source_target_pairs={{1,0},{2,1},{3,2},{4,3},{5,4},{6,5},{7,6},{8,7},{9,8},{10,9},{11,1... | collective-permute-start | bytes 393224 | tf_op jit(solution)/shard_map/ppermute | solution.py:24
  132.3 7.1 %collective-permute-start.12 = (f32[2,64,1,256]{3,2,1,0:T(1,128)}, f32[2,64,1,256]{3,2,1,0:T(1,128)}, u32[]{:S(2)}, u32[]{:S(2)}) collective-permute-start(f32[2,64,1,256]{3,2,1,0:T(1,128)} %get-tuple-element.23), channel_id=1, source_target_pairs={{0,1},{1,2},{2,3},{3,4},{4,5},{5,6},{6,7},{7,8},{8,9},{9,10},{10,1... | collective-permute-start | bytes 393224 | tf_op jit(solution)/shard_map/ppermute | solution.py:23
  147.2 6.7 %collective-permute-start.15 = (f32[2,64,1,256]{3,2,1,0:T(1,128)S(1)}, f32[2,64,1,256]{3,2,1,0:T(1,128)S(1)}, u32[]{:S(2)}, u32[]{:S(2)}) collective-permute-start(f32[2,64,1,256]{3,2,1,0:T(1,128)S(1)} %get-tuple-element.20), channel_id=1, source_target_pairs={{1,0},{2,1},{3,2},{4,3},{5,4},{6,5},{7,6},{8,7},{9,8},{10,9},{11,1... | collective-permute-start | bytes 393224 | tf_op jit(solution)/shard_map/ppermute | solution.py:24
  151.1 5.2 %collective-permute-start.14 = (f32[2,64,1,256]{3,2,1,0:T(1,128)S(1)}, f32[2,64,1,256]{3,2,1,0:T(1,128)S(1)}, u32[]{:S(2)}, u32[]{:S(2)}) collective-permute-start(f32[2,64,1,256]{3,2,1,0:T(1,128)S(1)} %get-tuple-element.21), channel_id=1, source_target_pairs={{0,1},{1,2},{2,3},{3,4},{4,5},{5,6},{6,7},{7,8},{8,9},{9,10},{10,1... | collective-permute-start | bytes 393224 | tf_op jit(solution)/shard_map/ppermute | solution.py:23
  153.9 7.5 %copy-start.28 = (f32[2,64,8,256]{3,2,1,0:T(8,128)S(1)}, f32[2,64,8,256]{3,2,1,0:T(8,128)}, u32[]{:S(2)}) copy-start(f32[2,64,8,256]{3,2,1,0:T(8,128)} %shard_map.73) | copy-start | bytes 3145732
  165.0 21.2 %collective-permute-start.16 = (f32[2,32,8,256]{3,2,1,0:T(8,128)S(1)}, f32[2,32,8,256]{3,2,1,0:T(8,128)S(1)}, u32[]{:S(2)}, u32[]{:S(2)}) collective-permute-start(f32[2,32,8,256]{3,2,1,0:T(8,128)S(1)} %get-tuple-element.5), channel_id=1, source_target_pairs={{0,16},{1,17},{2,18},{3,19},{4,20},{5,21},{6,22},{7,23},{8,24},{9,... | collective-permute-start | bytes 1572872 | tf_op jit(solution)/shard_map/ppermute | solution.py:296
  166.3 18.6 %collective-permute-start.18 = (f32[2,32,1,256]{3,2,1,0:T(1,128)S(1)}, f32[2,32,1,256]{3,2,1,0:T(1,128)S(1)}, u32[]{:S(2)}, u32[]{:S(2)}) collective-permute-start(f32[2,32,1,256]{3,2,1,0:T(1,128)S(1)} %get-tuple-element.33), channel_id=1, source_target_pairs={{1,16},{2,17},{3,18},{4,19},{5,20},{6,21},{7,22},{8,23},{9,24},{10... | collective-permute-start | bytes 196616 | tf_op jit(solution)/shard_map/ppermute | solution.py:298
  167.7 17.9 %collective-permute-start.17 = (f32[2,32,1,256]{3,2,1,0:T(1,128)S(1)}, f32[2,32,1,256]{3,2,1,0:T(1,128)S(1)}, u32[]{:S(2)}, u32[]{:S(2)}) collective-permute-start(f32[2,32,1,256]{3,2,1,0:T(1,128)S(1)} %get-tuple-element.34), channel_id=1, source_target_pairs={{0,17},{1,18},{2,19},{3,20},{4,21},{5,22},{6,23},{7,24},{8,25},{9,... | collective-permute-start | bytes 196616 | tf_op jit(solution)/shard_map/ppermute | solution.py:297
  (53 other events, 131.3 us)

commit v3 on v0

--- a/solution.py
+++ b/solution.py
@@ -57,8 +57,9 @@
         + (northward - 2.0 * middle + southward)
     )
     vertical = v_spread * (upward - 2.0 * middle + downward) / (z_spacing * z_spacing)
-    reaction = coupling[:, 0].reshape(-1, 1, 1, 1) * middle[..., 0:1, :, :, :]
-    reaction = reaction + coupling[:, 1].reshape(-1, 1, 1, 1) * middle[..., 1:2, :, :, :]
+    own = jnp.stack([coupling[0, 0], coupling[1, 1]]).reshape(-1, 1, 1, 1)
+    other = jnp.stack([coupling[0, 1], coupling[1, 0]]).reshape(-1, 1, 1, 1)
+    reaction = own * middle + other * middle[::-1]
     return diffusion + vertical - advection + reaction
 
 
@@ -127,9 +128,16 @@
         )
 
     coarse_first = shrink(initial)
-    (init_b, first_b), (init_a, first_a) = exchange(
-        (hi(initial), hi(coarse_first)), (lo(initial), lo(coarse_first))
-    )
+    levels = initial.shape[-3]
+
+    def joined(fine, coarse):
+        return jnp.concatenate([fine, coarse], axis=-3)
+
+    before, after = exchange(
+        joined(hi(initial), hi(coarse_first)), joined(lo(initial), lo(coarse_first))
+    )
+    init_b, first_b = before[..., :levels, :, :], before[..., levels:, :, :]
+    init_a, first_a = after[..., :levels, :, :], after[..., levels:, :, :]
     halo_zero = (init_b, init_a)
     halo_first = (first_b, first_a)
     first_rate = fine_rate(initial, halo_zero)

time: 159 us -> 151 us (0.950)
  starting transfers between devices: 53.1 us -> 46.6 us
  other arithmetic: 44.5 us -> 48.7 us
  local copies, waits for them, and re-layouts: 31.9 us -> 28.7 us
  waiting for transfers between devices: 27.3 us -> 24.3 us
    mul x13 -> x0, local copies, waits for them, and re-layouts: 8.53 us -> none  [tendency(): reaction = coupling[:, 0].reshape(-1, 1, 1, 1) * middle[..., 0:1, :, :, :]]
    slice x10, local copies, waits for them, and re-layouts: 0.48 us -> 5.57 us  [pair_sum(): jnp.roll(field, 1, axis=-2)]
    add x2, other arithmetic: 14.6 us -> 10.2 us  [first_node(): node_zero + half_step * (rate_zero - s0)]
    slice x9 -> x7, local copies, waits for them, and re-layouts: 5.57 us -> 1.43 us  [lo(): return field[..., :width, :]]
    ppermute x8 -> x7, starting transfers between devices: 23 us -> 19.7 us  [exchange(): before = lax.ppermute(to_right, 'space', shift_pairs(count, 1))]
    slice x1 -> x5, local copies, waits for them, and re-layouts: 0.96 us -> 4.26 us  [the longest x2 1.84 us: body(): init_a, first_a = (after[..., :levels, :, :], after[..., levels:, :, :])]
    ppermute x8 -> x7, starting transfers between devices: 26.2 us -> 23 us  [exchange(): after = lax.ppermute(to_left, 'space', shift_pairs(count, -1))]
    broadcast_in_dim x16, local copies, waits for them, and re-layouts: 5.83 us -> 8.81 us  [expand_z(): return jnp.repeat(field, 2, axis=-3)]
  transfers between devices with their start and end apart: 19 -> 17, of which waited for: 9 -> 9; matrix products, arithmetic and copies ran while one was open for 18% -> 17% of each run, Pallas kernels for 0% -> 0%
where the time goes in v3:
time: 151 us; the launch traced here: 149 us
  other arithmetic  48.7 us (32%)
  starting transfers between devices  46.6 us (31%)
  local copies, waits for them, and re-layouts  28.7 us (19%)
  waiting for transfers between devices  24.3 us (16%)
    ppermute x7, starting transfers between devices, exchange(): after = lax.ppermute(to_left, 'space', shift_pairs(count, -1))  23 us
    ppermute x7, starting transfers between devices, exchange(): before = lax.ppermute(to_right, 'space', shift_pairs(count, 1))  19.7 us
    ppermute x1, waiting for transfers between devices, body(): passed_b = lax.ppermute(hi(after), ('tm', 'space'), to_east)  14.4 us
    add x2, other arithmetic, first_node(): node_zero + half_step * (rate_zero - s0)  10.2 us
    broadcast_in_dim x16, local copies, waits for them, and re-layouts, expand_z(): return jnp.repeat(field, 2, axis=-3)  8.81 us
    ppermute x7, waiting for transfers between devices, exchange(): before = lax.ppermute(to_right, 'space', shift_pairs(count, 1))  7.53 us
    slice x10, local copies, waits for them, and re-layouts, pair_sum(): jnp.roll(field, 1, axis=-2)  5.57 us
    mul x4, other arithmetic, shrink(): return pair_sum(levels) * 0.25  4.52 us
  transfers between devices with their start and end apart: 17, of which 9 were waited for; matrix products, arithmetic and copies ran while one was open for 17% of the time, Pallas kernels for 0%

profile of v3, /device:TPU:11, one launch (start us, length us, event | category | flops | bytes accessed | tf_op | source)
XLA Modules:
  0.0 149.4 jit_solution(7976480369965390330)
XLA Ops:
  4.7 2.6 %collective-permute-start = (f32[2,96,1,256]{3,2,1,0:T(1,128)}, f32[2,96,1,256]{3,2,1,0:T(1,128)}, u32[]{:S(2)}, u32[]{:S(2)}) collective-permute-start(f32[2,96,1,256]{3,2,1,0:T(1,128)} %pad_maximum_fusion.34), channel_id=1, source_target_pairs={{1,0},{2,1},{3,2},{4,3},{5,4},{6,5},{7,6},{8,7},{9,8},{10,9},{11,1... | collective-permute-start | bytes 589832 | tf_op jit(solution)/shard_map/ppermute | solution.py:20
  8.2 3.0 %collective-permute-start.1 = (f32[2,96,1,256]{3,2,1,0:T(1,128)}, f32[2,96,1,256]{3,2,1,0:T(1,128)}, u32[]{:S(2)}, u32[]{:S(2)}) collective-permute-start(f32[2,96,1,256]{3,2,1,0:T(1,128)} %pad_maximum_fusion.35), channel_id=1, source_target_pairs={{0,1},{1,2},{2,3},{3,4},{4,5},{5,6},{6,7},{7,8},{8,9},{9,10},{10,1... | collective-permute-start | bytes 589832 | tf_op jit(solution)/shard_map/ppermute | solution.py:19
  17.0 2.5 %broadcast_multiply_fusion.2 = (f32[2]{0:T(128)S(1)}, f32[2]{0:T(128)S(1)}, f32[2]{0:T(128)S(1)}, f32[2]{0:T(128)S(1)}) fusion(f32[1]{0:T(128)} %bitcast.3, f32[1]{0:T(128)} %bitcast.2, f32[1]{0:T(128)} %bitcast.1, f32[1]{0:T(128)} %bitcast), kind=kLoop, calls=%fused_computation.248 | loop fusion | flops 8 | bytes 48 | tf_op jit(solution)/shard_map/mul | solution.py:62
  19.5 1.9 %fusion.67 = (f32[32,8,256]{2,1,0:T(8,128)S(1)}, f32[32,8,256]{2,1,0:T(8,128)S(1)}, f32[32,8,256]{2,1,0:T(8,128)S(1)}) fusion(f32[32,1,256]{2,1,0:T(1,128)} %get-tuple-element.92, f32[32,7,256]{2,1,0:T(8,128)} %get-tuple-element.94, f32[32,7,256]{2,1,0:T(8,128)} %get-tuple-element.93, f32[32,1,256]{2,1,0:T(1,128)} %get-tuple-element.91, ...), kind=kLoop, calls=%fused_computation.180 | loop fusion | flops 1179648 | bytes 3407944 | tf_op jit(solution)/shard_map/mul | solution.py:76
  26.4 1.9 %collective-permute-start.2 = (f32[2,64,1,256]{3,2,1,0:T(1,128)S(1)}, f32[2,64,1,256]{3,2,1,0:T(1,128)S(1)}, u32[]{:S(2)}, u32[]{:S(2)}) collective-permute-start(f32[2,64,1,256]{3,2,1,0:T(1,128)S(1)} %get-tuple-element.49), channel_id=1, source_target_pairs={{1,0},{2,1},{3,2},{4,3},{5,4},{6,5},{7,6},{8,7},{9,8},{10,9},{11,1... | collective-permute-start | bytes 393224 | tf_op jit(solution)/shard_map/ppermute | solution.py:20
  28.4 3.6 %collective-permute-start.3 = (f32[2,64,1,256]{3,2,1,0:T(1,128)S(1)}, f32[2,64,1,256]{3,2,1,0:T(1,128)S(1)}, u32[]{:S(2)}, u32[]{:S(2)}) collective-permute-start(f32[2,64,1,256]{3,2,1,0:T(1,128)S(1)} %get-tuple-element.50), channel_id=1, source_target_pairs={{0,1},{1,2},{2,3},{3,4},{4,5},{5,6},{6,7},{7,8},{8,9},{9,10},{10,1... | collective-permute-start | bytes 393224 | tf_op jit(solution)/shard_map/ppermute | solution.py:19
  37.2 4.6 %collective-permute-start.4 = (f32[2,64,2,256]{3,2,1,0:T(2,128)S(1)}, f32[2,64,2,256]{3,2,1,0:T(2,128)S(1)}, u32[]{:S(2)}, u32[]{:S(2)}) collective-permute-start(f32[2,64,2,256]{3,2,1,0:T(2,128)S(1)} %get-tuple-element.48), channel_id=1, source_target_pairs={{1,0},{2,1},{3,2},{4,3},{5,4},{6,5},{7,6},{8,7},{9,8},{10,9},{11,1... | collective-permute-start | bytes 786440 | tf_op jit(solution)/shard_map/ppermute | solution.py:20
  41.8 1.9 %collective-permute-start.5 = (f32[2,64,2,256]{3,2,1,0:T(2,128)S(1)}, f32[2,64,2,256]{3,2,1,0:T(2,128)S(1)}, u32[]{:S(2)}, u32[]{:S(2)}) collective-permute-start(f32[2,64,2,256]{3,2,1,0:T(2,128)S(1)} %get-tuple-element.47), channel_id=1, source_target_pairs={{0,1},{1,2},{2,3},{3,4},{4,5},{5,6},{6,7},{7,8},{8,9},{9,10},{10,1... | collective-permute-start | bytes 786440 | tf_op jit(solution)/shard_map/ppermute | solution.py:19
  43.9 1.7 %collective-permute-done.4 = f32[2,64,2,256]{3,2,1,0:T(2,128)S(1)} collective-permute-done((f32[2,64,2,256]{3,2,1,0:T(2,128)S(1)}, f32[2,64,2,256]{3,2,1,0:T(2,128)S(1)}, u32[]{:S(2)}, u32[]{:S(2)}) %collective-permute-start.4) | collective-permute-done | bytes 262176 | tf_op jit(solution)/shard_map/ppermute | solution.py:20
  45.7 3.4 %collective-permute-done.5 = f32[2,64,2,256]{3,2,1,0:T(2,128)S(1)} collective-permute-done((f32[2,64,2,256]{3,2,1,0:T(2,128)S(1)}, f32[2,64,2,256]{3,2,1,0:T(2,128)S(1)}, u32[]{:S(2)}, u32[]{:S(2)}) %collective-permute-start.5) | collective-permute-done | bytes 262176 | tf_op jit(solution)/shard_map/ppermute | solution.py:19
  51.8 2.0 %fusion.90 = (f32[2,32,8,256]{3,2,1,0:T(8,128)S(1)}, f32[2,32,8,256]{3,2,1,0:T(8,128)S(1)}, f32[2,32,8,256]{3,2,1,0:T(8,128)}) fusion(f32[2,32,8,256]{3,2,1,0:T(8,128)S(1)} %copy-done.5, f32[2,32,7,256]{3,2,1,0:T(8,128)S(1)} %get-tuple-element.76, f32[2,32,1,256]{3,2,1,0:T(1,128)S(1)} %get-tuple-element.78, f32[2,32,1,256]{3,2,1,0:T(1,128)S(1)} %get-tuple-element.77, ...), kind=kLoop, calls=%fused_computation.261 | loop fusion | flops 5505024 | bytes 5898328 | tf_op jit(solution)/shard_map/add | solution.py:164
  53.9 3.2 %collective-permute-start.6 = (f32[2,32,1,256]{3,2,1,0:T(1,128)S(1)}, f32[2,32,1,256]{3,2,1,0:T(1,128)S(1)}, u32[]{:S(2)}, u32[]{:S(2)}) collective-permute-start(f32[2,32,1,256]{3,2,1,0:T(1,128)S(1)} %get-tuple-element.73), channel_id=1, source_target_pairs={{1,0},{2,1},{3,2},{4,3},{5,4},{6,5},{7,6},{8,7},{9,8},{10,9},{11,1... | collective-permute-start | bytes 196616 | tf_op jit(solution)/shard_map/ppermute | solution.py:20
  57.1 3.1 %collective-permute-start.7 = (f32[2,32,1,256]{3,2,1,0:T(1,128)S(1)}, f32[2,32,1,256]{3,2,1,0:T(1,128)S(1)}, u32[]{:S(2)}, u32[]{:S(2)}) collective-permute-start(f32[2,32,1,256]{3,2,1,0:T(1,128)S(1)} %get-tuple-element.74), channel_id=1, source_target_pairs={{0,1},{1,2},{2,3},{3,4},{4,5},{5,6},{6,7},{7,8},{8,9},{9,10},{10,1... | collective-permute-start | bytes 196616 | tf_op jit(solution)/shard_map/ppermute | solution.py:19
  66.0 4.0 %collective-permute-start.8 = (f32[2,32,1,256]{3,2,1,0:T(1,128)S(1)}, f32[2,32,1,256]{3,2,1,0:T(1,128)S(1)}, u32[]{:S(2)}, u32[]{:S(2)}) collective-permute-start(f32[2,32,1,256]{3,2,1,0:T(1,128)S(1)} %get-tuple-element.67), channel_id=1, source_target_pairs={{1,0},{2,1},{3,2},{4,3},{5,4},{6,5},{7,6},{8,7},{9,8},{10,9},{11,1... | collective-permute-start | bytes 196616 | tf_op jit(solution)/shard_map/ppermute | solution.py:20
  70.0 2.4 %collective-permute-start.9 = (f32[2,32,1,256]{3,2,1,0:T(1,128)}, f32[2,32,1,256]{3,2,1,0:T(1,128)S(1)}, u32[]{:S(2)}, u32[]{:S(2)}) collective-permute-start(f32[2,32,1,256]{3,2,1,0:T(1,128)} %get-tuple-element.68), channel_id=1, source_target_pairs={{0,1},{1,2},{2,3},{3,4},{4,5},{5,6},{6,7},{7,8},{8,9},{9,10},{10,1... | collective-permute-start | bytes 196616 | tf_op jit(solution)/shard_map/ppermute | solution.py:19
  85.9 1.8 %broadcast_in_dim.58 = f32[2,64,1,256]{3,2,1,0:T(1,128)} reshape(f32[2,32,2,256]{3,2,1,0:T(2,128)} %broadcast_in_dim.57) | data formatting | bytes 262144 | tf_op jit(solution)/shard_map/broadcast_in_dim | solution.py:84
  93.2 8.5 %multiply_add_fusion.1 = (f32[2,64,8,256]{3,2,1,0:T(8,128)S(1)}, f32[2,64,8,256]{3,2,1,0:T(8,128)S(1)}, f32[2,64,8,256]{3,2,1,0:T(8,128)S(1)}, f32[2,64,8,256]{3,2,1,0:T(8,128)S(1)}, f32[2,64,8,256]{3,2,1,0:T(8,128)S(1)}) fusion(f32[2,64,8,256]{3,2,1,0:T(8,128)S(1)} %copy-done.8, f32[2,64,8,256]{3,2,1,0:T(8,128)} %add.759, f32[2]{0:T(128)S(1)} %get-tuple-element.33, ...), kind=kLoop, calls=%fused_computation.44 | loop fusion | flops 27787264 | bytes 12582928 | tf_op jit(solution)/shard_map/add | solution.py:118
  101.9 2.1 %collective-permute-start.10 = (f32[2,64,1,256]{3,2,1,0:T(1,128)S(1)}, f32[2,64,1,256]{3,2,1,0:T(1,128)S(1)}, u32[]{:S(2)}, u32[]{:S(2)}) collective-permute-start(f32[2,64,1,256]{3,2,1,0:T(1,128)S(1)} %get-tuple-element.42), channel_id=1, source_target_pairs={{1,0},{2,1},{3,2},{4,3},{5,4},{6,5},{7,6},{8,7},{9,8},{10,9},{11,1... | collective-permute-start | bytes 393224 | tf_op jit(solution)/shard_map/ppermute | solution.py:20
  104.1 3.4 %collective-permute-start.11 = (f32[2,64,1,256]{3,2,1,0:T(1,128)S(1)}, f32[2,64,1,256]{3,2,1,0:T(1,128)S(1)}, u32[]{:S(2)}, u32[]{:S(2)}) collective-permute-start(f32[2,64,1,256]{3,2,1,0:T(1,128)S(1)} %get-tuple-element.43), channel_id=1, source_target_pairs={{0,1},{1,2},{2,3},{3,4},{4,5},{5,6},{6,7},{7,8},{8,9},{9,10},{10,1... | collective-permute-start | bytes 393224 | tf_op jit(solution)/shard_map/ppermute | solution.py:19
  110.7 1.7 %multiply_add_fusion = (f32[2,64,8,256]{3,2,1,0:T(8,128)S(1)}, f32[2,64,8,256]{3,2,1,0:T(8,128)S(1)}) fusion(f32[2,64,8,256]{3,2,1,0:T(8,128)S(1)} %get-tuple-element.15, f32[2,64,8,256]{3,2,1,0:T(8,128)S(1)} %get-tuple-element.14, f32[2,64,8,256]{3,2,1,0:T(8,128)S(1)} %get-tuple-element.11, f32[2,64,8,256]{3,2,1,0:T(8,128)S(1)} %get-tuple-element.12, ...), kind=kLoop, calls=%fused_computation.40 | loop fusion | flops 8912896 | bytes 8650768 | tf_op jit(solution)/shard_map/add | solution.py:125
  112.7 4.6 %collective-permute-start.12 = (f32[2,64,1,256]{3,2,1,0:T(1,128)S(1)}, f32[2,64,1,256]{3,2,1,0:T(1,128)S(1)}, u32[]{:S(2)}, u32[]{:S(2)}) collective-permute-start(f32[2,64,1,256]{3,2,1,0:T(1,128)S(1)} %get-tuple-element.41), channel_id=1, source_target_pairs={{1,0},{2,1},{3,2},{4,3},{5,4},{6,5},{7,6},{8,7},{9,8},{10,9},{11,1... | collective-permute-start | bytes 393224 | tf_op jit(solution)/shard_map/ppermute | solution.py:20
  117.3 2.1 %collective-permute-start.13 = (f32[2,64,1,256]{3,2,1,0:T(1,128)S(1)}, f32[2,64,1,256]{3,2,1,0:T(1,128)S(1)}, u32[]{:S(2)}, u32[]{:S(2)}) collective-permute-start(f32[2,64,1,256]{3,2,1,0:T(1,128)S(1)} %get-tuple-element.40), channel_id=1, source_target_pairs={{0,1},{1,2},{2,3},{3,4},{4,5},{5,6},{6,7},{7,8},{8,9},{9,10},{10,1... | collective-permute-start | bytes 393224 | tf_op jit(solution)/shard_map/ppermute | solution.py:19
  119.7 2.2 %collective-permute-done.13 = f32[2,64,1,256]{3,2,1,0:T(1,128)S(1)} collective-permute-done((f32[2,64,1,256]{3,2,1,0:T(1,128)S(1)}, f32[2,64,1,256]{3,2,1,0:T(1,128)S(1)}, u32[]{:S(2)}, u32[]{:S(2)}) %collective-permute-start.13) | collective-permute-done | bytes 131104 | tf_op jit(solution)/shard_map/ppermute | solution.py:19
  130.2 14.4 %collective-permute-done.16 = f32[2,32,1,256]{3,2,1,0:T(1,128)S(1)} collective-permute-done((f32[2,32,1,256]{3,2,1,0:T(1,128)S(1)}, f32[2,32,1,256]{3,2,1,0:T(1,128)S(1)}, u32[]{:S(2)}, u32[]{:S(2)}) %collective-permute-start.16) | collective-permute-done | bytes 65568 | tf_op jit(solution)/shard_map/ppermute | solution.py:233
  (222 shorter events, 65.5 us)
Async XLA Ops:
  4.7 17.9 %collective-permute-start = (f32[2,96,1,256]{3,2,1,0:T(1,128)}, f32[2,96,1,256]{3,2,1,0:T(1,128)}, u32[]{:S(2)}, u32[]{:S(2)}) collective-permute-start(f32[2,96,1,256]{3,2,1,0:T(1,128)} %pad_maximum_fusion.34), channel_id=1, source_target_pairs={{1,0},{2,1},{3,2},{4,3},{5,4},{6,5},{7,6},{8,7},{9,8},{10,9},{11,1... | collective-permute-start | bytes 589832 | tf_op jit(solution)/shard_map/ppermute | solution.py:20
  8.2 15.4 %collective-permute-start.1 = (f32[2,96,1,256]{3,2,1,0:T(1,128)}, f32[2,96,1,256]{3,2,1,0:T(1,128)}, u32[]{:S(2)}, u32[]{:S(2)}) collective-permute-start(f32[2,96,1,256]{3,2,1,0:T(1,128)} %pad_maximum_fusion.35), channel_id=1, source_target_pairs={{0,1},{1,2},{2,3},{3,4},{4,5},{5,6},{6,7},{7,8},{8,9},{9,10},{10,1... | collective-permute-start | bytes 589832 | tf_op jit(solution)/shard_map/ppermute | solution.py:19
  19.5 31.4 %copy-start.41 = (f32[2]{0:T(128)}, f32[2]{0:T(128)S(1)}, u32[]{:S(2)}) copy-start(f32[2]{0:T(128)S(1)} %get-tuple-element.32) | copy-start | bytes 28
  19.5 31.4 %copy-start.43 = (f32[2]{0:T(128)}, f32[2]{0:T(128)S(1)}, u32[]{:S(2)}) copy-start(f32[2]{0:T(128)S(1)} %get-tuple-element.126) | copy-start | bytes 28
  21.4 40.1 %copy-start.9 = (f32[32,8,256]{2,1,0:T(8,128)}, f32[32,8,256]{2,1,0:T(8,128)S(1)}, u32[]{:S(2)}) copy-start(f32[32,8,256]{2,1,0:T(8,128)S(1)} %get-tuple-element.118) | copy-start | bytes 786436
  21.4 40.1 %copy-start.11 = (f32[32,8,256]{2,1,0:T(8,128)}, f32[32,8,256]{2,1,0:T(8,128)S(1)}, u32[]{:S(2)}) copy-start(f32[32,8,256]{2,1,0:T(8,128)S(1)} %get-tuple-element.119) | copy-start | bytes 786436
  26.4 7.5 %collective-permute-start.2 = (f32[2,64,1,256]{3,2,1,0:T(1,128)S(1)}, f32[2,64,1,256]{3,2,1,0:T(1,128)S(1)}, u32[]{:S(2)}, u32[]{:S(2)}) collective-permute-start(f32[2,64,1,256]{3,2,1,0:T(1,128)S(1)} %get-tuple-element.49), channel_id=1, source_target_pairs={{1,0},{2,1},{3,2},{4,3},{5,4},{6,5},{7,6},{8,7},{9,8},{10,9},{11,1... | collective-permute-start | bytes 393224 | tf_op jit(solution)/shard_map/ppermute | solution.py:20
  28.4 6.8 %collective-permute-start.3 = (f32[2,64,1,256]{3,2,1,0:T(1,128)S(1)}, f32[2,64,1,256]{3,2,1,0:T(1,128)S(1)}, u32[]{:S(2)}, u32[]{:S(2)}) collective-permute-start(f32[2,64,1,256]{3,2,1,0:T(1,128)S(1)} %get-tuple-element.50), channel_id=1, source_target_pairs={{0,1},{1,2},{2,3},{3,4},{4,5},{5,6},{6,7},{7,8},{8,9},{9,10},{10,1... | collective-permute-start | bytes 393224 | tf_op jit(solution)/shard_map/ppermute | solution.py:19
  32.2 29.3 %copy-start.13 = (f32[32,8,256]{2,1,0:T(8,128)}, f32[32,8,256]{2,1,0:T(8,128)S(1)}, u32[]{:S(2)}) copy-start(f32[32,8,256]{2,1,0:T(8,128)S(1)} %fusion.73) | copy-start | bytes 786436
  37.2 8.4 %collective-permute-start.4 = (f32[2,64,2,256]{3,2,1,0:T(2,128)S(1)}, f32[2,64,2,256]{3,2,1,0:T(2,128)S(1)}, u32[]{:S(2)}, u32[]{:S(2)}) collective-permute-start(f32[2,64,2,256]{3,2,1,0:T(2,128)S(1)} %get-tuple-element.48), channel_id=1, source_target_pairs={{1,0},{2,1},{3,2},{4,3},{5,4},{6,5},{7,6},{8,7},{9,8},{10,9},{11,1... | collective-permute-start | bytes 786440 | tf_op jit(solution)/shard_map/ppermute | solution.py:20
  41.8 7.3 %collective-permute-start.5 = (f32[2,64,2,256]{3,2,1,0:T(2,128)S(1)}, f32[2,64,2,256]{3,2,1,0:T(2,128)S(1)}, u32[]{:S(2)}, u32[]{:S(2)}) collective-permute-start(f32[2,64,2,256]{3,2,1,0:T(2,128)S(1)} %get-tuple-element.47), channel_id=1, source_target_pairs={{0,1},{1,2},{2,3},{3,4},{4,5},{5,6},{6,7},{7,8},{8,9},{9,10},{10,1... | collective-permute-start | bytes 786440 | tf_op jit(solution)/shard_map/ppermute | solution.py:19
  45.6 14.6 %copy-start.24 = (f32[2,64,2,256]{3,2,1,0:T(2,128)}, f32[2,64,2,256]{3,2,1,0:T(2,128)S(1)}, u32[]{:S(2)}) copy-start(f32[2,64,2,256]{3,2,1,0:T(2,128)S(1)} %collective-permute-done.4) | copy-start | bytes 786436
  53.9 7.4 %collective-permute-start.6 = (f32[2,32,1,256]{3,2,1,0:T(1,128)S(1)}, f32[2,32,1,256]{3,2,1,0:T(1,128)S(1)}, u32[]{:S(2)}, u32[]{:S(2)}) collective-permute-start(f32[2,32,1,256]{3,2,1,0:T(1,128)S(1)} %get-tuple-element.73), channel_id=1, source_target_pairs={{1,0},{2,1},{3,2},{4,3},{5,4},{6,5},{7,6},{8,7},{9,8},{10,9},{11,1... | collective-permute-start | bytes 196616 | tf_op jit(solution)/shard_map/ppermute | solution.py:20
  57.1 4.4 %collective-permute-start.7 = (f32[2,32,1,256]{3,2,1,0:T(1,128)S(1)}, f32[2,32,1,256]{3,2,1,0:T(1,128)S(1)}, u32[]{:S(2)}, u32[]{:S(2)}) collective-permute-start(f32[2,32,1,256]{3,2,1,0:T(1,128)S(1)} %get-tuple-element.74), channel_id=1, source_target_pairs={{0,1},{1,2},{2,3},{3,4},{4,5},{5,6},{6,7},{7,8},{8,9},{9,10},{10,1... | collective-permute-start | bytes 196616 | tf_op jit(solution)/shard_map/ppermute | solution.py:19
  66.0 9.0 %collective-permute-start.8 = (f32[2,32,1,256]{3,2,1,0:T(1,128)S(1)}, f32[2,32,1,256]{3,2,1,0:T(1,128)S(1)}, u32[]{:S(2)}, u32[]{:S(2)}) collective-permute-start(f32[2,32,1,256]{3,2,1,0:T(1,128)S(1)} %get-tuple-element.67), channel_id=1, source_target_pairs={{1,0},{2,1},{3,2},{4,3},{5,4},{6,5},{7,6},{8,7},{9,8},{10,9},{11,1... | collective-permute-start | bytes 196616 | tf_op jit(solution)/shard_map/ppermute | solution.py:20
  70.0 7.8 %collective-permute-start.9 = (f32[2,32,1,256]{3,2,1,0:T(1,128)}, f32[2,32,1,256]{3,2,1,0:T(1,128)S(1)}, u32[]{:S(2)}, u32[]{:S(2)}) collective-permute-start(f32[2,32,1,256]{3,2,1,0:T(1,128)} %get-tuple-element.68), channel_id=1, source_target_pairs={{0,1},{1,2},{2,3},{3,4},{4,5},{5,6},{6,7},{7,8},{8,9},{9,10},{10,1... | collective-permute-start | bytes 196616 | tf_op jit(solution)/shard_map/ppermute | solution.py:19
  93.2 14.3 %copy-start.25 = (f32[2,64,2,256]{3,2,1,0:T(2,128)S(1)}, f32[2,64,2,256]{3,2,1,0:T(2,128)}, u32[]{:S(2)}) copy-start(f32[2,64,2,256]{3,2,1,0:T(2,128)} %copy-done.24) | copy-start | bytes 786436
  101.9 8.3 %collective-permute-start.10 = (f32[2,64,1,256]{3,2,1,0:T(1,128)S(1)}, f32[2,64,1,256]{3,2,1,0:T(1,128)S(1)}, u32[]{:S(2)}, u32[]{:S(2)}) collective-permute-start(f32[2,64,1,256]{3,2,1,0:T(1,128)S(1)} %get-tuple-element.42), channel_id=1, source_target_pairs={{1,0},{2,1},{3,2},{4,3},{5,4},{6,5},{7,6},{8,7},{9,8},{10,9},{11,1... | collective-permute-start | bytes 393224 | tf_op jit(solution)/shard_map/ppermute | solution.py:20
  104.1 6.6 %collective-permute-start.11 = (f32[2,64,1,256]{3,2,1,0:T(1,128)S(1)}, f32[2,64,1,256]{3,2,1,0:T(1,128)S(1)}, u32[]{:S(2)}, u32[]{:S(2)}) collective-permute-start(f32[2,64,1,256]{3,2,1,0:T(1,128)S(1)} %get-tuple-element.43), channel_id=1, source_target_pairs={{0,1},{1,2},{2,3},{3,4},{4,5},{5,6},{6,7},{7,8},{8,9},{9,10},{10,1... | collective-permute-start | bytes 393224 | tf_op jit(solution)/shard_map/ppermute | solution.py:19
  112.7 7.0 %collective-permute-start.12 = (f32[2,64,1,256]{3,2,1,0:T(1,128)S(1)}, f32[2,64,1,256]{3,2,1,0:T(1,128)S(1)}, u32[]{:S(2)}, u32[]{:S(2)}) collective-permute-start(f32[2,64,1,256]{3,2,1,0:T(1,128)S(1)} %get-tuple-element.41), channel_id=1, source_target_pairs={{1,0},{2,1},{3,2},{4,3},{5,4},{6,5},{7,6},{8,7},{9,8},{10,9},{11,1... | collective-permute-start | bytes 393224 | tf_op jit(solution)/shard_map/ppermute | solution.py:20
  117.3 4.6 %collective-permute-start.13 = (f32[2,64,1,256]{3,2,1,0:T(1,128)S(1)}, f32[2,64,1,256]{3,2,1,0:T(1,128)S(1)}, u32[]{:S(2)}, u32[]{:S(2)}) collective-permute-start(f32[2,64,1,256]{3,2,1,0:T(1,128)S(1)} %get-tuple-element.40), channel_id=1, source_target_pairs={{0,1},{1,2},{2,3},{3,4},{4,5},{5,6},{6,7},{7,8},{8,9},{9,10},{10,1... | collective-permute-start | bytes 393224 | tf_op jit(solution)/shard_map/ppermute | solution.py:19
  126.2 20.7 %collective-permute-start.14 = (f32[2,32,8,256]{3,2,1,0:T(8,128)S(1)}, f32[2,32,8,256]{3,2,1,0:T(8,128)S(1)}, u32[]{:S(2)}, u32[]{:S(2)}) collective-permute-start(f32[2,32,8,256]{3,2,1,0:T(8,128)S(1)} %get-tuple-element.5), channel_id=1, source_target_pairs={{0,16},{1,17},{2,18},{3,19},{4,20},{5,21},{6,22},{7,23},{8,24},{9,... | collective-permute-start | bytes 1572872 | tf_op jit(solution)/shard_map/ppermute | solution.py:232
  127.5 17.1 %collective-permute-start.16 = (f32[2,32,1,256]{3,2,1,0:T(1,128)S(1)}, f32[2,32,1,256]{3,2,1,0:T(1,128)S(1)}, u32[]{:S(2)}, u32[]{:S(2)}) collective-permute-start(f32[2,32,1,256]{3,2,1,0:T(1,128)S(1)} %get-tuple-element.53), channel_id=1, source_target_pairs={{0,17},{1,18},{2,19},{3,20},{4,21},{5,22},{6,23},{7,24},{8,25},{9,... | collective-permute-start | bytes 196616 | tf_op jit(solution)/shard_map/ppermute | solution.py:233
  128.9 17.1 %collective-permute-start.15 = (f32[2,32,1,256]{3,2,1,0:T(1,128)S(1)}, f32[2,32,1,256]{3,2,1,0:T(1,128)S(1)}, u32[]{:S(2)}, u32[]{:S(2)}) collective-permute-start(f32[2,32,1,256]{3,2,1,0:T(1,128)S(1)} %get-tuple-element.54), channel_id=1, source_target_pairs={{1,16},{2,17},{3,18},{4,19},{5,20},{6,21},{7,22},{8,23},{9,24},{10... | collective-permute-start | bytes 196616 | tf_op jit(solution)/shard_map/ppermute | solution.py:234
  (39 other events, 144.2 us)

commit v4 on v3

--- a/solution.py
+++ b/solution.py
@@ -133,11 +133,29 @@
     def joined(fine, coarse):
         return jnp.concatenate([fine, coarse], axis=-3)
 
+    coarse_coefs = (coarse_x, coarse_y, coarse_h, coarse_v)
+    coarse_levels = coarse_first.shape[-3]
+
+    def coef_edge(edge):
+        stacked = jnp.stack([edge(c) for c in coarse_coefs])
+        return stacked.reshape((2, -1) + stacked.shape[-2:])
+
     before, after = exchange(
-        joined(hi(initial), hi(coarse_first)), joined(lo(initial), lo(coarse_first))
-    )
-    init_b, first_b = before[..., :levels, :, :], before[..., levels:, :, :]
-    init_a, first_a = after[..., :levels, :, :], after[..., levels:, :, :]
+        joined(joined(hi(initial), hi(coarse_first)), coef_edge(hi)),
+        joined(joined(lo(initial), lo(coarse_first)), coef_edge(lo)),
+    )
+    split = (levels, levels + coarse_levels)
+
+    def parts(received):
+        coefs = received[..., split[1]:, :, :].reshape((4, coarse_levels) + received.shape[-2:])
+        return (
+            received[..., : split[0], :, :],
+            received[..., split[0] : split[1], :, :],
+            tuple(coefs[k] for k in range(4)),
+        )
+
+    init_b, first_b, coefs_b = parts(before)
+    init_a, first_a, coefs_a = parts(after)
     halo_zero = (init_b, init_a)
     halo_first = (first_b, first_a)
     first_rate = fine_rate(initial, halo_zero)
@@ -160,9 +178,30 @@
     chain = [coarse_first]
     chain_halo = [halo_first]
     rate = coarse_first_rate
+    wide = None
     for count in range(slabs):
         after = chain[-1] + slab_step * rate + offset
-        after_halo = halo_of(after)
+        if wide is not None:
+            strip_b, strip_a, offset_b, offset_a = wide
+            rate_b = tendency(strip_b, (jnp.zeros_like(offset_b), lo(chain[-1])), *coefs_b,
+                              coupling, 2.0, 2.0)
+            rate_a = tendency(strip_a, (hi(chain[-1]), jnp.zeros_like(offset_a)), *coefs_a,
+                              coupling, 2.0, 2.0)
+            after_halo = (
+                hi(strip_b) + slab_step * hi(rate_b) + offset_b,
+                lo(strip_a) + slab_step * lo(rate_a) + offset_a,
+            )
+        elif count + 2 == slabs:
+            packed_b, packed_a = exchange(
+                jnp.concatenate([hi(after, 3), hi(offset)], axis=-2),
+                jnp.concatenate([lo(after, 3), lo(offset)], axis=-2),
+            )
+            strip_b, offset_b = packed_b[..., :3, :], packed_b[..., 3:, :]
+            strip_a, offset_a = packed_a[..., :3, :], packed_a[..., 3:, :]
+            wide = (strip_b, strip_a, offset_b, offset_a)
+            after_halo = (hi(strip_b), lo(strip_a))
+        else:
+            after_halo = halo_of(after)
         chain.append(after)
         chain_halo.append(after_halo)
         if count + 1 < slabs:

time: 151 us -> 169 us (1.12)
  other arithmetic: 48.7 us -> 67.5 us
  local copies, waits for them, and re-layouts: 28.7 us -> 37 us
  starting transfers between devices: 46.6 us -> 39.1 us
    unnamed x100 -> x154, local copies, waits for them, and re-layouts: 4.37 us -> 12.2 us
    add x2 -> x4, other arithmetic: 3.26 us -> 9.94 us  [the longest x2 6.96 us: tendency(): eastward - 2.0 * middle + westward]
    ppermute x7 -> x6, starting transfers between devices: 23 us -> 16.6 us  [exchange(): after = lax.ppermute(to_left, 'space', shift_pairs(count, -1))]
    slice x10, local copies, waits for them, and re-layouts: 5.57 us -> 0.48 us  [pair_sum(): jnp.roll(field, 1, axis=-2)]
    mul x1, other arithmetic: 1.41 us -> 6.15 us  [body(): fixed_one = node_one + expand((delta_zero + delta_one) * 0.5)]
    mul x2, other arithmetic: 2.32 us -> 6.09 us  [body(): (d0 + d1) * 0.5]
    sub x0 -> x2, other arithmetic: none -> 3.64 us  [body(): halo_earlier_delta = pair_map(lambda y, v: y - v, begins_halo, halo_end)]
    rev x0 -> x2, local copies, waits for them, and re-layouts: none -> 3.39 us  [tendency(): reaction = own * middle + other * middle[::-1]]
  transfers between devices with their start and end apart: 17 -> 15, of which waited for: 9 -> 7; matrix products, arithmetic and copies ran while one was open for 17% -> 20% of each run, Pallas kernels for 0% -> 0%
where the time goes in v4:
time: 169 us; the launch traced here: 168 us
  other arithmetic  67.5 us (40%)
  starting transfers between devices  39.1 us (23%)
  local copies, waits for them, and re-layouts  37 us (22%)
  waiting for transfers between devices  22.7 us (13%)
    ppermute x6, starting transfers between devices, exchange(): before = lax.ppermute(to_right, 'space', shift_pairs(count, 1))  18.6 us
    ppermute x6, starting transfers between devices, exchange(): after = lax.ppermute(to_left, 'space', shift_pairs(count, -1))  16.6 us
    ppermute x1, waiting for transfers between devices, body(): passed_b = lax.ppermute(hi(after), ('tm', 'space'), to_east)  14.4 us
    add x2, other arithmetic, first_node(): node_zero + half_step * (rate_zero - s0)  12.9 us
    unnamed x154, local copies, waits for them, and re-layouts  12.2 us
    add x2, other arithmetic, tendency(): eastward - 2.0 * middle + westward  6.96 us
    ppermute x6, waiting for transfers between devices, exchange(): before = lax.ppermute(to_right, 'space', shift_pairs(count, 1))  6.92 us
    mul x1, other arithmetic, body(): fixed_one = node_one + expand((delta_zero + delta_one) * 0.5)  6.15 us
  transfers between devices with their start and end apart: 15, of which 7 were waited for; matrix products, arithmetic and copies ran while one was open for 20% of the time, Pallas kernels for 0%

profile of v4, /device:TPU:11, one launch (start us, length us, event | category | flops | bytes accessed | tf_op | source)
XLA Modules:
  0.0 167.8 jit_solution(15327620123356709226)
XLA Ops:
  7.2 2.7 %collective-permute-start = (f32[2,160,1,256]{3,2,1,0:T(1,128)}, f32[2,160,1,256]{3,2,1,0:T(1,128)}, u32[]{:S(2)}, u32[]{:S(2)}) collective-permute-start(f32[2,160,1,256]{3,2,1,0:T(1,128)} %pad_maximum_fusion.34), channel_id=1, source_target_pairs={{1,0},{2,1},{3,2},{4,3},{5,4},{6,5},{7,6},{8,7},{9,8},{10,9},{11,1... | collective-permute-start | bytes 983048 | tf_op jit(solution)/shard_map/ppermute | solution.py:20
  11.1 3.0 %collective-permute-start.1 = (f32[2,160,1,256]{3,2,1,0:T(1,128)}, f32[2,160,1,256]{3,2,1,0:T(1,128)}, u32[]{:S(2)}, u32[]{:S(2)}) collective-permute-start(f32[2,160,1,256]{3,2,1,0:T(1,128)} %pad_maximum_fusion.35), channel_id=1, source_target_pairs={{0,1},{1,2},{2,3},{3,4},{4,5},{5,6},{6,7},{7,8},{8,9},{9,10},{10,1... | collective-permute-start | bytes 983048 | tf_op jit(solution)/shard_map/ppermute | solution.py:19
  14.9 2.7 %broadcast_multiply_fusion.2 = (f32[2]{0:T(128)S(1)}, f32[2]{0:T(128)S(1)}, f32[2]{0:T(128)S(1)}, f32[2]{0:T(128)S(1)}) fusion(f32[1]{0:T(128)} %bitcast.13, f32[1]{0:T(128)} %bitcast.12, f32[1]{0:T(128)} %bitcast.11, f32[1]{0:T(128)} %bitcast.10), kind=kLoop, calls=%fused_computation.314 | loop fusion | flops 8 | bytes 48 | tf_op jit(solution)/shard_map/mul | solution.py:62
  22.9 3.7 %collective-permute-start.2 = (f32[2,64,1,256]{3,2,1,0:T(1,128)S(1)}, f32[2,64,1,256]{3,2,1,0:T(1,128)S(1)}, u32[]{:S(2)}, u32[]{:S(2)}) collective-permute-start(f32[2,64,1,256]{3,2,1,0:T(1,128)S(1)} %get-tuple-element.51), channel_id=1, source_target_pairs={{1,0},{2,1},{3,2},{4,3},{5,4},{6,5},{7,6},{8,7},{9,8},{10,9},{11,1... | collective-permute-start | bytes 393224 | tf_op jit(solution)/shard_map/ppermute | solution.py:20
  26.6 2.7 %collective-permute-start.3 = (f32[2,64,1,256]{3,2,1,0:T(1,128)S(1)}, f32[2,64,1,256]{3,2,1,0:T(1,128)S(1)}, u32[]{:S(2)}, u32[]{:S(2)}) collective-permute-start(f32[2,64,1,256]{3,2,1,0:T(1,128)S(1)} %get-tuple-element.52), channel_id=1, source_target_pairs={{0,1},{1,2},{2,3},{3,4},{4,5},{5,6},{6,7},{7,8},{8,9},{9,10},{10,1... | collective-permute-start | bytes 393224 | tf_op jit(solution)/shard_map/ppermute | solution.py:19
  37.8 1.9 %collective-permute-start.4 = (f32[2,64,2,256]{3,2,1,0:T(2,128)S(1)}, f32[2,64,2,256]{3,2,1,0:T(2,128)S(1)}, u32[]{:S(2)}, u32[]{:S(2)}) collective-permute-start(f32[2,64,2,256]{3,2,1,0:T(2,128)S(1)} %get-tuple-element.50), channel_id=1, source_target_pairs={{1,0},{2,1},{3,2},{4,3},{5,4},{6,5},{7,6},{8,7},{9,8},{10,9},{11,1... | collective-permute-start | bytes 786440 | tf_op jit(solution)/shard_map/ppermute | solution.py:20
  39.8 3.6 %collective-permute-start.5 = (f32[2,64,2,256]{3,2,1,0:T(2,128)S(1)}, f32[2,64,2,256]{3,2,1,0:T(2,128)S(1)}, u32[]{:S(2)}, u32[]{:S(2)}) collective-permute-start(f32[2,64,2,256]{3,2,1,0:T(2,128)S(1)} %get-tuple-element.49), channel_id=1, source_target_pairs={{0,1},{1,2},{2,3},{3,4},{4,5},{5,6},{6,7},{7,8},{8,9},{9,10},{10,1... | collective-permute-start | bytes 786440 | tf_op jit(solution)/shard_map/ppermute | solution.py:19
  45.6 3.3 %collective-permute-done.5 = f32[2,64,2,256]{3,2,1,0:T(2,128)S(1)} collective-permute-done((f32[2,64,2,256]{3,2,1,0:T(2,128)S(1)}, f32[2,64,2,256]{3,2,1,0:T(2,128)S(1)}, u32[]{:S(2)}, u32[]{:S(2)}) %collective-permute-start.5) | collective-permute-done | bytes 262176 | tf_op jit(solution)/shard_map/ppermute | solution.py:19
  52.0 2.0 %fusion.102 = (f32[2,32,8,256]{3,2,1,0:T(8,128)S(1)}, f32[2,32,8,256]{3,2,1,0:T(8,128)S(1)}, f32[2,32,8,256]{3,2,1,0:T(8,128)}) fusion(f32[2,32,8,256]{3,2,1,0:T(8,128)S(1)} %copy-done.6, f32[2,32,7,256]{3,2,1,0:T(8,128)S(1)} %get-tuple-element.80, f32[2,32,1,256]{3,2,1,0:T(1,128)S(1)} %get-tuple-element.82, f32[2,32,1,256]{3,2,1,0:T(1,128)S(1)} %get-tuple-element.81, ...), kind=kLoop, calls=%fused_computation.327 | loop fusion | flops 5505024 | bytes 5898328 | tf_op jit(solution)/shard_map/add | solution.py:183
  54.3 3.2 %collective-permute-start.6 = (f32[2,32,4,256]{3,2,1,0:T(4,128)S(1)}, f32[2,32,4,256]{3,2,1,0:T(4,128)}, u32[]{:S(2)}, u32[]{:S(2)}) collective-permute-start(f32[2,32,4,256]{3,2,1,0:T(4,128)S(1)} %pad_maximum_fusion.40), channel_id=1, source_target_pairs={{1,0},{2,1},{3,2},{4,3},{5,4},{6,5},{7,6},{8,7},{9,8},{10,9},{11,1... | collective-permute-start | bytes 786440 | tf_op jit(solution)/shard_map/ppermute | solution.py:20
  58.5 3.3 %collective-permute-start.7 = (f32[2,32,4,256]{3,2,1,0:T(4,128)}, f32[2,32,4,256]{3,2,1,0:T(4,128)}, u32[]{:S(2)}, u32[]{:S(2)}) collective-permute-start(f32[2,32,4,256]{3,2,1,0:T(4,128)} %pad_maximum_fusion.41), channel_id=1, source_target_pairs={{0,1},{1,2},{2,3},{3,4},{4,5},{5,6},{6,7},{7,8},{8,9},{9,10},{10,1... | collective-permute-start | bytes 786440 | tf_op jit(solution)/shard_map/ppermute | solution.py:19
  65.1 3.6 %subtract_add_fusion.1 = (f32[2,32,3,256]{3,2,1,0:T(4,128)S(1)}, f32[2,32,3,256]{3,2,1,0:T(4,128)S(1)}, f32[2,32,3,256]{3,2,1,0:T(4,128)S(1)}, f32[2,32,3,256]{3...) fusion(f32[2,32,3,256]{3,2,1,0:T(4,128)} %bitcast.80, ...), kind=kLoop, calls=%fused_computation.207 | loop fusion | flops 393216 | bytes 2031616 | tf_op jit(solution)/shard_map/add | solution.py:56
  68.7 2.9 %add_multiply_fusion.4 = (f32[2,32,1,256]{3,2,1,0:T(1,128)}, f32[2,32,1,256]{3,2,1,0:T(1,128)}, f32[2,32,1,256]{3,2,1,0:T(1,128)}, f32[2,32,1,256]{3,2,1,0:T(1,128)S(1)}) fusion(f32[2,160,1,256]{3,2,1,0:T(1,128)} %collective-permute-done, f32[2,32,4,256]{3,2,1,0:T(4,128)} %collective-permute-done.6, pred[]{:T(512)S(6)} %eq.78, pred[]{:T(512)S(6)} %eq.77, ...), kind=kLoop, calls=%fused_computation.291 | loop fusion | flops 557056 | bytes 1376276 | tf_op jit(solution)/shard_map/mul | solution.py:223
  76.8 3.4 %subtract_add_fusion = (f32[2,32,3,256]{3,2,1,0:T(4,128)S(1)}, f32[2,32,3,256]{3,2,1,0:T(4,128)S(1)}, f32[2,32,3,256]{3,2,1,0:T(4,128)S(1)}, f32[2,32,3,256]{3,2...) fusion(f32[2,32,3,256]{3,2,1,0:T(4,128)} %bitcast.79, ...), kind=kLoop, calls=%fused_computation.205 | loop fusion | flops 393216 | bytes 2031616 | tf_op jit(solution)/shard_map/add | solution.py:56
  80.2 3.2 %add_multiply_fusion.3 = (f32[2,32,1,256]{3,2,1,0:T(1,128)}, f32[2,32,1,256]{3,2,1,0:T(1,128)}, f32[2,32,1,256]{3,2,1,0:T(1,128)}, f32[2,32,1,256]{3,2,1,0:T(1,128)S(1)}) fusion(f32[2,160,1,256]{3,2,1,0:T(1,128)} %collective-permute-done.1, f32[2,32,4,256]{3,2,1,0:T(4,128)} %collective-permute-done.7, pred[]{:T(512)S(6)} %eq.78, pred[]{:T(512)S(6)} %eq.77, ...), kind=kLoop, calls=%fused_computation.290 | loop fusion | flops 557056 | bytes 1376276 | tf_op jit(solution)/shard_map/mul | solution.py:223
  83.4 1.8 %fusion.99 = (f32[2,32,1,256]{3,2,1,0:T(1,128)S(1)}, f32[2,32,1,256]{3,2,1,0:T(1,128)}) fusion(f32[2,32,1,256]{3,2,1,0:T(1,128)S(1)} %get-tuple-element.19, pred[]{:T(512)S(6)} %eq.78, pred[]{:T(512)S(6)} %eq.77, f32[2,32,1,256]{3,2,1,0:T(1,128)S(1)} %copy-done.36, f32[2,32,1,256]{3,2,1,0:T(1,128)S(1)} %copy-done.35, ...), kind=kLoop, calls=%fused_computation.320 | loop fusion | flops 98304 | bytes 458754 | tf_op jit(solution)/shard_map/sub | solution.py:229
  86.9 6.2 %add_multiply_fusion.2 = (f32[2,32,8,256]{3,2,1,0:T(8,128)}, f32[2,32,8,256]{3,2,1,0:T(8,128)S(1)}, f32[2,32,8,256]{3,2,1,0:T(8,128)S(1)}, f32[2,32,8,256]{3,2,1,0:T(8,128)S(1)}, f32[2,32,8,256]{3,2,1,0:T(8,128)S(1)}) fusion(f32[2,32,8,256]{3,2,1,0:T(8,128)} %copy-done.13, f32[2,32,8,256]{3,2,1,0:T(8,128)} %get-tuple-element.41, pred[]{:T(512)S(6)} %eq.78, ...), kind=kLoop, calls=%fused_computation.165 | loop fusion | flops 6422528 | bytes 7471196 | tf_op jit(solution)/shard_map/mul | solution.py:217
  109.1 11.2 %multiply_add_fusion.1 = (f32[2,64,8,256]{3,2,1,0:T(8,128)S(1)}, f32[2,64,8,256]{3,2,1,0:T(8,128)S(1)}, f32[2,64,8,256]{3,2,1,0:T(8,128)S(1)}, f32[2,64,8,256]{3,2,1,0:T(8,128)S(1)}, f32[2,64,8,256]{3,2,1,0:T(8,128)S(1)}) fusion(f32[2,64,8,256]{3,2,1,0:T(8,128)S(1)} %copy-done.10, f32[2,64,8,256]{3,2,1,0:T(8,128)} %add.851, f32[2]{0:T(128)S(1)} %get-tuple-element.35, ...), kind=kLoop, calls=%fused_computation.44 | loop fusion | flops 27787264 | bytes 12582928 | tf_op jit(solution)/shard_map/add | solution.py:118
  120.5 1.9 %collective-permute-start.8 = (f32[2,64,1,256]{3,2,1,0:T(1,128)S(1)}, f32[2,64,1,256]{3,2,1,0:T(1,128)S(1)}, u32[]{:S(2)}, u32[]{:S(2)}) collective-permute-start(f32[2,64,1,256]{3,2,1,0:T(1,128)S(1)} %get-tuple-element.44), channel_id=1, source_target_pairs={{1,0},{2,1},{3,2},{4,3},{5,4},{6,5},{7,6},{8,7},{9,8},{10,9},{11,1... | collective-permute-start | bytes 393224 | tf_op jit(solution)/shard_map/ppermute | solution.py:20
  122.5 3.6 %collective-permute-start.9 = (f32[2,64,1,256]{3,2,1,0:T(1,128)S(1)}, f32[2,64,1,256]{3,2,1,0:T(1,128)S(1)}, u32[]{:S(2)}, u32[]{:S(2)}) collective-permute-start(f32[2,64,1,256]{3,2,1,0:T(1,128)S(1)} %get-tuple-element.45), channel_id=1, source_target_pairs={{0,1},{1,2},{2,3},{3,4},{4,5},{5,6},{6,7},{7,8},{8,9},{9,10},{10,1... | collective-permute-start | bytes 393224 | tf_op jit(solution)/shard_map/ppermute | solution.py:19
  131.8 3.2 %collective-permute-start.10 = (f32[2,64,1,256]{3,2,1,0:T(1,128)S(1)}, f32[2,64,1,256]{3,2,1,0:T(1,128)S(1)}, u32[]{:S(2)}, u32[]{:S(2)}) collective-permute-start(f32[2,64,1,256]{3,2,1,0:T(1,128)S(1)} %get-tuple-element.43), channel_id=1, source_target_pairs={{1,0},{2,1},{3,2},{4,3},{5,4},{6,5},{7,6},{8,7},{9,8},{10,9},{11,1... | collective-permute-start | bytes 393224 | tf_op jit(solution)/shard_map/ppermute | solution.py:20
  135.0 2.4 %collective-permute-start.11 = (f32[2,64,1,256]{3,2,1,0:T(1,128)S(1)}, f32[2,64,1,256]{3,2,1,0:T(1,128)S(1)}, u32[]{:S(2)}, u32[]{:S(2)}) collective-permute-start(f32[2,64,1,256]{3,2,1,0:T(1,128)S(1)} %get-tuple-element.42), channel_id=1, source_target_pairs={{0,1},{1,2},{2,3},{3,4},{4,5},{5,6},{6,7},{7,8},{8,9},{9,10},{10,1... | collective-permute-start | bytes 393224 | tf_op jit(solution)/shard_map/ppermute | solution.py:19
  138.1 2.5 %collective-permute-done.11 = f32[2,64,1,256]{3,2,1,0:T(1,128)S(1)} collective-permute-done((f32[2,64,1,256]{3,2,1,0:T(1,128)S(1)}, f32[2,64,1,256]{3,2,1,0:T(1,128)S(1)}, u32[]{:S(2)}, u32[]{:S(2)}) %collective-permute-start.11) | collective-permute-done | bytes 131104 | tf_op jit(solution)/shard_map/ppermute | solution.py:19
  148.6 14.4 %collective-permute-done.14 = f32[2,32,1,256]{3,2,1,0:T(1,128)S(1)} collective-permute-done((f32[2,32,1,256]{3,2,1,0:T(1,128)S(1)}, f32[2,32,1,256]{3,2,1,0:T(1,128)S(1)}, u32[]{:S(2)}, u32[]{:S(2)}) %collective-permute-start.14) | collective-permute-done | bytes 65568 | tf_op jit(solution)/shard_map/ppermute | solution.py:272
  (289 shorter events, 74.0 us)
Async XLA Ops:
  0.0 50.7 %copy-start.62 = (pred[8]{0:T(512)(128)(4,1)}, pred[8]{0:T(512)(128)(4,1)S(1)}, u32[]{:S(2)}) copy-start(pred[8]{0:T(512)(128)(4,1)S(1)} %compare_and_fusion) | copy-start | bytes 28
  7.2 13.7 %copy-start.2 = (f32[64,8,256]{2,1,0:T(8,128)S(1)}, f32[64,8,256]{2,1,0:T(8,128)}, u32[]{:S(2)}) copy-start(f32[64,8,256]{2,1,0:T(8,128)} %param.8) | copy-start | bytes 1572868
  7.2 13.7 %copy-start.3 = (f32[64,8,256]{2,1,0:T(8,128)S(1)}, f32[64,8,256]{2,1,0:T(8,128)}, u32[]{:S(2)}) copy-start(f32[64,8,256]{2,1,0:T(8,128)} %param.9) | copy-start | bytes 1572868
  7.2 10.3 %collective-permute-start = (f32[2,160,1,256]{3,2,1,0:T(1,128)}, f32[2,160,1,256]{3,2,1,0:T(1,128)}, u32[]{:S(2)}, u32[]{:S(2)}) collective-permute-start(f32[2,160,1,256]{3,2,1,0:T(1,128)} %pad_maximum_fusion.34), channel_id=1, source_target_pairs={{1,0},{2,1},{3,2},{4,3},{5,4},{6,5},{7,6},{8,7},{9,8},{10,9},{11,1... | collective-permute-start | bytes 983048 | tf_op jit(solution)/shard_map/ppermute | solution.py:20
  11.1 8.7 %collective-permute-start.1 = (f32[2,160,1,256]{3,2,1,0:T(1,128)}, f32[2,160,1,256]{3,2,1,0:T(1,128)}, u32[]{:S(2)}, u32[]{:S(2)}) collective-permute-start(f32[2,160,1,256]{3,2,1,0:T(1,128)} %pad_maximum_fusion.35), channel_id=1, source_target_pairs={{0,1},{1,2},{2,3},{3,4},{4,5},{5,6},{6,7},{7,8},{8,9},{9,10},{10,1... | collective-permute-start | bytes 983048 | tf_op jit(solution)/shard_map/ppermute | solution.py:19
  17.5 33.2 %copy-start.64 = (f32[2]{0:T(128)}, f32[2]{0:T(128)S(1)}, u32[]{:S(2)}) copy-start(f32[2]{0:T(128)S(1)} %get-tuple-element.34) | copy-start | bytes 28
  17.5 33.2 %copy-start.66 = (f32[2]{0:T(128)}, f32[2]{0:T(128)S(1)}, u32[]{:S(2)}) copy-start(f32[2]{0:T(128)S(1)} %get-tuple-element.170) | copy-start | bytes 28
  22.7 14.9 %copy-start.11 = (f32[2,64,8,256]{3,2,1,0:T(8,128)}, f32[2,64,8,256]{3,2,1,0:T(8,128)S(1)}, u32[]{:S(2)}) copy-start(f32[2,64,8,256]{3,2,1,0:T(8,128)S(1)} %get-tuple-element.38) | copy-start | bytes 3145732
  22.9 13.0 %collective-permute-start.2 = (f32[2,64,1,256]{3,2,1,0:T(1,128)S(1)}, f32[2,64,1,256]{3,2,1,0:T(1,128)S(1)}, u32[]{:S(2)}, u32[]{:S(2)}) collective-permute-start(f32[2,64,1,256]{3,2,1,0:T(1,128)S(1)} %get-tuple-element.51), channel_id=1, source_target_pairs={{1,0},{2,1},{3,2},{4,3},{5,4},{6,5},{7,6},{8,7},{9,8},{10,9},{11,1... | collective-permute-start | bytes 393224 | tf_op jit(solution)/shard_map/ppermute | solution.py:20
  26.6 9.3 %collective-permute-start.3 = (f32[2,64,1,256]{3,2,1,0:T(1,128)S(1)}, f32[2,64,1,256]{3,2,1,0:T(1,128)S(1)}, u32[]{:S(2)}, u32[]{:S(2)}) collective-permute-start(f32[2,64,1,256]{3,2,1,0:T(1,128)S(1)} %get-tuple-element.52), channel_id=1, source_target_pairs={{0,1},{1,2},{2,3},{3,4},{4,5},{5,6},{6,7},{7,8},{8,9},{9,10},{10,1... | collective-permute-start | bytes 393224 | tf_op jit(solution)/shard_map/ppermute | solution.py:19
  37.8 7.7 %collective-permute-start.4 = (f32[2,64,2,256]{3,2,1,0:T(2,128)S(1)}, f32[2,64,2,256]{3,2,1,0:T(2,128)S(1)}, u32[]{:S(2)}, u32[]{:S(2)}) collective-permute-start(f32[2,64,2,256]{3,2,1,0:T(2,128)S(1)} %get-tuple-element.50), channel_id=1, source_target_pairs={{1,0},{2,1},{3,2},{4,3},{5,4},{6,5},{7,6},{8,7},{9,8},{10,9},{11,1... | collective-permute-start | bytes 786440 | tf_op jit(solution)/shard_map/ppermute | solution.py:20
  39.8 9.2 %collective-permute-start.5 = (f32[2,64,2,256]{3,2,1,0:T(2,128)S(1)}, f32[2,64,2,256]{3,2,1,0:T(2,128)S(1)}, u32[]{:S(2)}, u32[]{:S(2)}) collective-permute-start(f32[2,64,2,256]{3,2,1,0:T(2,128)S(1)} %get-tuple-element.49), channel_id=1, source_target_pairs={{0,1},{1,2},{2,3},{3,4},{4,5},{5,6},{6,7},{7,8},{8,9},{9,10},{10,1... | collective-permute-start | bytes 786440 | tf_op jit(solution)/shard_map/ppermute | solution.py:19
  49.0 12.8 %copy-start.28 = (f32[2,64,2,256]{3,2,1,0:T(2,128)}, f32[2,64,2,256]{3,2,1,0:T(2,128)S(1)}, u32[]{:S(2)}) copy-start(f32[2,64,2,256]{3,2,1,0:T(2,128)S(1)} %collective-permute-done.5) | copy-start | bytes 786436
  54.3 9.1 %collective-permute-start.6 = (f32[2,32,4,256]{3,2,1,0:T(4,128)S(1)}, f32[2,32,4,256]{3,2,1,0:T(4,128)}, u32[]{:S(2)}, u32[]{:S(2)}) collective-permute-start(f32[2,32,4,256]{3,2,1,0:T(4,128)S(1)} %pad_maximum_fusion.40), channel_id=1, source_target_pairs={{1,0},{2,1},{3,2},{4,3},{5,4},{6,5},{7,6},{8,7},{9,8},{10,9},{11,1... | collective-permute-start | bytes 786440 | tf_op jit(solution)/shard_map/ppermute | solution.py:20
  58.5 16.6 %collective-permute-start.7 = (f32[2,32,4,256]{3,2,1,0:T(4,128)}, f32[2,32,4,256]{3,2,1,0:T(4,128)}, u32[]{:S(2)}, u32[]{:S(2)}) collective-permute-start(f32[2,32,4,256]{3,2,1,0:T(4,128)} %pad_maximum_fusion.41), channel_id=1, source_target_pairs={{0,1},{1,2},{2,3},{3,4},{4,5},{5,6},{6,7},{7,8},{8,9},{9,10},{10,1... | collective-permute-start | bytes 786440 | tf_op jit(solution)/shard_map/ppermute | solution.py:19
  109.1 17.0 %copy-start.31 = (f32[2,64,2,256]{3,2,1,0:T(2,128)S(1)}, f32[2,64,2,256]{3,2,1,0:T(2,128)}, u32[]{:S(2)}) copy-start(f32[2,64,2,256]{3,2,1,0:T(2,128)} %copy-done.30) | copy-start | bytes 786436
  109.1 17.0 %copy-start.41 = (f32[2,64,256]{2,1,0:T(8,128)S(1)}, f32[2,64,256]{2,1,0:T(8,128)}, u32[]{:S(2)}) copy-start(f32[2,64,256]{2,1,0:T(8,128)} %add.903) | copy-start | bytes 393220
  120.5 9.3 %collective-permute-start.8 = (f32[2,64,1,256]{3,2,1,0:T(1,128)S(1)}, f32[2,64,1,256]{3,2,1,0:T(1,128)S(1)}, u32[]{:S(2)}, u32[]{:S(2)}) collective-permute-start(f32[2,64,1,256]{3,2,1,0:T(1,128)S(1)} %get-tuple-element.44), channel_id=1, source_target_pairs={{1,0},{2,1},{3,2},{4,3},{5,4},{6,5},{7,6},{8,7},{9,8},{10,9},{11,1... | collective-permute-start | bytes 393224 | tf_op jit(solution)/shard_map/ppermute | solution.py:20
  122.5 7.3 %collective-permute-start.9 = (f32[2,64,1,256]{3,2,1,0:T(1,128)S(1)}, f32[2,64,1,256]{3,2,1,0:T(1,128)S(1)}, u32[]{:S(2)}, u32[]{:S(2)}) collective-permute-start(f32[2,64,1,256]{3,2,1,0:T(1,128)S(1)} %get-tuple-element.45), channel_id=1, source_target_pairs={{0,1},{1,2},{2,3},{3,4},{4,5},{5,6},{6,7},{7,8},{8,9},{9,10},{10,1... | collective-permute-start | bytes 393224 | tf_op jit(solution)/shard_map/ppermute | solution.py:19
  131.8 6.3 %collective-permute-start.10 = (f32[2,64,1,256]{3,2,1,0:T(1,128)S(1)}, f32[2,64,1,256]{3,2,1,0:T(1,128)S(1)}, u32[]{:S(2)}, u32[]{:S(2)}) collective-permute-start(f32[2,64,1,256]{3,2,1,0:T(1,128)S(1)} %get-tuple-element.43), channel_id=1, source_target_pairs={{1,0},{2,1},{3,2},{4,3},{5,4},{6,5},{7,6},{8,7},{9,8},{10,9},{11,1... | collective-permute-start | bytes 393224 | tf_op jit(solution)/shard_map/ppermute | solution.py:20
  135.0 5.6 %collective-permute-start.11 = (f32[2,64,1,256]{3,2,1,0:T(1,128)S(1)}, f32[2,64,1,256]{3,2,1,0:T(1,128)S(1)}, u32[]{:S(2)}, u32[]{:S(2)}) collective-permute-start(f32[2,64,1,256]{3,2,1,0:T(1,128)S(1)} %get-tuple-element.42), channel_id=1, source_target_pairs={{0,1},{1,2},{2,3},{3,4},{4,5},{5,6},{6,7},{7,8},{8,9},{9,10},{10,1... | collective-permute-start | bytes 393224 | tf_op jit(solution)/shard_map/ppermute | solution.py:19
  144.6 20.7 %collective-permute-start.12 = (f32[2,32,8,256]{3,2,1,0:T(8,128)S(1)}, f32[2,32,8,256]{3,2,1,0:T(8,128)S(1)}, u32[]{:S(2)}, u32[]{:S(2)}) collective-permute-start(f32[2,32,8,256]{3,2,1,0:T(8,128)S(1)} %get-tuple-element.5), channel_id=1, source_target_pairs={{0,16},{1,17},{2,18},{3,19},{4,20},{5,21},{6,22},{7,23},{8,24},{9,... | collective-permute-start | bytes 1572872 | tf_op jit(solution)/shard_map/ppermute | solution.py:271
  145.9 17.1 %collective-permute-start.14 = (f32[2,32,1,256]{3,2,1,0:T(1,128)S(1)}, f32[2,32,1,256]{3,2,1,0:T(1,128)S(1)}, u32[]{:S(2)}, u32[]{:S(2)}) collective-permute-start(f32[2,32,1,256]{3,2,1,0:T(1,128)S(1)} %get-tuple-element.55), channel_id=1, source_target_pairs={{0,17},{1,18},{2,19},{3,20},{4,21},{5,22},{6,23},{7,24},{8,25},{9,... | collective-permute-start | bytes 196616 | tf_op jit(solution)/shard_map/ppermute | solution.py:272
  147.3 17.1 %collective-permute-start.13 = (f32[2,32,1,256]{3,2,1,0:T(1,128)S(1)}, f32[2,32,1,256]{3,2,1,0:T(1,128)S(1)}, u32[]{:S(2)}, u32[]{:S(2)}) collective-permute-start(f32[2,32,1,256]{3,2,1,0:T(1,128)S(1)} %get-tuple-element.56), channel_id=1, source_target_pairs={{1,16},{2,17},{3,18},{4,19},{5,20},{6,21},{7,22},{8,23},{9,24},{10... | collective-permute-start | bytes 196616 | tf_op jit(solution)/shard_map/ppermute | solution.py:273
  (60 other events, 158.0 us)

commit v5 on v4

--- a/solution.py
+++ b/solution.py
@@ -37,9 +37,14 @@
     reach = int(x_spacing)
     padded = jnp.concatenate([halo[0]] * reach + [field] + [halo[1]] * reach, axis=-2)
     width = field.shape[-2]
-    middle = field
-    eastward = padded[..., 2 * reach:, :]
-    westward = padded[..., :width, :]
+    return stencil(
+        field, padded[..., 2 * reach:, :], padded[..., :width, :],
+        x_speed, y_speed, h_spread, v_spread, coupling, x_spacing, z_spacing,
+    )
+
+
+def stencil(middle, eastward, westward, x_speed, y_speed, h_spread, v_spread, coupling,
+            x_spacing, z_spacing):
     y_widths = [(0, 0)] * (middle.ndim - 1) + [(1, 1)]
     y_padded = jnp.pad(middle, y_widths)
     northward = y_padded[..., 2:]
@@ -183,13 +188,15 @@
         after = chain[-1] + slab_step * rate + offset
         if wide is not None:
             strip_b, strip_a, offset_b, offset_a = wide
-            rate_b = tendency(strip_b, (jnp.zeros_like(offset_b), lo(chain[-1])), *coefs_b,
-                              coupling, 2.0, 2.0)
-            rate_a = tendency(strip_a, (hi(chain[-1]), jnp.zeros_like(offset_a)), *coefs_a,
-                              coupling, 2.0, 2.0)
+            edge_b = strip_b[..., 2:3, :]
+            edge_a = strip_a[..., 0:1, :]
+            rate_b = stencil(edge_b, lo(chain[-1]), strip_b[..., 0:1, :], *coefs_b,
+                             coupling, 2.0, 2.0)
+            rate_a = stencil(edge_a, strip_a[..., 2:3, :], hi(chain[-1]), *coefs_a,
+                             coupling, 2.0, 2.0)
             after_halo = (
-                hi(strip_b) + slab_step * hi(rate_b) + offset_b,
-                lo(strip_a) + slab_step * lo(rate_a) + offset_a,
+                edge_b + slab_step * rate_b + offset_b,
+                edge_a + slab_step * rate_a + offset_a,
             )
         elif count + 2 == slabs:
             packed_b, packed_a = exchange(

time: 169 us -> 153 us (0.905)
  other arithmetic: 67.5 us -> 54.2 us
  local copies, waits for them, and re-layouts: 37 us -> 33.6 us
    add x2 -> x0, other arithmetic: 6.96 us -> none  [tendency(): eastward - 2.0 * middle + westward]
    add x2, other arithmetic: 12.9 us -> 8.26 us  [first_node(): node_zero + half_step * (rate_zero - s0)]
    rev x2 -> x0, local copies, waits for them, and re-layouts: 3.39 us -> none  [tendency(): reaction = own * middle + other * middle[::-1]]
    unnamed x154 -> x152, local copies, waits for them, and re-layouts: 12.2 us -> 9.65 us
    broadcast_in_dim x16, local copies, waits for them, and re-layouts: 5.85 us -> 8.08 us  [expand_z(): return jnp.repeat(field, 2, axis=-3)]
  transfers between devices with their start and end apart: 15 -> 15, of which waited for: 7 -> 8; matrix products, arithmetic and copies ran while one was open for 20% -> 16% of each run, Pallas kernels for 0% -> 0%
where the time goes in v5:
time: 153 us; the launch traced here: 151 us
  other arithmetic  54.2 us (35%)
  starting transfers between devices  39.3 us (26%)
  local copies, waits for them, and re-layouts  33.6 us (22%)
  waiting for transfers between devices  22.8 us (15%)
    ppermute x6, starting transfers between devices, exchange(): before = lax.ppermute(to_right, 'space', shift_pairs(count, 1))  19.7 us
    ppermute x6, starting transfers between devices, exchange(): after = lax.ppermute(to_left, 'space', shift_pairs(count, -1))  15.7 us
    ppermute x1, waiting for transfers between devices, body(): passed_b = lax.ppermute(hi(after), ('tm', 'space'), to_east)  14.4 us
    unnamed x152, local copies, waits for them, and re-layouts  9.65 us
    add x2, other arithmetic, first_node(): node_zero + half_step * (rate_zero - s0)  8.26 us
    broadcast_in_dim x16, local copies, waits for them, and re-layouts, expand_z(): return jnp.repeat(field, 2, axis=-3)  8.08 us
    ppermute x6, waiting for transfers between devices, exchange(): before = lax.ppermute(to_right, 'space', shift_pairs(count, 1))  6.92 us
    mul x1, other arithmetic, body(): fixed_one = node_one + expand((delta_zero + delta_one) * 0.5)  5.78 us
  transfers between devices with their start and end apart: 15, of which 8 were waited for; matrix products, arithmetic and copies ran while one was open for 16% of the time, Pallas kernels for 0%

profile of v5, /device:TPU:11, one launch (start us, length us, event | category | flops | bytes accessed | tf_op | source)
XLA Modules:
  0.0 151.4 jit_solution(12495103230454131853)
XLA Ops:
  7.3 2.7 %collective-permute-start = (f32[2,160,1,256]{3,2,1,0:T(1,128)}, f32[2,160,1,256]{3,2,1,0:T(1,128)}, u32[]{:S(2)}, u32[]{:S(2)}) collective-permute-start(f32[2,160,1,256]{3,2,1,0:T(1,128)} %pad_maximum_fusion.34), channel_id=1, source_target_pairs={{1,0},{2,1},{3,2},{4,3},{5,4},{6,5},{7,6},{8,7},{9,8},{10,9},{11,1... | collective-permute-start | bytes 983048 | tf_op jit(solution)/shard_map/ppermute | solution.py:20
  11.2 3.0 %collective-permute-start.1 = (f32[2,160,1,256]{3,2,1,0:T(1,128)}, f32[2,160,1,256]{3,2,1,0:T(1,128)}, u32[]{:S(2)}, u32[]{:S(2)}) collective-permute-start(f32[2,160,1,256]{3,2,1,0:T(1,128)} %pad_maximum_fusion.35), channel_id=1, source_target_pairs={{0,1},{1,2},{2,3},{3,4},{4,5},{5,6},{6,7},{7,8},{8,9},{9,10},{10,1... | collective-permute-start | bytes 983048 | tf_op jit(solution)/shard_map/ppermute | solution.py:19
  14.9 2.7 %broadcast_multiply_fusion.2 = (f32[2]{0:T(128)S(1)}, f32[2]{0:T(128)S(1)}, f32[2]{0:T(128)S(1)}, f32[2]{0:T(128)S(1)}) fusion(f32[1]{0:T(128)} %bitcast.13, f32[1]{0:T(128)} %bitcast.12, f32[1]{0:T(128)} %bitcast.11, f32[1]{0:T(128)} %bitcast.10), kind=kLoop, calls=%fused_computation.278 | loop fusion | flops 8 | bytes 48 | tf_op jit(solution)/shard_map/mul | solution.py:67
  22.9 3.7 %collective-permute-start.2 = (f32[2,64,1,256]{3,2,1,0:T(1,128)S(1)}, f32[2,64,1,256]{3,2,1,0:T(1,128)S(1)}, u32[]{:S(2)}, u32[]{:S(2)}) collective-permute-start(f32[2,64,1,256]{3,2,1,0:T(1,128)S(1)} %get-tuple-element.51), channel_id=1, source_target_pairs={{1,0},{2,1},{3,2},{4,3},{5,4},{6,5},{7,6},{8,7},{9,8},{10,9},{11,1... | collective-permute-start | bytes 393224 | tf_op jit(solution)/shard_map/ppermute | solution.py:20
  26.6 2.7 %collective-permute-start.3 = (f32[2,64,1,256]{3,2,1,0:T(1,128)S(1)}, f32[2,64,1,256]{3,2,1,0:T(1,128)S(1)}, u32[]{:S(2)}, u32[]{:S(2)}) collective-permute-start(f32[2,64,1,256]{3,2,1,0:T(1,128)S(1)} %get-tuple-element.52), channel_id=1, source_target_pairs={{0,1},{1,2},{2,3},{3,4},{4,5},{5,6},{6,7},{7,8},{8,9},{9,10},{10,1... | collective-permute-start | bytes 393224 | tf_op jit(solution)/shard_map/ppermute | solution.py:19
  35.5 2.2 %collective-permute-start.4 = (f32[2,64,2,256]{3,2,1,0:T(2,128)S(1)}, f32[2,64,2,256]{3,2,1,0:T(2,128)S(1)}, u32[]{:S(2)}, u32[]{:S(2)}) collective-permute-start(f32[2,64,2,256]{3,2,1,0:T(2,128)S(1)} %get-tuple-element.50), channel_id=1, source_target_pairs={{1,0},{2,1},{3,2},{4,3},{5,4},{6,5},{7,6},{8,7},{9,8},{10,9},{11,1... | collective-permute-start | bytes 786440 | tf_op jit(solution)/shard_map/ppermute | solution.py:20
  37.7 3.4 %collective-permute-start.5 = (f32[2,64,2,256]{3,2,1,0:T(2,128)S(1)}, f32[2,64,2,256]{3,2,1,0:T(2,128)S(1)}, u32[]{:S(2)}, u32[]{:S(2)}) collective-permute-start(f32[2,64,2,256]{3,2,1,0:T(2,128)S(1)} %get-tuple-element.49), channel_id=1, source_target_pairs={{0,1},{1,2},{2,3},{3,4},{4,5},{5,6},{6,7},{7,8},{8,9},{9,10},{10,1... | collective-permute-start | bytes 786440 | tf_op jit(solution)/shard_map/ppermute | solution.py:19
  43.3 3.3 %collective-permute-done.5 = f32[2,64,2,256]{3,2,1,0:T(2,128)S(1)} collective-permute-done((f32[2,64,2,256]{3,2,1,0:T(2,128)S(1)}, f32[2,64,2,256]{3,2,1,0:T(2,128)S(1)}, u32[]{:S(2)}, u32[]{:S(2)}) %collective-permute-start.5) | collective-permute-done | bytes 262176 | tf_op jit(solution)/shard_map/ppermute | solution.py:19
  49.6 2.0 %fusion.92 = (f32[2,32,8,256]{3,2,1,0:T(8,128)S(1)}, f32[2,32,8,256]{3,2,1,0:T(8,128)S(1)}, f32[2,32,8,256]{3,2,1,0:T(8,128)}) fusion(f32[2,32,8,256]{3,2,1,0:T(8,128)S(1)} %copy-done.6, f32[2,32,7,256]{3,2,1,0:T(8,128)S(1)} %get-tuple-element.78, f32[2,32,1,256]{3,2,1,0:T(1,128)S(1)} %get-tuple-element.80, f32[2,32,1,256]{3,2,1,0:T(1,128)S(1)} %get-tuple-element.79, ...), kind=kLoop, calls=%fused_computation.291 | loop fusion | flops 5505024 | bytes 5898328 | tf_op jit(solution)/shard_map/add | solution.py:188
  51.9 3.2 %collective-permute-start.6 = (f32[2,32,4,256]{3,2,1,0:T(4,128)S(1)}, f32[2,32,4,256]{3,2,1,0:T(4,128)S(1)}, u32[]{:S(2)}, u32[]{:S(2)}) collective-permute-start(f32[2,32,4,256]{3,2,1,0:T(4,128)S(1)} %pad_maximum_fusion.36), channel_id=1, source_target_pairs={{1,0},{2,1},{3,2},{4,3},{5,4},{6,5},{7,6},{8,7},{9,8},{10,9},{11,1... | collective-permute-start | bytes 786440 | tf_op jit(solution)/shard_map/ppermute | solution.py:20
  56.2 3.3 %collective-permute-start.7 = (f32[2,32,4,256]{3,2,1,0:T(4,128)}, f32[2,32,4,256]{3,2,1,0:T(4,128)}, u32[]{:S(2)}, u32[]{:S(2)}) collective-permute-start(f32[2,32,4,256]{3,2,1,0:T(4,128)} %pad_maximum_fusion.37), channel_id=1, source_target_pairs={{0,1},{1,2},{2,3},{3,4},{4,5},{5,6},{6,7},{7,8},{8,9},{9,10},{10,1... | collective-permute-start | bytes 786440 | tf_op jit(solution)/shard_map/ppermute | solution.py:19
  60.4 2.5 %add_multiply_fusion.4 = (f32[2,32,1,256]{3,2,1,0:T(1,128)}, f32[2,32,1,256]{3,2,1,0:T(1,128)}, f32[2,32,1,256]{3,2,1,0:T(1,128)}, f32[2,32,1,256]{3,2,1,0:T(1,128)S(1)}) fusion(f32[2,160,1,256]{3,2,1,0:T(1,128)} %collective-permute-done, f32[2,32,4,256]{3,2,1,0:T(4,128)S(1)} %collective-permute-done.6, pred[]{:T(512)S(6)} %eq.78, pred[]{:T(512)S(6)} %eq.77, ...), kind=kLoop, calls=%fused_computation.251 | loop fusion | flops 638976 | bytes 917524 | tf_op jit(solution)/shard_map/mul | solution.py:230
  66.7 3.0 %add_multiply_fusion.3 = (f32[2,32,1,256]{3,2,1,0:T(1,128)}, f32[2,32,1,256]{3,2,1,0:T(1,128)}, f32[2,32,1,256]{3,2,1,0:T(1,128)}, f32[2,32,1,256]{3,2,1,0:T(1,128)S(1)}) fusion(f32[2,160,1,256]{3,2,1,0:T(1,128)} %collective-permute-done.1, f32[2,32,4,256]{3,2,1,0:T(4,128)} %collective-permute-done.7, pred[]{:T(512)S(6)} %eq.78, pred[]{:T(512)S(6)} %eq.77, ...), kind=kLoop, calls=%fused_computation.250 | loop fusion | flops 638976 | bytes 917524 | tf_op jit(solution)/shard_map/mul | solution.py:230
  72.6 5.8 %add_multiply_fusion.2 = (f32[2,32,8,256]{3,2,1,0:T(8,128)}, f32[2,32,8,256]{3,2,1,0:T(8,128)S(1)}, f32[2,32,8,256]{3,2,1,0:T(8,128)S(1)}, f32[2,32,8,256]{3,2,1,0:T(8,128)S(1)}, f32[2,32,8,256]{3,2,1,0:T(8,128)S(1)}) fusion(f32[2,32,8,256]{3,2,1,0:T(8,128)} %copy-done.13, f32[2,32,8,256]{3,2,1,0:T(8,128)} %get-tuple-element.41, pred[]{:T(512)S(6)} %eq.78, ...), kind=kLoop, calls=%fused_computation.165 | loop fusion | flops 6422528 | bytes 7471196 | tf_op jit(solution)/shard_map/mul | solution.py:224
  88.4 1.7 %broadcast_in_dim.58 = f32[2,64,1,256]{3,2,1,0:T(1,128)} reshape(f32[2,32,2,256]{3,2,1,0:T(2,128)} %broadcast_in_dim.57) | data formatting | bytes 262144 | tf_op jit(solution)/shard_map/broadcast_in_dim | solution.py:89
  94.1 2.2 %slice_add_fusion.18 = (f32[2,64,1,256]{3,2,1,0:T(1,128)}, f32[2,64,1,256]{3,2,1,0:T(1,128)}, f32[2,64,1,256]{3,2,1,0:T(1,128)}) fusion(f32[2,64,1,256]{3,2,1,0:T(1,128)S(1)} %copy-done.51, f32[2,160,1,256]{3,2,1,0:T(1,128)} %collective-permute-done.1, f32[2,64,1,256]{3,2,1,0:T(1,128)S(1)} %copy-done.48, f32[2,64,2,256]{3,2,1,0:T(2,128)S(1)} %copy-done.30, ...), kind=kLoop, calls=%fused_computation.287 | loop fusion | flops 131072 | bytes 1048577 | tf_op jit(solution)/shard_map/add | solution.py:228
  96.3 6.5 %multiply_add_fusion.1 = (f32[2,64,8,256]{3,2,1,0:T(8,128)S(1)}, f32[2,64,8,256]{3,2,1,0:T(8,128)S(1)}, f32[2,64,8,256]{3,2,1,0:T(8,128)S(1)}, f32[2,64,8,256]{3,2,1,0:T(8,128)S(1)}, f32[2,64,8,256]{3,2,1,0:T(8,128)S(1)}) fusion(f32[2,64,8,256]{3,2,1,0:T(8,128)S(1)} %copy-done.10, f32[2,64,8,256]{3,2,1,0:T(8,128)S(1)} %add.847, f32[2]{0:T(128)S(1)} %get-tuple-element.35, ...), kind=kLoop, calls=%fused_computation.44 | loop fusion | flops 27787264 | bytes 12582928 | tf_op jit(solution)/shard_map/add | solution.py:123
  103.0 1.9 %collective-permute-start.8 = (f32[2,64,1,256]{3,2,1,0:T(1,128)S(1)}, f32[2,64,1,256]{3,2,1,0:T(1,128)S(1)}, u32[]{:S(2)}, u32[]{:S(2)}) collective-permute-start(f32[2,64,1,256]{3,2,1,0:T(1,128)S(1)} %get-tuple-element.44), channel_id=1, source_target_pairs={{1,0},{2,1},{3,2},{4,3},{5,4},{6,5},{7,6},{8,7},{9,8},{10,9},{11,1... | collective-permute-start | bytes 393224 | tf_op jit(solution)/shard_map/ppermute | solution.py:20
  104.9 3.9 %collective-permute-start.9 = (f32[2,64,1,256]{3,2,1,0:T(1,128)S(1)}, f32[2,64,1,256]{3,2,1,0:T(1,128)S(1)}, u32[]{:S(2)}, u32[]{:S(2)}) collective-permute-start(f32[2,64,1,256]{3,2,1,0:T(1,128)S(1)} %get-tuple-element.45), channel_id=1, source_target_pairs={{0,1},{1,2},{2,3},{3,4},{4,5},{5,6},{6,7},{7,8},{8,9},{9,10},{10,1... | collective-permute-start | bytes 393224 | tf_op jit(solution)/shard_map/ppermute | solution.py:19
  113.4 1.8 %multiply_add_fusion = (f32[2,64,8,256]{3,2,1,0:T(8,128)S(1)}, f32[2,64,8,256]{3,2,1,0:T(8,128)S(1)}) fusion(f32[2,64,8,256]{3,2,1,0:T(8,128)S(1)} %get-tuple-element.15, f32[2,64,8,256]{3,2,1,0:T(8,128)S(1)} %get-tuple-element.14, f32[2,64,8,256]{3,2,1,0:T(8,128)S(1)} %get-tuple-element.11, f32[2,64,8,256]{3,2,1,0:T(8,128)S(1)} %get-tuple-element.12, ...), kind=kLoop, calls=%fused_computation.40 | loop fusion | flops 8912896 | bytes 8650768 | tf_op jit(solution)/shard_map/add | solution.py:130
  115.4 2.1 %collective-permute-start.10 = (f32[2,64,1,256]{3,2,1,0:T(1,128)S(1)}, f32[2,64,1,256]{3,2,1,0:T(1,128)S(1)}, u32[]{:S(2)}, u32[]{:S(2)}) collective-permute-start(f32[2,64,1,256]{3,2,1,0:T(1,128)S(1)} %get-tuple-element.43), channel_id=1, source_target_pairs={{1,0},{2,1},{3,2},{4,3},{5,4},{6,5},{7,6},{8,7},{9,8},{10,9},{11,1... | collective-permute-start | bytes 393224 | tf_op jit(solution)/shard_map/ppermute | solution.py:20
  117.5 3.5 %collective-permute-start.11 = (f32[2,64,1,256]{3,2,1,0:T(1,128)S(1)}, f32[2,64,1,256]{3,2,1,0:T(1,128)S(1)}, u32[]{:S(2)}, u32[]{:S(2)}) collective-permute-start(f32[2,64,1,256]{3,2,1,0:T(1,128)S(1)} %get-tuple-element.42), channel_id=1, source_target_pairs={{0,1},{1,2},{2,3},{3,4},{4,5},{5,6},{6,7},{7,8},{8,9},{9,10},{10,1... | collective-permute-start | bytes 393224 | tf_op jit(solution)/shard_map/ppermute | solution.py:19
  121.7 2.5 %collective-permute-done.11 = f32[2,64,1,256]{3,2,1,0:T(1,128)S(1)} collective-permute-done((f32[2,64,1,256]{3,2,1,0:T(1,128)S(1)}, f32[2,64,1,256]{3,2,1,0:T(1,128)S(1)}, u32[]{:S(2)}, u32[]{:S(2)}) %collective-permute-start.11) | collective-permute-done | bytes 131104 | tf_op jit(solution)/shard_map/ppermute | solution.py:19
  132.2 14.4 %collective-permute-done.14 = f32[2,32,1,256]{3,2,1,0:T(1,128)S(1)} collective-permute-done((f32[2,32,1,256]{3,2,1,0:T(1,128)S(1)}, f32[2,32,1,256]{3,2,1,0:T(1,128)S(1)}, u32[]{:S(2)}, u32[]{:S(2)}) %collective-permute-start.14) | collective-permute-done | bytes 65568 | tf_op jit(solution)/shard_map/ppermute | solution.py:279
  (284 shorter events, 66.1 us)
Async XLA Ops:
  0.0 48.4 %copy-start.61 = (pred[8]{0:T(512)(128)(4,1)}, pred[8]{0:T(512)(128)(4,1)S(1)}, u32[]{:S(2)}) copy-start(pred[8]{0:T(512)(128)(4,1)S(1)} %compare_and_fusion) | copy-start | bytes 28
  7.3 13.7 %copy-start.2 = (f32[64,8,256]{2,1,0:T(8,128)S(1)}, f32[64,8,256]{2,1,0:T(8,128)}, u32[]{:S(2)}) copy-start(f32[64,8,256]{2,1,0:T(8,128)} %param.8) | copy-start | bytes 1572868
  7.3 13.7 %copy-start.3 = (f32[64,8,256]{2,1,0:T(8,128)S(1)}, f32[64,8,256]{2,1,0:T(8,128)}, u32[]{:S(2)}) copy-start(f32[64,8,256]{2,1,0:T(8,128)} %param.9) | copy-start | bytes 1572868
  7.3 10.3 %collective-permute-start = (f32[2,160,1,256]{3,2,1,0:T(1,128)}, f32[2,160,1,256]{3,2,1,0:T(1,128)}, u32[]{:S(2)}, u32[]{:S(2)}) collective-permute-start(f32[2,160,1,256]{3,2,1,0:T(1,128)} %pad_maximum_fusion.34), channel_id=1, source_target_pairs={{1,0},{2,1},{3,2},{4,3},{5,4},{6,5},{7,6},{8,7},{9,8},{10,9},{11,1... | collective-permute-start | bytes 983048 | tf_op jit(solution)/shard_map/ppermute | solution.py:20
  11.2 8.7 %collective-permute-start.1 = (f32[2,160,1,256]{3,2,1,0:T(1,128)}, f32[2,160,1,256]{3,2,1,0:T(1,128)}, u32[]{:S(2)}, u32[]{:S(2)}) collective-permute-start(f32[2,160,1,256]{3,2,1,0:T(1,128)} %pad_maximum_fusion.35), channel_id=1, source_target_pairs={{0,1},{1,2},{2,3},{3,4},{4,5},{5,6},{6,7},{7,8},{8,9},{9,10},{10,1... | collective-permute-start | bytes 983048 | tf_op jit(solution)/shard_map/ppermute | solution.py:19
  17.6 30.8 %copy-start.63 = (f32[2]{0:T(128)}, f32[2]{0:T(128)S(1)}, u32[]{:S(2)}) copy-start(f32[2]{0:T(128)S(1)} %get-tuple-element.34) | copy-start | bytes 28
  17.6 30.8 %copy-start.65 = (f32[2]{0:T(128)}, f32[2]{0:T(128)S(1)}, u32[]{:S(2)}) copy-start(f32[2]{0:T(128)S(1)} %get-tuple-element.148) | copy-start | bytes 28
  22.8 12.5 %copy-start.11 = (f32[2,64,8,256]{3,2,1,0:T(8,128)}, f32[2,64,8,256]{3,2,1,0:T(8,128)S(1)}, u32[]{:S(2)}) copy-start(f32[2,64,8,256]{3,2,1,0:T(8,128)S(1)} %get-tuple-element.38) | copy-start | bytes 3145732
  22.9 10.6 %collective-permute-start.2 = (f32[2,64,1,256]{3,2,1,0:T(1,128)S(1)}, f32[2,64,1,256]{3,2,1,0:T(1,128)S(1)}, u32[]{:S(2)}, u32[]{:S(2)}) collective-permute-start(f32[2,64,1,256]{3,2,1,0:T(1,128)S(1)} %get-tuple-element.51), channel_id=1, source_target_pairs={{1,0},{2,1},{3,2},{4,3},{5,4},{6,5},{7,6},{8,7},{9,8},{10,9},{11,1... | collective-permute-start | bytes 393224 | tf_op jit(solution)/shard_map/ppermute | solution.py:20
  26.6 6.9 %collective-permute-start.3 = (f32[2,64,1,256]{3,2,1,0:T(1,128)S(1)}, f32[2,64,1,256]{3,2,1,0:T(1,128)S(1)}, u32[]{:S(2)}, u32[]{:S(2)}) collective-permute-start(f32[2,64,1,256]{3,2,1,0:T(1,128)S(1)} %get-tuple-element.52), channel_id=1, source_target_pairs={{0,1},{1,2},{2,3},{3,4},{4,5},{5,6},{6,7},{7,8},{8,9},{9,10},{10,1... | collective-permute-start | bytes 393224 | tf_op jit(solution)/shard_map/ppermute | solution.py:19
  35.5 7.7 %collective-permute-start.4 = (f32[2,64,2,256]{3,2,1,0:T(2,128)S(1)}, f32[2,64,2,256]{3,2,1,0:T(2,128)S(1)}, u32[]{:S(2)}, u32[]{:S(2)}) collective-permute-start(f32[2,64,2,256]{3,2,1,0:T(2,128)S(1)} %get-tuple-element.50), channel_id=1, source_target_pairs={{1,0},{2,1},{3,2},{4,3},{5,4},{6,5},{7,6},{8,7},{9,8},{10,9},{11,1... | collective-permute-start | bytes 786440 | tf_op jit(solution)/shard_map/ppermute | solution.py:20
  37.7 9.0 %collective-permute-start.5 = (f32[2,64,2,256]{3,2,1,0:T(2,128)S(1)}, f32[2,64,2,256]{3,2,1,0:T(2,128)S(1)}, u32[]{:S(2)}, u32[]{:S(2)}) collective-permute-start(f32[2,64,2,256]{3,2,1,0:T(2,128)S(1)} %get-tuple-element.49), channel_id=1, source_target_pairs={{0,1},{1,2},{2,3},{3,4},{4,5},{5,6},{6,7},{7,8},{8,9},{9,10},{10,1... | collective-permute-start | bytes 786440 | tf_op jit(solution)/shard_map/ppermute | solution.py:19
  43.2 11.9 %copy-start.31 = (f32[2,64,2,256]{3,2,1,0:T(2,128)}, f32[2,64,2,256]{3,2,1,0:T(2,128)S(1)}, u32[]{:S(2)}) copy-start(f32[2,64,2,256]{3,2,1,0:T(2,128)S(1)} %collective-permute-done.4) | copy-start | bytes 786436
  46.6 12.8 %copy-start.29 = (f32[2,64,2,256]{3,2,1,0:T(2,128)}, f32[2,64,2,256]{3,2,1,0:T(2,128)S(1)}, u32[]{:S(2)}) copy-start(f32[2,64,2,256]{3,2,1,0:T(2,128)S(1)} %collective-permute-done.5) | copy-start | bytes 786436
  51.9 8.4 %collective-permute-start.6 = (f32[2,32,4,256]{3,2,1,0:T(4,128)S(1)}, f32[2,32,4,256]{3,2,1,0:T(4,128)S(1)}, u32[]{:S(2)}, u32[]{:S(2)}) collective-permute-start(f32[2,32,4,256]{3,2,1,0:T(4,128)S(1)} %pad_maximum_fusion.36), channel_id=1, source_target_pairs={{1,0},{2,1},{3,2},{4,3},{5,4},{6,5},{7,6},{8,7},{9,8},{10,9},{11,1... | collective-permute-start | bytes 786440 | tf_op jit(solution)/shard_map/ppermute | solution.py:20
  56.2 9.5 %collective-permute-start.7 = (f32[2,32,4,256]{3,2,1,0:T(4,128)}, f32[2,32,4,256]{3,2,1,0:T(4,128)}, u32[]{:S(2)}, u32[]{:S(2)}) collective-permute-start(f32[2,32,4,256]{3,2,1,0:T(4,128)} %pad_maximum_fusion.37), channel_id=1, source_target_pairs={{0,1},{1,2},{2,3},{3,4},{4,5},{5,6},{6,7},{7,8},{8,9},{9,10},{10,1... | collective-permute-start | bytes 786440 | tf_op jit(solution)/shard_map/ppermute | solution.py:19
  96.3 12.5 %copy-start.33 = (f32[2,64,2,256]{3,2,1,0:T(2,128)S(1)}, f32[2,64,2,256]{3,2,1,0:T(2,128)}, u32[]{:S(2)}) copy-start(f32[2,64,2,256]{3,2,1,0:T(2,128)} %copy-done.31) | copy-start | bytes 786436
  103.0 10.4 %collective-permute-start.8 = (f32[2,64,1,256]{3,2,1,0:T(1,128)S(1)}, f32[2,64,1,256]{3,2,1,0:T(1,128)S(1)}, u32[]{:S(2)}, u32[]{:S(2)}) collective-permute-start(f32[2,64,1,256]{3,2,1,0:T(1,128)S(1)} %get-tuple-element.44), channel_id=1, source_target_pairs={{1,0},{2,1},{3,2},{4,3},{5,4},{6,5},{7,6},{8,7},{9,8},{10,9},{11,1... | collective-permute-start | bytes 393224 | tf_op jit(solution)/shard_map/ppermute | solution.py:20
  104.9 8.4 %collective-permute-start.9 = (f32[2,64,1,256]{3,2,1,0:T(1,128)S(1)}, f32[2,64,1,256]{3,2,1,0:T(1,128)S(1)}, u32[]{:S(2)}, u32[]{:S(2)}) collective-permute-start(f32[2,64,1,256]{3,2,1,0:T(1,128)S(1)} %get-tuple-element.45), channel_id=1, source_target_pairs={{0,1},{1,2},{2,3},{3,4},{4,5},{5,6},{6,7},{7,8},{8,9},{9,10},{10,1... | collective-permute-start | bytes 393224 | tf_op jit(solution)/shard_map/ppermute | solution.py:19
  115.4 6.3 %collective-permute-start.10 = (f32[2,64,1,256]{3,2,1,0:T(1,128)S(1)}, f32[2,64,1,256]{3,2,1,0:T(1,128)S(1)}, u32[]{:S(2)}, u32[]{:S(2)}) collective-permute-start(f32[2,64,1,256]{3,2,1,0:T(1,128)S(1)} %get-tuple-element.43), channel_id=1, source_target_pairs={{1,0},{2,1},{3,2},{4,3},{5,4},{6,5},{7,6},{8,7},{9,8},{10,9},{11,1... | collective-permute-start | bytes 393224 | tf_op jit(solution)/shard_map/ppermute | solution.py:20
  117.5 6.7 %collective-permute-start.11 = (f32[2,64,1,256]{3,2,1,0:T(1,128)S(1)}, f32[2,64,1,256]{3,2,1,0:T(1,128)S(1)}, u32[]{:S(2)}, u32[]{:S(2)}) collective-permute-start(f32[2,64,1,256]{3,2,1,0:T(1,128)S(1)} %get-tuple-element.42), channel_id=1, source_target_pairs={{0,1},{1,2},{2,3},{3,4},{4,5},{5,6},{6,7},{7,8},{8,9},{9,10},{10,1... | collective-permute-start | bytes 393224 | tf_op jit(solution)/shard_map/ppermute | solution.py:19
  128.2 20.7 %collective-permute-start.12 = (f32[2,32,8,256]{3,2,1,0:T(8,128)S(1)}, f32[2,32,8,256]{3,2,1,0:T(8,128)S(1)}, u32[]{:S(2)}, u32[]{:S(2)}) collective-permute-start(f32[2,32,8,256]{3,2,1,0:T(8,128)S(1)} %get-tuple-element.5), channel_id=1, source_target_pairs={{0,16},{1,17},{2,18},{3,19},{4,20},{5,21},{6,22},{7,23},{8,24},{9,... | collective-permute-start | bytes 1572872 | tf_op jit(solution)/shard_map/ppermute | solution.py:278
  129.5 17.1 %collective-permute-start.14 = (f32[2,32,1,256]{3,2,1,0:T(1,128)S(1)}, f32[2,32,1,256]{3,2,1,0:T(1,128)S(1)}, u32[]{:S(2)}, u32[]{:S(2)}) collective-permute-start(f32[2,32,1,256]{3,2,1,0:T(1,128)S(1)} %get-tuple-element.55), channel_id=1, source_target_pairs={{0,17},{1,18},{2,19},{3,20},{4,21},{5,22},{6,23},{7,24},{8,25},{9,... | collective-permute-start | bytes 196616 | tf_op jit(solution)/shard_map/ppermute | solution.py:279
  130.9 17.1 %collective-permute-start.13 = (f32[2,32,1,256]{3,2,1,0:T(1,128)S(1)}, f32[2,32,1,256]{3,2,1,0:T(1,128)S(1)}, u32[]{:S(2)}, u32[]{:S(2)}) collective-permute-start(f32[2,32,1,256]{3,2,1,0:T(1,128)S(1)} %get-tuple-element.56), channel_id=1, source_target_pairs={{1,16},{2,17},{3,18},{4,19},{5,20},{6,21},{7,22},{8,23},{9,24},{10... | collective-permute-start | bytes 196616 | tf_op jit(solution)/shard_map/ppermute | solution.py:280
  (59 other events, 143.3 us)

commit v6 on v3

--- a/solution.py
+++ b/solution.py
@@ -29,13 +29,25 @@
     return field[..., field.shape[-2] - width:, :]
 
 
+def pack(before, after):
+    return jnp.concatenate([before, after], axis=-2)
+
+
+def west(halo):
+    return halo[..., 0:1, :]
+
+
+def east(halo):
+    return halo[..., 1:2, :]
+
+
 def halo_of(field):
-    return exchange(hi(field), lo(field))
+    return pack(*exchange(hi(field), lo(field)))
 
 
 def tendency(field, halo, x_speed, y_speed, h_spread, v_spread, coupling, x_spacing, z_spacing):
     reach = int(x_spacing)
-    padded = jnp.concatenate([halo[0]] * reach + [field] + [halo[1]] * reach, axis=-2)
+    padded = jnp.concatenate([west(halo)] * reach + [field] + [east(halo)] * reach, axis=-2)
     width = field.shape[-2]
     middle = field
     eastward = padded[..., 2 * reach:, :]
@@ -91,8 +103,8 @@
     return out
 
 
-def pair_map(fn, *pairs):
-    return tuple(fn(*parts) for parts in zip(*pairs))
+def pair_map(fn, *halos):
+    return fn(*halos)
 
 
 def body(initial, x_velocity, y_velocity, h_diffusion, v_diffusion, coupling):
@@ -138,8 +150,8 @@
     )
     init_b, first_b = before[..., :levels, :, :], before[..., levels:, :, :]
     init_a, first_a = after[..., :levels, :, :], after[..., levels:, :, :]
-    halo_zero = (init_b, init_a)
-    halo_first = (first_b, first_a)
+    halo_zero = pack(init_b, init_a)
+    halo_first = pack(first_b, first_a)
     first_rate = fine_rate(initial, halo_zero)
     coarse_first_rate = coarse_rate(coarse_first, halo_first)
 
@@ -150,9 +162,9 @@
     rate_one = fine_rate(node_one, halo_one)
     node_two = second_node(node_one, rate_one, first_rate, first_rate, first_rate)
     two_b, two_a = exchange(hi(node_two, 2), lo(node_two, 2))
-    halo_two = (hi(two_b), lo(two_a))
+    halo_two = pack(hi(two_b), lo(two_a))
     coarse_end = shrink(node_two)
-    halo_end = (hi(shrink(two_b)), lo(shrink(two_a)))
+    halo_end = pack(hi(shrink(two_b)), lo(shrink(two_a)))
     rate_two = fine_rate(node_two, halo_two)
     source = shrink(slab_step * (rate_zero + 4.0 * rate_one + rate_two) / 6.0)
     offset = source - slab_step * coarse_first_rate
@@ -190,13 +202,13 @@
     halo_earlier_delta = pair_map(lambda y, v: y - v, begins_halo, halo_end)
     halo_earlier = pair_map(lambda w, d: w + expand_z(d), halo_two, halo_earlier_delta)
     wide_earlier = (
-        two_b + expand(halo_earlier_delta[0]),
-        two_a + expand(halo_earlier_delta[1]),
+        two_b + expand(west(halo_earlier_delta)),
+        two_a + expand(east(halo_earlier_delta)),
     )
     start = jnp.where(first, initial, earlier_end)
     halo_start = pair_map(lambda a, b: jnp.where(first, a, b), halo_zero, halo_earlier)
-    halo_start_coarse = pair_map(
-        lambda a, w: jnp.where(first, a, lo(shrink(w))), halo_first, wide_earlier
+    halo_start_coarse = jnp.where(
+        first, halo_first, pack(lo(shrink(wide_earlier[0])), lo(shrink(wide_earlier[1])))
     )
 
     slope_zero = fine_rate(fixed_zero, halo_f0)
@@ -233,9 +245,7 @@
         passed_b = lax.ppermute(hi(after), ("tm", "space"), to_east)
         passed_a = lax.ppermute(lo(after), ("tm", "space"), to_west)
         carried = jnp.where(first, coarse_first, passed)
-        carried_halo = pair_map(
-            lambda a, b: jnp.where(first, a, b), halo_first, (passed_b, passed_a)
-        )
+        carried_halo = jnp.where(first, halo_first, pack(passed_b, passed_a))
         rate = coarse_rate(carried, carried_halo)
     finals = carried + slab_step * rate + offset
     result = node_two + expand(finals - coarse_end)

time: 151 us -> 140 us (0.927)
  other arithmetic: 48.7 us -> 39.9 us
  local copies, waits for them, and re-layouts: 28.7 us -> 25.3 us
  waiting for transfers between devices: 24.3 us -> 26.5 us
    broadcast_in_dim x16 -> x4, local copies, waits for them, and re-layouts: 8.81 us -> 0.28 us  [expand_z(): return jnp.repeat(field, 2, axis=-3)]
    broadcast_in_dim x5 -> x9, local copies, waits for them, and re-layouts: 0.4 us -> 5.12 us  [expand(): return jnp.repeat(field, 2, axis=-3)]
    select_n x4 -> x2, other arithmetic: 3.83 us -> 0.43 us  [the longest x1 0.22 us: body(): jnp.where(first, halo_first, pack(lo(shrink(wide_earlier[0])), lo(shrink(...]
    ppermute x7, starting transfers between devices: 23 us -> 20.1 us  [exchange(): after = lax.ppermute(to_left, 'space', shift_pairs(count, -1))]
    add x2 -> x1, other arithmetic: 3.26 us -> 0.67 us  [body(): halo_f2 = pair_map(lambda w, d: w + expand_z(d), halo_two, halo_d1)]
    ppermute x7, waiting for transfers between devices: 1.91 us -> 4.16 us  [exchange(): after = lax.ppermute(to_left, 'space', shift_pairs(count, -1))]
    add x2, other arithmetic: 0.28 us -> 2.42 us  [the longest x1 1.27 us: body(): two_a + expand(east(halo_earlier_delta))]
    ppermute x7, starting transfers between devices: 19.7 us -> 21.7 us  [exchange(): before = lax.ppermute(to_right, 'space', shift_pairs(count, 1))]
  transfers between devices with their start and end apart: 17 -> 17, of which waited for: 9 -> 9; matrix products, arithmetic and copies ran while one was open for 17% -> 19% of each run, Pallas kernels for 0% -> 0%
where the time goes in v6:
time: 140 us; the launch traced here: 139 us
  starting transfers between devices  45.7 us (33%)
  other arithmetic  39.9 us (28%)
  waiting for transfers between devices  26.5 us (19%)
  local copies, waits for them, and re-layouts  25.3 us (18%)
    ppermute x7, starting transfers between devices, exchange(): before = lax.ppermute(to_right, 'space', shift_pairs(count, 1))  21.7 us
    ppermute x7, starting transfers between devices, exchange(): after = lax.ppermute(to_left, 'space', shift_pairs(count, -1))  20.1 us
    ppermute x1, waiting for transfers between devices, body(): passed_b = lax.ppermute(hi(after), ('tm', 'space'), to_east)  14.4 us
    add x2, other arithmetic, first_node(): node_zero + half_step * (rate_zero - s0)  8.51 us
    ppermute x7, waiting for transfers between devices, exchange(): before = lax.ppermute(to_right, 'space', shift_pairs(count, 1))  7.72 us
    mul x8, other arithmetic, shrink(): return pair_sum(levels) * 0.25  5.86 us
    slice x10, local copies, waits for them, and re-layouts, pair_sum(): jnp.roll(field, 1, axis=-2)  5.55 us
    broadcast_in_dim x9, local copies, waits for them, and re-layouts, expand(): return jnp.repeat(field, 2, axis=-3)  5.12 us
  transfers between devices with their start and end apart: 17, of which 9 were waited for; matrix products, arithmetic and copies ran while one was open for 19% of the time, Pallas kernels for 0%

profile of v6, /device:TPU:11, one launch (start us, length us, event | category | flops | bytes accessed | tf_op | source)
XLA Modules:
  0.0 138.6 jit_solution(10606039089760212021)
XLA Ops:
  4.7 2.6 %collective-permute-start = (f32[2,96,1,256]{3,2,1,0:T(1,128)}, f32[2,96,1,256]{3,2,1,0:T(1,128)}, u32[]{:S(2)}, u32[]{:S(2)}) collective-permute-start(f32[2,96,1,256]{3,2,1,0:T(1,128)} %pad_maximum_fusion.36), channel_id=1, source_target_pairs={{1,0},{2,1},{3,2},{4,3},{5,4},{6,5},{7,6},{8,7},{9,8},{10,9},{11,1... | collective-permute-start | bytes 589832 | tf_op jit(solution)/shard_map/ppermute | solution.py:20
  8.2 3.0 %collective-permute-start.1 = (f32[2,96,1,256]{3,2,1,0:T(1,128)}, f32[2,96,1,256]{3,2,1,0:T(1,128)}, u32[]{:S(2)}, u32[]{:S(2)}) collective-permute-start(f32[2,96,1,256]{3,2,1,0:T(1,128)} %pad_maximum_fusion.37), channel_id=1, source_target_pairs={{0,1},{1,2},{2,3},{3,4},{4,5},{5,6},{6,7},{7,8},{8,9},{9,10},{10,1... | collective-permute-start | bytes 589832 | tf_op jit(solution)/shard_map/ppermute | solution.py:19
  17.0 2.7 %broadcast_multiply_fusion.2 = (f32[2]{0:T(128)S(1)}, f32[2]{0:T(128)S(1)}, f32[2]{0:T(128)S(1)}, f32[2]{0:T(128)S(1)}) fusion(f32[1]{0:T(128)} %bitcast.3, f32[1]{0:T(128)} %bitcast.2, f32[1]{0:T(128)} %bitcast.1, f32[1]{0:T(128)} %bitcast), kind=kLoop, calls=%fused_computation.242 | loop fusion | flops 8 | bytes 48 | tf_op jit(solution)/shard_map/mul | solution.py:74
  19.7 1.9 %fusion.67 = (f32[32,8,256]{2,1,0:T(8,128)S(1)}, f32[32,8,256]{2,1,0:T(8,128)S(1)}, f32[32,8,256]{2,1,0:T(8,128)S(1)}) fusion(f32[32,1,256]{2,1,0:T(1,128)} %get-tuple-element.95, f32[32,7,256]{2,1,0:T(8,128)} %get-tuple-element.97, f32[32,7,256]{2,1,0:T(8,128)} %get-tuple-element.96, f32[32,1,256]{2,1,0:T(1,128)} %get-tuple-element.94, ...), kind=kLoop, calls=%fused_computation.180 | loop fusion | flops 1179648 | bytes 3407944 | tf_op jit(solution)/shard_map/mul | solution.py:88
  26.7 1.9 %collective-permute-start.2 = (f32[2,64,1,256]{3,2,1,0:T(1,128)S(1)}, f32[2,64,1,256]{3,2,1,0:T(1,128)S(1)}, u32[]{:S(2)}, u32[]{:S(2)}) collective-permute-start(f32[2,64,1,256]{3,2,1,0:T(1,128)S(1)} %get-tuple-element.47), channel_id=1, source_target_pairs={{1,0},{2,1},{3,2},{4,3},{5,4},{6,5},{7,6},{8,7},{9,8},{10,9},{11,1... | collective-permute-start | bytes 393224 | tf_op jit(solution)/shard_map/ppermute | solution.py:20
  28.6 3.6 %collective-permute-start.3 = (f32[2,64,1,256]{3,2,1,0:T(1,128)S(1)}, f32[2,64,1,256]{3,2,1,0:T(1,128)S(1)}, u32[]{:S(2)}, u32[]{:S(2)}) collective-permute-start(f32[2,64,1,256]{3,2,1,0:T(1,128)S(1)} %get-tuple-element.48), channel_id=1, source_target_pairs={{0,1},{1,2},{2,3},{3,4},{4,5},{5,6},{6,7},{7,8},{8,9},{9,10},{10,1... | collective-permute-start | bytes 393224 | tf_op jit(solution)/shard_map/ppermute | solution.py:19
  37.4 4.6 %collective-permute-start.4 = (f32[2,64,2,256]{3,2,1,0:T(2,128)S(1)}, f32[2,64,2,256]{3,2,1,0:T(2,128)S(1)}, u32[]{:S(2)}, u32[]{:S(2)}) collective-permute-start(f32[2,64,2,256]{3,2,1,0:T(2,128)S(1)} %get-tuple-element.46), channel_id=1, source_target_pairs={{1,0},{2,1},{3,2},{4,3},{5,4},{6,5},{7,6},{8,7},{9,8},{10,9},{11,1... | collective-permute-start | bytes 786440 | tf_op jit(solution)/shard_map/ppermute | solution.py:20
  42.0 1.9 %collective-permute-start.5 = (f32[2,64,2,256]{3,2,1,0:T(2,128)S(1)}, f32[2,64,2,256]{3,2,1,0:T(2,128)S(1)}, u32[]{:S(2)}, u32[]{:S(2)}) collective-permute-start(f32[2,64,2,256]{3,2,1,0:T(2,128)S(1)} %get-tuple-element.45), channel_id=1, source_target_pairs={{0,1},{1,2},{2,3},{3,4},{4,5},{5,6},{6,7},{7,8},{8,9},{9,10},{10,1... | collective-permute-start | bytes 786440 | tf_op jit(solution)/shard_map/ppermute | solution.py:19
  44.1 1.7 %collective-permute-done.4 = f32[2,64,2,256]{3,2,1,0:T(2,128)S(1)} collective-permute-done((f32[2,64,2,256]{3,2,1,0:T(2,128)S(1)}, f32[2,64,2,256]{3,2,1,0:T(2,128)S(1)}, u32[]{:S(2)}, u32[]{:S(2)}) %collective-permute-start.4) | collective-permute-done | bytes 262176 | tf_op jit(solution)/shard_map/ppermute | solution.py:20
  45.9 3.4 %collective-permute-done.5 = f32[2,64,2,256]{3,2,1,0:T(2,128)S(1)} collective-permute-done((f32[2,64,2,256]{3,2,1,0:T(2,128)S(1)}, f32[2,64,2,256]{3,2,1,0:T(2,128)S(1)}, u32[]{:S(2)}, u32[]{:S(2)}) %collective-permute-start.5) | collective-permute-done | bytes 262176 | tf_op jit(solution)/shard_map/ppermute | solution.py:19
  52.1 2.0 %fusion.89 = (f32[2,32,8,256]{3,2,1,0:T(8,128)S(1)}, f32[2,32,8,256]{3,2,1,0:T(8,128)S(1)}, f32[2,32,8,256]{3,2,1,0:T(8,128)}) fusion(f32[2,32,8,256]{3,2,1,0:T(8,128)S(1)} %copy-done.5, f32[2,32,7,256]{3,2,1,0:T(8,128)S(1)} %get-tuple-element.74, f32[2,32,1,256]{3,2,1,0:T(1,128)S(1)} %get-tuple-element.76, f32[2,32,1,256]{3,2,1,0:T(1,128)S(1)} %get-tuple-element.75, ...), kind=kLoop, calls=%fused_computation.247 | loop fusion | flops 5505024 | bytes 5898328 | tf_op jit(solution)/shard_map/add | solution.py:176
  54.1 3.2 %collective-permute-start.6 = (f32[2,32,1,256]{3,2,1,0:T(1,128)S(1)}, f32[2,32,1,256]{3,2,1,0:T(1,128)S(1)}, u32[]{:S(2)}, u32[]{:S(2)}) collective-permute-start(f32[2,32,1,256]{3,2,1,0:T(1,128)S(1)} %get-tuple-element.71), channel_id=1, source_target_pairs={{1,0},{2,1},{3,2},{4,3},{5,4},{6,5},{7,6},{8,7},{9,8},{10,9},{11,1... | collective-permute-start | bytes 196616 | tf_op jit(solution)/shard_map/ppermute | solution.py:20
  57.3 3.3 %collective-permute-start.7 = (f32[2,32,1,256]{3,2,1,0:T(1,128)S(1)}, f32[2,32,1,256]{3,2,1,0:T(1,128)S(1)}, u32[]{:S(2)}, u32[]{:S(2)}) collective-permute-start(f32[2,32,1,256]{3,2,1,0:T(1,128)S(1)} %get-tuple-element.72), channel_id=1, source_target_pairs={{0,1},{1,2},{2,3},{3,4},{4,5},{5,6},{6,7},{7,8},{8,9},{9,10},{10,1... | collective-permute-start | bytes 196616 | tf_op jit(solution)/shard_map/ppermute | solution.py:19
  64.3 4.3 %collective-permute-start.8 = (f32[2,32,1,256]{3,2,1,0:T(1,128)S(1)}, f32[2,32,1,256]{3,2,1,0:T(1,128)S(1)}, u32[]{:S(2)}, u32[]{:S(2)}) collective-permute-start(f32[2,32,1,256]{3,2,1,0:T(1,128)S(1)} %get-tuple-element.65), channel_id=1, source_target_pairs={{0,1},{1,2},{2,3},{3,4},{4,5},{5,6},{6,7},{7,8},{8,9},{9,10},{10,1... | collective-permute-start | bytes 196616 | tf_op jit(solution)/shard_map/ppermute | solution.py:19
  68.5 1.9 %collective-permute-start.9 = (f32[2,32,1,256]{3,2,1,0:T(1,128)S(1)}, f32[2,32,1,256]{3,2,1,0:T(1,128)S(1)}, u32[]{:S(2)}, u32[]{:S(2)}) collective-permute-start(f32[2,32,1,256]{3,2,1,0:T(1,128)S(1)} %get-tuple-element.66), channel_id=1, source_target_pairs={{1,0},{2,1},{3,2},{4,3},{5,4},{6,5},{7,6},{8,7},{9,8},{10,9},{11,1... | collective-permute-start | bytes 196616 | tf_op jit(solution)/shard_map/ppermute | solution.py:20
  72.0 2.2 %collective-permute-done.9 = f32[2,32,1,256]{3,2,1,0:T(1,128)S(1)} collective-permute-done((f32[2,32,1,256]{3,2,1,0:T(1,128)S(1)}, f32[2,32,1,256]{3,2,1,0:T(1,128)S(1)}, u32[]{:S(2)}, u32[]{:S(2)}) %collective-permute-start.9) | collective-permute-done | bytes 65568 | tf_op jit(solution)/shard_map/ppermute | solution.py:20
  77.6 6.8 %multiply_add_fusion.1 = (f32[2,64,8,256]{3,2,1,0:T(8,128)S(1)}, f32[2,64,8,256]{3,2,1,0:T(8,128)}, f32[2,64,8,256]{3,2,1,0:T(8,128)}, f32[2,64,8,256]{3,2,1,0:T(8,128)}, f32[2,64,8,256]{3,2,1,0:T(8,128)}) fusion(f32[2,64,8,256]{3,2,1,0:T(8,128)S(1)} %get-tuple-element.43, f32[2,64,8,256]{3,2,1,0:T(8,128)S(1)} %add.738, f32[2]{0:T(128)S(1)} %get-tuple-element.31, ...), kind=kLoop, calls=%fused_computation.44 | loop fusion | flops 27787264 | bytes 12582928 | tf_op jit(solution)/shard_map/add | solution.py:130
  85.3 2.5 %collective-permute-start.10 = (f32[2,64,1,256]{3,2,1,0:T(1,128)}, f32[2,64,1,256]{3,2,1,0:T(1,128)}, u32[]{:S(2)}, u32[]{:S(2)}) collective-permute-start(f32[2,64,1,256]{3,2,1,0:T(1,128)} %get-tuple-element.40), channel_id=1, source_target_pairs={{1,0},{2,1},{3,2},{4,3},{5,4},{6,5},{7,6},{8,7},{9,8},{10,9},{11,1... | collective-permute-start | bytes 393224 | tf_op jit(solution)/shard_map/ppermute | solution.py:20
  87.8 3.1 %collective-permute-start.11 = (f32[2,64,1,256]{3,2,1,0:T(1,128)}, f32[2,64,1,256]{3,2,1,0:T(1,128)}, u32[]{:S(2)}, u32[]{:S(2)}) collective-permute-start(f32[2,64,1,256]{3,2,1,0:T(1,128)} %get-tuple-element.41), channel_id=1, source_target_pairs={{0,1},{1,2},{2,3},{3,4},{4,5},{5,6},{6,7},{7,8},{8,9},{9,10},{10,1... | collective-permute-start | bytes 393224 | tf_op jit(solution)/shard_map/ppermute | solution.py:19
  100.7 2.8 %multiply_add_fusion = (f32[2,64,8,256]{3,2,1,0:T(8,128)S(1)}, f32[2,64,8,256]{3,2,1,0:T(8,128)S(1)}) fusion(f32[2,64,8,256]{3,2,1,0:T(8,128)} %get-tuple-element.15, f32[2,64,8,256]{3,2,1,0:T(8,128)S(1)} %copy-done.16, f32[2,64,8,256]{3,2,1,0:T(8,128)S(1)} %get-tuple-element.11, f32[2,64,8,256]{3,2,1,0:T(8,128)S(1)} %copy-done.15, ...), kind=kLoop, calls=%fused_computation.40 | loop fusion | flops 8912896 | bytes 8650768 | tf_op jit(solution)/shard_map/add | solution.py:137
  103.8 3.4 %collective-permute-start.12 = (f32[2,64,1,256]{3,2,1,0:T(1,128)S(1)}, f32[2,64,1,256]{3,2,1,0:T(1,128)S(1)}, u32[]{:S(2)}, u32[]{:S(2)}) collective-permute-start(f32[2,64,1,256]{3,2,1,0:T(1,128)S(1)} %get-tuple-element.39), channel_id=1, source_target_pairs={{1,0},{2,1},{3,2},{4,3},{5,4},{6,5},{7,6},{8,7},{9,8},{10,9},{11,1... | collective-permute-start | bytes 393224 | tf_op jit(solution)/shard_map/ppermute | solution.py:20
  107.2 2.5 %collective-permute-start.13 = (f32[2,64,1,256]{3,2,1,0:T(1,128)S(1)}, f32[2,64,1,256]{3,2,1,0:T(1,128)S(1)}, u32[]{:S(2)}, u32[]{:S(2)}) collective-permute-start(f32[2,64,1,256]{3,2,1,0:T(1,128)S(1)} %get-tuple-element.38), channel_id=1, source_target_pairs={{0,1},{1,2},{2,3},{3,4},{4,5},{5,6},{6,7},{7,8},{8,9},{9,10},{10,1... | collective-permute-start | bytes 393224 | tf_op jit(solution)/shard_map/ppermute | solution.py:19
  110.1 2.7 %collective-permute-done.13 = f32[2,64,1,256]{3,2,1,0:T(1,128)S(1)} collective-permute-done((f32[2,64,1,256]{3,2,1,0:T(1,128)S(1)}, f32[2,64,1,256]{3,2,1,0:T(1,128)S(1)}, u32[]{:S(2)}, u32[]{:S(2)}) %collective-permute-start.13) | collective-permute-done | bytes 131104 | tf_op jit(solution)/shard_map/ppermute | solution.py:19
  121.1 14.4 %collective-permute-done.15 = f32[2,32,1,256]{3,2,1,0:T(1,128)S(1)} collective-permute-done((f32[2,32,1,256]{3,2,1,0:T(1,128)S(1)}, f32[2,32,1,256]{3,2,1,0:T(1,128)S(1)}, u32[]{:S(2)}, u32[]{:S(2)}) %collective-permute-start.15) | collective-permute-done | bytes 65568 | tf_op jit(solution)/shard_map/ppermute | solution.py:245
  (195 shorter events, 55.1 us)
Async XLA Ops:
  4.7 18.2 %collective-permute-start = (f32[2,96,1,256]{3,2,1,0:T(1,128)}, f32[2,96,1,256]{3,2,1,0:T(1,128)}, u32[]{:S(2)}, u32[]{:S(2)}) collective-permute-start(f32[2,96,1,256]{3,2,1,0:T(1,128)} %pad_maximum_fusion.36), channel_id=1, source_target_pairs={{1,0},{2,1},{3,2},{4,3},{5,4},{6,5},{7,6},{8,7},{9,8},{10,9},{11,1... | collective-permute-start | bytes 589832 | tf_op jit(solution)/shard_map/ppermute | solution.py:20
  8.2 15.7 %collective-permute-start.1 = (f32[2,96,1,256]{3,2,1,0:T(1,128)}, f32[2,96,1,256]{3,2,1,0:T(1,128)}, u32[]{:S(2)}, u32[]{:S(2)}) collective-permute-start(f32[2,96,1,256]{3,2,1,0:T(1,128)} %pad_maximum_fusion.37), channel_id=1, source_target_pairs={{0,1},{1,2},{2,3},{3,4},{4,5},{5,6},{6,7},{7,8},{8,9},{9,10},{10,1... | collective-permute-start | bytes 589832 | tf_op jit(solution)/shard_map/ppermute | solution.py:19
  19.7 31.3 %copy-start.32 = (f32[2]{0:T(128)}, f32[2]{0:T(128)S(1)}, u32[]{:S(2)}) copy-start(f32[2]{0:T(128)S(1)} %get-tuple-element.30) | copy-start | bytes 28
  19.7 31.3 %copy-start.34 = (f32[2]{0:T(128)}, f32[2]{0:T(128)S(1)}, u32[]{:S(2)}) copy-start(f32[2]{0:T(128)S(1)} %get-tuple-element.133) | copy-start | bytes 28
  21.6 40.1 %copy-start.7 = (f32[32,8,256]{2,1,0:T(8,128)}, f32[32,8,256]{2,1,0:T(8,128)S(1)}, u32[]{:S(2)}) copy-start(f32[32,8,256]{2,1,0:T(8,128)S(1)} %get-tuple-element.125) | copy-start | bytes 786436
  21.6 40.1 %copy-start.9 = (f32[32,8,256]{2,1,0:T(8,128)}, f32[32,8,256]{2,1,0:T(8,128)S(1)}, u32[]{:S(2)}) copy-start(f32[32,8,256]{2,1,0:T(8,128)S(1)} %get-tuple-element.126) | copy-start | bytes 786436
  26.7 7.5 %collective-permute-start.2 = (f32[2,64,1,256]{3,2,1,0:T(1,128)S(1)}, f32[2,64,1,256]{3,2,1,0:T(1,128)S(1)}, u32[]{:S(2)}, u32[]{:S(2)}) collective-permute-start(f32[2,64,1,256]{3,2,1,0:T(1,128)S(1)} %get-tuple-element.47), channel_id=1, source_target_pairs={{1,0},{2,1},{3,2},{4,3},{5,4},{6,5},{7,6},{8,7},{9,8},{10,9},{11,1... | collective-permute-start | bytes 393224 | tf_op jit(solution)/shard_map/ppermute | solution.py:20
  28.6 6.8 %collective-permute-start.3 = (f32[2,64,1,256]{3,2,1,0:T(1,128)S(1)}, f32[2,64,1,256]{3,2,1,0:T(1,128)S(1)}, u32[]{:S(2)}, u32[]{:S(2)}) collective-permute-start(f32[2,64,1,256]{3,2,1,0:T(1,128)S(1)} %get-tuple-element.48), channel_id=1, source_target_pairs={{0,1},{1,2},{2,3},{3,4},{4,5},{5,6},{6,7},{7,8},{8,9},{9,10},{10,1... | collective-permute-start | bytes 393224 | tf_op jit(solution)/shard_map/ppermute | solution.py:19
  32.4 29.3 %copy-start.11 = (f32[32,8,256]{2,1,0:T(8,128)}, f32[32,8,256]{2,1,0:T(8,128)S(1)}, u32[]{:S(2)}) copy-start(f32[32,8,256]{2,1,0:T(8,128)S(1)} %fusion.73) | copy-start | bytes 786436
  37.4 8.4 %collective-permute-start.4 = (f32[2,64,2,256]{3,2,1,0:T(2,128)S(1)}, f32[2,64,2,256]{3,2,1,0:T(2,128)S(1)}, u32[]{:S(2)}, u32[]{:S(2)}) collective-permute-start(f32[2,64,2,256]{3,2,1,0:T(2,128)S(1)} %get-tuple-element.46), channel_id=1, source_target_pairs={{1,0},{2,1},{3,2},{4,3},{5,4},{6,5},{7,6},{8,7},{9,8},{10,9},{11,1... | collective-permute-start | bytes 786440 | tf_op jit(solution)/shard_map/ppermute | solution.py:20
  42.0 7.3 %collective-permute-start.5 = (f32[2,64,2,256]{3,2,1,0:T(2,128)S(1)}, f32[2,64,2,256]{3,2,1,0:T(2,128)S(1)}, u32[]{:S(2)}, u32[]{:S(2)}) collective-permute-start(f32[2,64,2,256]{3,2,1,0:T(2,128)S(1)} %get-tuple-element.45), channel_id=1, source_target_pairs={{0,1},{1,2},{2,3},{3,4},{4,5},{5,6},{6,7},{7,8},{8,9},{9,10},{10,1... | collective-permute-start | bytes 786440 | tf_op jit(solution)/shard_map/ppermute | solution.py:19
  45.8 15.0 %copy-start.24 = (f32[2,64,2,256]{3,2,1,0:T(2,128)}, f32[2,64,2,256]{3,2,1,0:T(2,128)S(1)}, u32[]{:S(2)}) copy-start(f32[2,64,2,256]{3,2,1,0:T(2,128)S(1)} %collective-permute-done.4) | copy-start | bytes 786436
  49.3 11.3 %copy-start.25 = (f32[2,64,2,256]{3,2,1,0:T(2,128)}, f32[2,64,2,256]{3,2,1,0:T(2,128)S(1)}, u32[]{:S(2)}) copy-start(f32[2,64,2,256]{3,2,1,0:T(2,128)S(1)} %collective-permute-done.5) | copy-start | bytes 786436
  54.1 7.2 %collective-permute-start.6 = (f32[2,32,1,256]{3,2,1,0:T(1,128)S(1)}, f32[2,32,1,256]{3,2,1,0:T(1,128)S(1)}, u32[]{:S(2)}, u32[]{:S(2)}) collective-permute-start(f32[2,32,1,256]{3,2,1,0:T(1,128)S(1)} %get-tuple-element.71), channel_id=1, source_target_pairs={{1,0},{2,1},{3,2},{4,3},{5,4},{6,5},{7,6},{8,7},{9,8},{10,9},{11,1... | collective-permute-start | bytes 196616 | tf_op jit(solution)/shard_map/ppermute | solution.py:20
  57.3 4.4 %collective-permute-start.7 = (f32[2,32,1,256]{3,2,1,0:T(1,128)S(1)}, f32[2,32,1,256]{3,2,1,0:T(1,128)S(1)}, u32[]{:S(2)}, u32[]{:S(2)}) collective-permute-start(f32[2,32,1,256]{3,2,1,0:T(1,128)S(1)} %get-tuple-element.72), channel_id=1, source_target_pairs={{0,1},{1,2},{2,3},{3,4},{4,5},{5,6},{6,7},{7,8},{8,9},{9,10},{10,1... | collective-permute-start | bytes 196616 | tf_op jit(solution)/shard_map/ppermute | solution.py:19
  64.3 7.7 %collective-permute-start.8 = (f32[2,32,1,256]{3,2,1,0:T(1,128)S(1)}, f32[2,32,1,256]{3,2,1,0:T(1,128)S(1)}, u32[]{:S(2)}, u32[]{:S(2)}) collective-permute-start(f32[2,32,1,256]{3,2,1,0:T(1,128)S(1)} %get-tuple-element.65), channel_id=1, source_target_pairs={{0,1},{1,2},{2,3},{3,4},{4,5},{5,6},{6,7},{7,8},{8,9},{9,10},{10,1... | collective-permute-start | bytes 196616 | tf_op jit(solution)/shard_map/ppermute | solution.py:19
  68.5 5.6 %collective-permute-start.9 = (f32[2,32,1,256]{3,2,1,0:T(1,128)S(1)}, f32[2,32,1,256]{3,2,1,0:T(1,128)S(1)}, u32[]{:S(2)}, u32[]{:S(2)}) collective-permute-start(f32[2,32,1,256]{3,2,1,0:T(1,128)S(1)} %get-tuple-element.66), channel_id=1, source_target_pairs={{1,0},{2,1},{3,2},{4,3},{5,4},{6,5},{7,6},{8,7},{9,8},{10,9},{11,1... | collective-permute-start | bytes 196616 | tf_op jit(solution)/shard_map/ppermute | solution.py:20
  85.3 15.3 %collective-permute-start.10 = (f32[2,64,1,256]{3,2,1,0:T(1,128)}, f32[2,64,1,256]{3,2,1,0:T(1,128)}, u32[]{:S(2)}, u32[]{:S(2)}) collective-permute-start(f32[2,64,1,256]{3,2,1,0:T(1,128)} %get-tuple-element.40), channel_id=1, source_target_pairs={{1,0},{2,1},{3,2},{4,3},{5,4},{6,5},{7,6},{8,7},{9,8},{10,9},{11,1... | collective-permute-start | bytes 393224 | tf_op jit(solution)/shard_map/ppermute | solution.py:20
  87.8 12.9 %collective-permute-start.11 = (f32[2,64,1,256]{3,2,1,0:T(1,128)}, f32[2,64,1,256]{3,2,1,0:T(1,128)}, u32[]{:S(2)}, u32[]{:S(2)}) collective-permute-start(f32[2,64,1,256]{3,2,1,0:T(1,128)} %get-tuple-element.41), channel_id=1, source_target_pairs={{0,1},{1,2},{2,3},{3,4},{4,5},{5,6},{6,7},{7,8},{8,9},{9,10},{10,1... | collective-permute-start | bytes 393224 | tf_op jit(solution)/shard_map/ppermute | solution.py:19
  103.8 6.3 %collective-permute-start.12 = (f32[2,64,1,256]{3,2,1,0:T(1,128)S(1)}, f32[2,64,1,256]{3,2,1,0:T(1,128)S(1)}, u32[]{:S(2)}, u32[]{:S(2)}) collective-permute-start(f32[2,64,1,256]{3,2,1,0:T(1,128)S(1)} %get-tuple-element.39), channel_id=1, source_target_pairs={{1,0},{2,1},{3,2},{4,3},{5,4},{6,5},{7,6},{8,7},{9,8},{10,9},{11,1... | collective-permute-start | bytes 393224 | tf_op jit(solution)/shard_map/ppermute | solution.py:20
  107.2 5.5 %collective-permute-start.13 = (f32[2,64,1,256]{3,2,1,0:T(1,128)S(1)}, f32[2,64,1,256]{3,2,1,0:T(1,128)S(1)}, u32[]{:S(2)}, u32[]{:S(2)}) collective-permute-start(f32[2,64,1,256]{3,2,1,0:T(1,128)S(1)} %get-tuple-element.38), channel_id=1, source_target_pairs={{0,1},{1,2},{2,3},{3,4},{4,5},{5,6},{6,7},{7,8},{8,9},{9,10},{10,1... | collective-permute-start | bytes 393224 | tf_op jit(solution)/shard_map/ppermute | solution.py:19
  117.1 19.0 %collective-permute-start.14 = (f32[2,32,8,256]{3,2,1,0:T(8,128)S(1)}, f32[2,32,8,256]{3,2,1,0:T(8,128)S(1)}, u32[]{:S(2)}, u32[]{:S(2)}) collective-permute-start(f32[2,32,8,256]{3,2,1,0:T(8,128)S(1)} %get-tuple-element.5), channel_id=1, source_target_pairs={{0,16},{1,17},{2,18},{3,19},{4,20},{5,21},{6,22},{7,23},{8,24},{9,... | collective-permute-start | bytes 1572872 | tf_op jit(solution)/shard_map/ppermute | solution.py:244
  118.4 17.1 %collective-permute-start.15 = (f32[2,32,1,256]{3,2,1,0:T(1,128)S(1)}, f32[2,32,1,256]{3,2,1,0:T(1,128)S(1)}, u32[]{:S(2)}, u32[]{:S(2)}) collective-permute-start(f32[2,32,1,256]{3,2,1,0:T(1,128)S(1)} %get-tuple-element.51), channel_id=1, source_target_pairs={{0,17},{1,18},{2,19},{3,20},{4,21},{5,22},{6,23},{7,24},{8,25},{9,... | collective-permute-start | bytes 196616 | tf_op jit(solution)/shard_map/ppermute | solution.py:245
  119.7 16.1 %collective-permute-start.16 = (f32[2,32,1,256]{3,2,1,0:T(1,128)S(1)}, f32[2,32,1,256]{3,2,1,0:T(1,128)S(1)}, u32[]{:S(2)}, u32[]{:S(2)}) collective-permute-start(f32[2,32,1,256]{3,2,1,0:T(1,128)S(1)} %get-tuple-element.52), channel_id=1, source_target_pairs={{1,16},{2,17},{3,18},{4,19},{5,20},{6,21},{7,22},{8,23},{9,24},{10... | collective-permute-start | bytes 196616 | tf_op jit(solution)/shard_map/ppermute | solution.py:246
  (30 other events, 87.7 us)

commit v7 on v6

--- a/solution.py
+++ b/solution.py
@@ -49,9 +49,14 @@
     reach = int(x_spacing)
     padded = jnp.concatenate([west(halo)] * reach + [field] + [east(halo)] * reach, axis=-2)
     width = field.shape[-2]
-    middle = field
-    eastward = padded[..., 2 * reach:, :]
-    westward = padded[..., :width, :]
+    return stencil(
+        field, padded[..., 2 * reach:, :], padded[..., :width, :],
+        x_speed, y_speed, h_spread, v_spread, coupling, x_spacing, z_spacing,
+    )
+
+
+def stencil(middle, eastward, westward, x_speed, y_speed, h_spread, v_spread, coupling,
+            x_spacing, z_spacing):
     y_widths = [(0, 0)] * (middle.ndim - 1) + [(1, 1)]
     y_padded = jnp.pad(middle, y_widths)
     northward = y_padded[..., 2:]
@@ -145,11 +150,22 @@
     def joined(fine, coarse):
         return jnp.concatenate([fine, coarse], axis=-3)
 
+    coarse_coefs = (coarse_x, coarse_y, coarse_h, coarse_v)
+    coarse_levels = coarse_first.shape[-3]
+
+    def coef_edge(edge):
+        stacked = jnp.stack([edge(c) for c in coarse_coefs])
+        return stacked.reshape((2, -1) + stacked.shape[-2:])
+
     before, after = exchange(
-        joined(hi(initial), hi(coarse_first)), joined(lo(initial), lo(coarse_first))
-    )
-    init_b, first_b = before[..., :levels, :, :], before[..., levels:, :, :]
-    init_a, first_a = after[..., :levels, :, :], after[..., levels:, :, :]
+        joined(joined(hi(initial), hi(coarse_first)), coef_edge(hi)),
+        joined(joined(lo(initial), lo(coarse_first)), coef_edge(lo)),
+    )
+    split = (levels, levels + coarse_levels)
+    init_b, first_b = before[..., : split[0], :, :], before[..., split[0] : split[1], :, :]
+    init_a, first_a = after[..., : split[0], :, :], after[..., split[0] : split[1], :, :]
+    edge_coefs = pack(before[..., split[1] :, :, :], after[..., split[1] :, :, :])
+    edge_coefs = edge_coefs.reshape((4, coarse_levels) + edge_coefs.shape[-2:])
     halo_zero = pack(init_b, init_a)
     halo_first = pack(first_b, first_a)
     first_rate = fine_rate(initial, halo_zero)
@@ -172,9 +188,30 @@
     chain = [coarse_first]
     chain_halo = [halo_first]
     rate = coarse_first_rate
+    wide = None
     for count in range(slabs):
         after = chain[-1] + slab_step * rate + offset
-        after_halo = halo_of(after)
+        if wide is not None:
+            strip_b, strip_a, offset_edge = wide
+            edge = pack(strip_b[..., 2:3, :], strip_a[..., 0:1, :])
+            edge_rate = stencil(
+                edge,
+                pack(lo(chain[-1]), strip_a[..., 2:3, :]),
+                pack(strip_b[..., 0:1, :], hi(chain[-1])),
+                *(edge_coefs[k] for k in range(4)),
+                coupling, 2.0, 2.0,
+            )
+            after_halo = edge + slab_step * edge_rate + offset_edge
+        elif count + 2 == slabs:
+            packed_b, packed_a = exchange(
+                jnp.concatenate([hi(after, 3), hi(offset)], axis=-2),
+                jnp.concatenate([lo(after, 3), lo(offset)], axis=-2),
+            )
+            strip_b, strip_a = packed_b[..., :3, :], packed_a[..., :3, :]
+            wide = (strip_b, strip_a, pack(packed_b[..., 3:, :], packed_a[..., 3:, :]))
+            after_halo = pack(strip_b[..., 2:3, :], strip_a[..., 0:1, :])
+        else:
+            after_halo = halo_of(after)
         chain.append(after)
         chain_halo.append(after_halo)
         if count + 1 < slabs:

time: 140 us -> 134 us (0.957)
  starting transfers between devices: 45.7 us -> 41 us
  local copies, waits for them, and re-layouts: 25.3 us -> 23.3 us
    slice x10, local copies, waits for them, and re-layouts: 5.55 us -> 0.48 us  [pair_sum(): jnp.roll(field, 1, axis=-2)]
    ppermute x7 -> x6, starting transfers between devices: 21.7 us -> 17.9 us  [exchange(): before = lax.ppermute(to_right, 'space', shift_pairs(count, 1))]
    slice x14, local copies, waits for them, and re-layouts: 1.88 us -> 3.64 us  [pair_sum(): jnp.roll(field, -1, axis=-2)]
    mul x8, other arithmetic: 5.86 us -> 4.42 us  [shrink(): return pair_sum(levels) * 0.25]
    ppermute x7 -> x6, starting transfers between devices: 20.1 us -> 19.3 us  [exchange(): after = lax.ppermute(to_left, 'space', shift_pairs(count, -1))]
    ppermute x7 -> x6, waiting for transfers between devices: 4.16 us -> 3.38 us  [exchange(): after = lax.ppermute(to_left, 'space', shift_pairs(count, -1))]
    slice x5 -> x7, local copies, waits for them, and re-layouts: 4.28 us -> 4.93 us  [the longest x2 2.3 us: body(): edge_coefs = pack(before[..., split[1]:, :, :], after[..., split[1]:, :, :])]
    ppermute x7 -> x6, waiting for transfers between devices: 7.72 us -> 8.29 us  [exchange(): before = lax.ppermute(to_right, 'space', shift_pairs(count, 1))]
  transfers between devices with their start and end apart: 17 -> 15, of which waited for: 9 -> 9; matrix products, arithmetic and copies ran while one was open for 19% -> 15% of each run, Pallas kernels for 0% -> 0%
where the time goes in v7:
time: 134 us
  starting transfers between devices  41 us (31%)
  other arithmetic  40.4 us (30%)
  waiting for transfers between devices  27.6 us (21%)
  local copies, waits for them, and re-layouts  23.3 us (17%)
    ppermute x6, starting transfers between devices, exchange(): after = lax.ppermute(to_left, 'space', shift_pairs(count, -1))  19.3 us
    ppermute x6, starting transfers between devices, exchange(): before = lax.ppermute(to_right, 'space', shift_pairs(count, 1))  17.9 us
    ppermute x1, waiting for transfers between devices, body(): passed_b = lax.ppermute(hi(after), ('tm', 'space'), to_east)  14.4 us
    add x2, other arithmetic, first_node(): node_zero + half_step * (rate_zero - s0)  8.52 us
    ppermute x6, waiting for transfers between devices, exchange(): before = lax.ppermute(to_right, 'space', shift_pairs(count, 1))  8.29 us
    broadcast_in_dim x9, local copies, waits for them, and re-layouts, expand(): return jnp.repeat(field, 2, axis=-3)  5.08 us
    unnamed x78, local copies, waits for them, and re-layouts  4.88 us
    mul x8, other arithmetic, shrink(): return pair_sum(levels) * 0.25  4.42 us
  transfers between devices with their start and end apart: 15, of which 9 were waited for; matrix products, arithmetic and copies ran while one was open for 15% of the time, Pallas kernels for 0%

profile of v7, /device:TPU:11, one launch (start us, length us, event | category | flops | bytes accessed | tf_op | source)
XLA Modules:
  0.0 133.6 jit_solution(3559161579645547238)
XLA Ops:
  7.3 2.7 %collective-permute-start = (f32[2,160,1,256]{3,2,1,0:T(1,128)}, f32[2,160,1,256]{3,2,1,0:T(1,128)}, u32[]{:S(2)}, u32[]{:S(2)}) collective-permute-start(f32[2,160,1,256]{3,2,1,0:T(1,128)} %pad_maximum_fusion.34), channel_id=1, source_target_pairs={{1,0},{2,1},{3,2},{4,3},{5,4},{6,5},{7,6},{8,7},{9,8},{10,9},{11,1... | collective-permute-start | bytes 983048 | tf_op jit(solution)/shard_map/ppermute | solution.py:20
  11.1 3.0 %collective-permute-start.1 = (f32[2,160,1,256]{3,2,1,0:T(1,128)}, f32[2,160,1,256]{3,2,1,0:T(1,128)}, u32[]{:S(2)}, u32[]{:S(2)}) collective-permute-start(f32[2,160,1,256]{3,2,1,0:T(1,128)} %pad_maximum_fusion.35), channel_id=1, source_target_pairs={{0,1},{1,2},{2,3},{3,4},{4,5},{5,6},{6,7},{7,8},{8,9},{9,10},{10,1... | collective-permute-start | bytes 983048 | tf_op jit(solution)/shard_map/ppermute | solution.py:19
  14.9 2.5 %broadcast_multiply_fusion.2 = (f32[2]{0:T(128)S(1)}, f32[2]{0:T(128)S(1)}, f32[2]{0:T(128)S(1)}, f32[2]{0:T(128)S(1)}) fusion(f32[1]{0:T(128)} %bitcast.13, f32[1]{0:T(128)} %bitcast.12, f32[1]{0:T(128)} %bitcast.11, f32[1]{0:T(128)} %bitcast.10), kind=kLoop, calls=%fused_computation.267 | loop fusion | flops 8 | bytes 48 | tf_op jit(solution)/shard_map/mul | solution.py:79
  21.0 1.7 %multiply_add_fusion.3 = (f32[2,64,8,256]{3,2,1,0:T(8,128)S(1)}, f32[2,64,8,256]{3,2,1,0:T(8,128)S(1)}) fusion(f32[2,64,8,256]{3,2,1,0:T(8,128)S(1)} %copy-done.4, f32[2]{0:T(128)S(1)} %get-tuple-element.31, f32[2]{0:T(128)S(1)} %get-tuple-element.160, f32[64,8,256]{2,1,0:T(8,128)S(1)} %copy-done.2, f32[64,8,256]{2,1,0:T(8,128)S(1)} %copy-done.1, ...), kind=kLoop, calls=%fused_computation.65 | loop fusion | flops 8912896 | bytes 5505040 | tf_op jit(solution)/shard_map/add | solution.py:135
  22.9 3.7 %collective-permute-start.2 = (f32[2,64,1,256]{3,2,1,0:T(1,128)S(1)}, f32[2,64,1,256]{3,2,1,0:T(1,128)S(1)}, u32[]{:S(2)}, u32[]{:S(2)}) collective-permute-start(f32[2,64,1,256]{3,2,1,0:T(1,128)S(1)} %get-tuple-element.47), channel_id=1, source_target_pairs={{1,0},{2,1},{3,2},{4,3},{5,4},{6,5},{7,6},{8,7},{9,8},{10,9},{11,1... | collective-permute-start | bytes 393224 | tf_op jit(solution)/shard_map/ppermute | solution.py:20
  26.5 2.6 %collective-permute-start.3 = (f32[2,64,1,256]{3,2,1,0:T(1,128)S(1)}, f32[2,64,1,256]{3,2,1,0:T(1,128)S(1)}, u32[]{:S(2)}, u32[]{:S(2)}) collective-permute-start(f32[2,64,1,256]{3,2,1,0:T(1,128)S(1)} %get-tuple-element.48), channel_id=1, source_target_pairs={{0,1},{1,2},{2,3},{3,4},{4,5},{5,6},{6,7},{7,8},{8,9},{9,10},{10,1... | collective-permute-start | bytes 393224 | tf_op jit(solution)/shard_map/ppermute | solution.py:19
  31.2 1.7 %multiply_add_fusion.2 = (f32[2,64,8,256]{3,2,1,0:T(8,128)S(1)}, f32[2,64,8,256]{3,2,1,0:T(8,128)S(1)}) fusion(f32[2,64,8,256]{3,2,1,0:T(8,128)S(1)} %get-tuple-element.35, f32[2,64,8,256]{3,2,1,0:T(8,128)S(1)} %get-tuple-element.34, f32[2]{0:T(128)S(1)} %get-tuple-element.31, f32[2]{0:T(128)S(1)} %get-tuple-element.160, f32[64,8,256]{2,1,0:T(8,128)S(1)} %copy-done.2, ...), kind=kLoop, calls=%fused_computation.61 | loop fusion | flops 8912896 | bytes 6553616 | tf_op jit(solution)/shard_map/add | solution.py:142
  33.1 4.4 %collective-permute-start.4 = (f32[2,64,2,256]{3,2,1,0:T(2,128)S(1)}, f32[2,64,2,256]{3,2,1,0:T(2,128)S(1)}, u32[]{:S(2)}, u32[]{:S(2)}) collective-permute-start(f32[2,64,2,256]{3,2,1,0:T(2,128)S(1)} %get-tuple-element.46), channel_id=1, source_target_pairs={{1,0},{2,1},{3,2},{4,3},{5,4},{6,5},{7,6},{8,7},{9,8},{10,9},{11,1... | collective-permute-start | bytes 786440 | tf_op jit(solution)/shard_map/ppermute | solution.py:20
  37.6 1.9 %collective-permute-start.5 = (f32[2,64,2,256]{3,2,1,0:T(2,128)S(1)}, f32[2,64,2,256]{3,2,1,0:T(2,128)S(1)}, u32[]{:S(2)}, u32[]{:S(2)}) collective-permute-start(f32[2,64,2,256]{3,2,1,0:T(2,128)S(1)} %get-tuple-element.45), channel_id=1, source_target_pairs={{0,1},{1,2},{2,3},{3,4},{4,5},{5,6},{6,7},{7,8},{8,9},{9,10},{10,1... | collective-permute-start | bytes 786440 | tf_op jit(solution)/shard_map/ppermute | solution.py:19
  39.7 1.8 %collective-permute-done.4 = f32[2,64,2,256]{3,2,1,0:T(2,128)S(1)} collective-permute-done((f32[2,64,2,256]{3,2,1,0:T(2,128)S(1)}, f32[2,64,2,256]{3,2,1,0:T(2,128)S(1)}, u32[]{:S(2)}, u32[]{:S(2)}) %collective-permute-start.4) | collective-permute-done | bytes 262176 | tf_op jit(solution)/shard_map/ppermute | solution.py:20
  41.6 3.3 %collective-permute-done.5 = f32[2,64,2,256]{3,2,1,0:T(2,128)S(1)} collective-permute-done((f32[2,64,2,256]{3,2,1,0:T(2,128)S(1)}, f32[2,64,2,256]{3,2,1,0:T(2,128)S(1)}, u32[]{:S(2)}, u32[]{:S(2)}) %collective-permute-start.5) | collective-permute-done | bytes 262176 | tf_op jit(solution)/shard_map/ppermute | solution.py:19
  47.9 2.0 %fusion.92 = (f32[2,32,8,256]{3,2,1,0:T(8,128)S(1)}, f32[2,32,8,256]{3,2,1,0:T(8,128)S(1)}, f32[2,32,8,256]{3,2,1,0:T(8,128)}) fusion(f32[2,32,8,256]{3,2,1,0:T(8,128)S(1)} %copy-done.5, f32[2,32,7,256]{3,2,1,0:T(8,128)S(1)} %get-tuple-element.76, f32[2,32,1,256]{3,2,1,0:T(1,128)S(1)} %get-tuple-element.78, f32[2,32,1,256]{3,2,1,0:T(1,128)S(1)} %get-tuple-element.77, ...), kind=kLoop, calls=%fused_computation.272 | loop fusion | flops 5505024 | bytes 5898328 | tf_op jit(solution)/shard_map/add | solution.py:193
  50.3 3.2 %collective-permute-start.6 = (f32[2,32,4,256]{3,2,1,0:T(4,128)S(1)}, f32[2,32,4,256]{3,2,1,0:T(4,128)S(1)}, u32[]{:S(2)}, u32[]{:S(2)}) collective-permute-start(f32[2,32,4,256]{3,2,1,0:T(4,128)S(1)} %pad_maximum_fusion.36), channel_id=1, source_target_pairs={{1,0},{2,1},{3,2},{4,3},{5,4},{6,5},{7,6},{8,7},{9,8},{10,9},{11,1... | collective-permute-start | bytes 786440 | tf_op jit(solution)/shard_map/ppermute | solution.py:20
  53.6 3.3 %collective-permute-start.7 = (f32[2,32,4,256]{3,2,1,0:T(4,128)S(1)}, f32[2,32,4,256]{3,2,1,0:T(4,128)S(1)}, u32[]{:S(2)}, u32[]{:S(2)}) collective-permute-start(f32[2,32,4,256]{3,2,1,0:T(4,128)S(1)} %pad_maximum_fusion.37), channel_id=1, source_target_pairs={{0,1},{1,2},{2,3},{3,4},{4,5},{5,6},{6,7},{7,8},{8,9},{9,10},{10,1... | collective-permute-start | bytes 786440 | tf_op jit(solution)/shard_map/ppermute | solution.py:19
  58.9 1.9 %collective-permute-done.7 = f32[2,32,4,256]{3,2,1,0:T(4,128)S(1)} collective-permute-done((f32[2,32,4,256]{3,2,1,0:T(4,128)S(1)}, f32[2,32,4,256]{3,2,1,0:T(4,128)S(1)}, u32[]{:S(2)}, u32[]{:S(2)}) %collective-permute-start.7) | collective-permute-done | bytes 262176 | tf_op jit(solution)/shard_map/ppermute | solution.py:19
  70.1 6.8 %multiply_add_fusion.1 = (f32[2,64,8,256]{3,2,1,0:T(8,128)S(1)}, f32[2,64,8,256]{3,2,1,0:T(8,128)}, f32[2,64,8,256]{3,2,1,0:T(8,128)}, f32[2,64,8,256]{3,2,1,0:T(8,128)}, f32[2,64,8,256]{3,2,1,0:T(8,128)}) fusion(f32[2,64,8,256]{3,2,1,0:T(8,128)S(1)} %get-tuple-element.43, f32[2,64,8,256]{3,2,1,0:T(8,128)S(1)} %add.782, f32[2]{0:T(128)S(1)} %get-tuple-element.31, ...), kind=kLoop, calls=%fused_computation.44 | loop fusion | flops 27787264 | bytes 12582928 | tf_op jit(solution)/shard_map/add | solution.py:135
  77.8 3.3 %collective-permute-start.8 = (f32[2,64,1,256]{3,2,1,0:T(1,128)}, f32[2,64,1,256]{3,2,1,0:T(1,128)}, u32[]{:S(2)}, u32[]{:S(2)}) collective-permute-start(f32[2,64,1,256]{3,2,1,0:T(1,128)} %get-tuple-element.40), channel_id=1, source_target_pairs={{1,0},{2,1},{3,2},{4,3},{5,4},{6,5},{7,6},{8,7},{9,8},{10,9},{11,1... | collective-permute-start | bytes 393224 | tf_op jit(solution)/shard_map/ppermute | solution.py:20
  81.1 3.2 %collective-permute-start.9 = (f32[2,64,1,256]{3,2,1,0:T(1,128)}, f32[2,64,1,256]{3,2,1,0:T(1,128)}, u32[]{:S(2)}, u32[]{:S(2)}) collective-permute-start(f32[2,64,1,256]{3,2,1,0:T(1,128)} %get-tuple-element.41), channel_id=1, source_target_pairs={{0,1},{1,2},{2,3},{3,4},{4,5},{5,6},{6,7},{7,8},{8,9},{9,10},{10,1... | collective-permute-start | bytes 393224 | tf_op jit(solution)/shard_map/ppermute | solution.py:19
  89.4 1.6 %broadcast_in_dim.39 = f32[2,64,256]{2,1,0:T(8,128)} reshape(f32[2,32,2,256]{3,2,1,0:T(2,128)} %broadcast_in_dim.38) | data formatting | bytes 262144 | tf_op jit(solution)/shard_map/broadcast_in_dim | solution.py:97
  95.9 2.6 %multiply_add_fusion = (f32[2,64,8,256]{3,2,1,0:T(8,128)S(1)}, f32[2,64,8,256]{3,2,1,0:T(8,128)S(1)}) fusion(f32[2,64,8,256]{3,2,1,0:T(8,128)S(1)} %copy-done.20, f32[2,64,8,256]{3,2,1,0:T(8,128)S(1)} %copy-done.19, f32[2,64,8,256]{3,2,1,0:T(8,128)S(1)} %get-tuple-element.11, f32[2,64,8,256]{3,2,1,0:T(8,128)S(1)} %copy-done.18, f32[2]{0:T(128)S(1)} %get-tuple-element.31, ...), kind=kLoop, calls=%fused_computation.40 | loop fusion | flops 8912896 | bytes 8650768 | tf_op jit(solution)/shard_map/add | solution.py:142
  98.7 1.9 %collective-permute-start.10 = (f32[2,64,1,256]{3,2,1,0:T(1,128)S(1)}, f32[2,64,1,256]{3,2,1,0:T(1,128)S(1)}, u32[]{:S(2)}, u32[]{:S(2)}) collective-permute-start(f32[2,64,1,256]{3,2,1,0:T(1,128)S(1)} %get-tuple-element.39), channel_id=1, source_target_pairs={{1,0},{2,1},{3,2},{4,3},{5,4},{6,5},{7,6},{8,7},{9,8},{10,9},{11,1... | collective-permute-start | bytes 393224 | tf_op jit(solution)/shard_map/ppermute | solution.py:20
  100.7 3.8 %collective-permute-start.11 = (f32[2,64,1,256]{3,2,1,0:T(1,128)S(1)}, f32[2,64,1,256]{3,2,1,0:T(1,128)S(1)}, u32[]{:S(2)}, u32[]{:S(2)}) collective-permute-start(f32[2,64,1,256]{3,2,1,0:T(1,128)S(1)} %get-tuple-element.38), channel_id=1, source_target_pairs={{0,1},{1,2},{2,3},{3,4},{4,5},{5,6},{6,7},{7,8},{8,9},{9,10},{10,1... | collective-permute-start | bytes 393224 | tf_op jit(solution)/shard_map/ppermute | solution.py:19
  105.0 1.7 %collective-permute-done.11 = f32[2,64,1,256]{3,2,1,0:T(1,128)S(1)} collective-permute-done((f32[2,64,1,256]{3,2,1,0:T(1,128)S(1)}, f32[2,64,1,256]{3,2,1,0:T(1,128)S(1)}, u32[]{:S(2)}, u32[]{:S(2)}) %collective-permute-start.11) | collective-permute-done | bytes 131104 | tf_op jit(solution)/shard_map/ppermute | solution.py:19
  114.8 14.4 %collective-permute-done.13 = f32[2,32,1,256]{3,2,1,0:T(1,128)S(1)} collective-permute-done((f32[2,32,1,256]{3,2,1,0:T(1,128)S(1)}, f32[2,32,1,256]{3,2,1,0:T(1,128)S(1)}, u32[]{:S(2)}, u32[]{:S(2)}) %collective-permute-start.13) | collective-permute-done | bytes 65568 | tf_op jit(solution)/shard_map/ppermute | solution.py:282
  (207 shorter events, 53.2 us)
Async XLA Ops:
  6.0 8.2 %copy-start.37 = (f32[2,2]{1,0:T(2,128)S(1)}, f32[2,2]{1,0:T(2,128)}, u32[]{:S(2)}) copy-start(f32[2,2]{1,0:T(2,128)} %param.11) | copy-start | bytes 52
  7.2 13.7 %copy-start.2 = (f32[64,8,256]{2,1,0:T(8,128)S(1)}, f32[64,8,256]{2,1,0:T(8,128)}, u32[]{:S(2)}) copy-start(f32[64,8,256]{2,1,0:T(8,128)} %param.8) | copy-start | bytes 1572868
  7.3 13.7 %copy-start.3 = (f32[64,8,256]{2,1,0:T(8,128)S(1)}, f32[64,8,256]{2,1,0:T(8,128)}, u32[]{:S(2)}) copy-start(f32[64,8,256]{2,1,0:T(8,128)} %param.9) | copy-start | bytes 1572868
  7.3 10.1 %collective-permute-start = (f32[2,160,1,256]{3,2,1,0:T(1,128)}, f32[2,160,1,256]{3,2,1,0:T(1,128)}, u32[]{:S(2)}, u32[]{:S(2)}) collective-permute-start(f32[2,160,1,256]{3,2,1,0:T(1,128)} %pad_maximum_fusion.34), channel_id=1, source_target_pairs={{1,0},{2,1},{3,2},{4,3},{5,4},{6,5},{7,6},{8,7},{9,8},{10,9},{11,1... | collective-permute-start | bytes 983048 | tf_op jit(solution)/shard_map/ppermute | solution.py:20
  11.1 8.7 %collective-permute-start.1 = (f32[2,160,1,256]{3,2,1,0:T(1,128)}, f32[2,160,1,256]{3,2,1,0:T(1,128)}, u32[]{:S(2)}, u32[]{:S(2)}) collective-permute-start(f32[2,160,1,256]{3,2,1,0:T(1,128)} %pad_maximum_fusion.35), channel_id=1, source_target_pairs={{0,1},{1,2},{2,3},{3,4},{4,5},{5,6},{6,7},{7,8},{8,9},{9,10},{10,1... | collective-permute-start | bytes 983048 | tf_op jit(solution)/shard_map/ppermute | solution.py:19
  17.4 29.3 %copy-start.33 = (f32[2]{0:T(128)}, f32[2]{0:T(128)S(1)}, u32[]{:S(2)}) copy-start(f32[2]{0:T(128)S(1)} %get-tuple-element.30) | copy-start | bytes 28
  17.4 29.3 %copy-start.35 = (f32[2]{0:T(128)}, f32[2]{0:T(128)S(1)}, u32[]{:S(2)}) copy-start(f32[2]{0:T(128)S(1)} %get-tuple-element.159) | copy-start | bytes 28
  22.9 8.3 %collective-permute-start.2 = (f32[2,64,1,256]{3,2,1,0:T(1,128)S(1)}, f32[2,64,1,256]{3,2,1,0:T(1,128)S(1)}, u32[]{:S(2)}, u32[]{:S(2)}) collective-permute-start(f32[2,64,1,256]{3,2,1,0:T(1,128)S(1)} %get-tuple-element.47), channel_id=1, source_target_pairs={{1,0},{2,1},{3,2},{4,3},{5,4},{6,5},{7,6},{8,7},{9,8},{10,9},{11,1... | collective-permute-start | bytes 393224 | tf_op jit(solution)/shard_map/ppermute | solution.py:20
  26.5 4.6 %collective-permute-start.3 = (f32[2,64,1,256]{3,2,1,0:T(1,128)S(1)}, f32[2,64,1,256]{3,2,1,0:T(1,128)S(1)}, u32[]{:S(2)}, u32[]{:S(2)}) collective-permute-start(f32[2,64,1,256]{3,2,1,0:T(1,128)S(1)} %get-tuple-element.48), channel_id=1, source_target_pairs={{0,1},{1,2},{2,3},{3,4},{4,5},{5,6},{6,7},{7,8},{8,9},{9,10},{10,1... | collective-permute-start | bytes 393224 | tf_op jit(solution)/shard_map/ppermute | solution.py:19
  33.1 8.3 %collective-permute-start.4 = (f32[2,64,2,256]{3,2,1,0:T(2,128)S(1)}, f32[2,64,2,256]{3,2,1,0:T(2,128)S(1)}, u32[]{:S(2)}, u32[]{:S(2)}) collective-permute-start(f32[2,64,2,256]{3,2,1,0:T(2,128)S(1)} %get-tuple-element.46), channel_id=1, source_target_pairs={{1,0},{2,1},{3,2},{4,3},{5,4},{6,5},{7,6},{8,7},{9,8},{10,9},{11,1... | collective-permute-start | bytes 786440 | tf_op jit(solution)/shard_map/ppermute | solution.py:20
  37.6 7.3 %collective-permute-start.5 = (f32[2,64,2,256]{3,2,1,0:T(2,128)S(1)}, f32[2,64,2,256]{3,2,1,0:T(2,128)S(1)}, u32[]{:S(2)}, u32[]{:S(2)}) collective-permute-start(f32[2,64,2,256]{3,2,1,0:T(2,128)S(1)} %get-tuple-element.45), channel_id=1, source_target_pairs={{0,1},{1,2},{2,3},{3,4},{4,5},{5,6},{6,7},{7,8},{8,9},{9,10},{10,1... | collective-permute-start | bytes 786440 | tf_op jit(solution)/shard_map/ppermute | solution.py:19
  41.5 15.7 %copy-start.27 = (f32[2,64,2,256]{3,2,1,0:T(2,128)}, f32[2,64,2,256]{3,2,1,0:T(2,128)S(1)}, u32[]{:S(2)}) copy-start(f32[2,64,2,256]{3,2,1,0:T(2,128)S(1)} %collective-permute-done.4) | copy-start | bytes 786436
  44.9 12.0 %copy-start.28 = (f32[2,64,2,256]{3,2,1,0:T(2,128)}, f32[2,64,2,256]{3,2,1,0:T(2,128)S(1)}, u32[]{:S(2)}) copy-start(f32[2,64,2,256]{3,2,1,0:T(2,128)S(1)} %collective-permute-done.5) | copy-start | bytes 786436
  50.3 8.4 %collective-permute-start.6 = (f32[2,32,4,256]{3,2,1,0:T(4,128)S(1)}, f32[2,32,4,256]{3,2,1,0:T(4,128)S(1)}, u32[]{:S(2)}, u32[]{:S(2)}) collective-permute-start(f32[2,32,4,256]{3,2,1,0:T(4,128)S(1)} %pad_maximum_fusion.36), channel_id=1, source_target_pairs={{1,0},{2,1},{3,2},{4,3},{5,4},{6,5},{7,6},{8,7},{9,8},{10,9},{11,1... | collective-permute-start | bytes 786440 | tf_op jit(solution)/shard_map/ppermute | solution.py:20
  53.6 7.2 %collective-permute-start.7 = (f32[2,32,4,256]{3,2,1,0:T(4,128)S(1)}, f32[2,32,4,256]{3,2,1,0:T(4,128)S(1)}, u32[]{:S(2)}, u32[]{:S(2)}) collective-permute-start(f32[2,32,4,256]{3,2,1,0:T(4,128)S(1)} %pad_maximum_fusion.37), channel_id=1, source_target_pairs={{0,1},{1,2},{2,3},{3,4},{4,5},{5,6},{6,7},{7,8},{8,9},{9,10},{10,1... | collective-permute-start | bytes 786440 | tf_op jit(solution)/shard_map/ppermute | solution.py:19
  63.4 6.7 %copy-start.7 = (f32[2,64,8,256]{3,2,1,0:T(8,128)}, f32[2,64,8,256]{3,2,1,0:T(8,128)S(1)}, u32[]{:S(2)}) copy-start(f32[2,64,8,256]{3,2,1,0:T(8,128)S(1)} %get-tuple-element.43) | copy-start | bytes 3145732
  77.8 17.6 %collective-permute-start.8 = (f32[2,64,1,256]{3,2,1,0:T(1,128)}, f32[2,64,1,256]{3,2,1,0:T(1,128)}, u32[]{:S(2)}, u32[]{:S(2)}) collective-permute-start(f32[2,64,1,256]{3,2,1,0:T(1,128)} %get-tuple-element.40), channel_id=1, source_target_pairs={{1,0},{2,1},{3,2},{4,3},{5,4},{6,5},{7,6},{8,7},{9,8},{10,9},{11,1... | collective-permute-start | bytes 393224 | tf_op jit(solution)/shard_map/ppermute | solution.py:20
  81.1 14.3 %collective-permute-start.9 = (f32[2,64,1,256]{3,2,1,0:T(1,128)}, f32[2,64,1,256]{3,2,1,0:T(1,128)}, u32[]{:S(2)}, u32[]{:S(2)}) collective-permute-start(f32[2,64,1,256]{3,2,1,0:T(1,128)} %get-tuple-element.41), channel_id=1, source_target_pairs={{0,1},{1,2},{2,3},{3,4},{4,5},{5,6},{6,7},{7,8},{8,9},{9,10},{10,1... | collective-permute-start | bytes 393224 | tf_op jit(solution)/shard_map/ppermute | solution.py:19
  98.7 6.3 %collective-permute-start.10 = (f32[2,64,1,256]{3,2,1,0:T(1,128)S(1)}, f32[2,64,1,256]{3,2,1,0:T(1,128)S(1)}, u32[]{:S(2)}, u32[]{:S(2)}) collective-permute-start(f32[2,64,1,256]{3,2,1,0:T(1,128)S(1)} %get-tuple-element.39), channel_id=1, source_target_pairs={{1,0},{2,1},{3,2},{4,3},{5,4},{6,5},{7,6},{8,7},{9,8},{10,9},{11,1... | collective-permute-start | bytes 393224 | tf_op jit(solution)/shard_map/ppermute | solution.py:20
  100.7 6.1 %copy-start.21 = (f32[2,64,8,256]{3,2,1,0:T(8,128)S(1)}, f32[2,64,8,256]{3,2,1,0:T(8,128)}, u32[]{:S(2)}) copy-start(f32[2,64,8,256]{3,2,1,0:T(8,128)} %get-tuple-element.13) | copy-start | bytes 3145732
  100.7 6.1 %collective-permute-start.11 = (f32[2,64,1,256]{3,2,1,0:T(1,128)S(1)}, f32[2,64,1,256]{3,2,1,0:T(1,128)S(1)}, u32[]{:S(2)}, u32[]{:S(2)}) collective-permute-start(f32[2,64,1,256]{3,2,1,0:T(1,128)S(1)} %get-tuple-element.38), channel_id=1, source_target_pairs={{0,1},{1,2},{2,3},{3,4},{4,5},{5,6},{6,7},{7,8},{8,9},{9,10},{10,1... | collective-permute-start | bytes 393224 | tf_op jit(solution)/shard_map/ppermute | solution.py:19
  110.8 20.3 %collective-permute-start.12 = (f32[2,32,8,256]{3,2,1,0:T(8,128)S(1)}, f32[2,32,8,256]{3,2,1,0:T(8,128)S(1)}, u32[]{:S(2)}, u32[]{:S(2)}) collective-permute-start(f32[2,32,8,256]{3,2,1,0:T(8,128)S(1)} %get-tuple-element.5), channel_id=1, source_target_pairs={{0,16},{1,17},{2,18},{3,19},{4,20},{5,21},{6,22},{7,23},{8,24},{9,... | collective-permute-start | bytes 1572872 | tf_op jit(solution)/shard_map/ppermute | solution.py:281
  112.1 17.1 %collective-permute-start.13 = (f32[2,32,1,256]{3,2,1,0:T(1,128)S(1)}, f32[2,32,1,256]{3,2,1,0:T(1,128)S(1)}, u32[]{:S(2)}, u32[]{:S(2)}) collective-permute-start(f32[2,32,1,256]{3,2,1,0:T(1,128)S(1)} %get-tuple-element.51), channel_id=1, source_target_pairs={{0,17},{1,18},{2,19},{3,20},{4,21},{5,22},{6,23},{7,24},{8,25},{9,... | collective-permute-start | bytes 196616 | tf_op jit(solution)/shard_map/ppermute | solution.py:282
  113.4 17.3 %collective-permute-start.14 = (f32[2,32,1,256]{3,2,1,0:T(1,128)S(1)}, f32[2,32,1,256]{3,2,1,0:T(1,128)S(1)}, u32[]{:S(2)}, u32[]{:S(2)}) collective-permute-start(f32[2,32,1,256]{3,2,1,0:T(1,128)S(1)} %get-tuple-element.52), channel_id=1, source_target_pairs={{1,16},{2,17},{3,18},{4,19},{5,20},{6,21},{7,22},{8,23},{9,24},{10... | collective-permute-start | bytes 196616 | tf_op jit(solution)/shard_map/ppermute | solution.py:283
  (29 other events, 52.3 us)

commit v8 on v7

--- a/solution.py
+++ b/solution.py
@@ -74,8 +74,9 @@
         + (northward - 2.0 * middle + southward)
     )
     vertical = v_spread * (upward - 2.0 * middle + downward) / (z_spacing * z_spacing)
-    own = jnp.stack([coupling[0, 0], coupling[1, 1]]).reshape(-1, 1, 1, 1)
-    other = jnp.stack([coupling[0, 1], coupling[1, 0]]).reshape(-1, 1, 1, 1)
+    tracer = lax.broadcasted_iota(jnp.int32, (2, 1, 1, 1), 0)
+    own = jnp.where(tracer == 0, coupling[0, 0], coupling[1, 1])
+    other = jnp.where(tracer == 0, coupling[0, 1], coupling[1, 0])
     reaction = own * middle + other * middle[::-1]
     return diffusion + vertical - advection + reaction
 
@@ -97,8 +98,10 @@
     return jnp.repeat(field, 2, axis=-3)
 
 
-def expand_z(field):
-    return jnp.repeat(field, 2, axis=-3)
+def add_coarse(fine, coarse):
+    shape = fine.shape
+    paired = fine.reshape(shape[:-3] + (shape[-3] // 2, 2) + shape[-2:])
+    return (paired + jnp.expand_dims(coarse, -3)).reshape(shape)
 
 
 def pick(items, index):
@@ -223,24 +226,22 @@
 
     delta_zero = begins - coarse_first
     delta_one = finals - coarse_end
-    fixed_zero = node_zero + expand(delta_zero)
-    fixed_one = node_one + expand((delta_zero + delta_one) * 0.5)
-    fixed_two = node_two + expand(delta_one)
+    fixed_zero = add_coarse(node_zero, delta_zero)
+    fixed_one = add_coarse(node_one, (delta_zero + delta_one) * 0.5)
+    fixed_two = add_coarse(node_two, delta_one)
     halo_dz = pair_map(lambda y, v: y - v, begins_halo, halo_first)
     halo_d1 = pair_map(lambda y, v: y - v, finals_halo, halo_end)
-    halo_f0 = pair_map(lambda w, d: w + expand_z(d), halo_zero, halo_dz)
-    halo_f1 = pair_map(
-        lambda w, d0, d1: w + expand_z((d0 + d1) * 0.5), halo_one, halo_dz, halo_d1
-    )
-    halo_f2 = pair_map(lambda w, d: w + expand_z(d), halo_two, halo_d1)
+    halo_f0 = add_coarse(halo_zero, halo_dz)
+    halo_f1 = add_coarse(halo_one, (halo_dz + halo_d1) * 0.5)
+    halo_f2 = add_coarse(halo_two, halo_d1)
 
     earlier_delta = begins - coarse_end
-    earlier_end = node_two + expand(earlier_delta)
+    earlier_end = add_coarse(node_two, earlier_delta)
     halo_earlier_delta = pair_map(lambda y, v: y - v, begins_halo, halo_end)
-    halo_earlier = pair_map(lambda w, d: w + expand_z(d), halo_two, halo_earlier_delta)
+    halo_earlier = add_coarse(halo_two, halo_earlier_delta)
     wide_earlier = (
-        two_b + expand(west(halo_earlier_delta)),
-        two_a + expand(east(halo_earlier_delta)),
+        add_coarse(two_b, west(halo_earlier_delta)),
+        add_coarse(two_a, east(halo_earlier_delta)),
     )
     start = jnp.where(first, initial, earlier_end)
     halo_start = pair_map(lambda a, b: jnp.where(first, a, b), halo_zero, halo_earlier)
@@ -285,7 +286,7 @@
         carried_halo = jnp.where(first, halo_first, pack(passed_b, passed_a))
         rate = coarse_rate(carried, carried_halo)
     finals = carried + slab_step * rate + offset
-    result = node_two + expand(finals - coarse_end)
+    result = add_coarse(node_two, finals - coarse_end)
     return result[None]
 
 

time: 134 us -> 134 us (level)
    add x0 -> x13, local copies, waits for them, and re-layouts: none -> 5.36 us  [add_coarse(): return (paired + jnp.expand_dims(coarse, -3)).reshape(shape)]
    broadcast_in_dim x13 -> x0, local copies, waits for them, and re-layouts: 5.36 us -> none  [the longest x9 5.08 us: expand(): return jnp.repeat(field, 2, axis=-3)]
    add x6 -> x7, other arithmetic: 4.01 us -> 5.12 us  [add_coarse(): return (paired + jnp.expand_dims(coarse, -3)).reshape(shape)]
where the time goes in v8:
time: 134 us
  starting transfers between devices  41 us (31%)
  other arithmetic  40.4 us (30%)
  waiting for transfers between devices  27.7 us (21%)
  local copies, waits for them, and re-layouts  23.3 us (17%)
    ppermute x6, starting transfers between devices, exchange(): after = lax.ppermute(to_left, 'space', shift_pairs(count, -1))  19.3 us
    ppermute x6, starting transfers between devices, exchange(): before = lax.ppermute(to_right, 'space', shift_pairs(count, 1))  17.9 us
    ppermute x1, waiting for transfers between devices, body(): passed_b = lax.ppermute(hi(after), ('tm', 'space'), to_east)  14.4 us
    add x2, other arithmetic, first_node(): node_zero + half_step * (rate_zero - s0)  8.52 us
    ppermute x6, waiting for transfers between devices, exchange(): before = lax.ppermute(to_right, 'space', shift_pairs(count, 1))  8.34 us
    add x13, local copies, waits for them, and re-layouts, add_coarse(): return (paired + jnp.expand_dims(coarse, -3)).reshape(shape)  5.36 us
    add x7, other arithmetic, add_coarse(): return (paired + jnp.expand_dims(coarse, -3)).reshape(shape)  5.12 us
    unnamed x78, local copies, waits for them, and re-layouts  4.88 us
  transfers between devices with their start and end apart: 15, of which 9 were waited for; matrix products, arithmetic and copies ran while one was open for 15% of the time, Pallas kernels for 0%

profile of v8, /device:TPU:11, one launch (start us, length us, event | category | flops | bytes accessed | tf_op | source)
XLA Modules:
  0.0 133.6 jit_solution(9629399237844756500)
XLA Ops:
  7.3 2.7 %collective-permute-start = (f32[2,160,1,256]{3,2,1,0:T(1,128)}, f32[2,160,1,256]{3,2,1,0:T(1,128)}, u32[]{:S(2)}, u32[]{:S(2)}) collective-permute-start(f32[2,160,1,256]{3,2,1,0:T(1,128)} %pad_maximum_fusion.34), channel_id=1, source_target_pairs={{1,0},{2,1},{3,2},{4,3},{5,4},{6,5},{7,6},{8,7},{9,8},{10,9},{11,1... | collective-permute-start | bytes 983048 | tf_op jit(solution)/shard_map/ppermute | solution.py:20
  11.1 3.0 %collective-permute-start.1 = (f32[2,160,1,256]{3,2,1,0:T(1,128)}, f32[2,160,1,256]{3,2,1,0:T(1,128)}, u32[]{:S(2)}, u32[]{:S(2)}) collective-permute-start(f32[2,160,1,256]{3,2,1,0:T(1,128)} %pad_maximum_fusion.35), channel_id=1, source_target_pairs={{0,1},{1,2},{2,3},{3,4},{4,5},{5,6},{6,7},{7,8},{8,9},{9,10},{10,1... | collective-permute-start | bytes 983048 | tf_op jit(solution)/shard_map/ppermute | solution.py:19
  14.9 2.4 %broadcast_multiply_fusion.2 = (f32[2]{0:T(128)S(1)}, f32[2]{0:T(128)S(1)}, f32[2]{0:T(128)S(1)}, f32[2]{0:T(128)S(1)}) fusion(f32[]{:T(128)} %bitcast.13, f32[]{:T(128)} %bitcast.12, f32[]{:T(128)} %bitcast.11, f32[]{:T(128)} %bitcast.10), kind=kLoop, calls=%fused_computation.267 | loop fusion | flops 10 | bytes 48 | tf_op jit(solution)/shard_map/mul | solution.py:80
  21.0 1.7 %multiply_add_fusion.3 = (f32[2,64,8,256]{3,2,1,0:T(8,128)S(1)}, f32[2,64,8,256]{3,2,1,0:T(8,128)S(1)}) fusion(f32[2,64,8,256]{3,2,1,0:T(8,128)S(1)} %copy-done.4, f32[2]{0:T(128)S(1)} %get-tuple-element.31, f32[2]{0:T(128)S(1)} %get-tuple-element.160, f32[64,8,256]{2,1,0:T(8,128)S(1)} %copy-done.2, f32[64,8,256]{2,1,0:T(8,128)S(1)} %copy-done.1, ...), kind=kLoop, calls=%fused_computation.65 | loop fusion | flops 8912896 | bytes 5505040 | tf_op jit(solution)/shard_map/add | solution.py:138
  22.9 3.7 %collective-permute-start.2 = (f32[2,64,1,256]{3,2,1,0:T(1,128)S(1)}, f32[2,64,1,256]{3,2,1,0:T(1,128)S(1)}, u32[]{:S(2)}, u32[]{:S(2)}) collective-permute-start(f32[2,64,1,256]{3,2,1,0:T(1,128)S(1)} %get-tuple-element.47), channel_id=1, source_target_pairs={{1,0},{2,1},{3,2},{4,3},{5,4},{6,5},{7,6},{8,7},{9,8},{10,9},{11,1... | collective-permute-start | bytes 393224 | tf_op jit(solution)/shard_map/ppermute | solution.py:20
  26.5 2.6 %collective-permute-start.3 = (f32[2,64,1,256]{3,2,1,0:T(1,128)S(1)}, f32[2,64,1,256]{3,2,1,0:T(1,128)S(1)}, u32[]{:S(2)}, u32[]{:S(2)}) collective-permute-start(f32[2,64,1,256]{3,2,1,0:T(1,128)S(1)} %get-tuple-element.48), channel_id=1, source_target_pairs={{0,1},{1,2},{2,3},{3,4},{4,5},{5,6},{6,7},{7,8},{8,9},{9,10},{10,1... | collective-permute-start | bytes 393224 | tf_op jit(solution)/shard_map/ppermute | solution.py:19
  31.2 1.7 %multiply_add_fusion.2 = (f32[2,64,8,256]{3,2,1,0:T(8,128)S(1)}, f32[2,64,8,256]{3,2,1,0:T(8,128)S(1)}) fusion(f32[2,64,8,256]{3,2,1,0:T(8,128)S(1)} %get-tuple-element.35, f32[2,64,8,256]{3,2,1,0:T(8,128)S(1)} %get-tuple-element.34, f32[2]{0:T(128)S(1)} %get-tuple-element.31, f32[2]{0:T(128)S(1)} %get-tuple-element.160, f32[64,8,256]{2,1,0:T(8,128)S(1)} %copy-done.2, ...), kind=kLoop, calls=%fused_computation.61 | loop fusion | flops 8912896 | bytes 6553616 | tf_op jit(solution)/shard_map/add | solution.py:145
  33.1 4.4 %collective-permute-start.4 = (f32[2,64,2,256]{3,2,1,0:T(2,128)S(1)}, f32[2,64,2,256]{3,2,1,0:T(2,128)S(1)}, u32[]{:S(2)}, u32[]{:S(2)}) collective-permute-start(f32[2,64,2,256]{3,2,1,0:T(2,128)S(1)} %get-tuple-element.46), channel_id=1, source_target_pairs={{1,0},{2,1},{3,2},{4,3},{5,4},{6,5},{7,6},{8,7},{9,8},{10,9},{11,1... | collective-permute-start | bytes 786440 | tf_op jit(solution)/shard_map/ppermute | solution.py:20
  37.6 1.9 %collective-permute-start.5 = (f32[2,64,2,256]{3,2,1,0:T(2,128)S(1)}, f32[2,64,2,256]{3,2,1,0:T(2,128)S(1)}, u32[]{:S(2)}, u32[]{:S(2)}) collective-permute-start(f32[2,64,2,256]{3,2,1,0:T(2,128)S(1)} %get-tuple-element.45), channel_id=1, source_target_pairs={{0,1},{1,2},{2,3},{3,4},{4,5},{5,6},{6,7},{7,8},{8,9},{9,10},{10,1... | collective-permute-start | bytes 786440 | tf_op jit(solution)/shard_map/ppermute | solution.py:19
  39.7 1.8 %collective-permute-done.4 = f32[2,64,2,256]{3,2,1,0:T(2,128)S(1)} collective-permute-done((f32[2,64,2,256]{3,2,1,0:T(2,128)S(1)}, f32[2,64,2,256]{3,2,1,0:T(2,128)S(1)}, u32[]{:S(2)}, u32[]{:S(2)}) %collective-permute-start.4) | collective-permute-done | bytes 262176 | tf_op jit(solution)/shard_map/ppermute | solution.py:20
  41.6 3.3 %collective-permute-done.5 = f32[2,64,2,256]{3,2,1,0:T(2,128)S(1)} collective-permute-done((f32[2,64,2,256]{3,2,1,0:T(2,128)S(1)}, f32[2,64,2,256]{3,2,1,0:T(2,128)S(1)}, u32[]{:S(2)}, u32[]{:S(2)}) %collective-permute-start.5) | collective-permute-done | bytes 262176 | tf_op jit(solution)/shard_map/ppermute | solution.py:19
  47.9 2.0 %fusion.92 = (f32[2,32,8,256]{3,2,1,0:T(8,128)S(1)}, f32[2,32,8,256]{3,2,1,0:T(8,128)S(1)}, f32[2,32,8,256]{3,2,1,0:T(8,128)}) fusion(f32[2,32,8,256]{3,2,1,0:T(8,128)S(1)} %copy-done.5, f32[2,32,7,256]{3,2,1,0:T(8,128)S(1)} %get-tuple-element.76, f32[2,32,1,256]{3,2,1,0:T(1,128)S(1)} %get-tuple-element.78, f32[2,32,1,256]{3,2,1,0:T(1,128)S(1)} %get-tuple-element.77, ...), kind=kLoop, calls=%fused_computation.272 | loop fusion | flops 5505024 | bytes 5898328 | tf_op jit(solution)/shard_map/add | solution.py:196
  50.3 3.2 %collective-permute-start.6 = (f32[2,32,4,256]{3,2,1,0:T(4,128)S(1)}, f32[2,32,4,256]{3,2,1,0:T(4,128)S(1)}, u32[]{:S(2)}, u32[]{:S(2)}) collective-permute-start(f32[2,32,4,256]{3,2,1,0:T(4,128)S(1)} %pad_maximum_fusion.36), channel_id=1, source_target_pairs={{1,0},{2,1},{3,2},{4,3},{5,4},{6,5},{7,6},{8,7},{9,8},{10,9},{11,1... | collective-permute-start | bytes 786440 | tf_op jit(solution)/shard_map/ppermute | solution.py:20
  53.6 3.3 %collective-permute-start.7 = (f32[2,32,4,256]{3,2,1,0:T(4,128)S(1)}, f32[2,32,4,256]{3,2,1,0:T(4,128)S(1)}, u32[]{:S(2)}, u32[]{:S(2)}) collective-permute-start(f32[2,32,4,256]{3,2,1,0:T(4,128)S(1)} %pad_maximum_fusion.37), channel_id=1, source_target_pairs={{0,1},{1,2},{2,3},{3,4},{4,5},{5,6},{6,7},{7,8},{8,9},{9,10},{10,1... | collective-permute-start | bytes 786440 | tf_op jit(solution)/shard_map/ppermute | solution.py:19
  58.9 1.9 %collective-permute-done.7 = f32[2,32,4,256]{3,2,1,0:T(4,128)S(1)} collective-permute-done((f32[2,32,4,256]{3,2,1,0:T(4,128)S(1)}, f32[2,32,4,256]{3,2,1,0:T(4,128)S(1)}, u32[]{:S(2)}, u32[]{:S(2)}) %collective-permute-start.7) | collective-permute-done | bytes 262176 | tf_op jit(solution)/shard_map/ppermute | solution.py:19
  70.1 6.8 %multiply_add_fusion.1 = (f32[2,64,8,256]{3,2,1,0:T(8,128)S(1)}, f32[2,64,8,256]{3,2,1,0:T(8,128)}, f32[2,64,8,256]{3,2,1,0:T(8,128)}, f32[2,64,8,256]{3,2,1,0:T(8,128)}, f32[2,64,8,256]{3,2,1,0:T(8,128)}) fusion(f32[2,64,8,256]{3,2,1,0:T(8,128)S(1)} %get-tuple-element.43, f32[2,64,8,256]{3,2,1,0:T(8,128)S(1)} %add.881, f32[2]{0:T(128)S(1)} %get-tuple-element.31, ...), kind=kLoop, calls=%fused_computation.44 | loop fusion | flops 27787264 | bytes 12582928 | tf_op jit(solution)/shard_map/add | solution.py:138
  77.8 3.3 %collective-permute-start.8 = (f32[2,64,1,256]{3,2,1,0:T(1,128)}, f32[2,64,1,256]{3,2,1,0:T(1,128)}, u32[]{:S(2)}, u32[]{:S(2)}) collective-permute-start(f32[2,64,1,256]{3,2,1,0:T(1,128)} %get-tuple-element.40), channel_id=1, source_target_pairs={{1,0},{2,1},{3,2},{4,3},{5,4},{6,5},{7,6},{8,7},{9,8},{10,9},{11,1... | collective-permute-start | bytes 393224 | tf_op jit(solution)/shard_map/ppermute | solution.py:20
  81.1 3.2 %collective-permute-start.9 = (f32[2,64,1,256]{3,2,1,0:T(1,128)}, f32[2,64,1,256]{3,2,1,0:T(1,128)}, u32[]{:S(2)}, u32[]{:S(2)}) collective-permute-start(f32[2,64,1,256]{3,2,1,0:T(1,128)} %get-tuple-element.41), channel_id=1, source_target_pairs={{0,1},{1,2},{2,3},{3,4},{4,5},{5,6},{6,7},{7,8},{8,9},{9,10},{10,1... | collective-permute-start | bytes 393224 | tf_op jit(solution)/shard_map/ppermute | solution.py:19
  89.4 1.6 %add.945 = f32[2,64,256]{2,1,0:T(8,128)} reshape(f32[2,32,2,256]{3,2,1,0:T(2,128)} %add.944) | data formatting | bytes 262144 | tf_op jit(solution)/shard_map/add | solution.py:104
  95.9 2.6 %multiply_add_fusion = (f32[2,64,8,256]{3,2,1,0:T(8,128)S(1)}, f32[2,64,8,256]{3,2,1,0:T(8,128)S(1)}) fusion(f32[2,64,8,256]{3,2,1,0:T(8,128)S(1)} %copy-done.20, f32[2,64,8,256]{3,2,1,0:T(8,128)S(1)} %copy-done.19, f32[2,64,8,256]{3,2,1,0:T(8,128)S(1)} %get-tuple-element.11, f32[2,64,8,256]{3,2,1,0:T(8,128)S(1)} %copy-done.18, f32[2]{0:T(128)S(1)} %get-tuple-element.31, ...), kind=kLoop, calls=%fused_computation.40 | loop fusion | flops 8912896 | bytes 8650768 | tf_op jit(solution)/shard_map/add | solution.py:145
  98.7 1.9 %collective-permute-start.10 = (f32[2,64,1,256]{3,2,1,0:T(1,128)S(1)}, f32[2,64,1,256]{3,2,1,0:T(1,128)S(1)}, u32[]{:S(2)}, u32[]{:S(2)}) collective-permute-start(f32[2,64,1,256]{3,2,1,0:T(1,128)S(1)} %get-tuple-element.39), channel_id=1, source_target_pairs={{1,0},{2,1},{3,2},{4,3},{5,4},{6,5},{7,6},{8,7},{9,8},{10,9},{11,1... | collective-permute-start | bytes 393224 | tf_op jit(solution)/shard_map/ppermute | solution.py:20
  100.7 3.8 %collective-permute-start.11 = (f32[2,64,1,256]{3,2,1,0:T(1,128)S(1)}, f32[2,64,1,256]{3,2,1,0:T(1,128)S(1)}, u32[]{:S(2)}, u32[]{:S(2)}) collective-permute-start(f32[2,64,1,256]{3,2,1,0:T(1,128)S(1)} %get-tuple-element.38), channel_id=1, source_target_pairs={{0,1},{1,2},{2,3},{3,4},{4,5},{5,6},{6,7},{7,8},{8,9},{9,10},{10,1... | collective-permute-start | bytes 393224 | tf_op jit(solution)/shard_map/ppermute | solution.py:19
  105.0 1.7 %collective-permute-done.11 = f32[2,64,1,256]{3,2,1,0:T(1,128)S(1)} collective-permute-done((f32[2,64,1,256]{3,2,1,0:T(1,128)S(1)}, f32[2,64,1,256]{3,2,1,0:T(1,128)S(1)}, u32[]{:S(2)}, u32[]{:S(2)}) %collective-permute-start.11) | collective-permute-done | bytes 131104 | tf_op jit(solution)/shard_map/ppermute | solution.py:19
  114.8 14.4 %collective-permute-done.13 = f32[2,32,1,256]{3,2,1,0:T(1,128)S(1)} collective-permute-done((f32[2,32,1,256]{3,2,1,0:T(1,128)S(1)}, f32[2,32,1,256]{3,2,1,0:T(1,128)S(1)}, u32[]{:S(2)}, u32[]{:S(2)}) %collective-permute-start.13) | collective-permute-done | bytes 65568 | tf_op jit(solution)/shard_map/ppermute | solution.py:283
  (207 shorter events, 53.2 us)
Async XLA Ops:
  6.0 8.2 %copy-start.37 = (f32[2,2]{1,0:T(2,128)S(1)}, f32[2,2]{1,0:T(2,128)}, u32[]{:S(2)}) copy-start(f32[2,2]{1,0:T(2,128)} %param.11) | copy-start | bytes 52
  7.2 13.7 %copy-start.2 = (f32[64,8,256]{2,1,0:T(8,128)S(1)}, f32[64,8,256]{2,1,0:T(8,128)}, u32[]{:S(2)}) copy-start(f32[64,8,256]{2,1,0:T(8,128)} %param.8) | copy-start | bytes 1572868
  7.3 13.7 %copy-start.3 = (f32[64,8,256]{2,1,0:T(8,128)S(1)}, f32[64,8,256]{2,1,0:T(8,128)}, u32[]{:S(2)}) copy-start(f32[64,8,256]{2,1,0:T(8,128)} %param.9) | copy-start | bytes 1572868
  7.3 10.1 %collective-permute-start = (f32[2,160,1,256]{3,2,1,0:T(1,128)}, f32[2,160,1,256]{3,2,1,0:T(1,128)}, u32[]{:S(2)}, u32[]{:S(2)}) collective-permute-start(f32[2,160,1,256]{3,2,1,0:T(1,128)} %pad_maximum_fusion.34), channel_id=1, source_target_pairs={{1,0},{2,1},{3,2},{4,3},{5,4},{6,5},{7,6},{8,7},{9,8},{10,9},{11,1... | collective-permute-start | bytes 983048 | tf_op jit(solution)/shard_map/ppermute | solution.py:20
  11.1 8.7 %collective-permute-start.1 = (f32[2,160,1,256]{3,2,1,0:T(1,128)}, f32[2,160,1,256]{3,2,1,0:T(1,128)}, u32[]{:S(2)}, u32[]{:S(2)}) collective-permute-start(f32[2,160,1,256]{3,2,1,0:T(1,128)} %pad_maximum_fusion.35), channel_id=1, source_target_pairs={{0,1},{1,2},{2,3},{3,4},{4,5},{5,6},{6,7},{7,8},{8,9},{9,10},{10,1... | collective-permute-start | bytes 983048 | tf_op jit(solution)/shard_map/ppermute | solution.py:19
  17.3 29.4 %copy-start.33 = (f32[2]{0:T(128)}, f32[2]{0:T(128)S(1)}, u32[]{:S(2)}) copy-start(f32[2]{0:T(128)S(1)} %get-tuple-element.30) | copy-start | bytes 28
  17.3 29.4 %copy-start.35 = (f32[2]{0:T(128)}, f32[2]{0:T(128)S(1)}, u32[]{:S(2)}) copy-start(f32[2]{0:T(128)S(1)} %get-tuple-element.159) | copy-start | bytes 28
  22.9 8.3 %collective-permute-start.2 = (f32[2,64,1,256]{3,2,1,0:T(1,128)S(1)}, f32[2,64,1,256]{3,2,1,0:T(1,128)S(1)}, u32[]{:S(2)}, u32[]{:S(2)}) collective-permute-start(f32[2,64,1,256]{3,2,1,0:T(1,128)S(1)} %get-tuple-element.47), channel_id=1, source_target_pairs={{1,0},{2,1},{3,2},{4,3},{5,4},{6,5},{7,6},{8,7},{9,8},{10,9},{11,1... | collective-permute-start | bytes 393224 | tf_op jit(solution)/shard_map/ppermute | solution.py:20
  26.5 4.6 %collective-permute-start.3 = (f32[2,64,1,256]{3,2,1,0:T(1,128)S(1)}, f32[2,64,1,256]{3,2,1,0:T(1,128)S(1)}, u32[]{:S(2)}, u32[]{:S(2)}) collective-permute-start(f32[2,64,1,256]{3,2,1,0:T(1,128)S(1)} %get-tuple-element.48), channel_id=1, source_target_pairs={{0,1},{1,2},{2,3},{3,4},{4,5},{5,6},{6,7},{7,8},{8,9},{9,10},{10,1... | collective-permute-start | bytes 393224 | tf_op jit(solution)/shard_map/ppermute | solution.py:19
  33.1 8.3 %collective-permute-start.4 = (f32[2,64,2,256]{3,2,1,0:T(2,128)S(1)}, f32[2,64,2,256]{3,2,1,0:T(2,128)S(1)}, u32[]{:S(2)}, u32[]{:S(2)}) collective-permute-start(f32[2,64,2,256]{3,2,1,0:T(2,128)S(1)} %get-tuple-element.46), channel_id=1, source_target_pairs={{1,0},{2,1},{3,2},{4,3},{5,4},{6,5},{7,6},{8,7},{9,8},{10,9},{11,1... | collective-permute-start | bytes 786440 | tf_op jit(solution)/shard_map/ppermute | solution.py:20
  37.6 7.3 %collective-permute-start.5 = (f32[2,64,2,256]{3,2,1,0:T(2,128)S(1)}, f32[2,64,2,256]{3,2,1,0:T(2,128)S(1)}, u32[]{:S(2)}, u32[]{:S(2)}) collective-permute-start(f32[2,64,2,256]{3,2,1,0:T(2,128)S(1)} %get-tuple-element.45), channel_id=1, source_target_pairs={{0,1},{1,2},{2,3},{3,4},{4,5},{5,6},{6,7},{7,8},{8,9},{9,10},{10,1... | collective-permute-start | bytes 786440 | tf_op jit(solution)/shard_map/ppermute | solution.py:19
  41.5 15.7 %copy-start.27 = (f32[2,64,2,256]{3,2,1,0:T(2,128)}, f32[2,64,2,256]{3,2,1,0:T(2,128)S(1)}, u32[]{:S(2)}) copy-start(f32[2,64,2,256]{3,2,1,0:T(2,128)S(1)} %collective-permute-done.4) | copy-start | bytes 786436
  44.9 12.0 %copy-start.28 = (f32[2,64,2,256]{3,2,1,0:T(2,128)}, f32[2,64,2,256]{3,2,1,0:T(2,128)S(1)}, u32[]{:S(2)}) copy-start(f32[2,64,2,256]{3,2,1,0:T(2,128)S(1)} %collective-permute-done.5) | copy-start | bytes 786436
  50.3 8.4 %collective-permute-start.6 = (f32[2,32,4,256]{3,2,1,0:T(4,128)S(1)}, f32[2,32,4,256]{3,2,1,0:T(4,128)S(1)}, u32[]{:S(2)}, u32[]{:S(2)}) collective-permute-start(f32[2,32,4,256]{3,2,1,0:T(4,128)S(1)} %pad_maximum_fusion.36), channel_id=1, source_target_pairs={{1,0},{2,1},{3,2},{4,3},{5,4},{6,5},{7,6},{8,7},{9,8},{10,9},{11,1... | collective-permute-start | bytes 786440 | tf_op jit(solution)/shard_map/ppermute | solution.py:20
  53.6 7.2 %collective-permute-start.7 = (f32[2,32,4,256]{3,2,1,0:T(4,128)S(1)}, f32[2,32,4,256]{3,2,1,0:T(4,128)S(1)}, u32[]{:S(2)}, u32[]{:S(2)}) collective-permute-start(f32[2,32,4,256]{3,2,1,0:T(4,128)S(1)} %pad_maximum_fusion.37), channel_id=1, source_target_pairs={{0,1},{1,2},{2,3},{3,4},{4,5},{5,6},{6,7},{7,8},{8,9},{9,10},{10,1... | collective-permute-start | bytes 786440 | tf_op jit(solution)/shard_map/ppermute | solution.py:19
  63.4 6.7 %copy-start.7 = (f32[2,64,8,256]{3,2,1,0:T(8,128)}, f32[2,64,8,256]{3,2,1,0:T(8,128)S(1)}, u32[]{:S(2)}) copy-start(f32[2,64,8,256]{3,2,1,0:T(8,128)S(1)} %get-tuple-element.43) | copy-start | bytes 3145732
  77.8 17.6 %collective-permute-start.8 = (f32[2,64,1,256]{3,2,1,0:T(1,128)}, f32[2,64,1,256]{3,2,1,0:T(1,128)}, u32[]{:S(2)}, u32[]{:S(2)}) collective-permute-start(f32[2,64,1,256]{3,2,1,0:T(1,128)} %get-tuple-element.40), channel_id=1, source_target_pairs={{1,0},{2,1},{3,2},{4,3},{5,4},{6,5},{7,6},{8,7},{9,8},{10,9},{11,1... | collective-permute-start | bytes 393224 | tf_op jit(solution)/shard_map/ppermute | solution.py:20
  81.1 14.3 %collective-permute-start.9 = (f32[2,64,1,256]{3,2,1,0:T(1,128)}, f32[2,64,1,256]{3,2,1,0:T(1,128)}, u32[]{:S(2)}, u32[]{:S(2)}) collective-permute-start(f32[2,64,1,256]{3,2,1,0:T(1,128)} %get-tuple-element.41), channel_id=1, source_target_pairs={{0,1},{1,2},{2,3},{3,4},{4,5},{5,6},{6,7},{7,8},{8,9},{9,10},{10,1... | collective-permute-start | bytes 393224 | tf_op jit(solution)/shard_map/ppermute | solution.py:19
  98.7 6.3 %collective-permute-start.10 = (f32[2,64,1,256]{3,2,1,0:T(1,128)S(1)}, f32[2,64,1,256]{3,2,1,0:T(1,128)S(1)}, u32[]{:S(2)}, u32[]{:S(2)}) collective-permute-start(f32[2,64,1,256]{3,2,1,0:T(1,128)S(1)} %get-tuple-element.39), channel_id=1, source_target_pairs={{1,0},{2,1},{3,2},{4,3},{5,4},{6,5},{7,6},{8,7},{9,8},{10,9},{11,1... | collective-permute-start | bytes 393224 | tf_op jit(solution)/shard_map/ppermute | solution.py:20
  100.7 6.1 %copy-start.21 = (f32[2,64,8,256]{3,2,1,0:T(8,128)S(1)}, f32[2,64,8,256]{3,2,1,0:T(8,128)}, u32[]{:S(2)}) copy-start(f32[2,64,8,256]{3,2,1,0:T(8,128)} %get-tuple-element.13) | copy-start | bytes 3145732
  100.7 6.1 %collective-permute-start.11 = (f32[2,64,1,256]{3,2,1,0:T(1,128)S(1)}, f32[2,64,1,256]{3,2,1,0:T(1,128)S(1)}, u32[]{:S(2)}, u32[]{:S(2)}) collective-permute-start(f32[2,64,1,256]{3,2,1,0:T(1,128)S(1)} %get-tuple-element.38), channel_id=1, source_target_pairs={{0,1},{1,2},{2,3},{3,4},{4,5},{5,6},{6,7},{7,8},{8,9},{9,10},{10,1... | collective-permute-start | bytes 393224 | tf_op jit(solution)/shard_map/ppermute | solution.py:19
  110.8 20.3 %collective-permute-start.12 = (f32[2,32,8,256]{3,2,1,0:T(8,128)S(1)}, f32[2,32,8,256]{3,2,1,0:T(8,128)S(1)}, u32[]{:S(2)}, u32[]{:S(2)}) collective-permute-start(f32[2,32,8,256]{3,2,1,0:T(8,128)S(1)} %get-tuple-element.5), channel_id=1, source_target_pairs={{0,16},{1,17},{2,18},{3,19},{4,20},{5,21},{6,22},{7,23},{8,24},{9,... | collective-permute-start | bytes 1572872 | tf_op jit(solution)/shard_map/ppermute | solution.py:282
  112.1 17.1 %collective-permute-start.13 = (f32[2,32,1,256]{3,2,1,0:T(1,128)S(1)}, f32[2,32,1,256]{3,2,1,0:T(1,128)S(1)}, u32[]{:S(2)}, u32[]{:S(2)}) collective-permute-start(f32[2,32,1,256]{3,2,1,0:T(1,128)S(1)} %get-tuple-element.51), channel_id=1, source_target_pairs={{0,17},{1,18},{2,19},{3,20},{4,21},{5,22},{6,23},{7,24},{8,25},{9,... | collective-permute-start | bytes 196616 | tf_op jit(solution)/shard_map/ppermute | solution.py:283
  113.4 17.3 %collective-permute-start.14 = (f32[2,32,1,256]{3,2,1,0:T(1,128)S(1)}, f32[2,32,1,256]{3,2,1,0:T(1,128)S(1)}, u32[]{:S(2)}, u32[]{:S(2)}) collective-permute-start(f32[2,32,1,256]{3,2,1,0:T(1,128)S(1)} %get-tuple-element.52), channel_id=1, source_target_pairs={{1,16},{2,17},{3,18},{4,19},{5,20},{6,21},{7,22},{8,23},{9,24},{10... | collective-permute-start | bytes 196616 | tf_op jit(solution)/shard_map/ppermute | solution.py:284
  (29 other events, 52.3 us)

commit v9 on v8

--- a/solution.py
+++ b/solution.py
@@ -191,6 +191,7 @@
     chain = [coarse_first]
     chain_halo = [halo_first]
     rate = coarse_first_rate
+    rates = [rate]
     wide = None
     for count in range(slabs):
         after = chain[-1] + slab_step * rate + offset
@@ -219,6 +220,7 @@
         chain_halo.append(after_halo)
         if count + 1 < slabs:
             rate = coarse_rate(after, after_halo)
+            rates.append(rate)
     begins = pick(chain, slab)
     finals = pick(chain, slab + 1)
     begins_halo = pick(chain_halo, slab)
@@ -239,15 +241,9 @@
     earlier_end = add_coarse(node_two, earlier_delta)
     halo_earlier_delta = pair_map(lambda y, v: y - v, begins_halo, halo_end)
     halo_earlier = add_coarse(halo_two, halo_earlier_delta)
-    wide_earlier = (
-        add_coarse(two_b, west(halo_earlier_delta)),
-        add_coarse(two_a, east(halo_earlier_delta)),
-    )
     start = jnp.where(first, initial, earlier_end)
     halo_start = pair_map(lambda a, b: jnp.where(first, a, b), halo_zero, halo_earlier)
-    halo_start_coarse = jnp.where(
-        first, halo_first, pack(lo(shrink(wide_earlier[0])), lo(shrink(wide_earlier[1])))
-    )
+    start_rate = pick(rates, slab)
 
     slope_zero = fine_rate(fixed_zero, halo_f0)
     slope_one = fine_rate(fixed_one, halo_f1)
@@ -258,10 +254,9 @@
     rate_one = fine_rate(node_one, halo_of(node_one))
     node_two = second_node(node_one, rate_one, slope_zero, slope_one, slope_two)
     rate_two = fine_rate(node_two, halo_of(node_two))
-    coarse_zero = shrink(node_zero)
     coarse_end = shrink(node_two)
     source = shrink(slab_step * (rate_zero + 4.0 * rate_one + rate_two) / 6.0)
-    offset = source - slab_step * coarse_rate(coarse_zero, halo_start_coarse)
+    offset = source - slab_step * start_rate
 
     down = shift_pairs(slabs, 1)
     to_east = [

time: 134 us -> 130 us (0.970)
  waiting for transfers between devices: 27.7 us -> 37.1 us
  local copies, waits for them, and re-layouts: 23.3 us -> 16.1 us
  other arithmetic: 40.4 us -> 36.1 us
  starting transfers between devices: 41 us -> 38.6 us
    ppermute x6, waiting for transfers between devices: 3.38 us -> 17.5 us  [exchange(): after = lax.ppermute(to_left, 'space', shift_pairs(count, -1))]
    ppermute x6, starting transfers between devices: 19.3 us -> 13 us  [exchange(): after = lax.ppermute(to_left, 'space', shift_pairs(count, -1))]
    add x13 -> x9, local copies, waits for them, and re-layouts: 5.36 us -> 0.68 us  [add_coarse(): return (paired + jnp.expand_dims(coarse, -3)).reshape(shape)]
    ppermute x6, starting transfers between devices: 17.9 us -> 21.7 us  [exchange(): before = lax.ppermute(to_right, 'space', shift_pairs(count, 1))]
    ppermute x6, waiting for transfers between devices: 8.34 us -> 5.21 us  [exchange(): before = lax.ppermute(to_right, 'space', shift_pairs(count, 1))]
    slice x14 -> x10, local copies, waits for them, and re-layouts: 3.64 us -> 0.85 us  [pair_sum(): jnp.roll(field, -1, axis=-2)]
    mul x8 -> x5, other arithmetic: 4.42 us -> 1.88 us  [shrink(): return pair_sum(levels) * 0.25]
    add x2, other arithmetic: 8.52 us -> 11 us  [first_node(): node_zero + half_step * (rate_zero - s0)]
  transfers between devices with their start and end apart: 15 -> 15, of which waited for: 9 -> 10; matrix products, arithmetic and copies ran while one was open for 15% -> 7% of each run, Pallas kernels for 0% -> 0%
where the time goes in v9:
time: 130 us; the launch traced here: 129 us
  starting transfers between devices  38.6 us (30%)
  waiting for transfers between devices  37.1 us (29%)
  other arithmetic  36.1 us (28%)
  local copies, waits for them, and re-layouts  16.1 us (12%)
    ppermute x6, starting transfers between devices, exchange(): before = lax.ppermute(to_right, 'space', shift_pairs(count, 1))  21.7 us
    ppermute x6, waiting for transfers between devices, exchange(): after = lax.ppermute(to_left, 'space', shift_pairs(count, -1))  17.5 us
    ppermute x1, waiting for transfers between devices, body(): passed_b = lax.ppermute(hi(after), ('tm', 'space'), to_east)  14.4 us
    ppermute x6, starting transfers between devices, exchange(): after = lax.ppermute(to_left, 'space', shift_pairs(count, -1))  13 us
    add x2, other arithmetic, first_node(): node_zero + half_step * (rate_zero - s0)  11 us
    unnamed x32, local copies, waits for them, and re-layouts  5.85 us
    ppermute x6, waiting for transfers between devices, exchange(): before = lax.ppermute(to_right, 'space', shift_pairs(count, 1))  5.21 us
    add x5, other arithmetic, add_coarse(): return (paired + jnp.expand_dims(coarse, -3)).reshape(shape)  3.57 us
  transfers between devices with their start and end apart: 15, of which 10 were waited for; matrix products, arithmetic and copies ran while one was open for 7% of the time, Pallas kernels for 0%

profile of v9, /device:TPU:11, one launch (start us, length us, event | category | flops | bytes accessed | tf_op | source)
XLA Modules:
  0.0 128.8 jit_solution(860601543671466397)
XLA Ops:
  9.7 3.7 %collective-permute-start.1 = (f32[2,160,1,256]{3,2,1,0:T(1,128)}, f32[2,160,1,256]{3,2,1,0:T(1,128)}, u32[]{:S(2)}, u32[]{:S(2)}) collective-permute-start(f32[2,160,1,256]{3,2,1,0:T(1,128)} %pad_maximum_fusion.31), channel_id=1, source_target_pairs={{0,1},{1,2},{2,3},{3,4},{4,5},{5,6},{6,7},{7,8},{8,9},{9,10},{10,1... | collective-permute-start | bytes 983048 | tf_op jit(solution)/shard_map/ppermute | solution.py:19
  14.6 1.9 %collective-permute-start = (f32[2,160,1,256]{3,2,1,0:T(1,128)}, f32[2,160,1,256]{3,2,1,0:T(1,128)}, u32[]{:S(2)}, u32[]{:S(2)}) collective-permute-start(f32[2,160,1,256]{3,2,1,0:T(1,128)} %pad_maximum_fusion.30), channel_id=1, source_target_pairs={{1,0},{2,1},{3,2},{4,3},{5,4},{6,5},{7,6},{8,7},{9,8},{10,9},{11,1... | collective-permute-start | bytes 983048 | tf_op jit(solution)/shard_map/ppermute | solution.py:20
  17.2 2.6 %broadcast_multiply_fusion.1 = (f32[2]{0:T(128)S(1)}, f32[2]{0:T(128)S(1)}, f32[2]{0:T(128)S(1)}, f32[2]{0:T(128)S(1)}) fusion(f32[]{:T(128)} %bitcast.13, f32[]{:T(128)} %bitcast.12, f32[]{:T(128)} %bitcast.11, f32[]{:T(128)} %bitcast.10), kind=kLoop, calls=%fused_computation.229 | loop fusion | flops 10 | bytes 48 | tf_op jit(solution)/shard_map/mul | solution.py:80
  21.0 2.3 %collective-permute-done = f32[2,160,1,256]{3,2,1,0:T(1,128)} collective-permute-done((f32[2,160,1,256]{3,2,1,0:T(1,128)}, f32[2,160,1,256]{3,2,1,0:T(1,128)}, u32[]{:S(2)}, u32[]{:S(2)}) %collective-permute-start) | collective-permute-done | bytes 327712 | tf_op jit(solution)/shard_map/ppermute | solution.py:20
  24.4 1.7 %multiply_add_fusion.3 = (f32[2,64,8,256]{3,2,1,0:T(8,128)S(1)}, f32[2,64,8,256]{3,2,1,0:T(8,128)S(1)}) fusion(f32[2,64,8,256]{3,2,1,0:T(8,128)S(1)} %copy-done.4, f32[2]{0:T(128)S(1)} %get-tuple-element.29, f32[2]{0:T(128)S(1)} %get-tuple-element.146, f32[64,8,256]{2,1,0:T(8,128)S(1)} %copy-done.2, f32[64,8,256]{2,1,0:T(8,128)S(1)} %copy-done.1, ...), kind=kLoop, calls=%fused_computation.65 | loop fusion | flops 8912896 | bytes 5505040 | tf_op jit(solution)/shard_map/add | solution.py:138
  26.3 1.9 %collective-permute-start.2 = (f32[2,64,1,256]{3,2,1,0:T(1,128)S(1)}, f32[2,64,1,256]{3,2,1,0:T(1,128)S(1)}, u32[]{:S(2)}, u32[]{:S(2)}) collective-permute-start(f32[2,64,1,256]{3,2,1,0:T(1,128)S(1)} %get-tuple-element.45), channel_id=1, source_target_pairs={{1,0},{2,1},{3,2},{4,3},{5,4},{6,5},{7,6},{8,7},{9,8},{10,9},{11,1... | collective-permute-start | bytes 393224 | tf_op jit(solution)/shard_map/ppermute | solution.py:20
  28.2 3.6 %collective-permute-start.3 = (f32[2,64,1,256]{3,2,1,0:T(1,128)S(1)}, f32[2,64,1,256]{3,2,1,0:T(1,128)S(1)}, u32[]{:S(2)}, u32[]{:S(2)}) collective-permute-start(f32[2,64,1,256]{3,2,1,0:T(1,128)S(1)} %get-tuple-element.46), channel_id=1, source_target_pairs={{0,1},{1,2},{2,3},{3,4},{4,5},{5,6},{6,7},{7,8},{8,9},{9,10},{10,1... | collective-permute-start | bytes 393224 | tf_op jit(solution)/shard_map/ppermute | solution.py:19
  35.1 1.7 %multiply_add_fusion.2 = (f32[2,64,8,256]{3,2,1,0:T(8,128)S(1)}, f32[2,64,8,256]{3,2,1,0:T(8,128)S(1)}) fusion(f32[2,64,8,256]{3,2,1,0:T(8,128)S(1)} %get-tuple-element.33, f32[2,64,8,256]{3,2,1,0:T(8,128)S(1)} %get-tuple-element.32, f32[2]{0:T(128)S(1)} %get-tuple-element.29, f32[2]{0:T(128)S(1)} %get-tuple-element.146, f32[64,8,256]{2,1,0:T(8,128)S(1)} %copy-done.2, ...), kind=kLoop, calls=%fused_computation.61 | loop fusion | flops 8912896 | bytes 6553616 | tf_op jit(solution)/shard_map/add | solution.py:145
  37.1 4.4 %collective-permute-start.5 = (f32[2,64,2,256]{3,2,1,0:T(2,128)S(1)}, f32[2,64,2,256]{3,2,1,0:T(2,128)S(1)}, u32[]{:S(2)}, u32[]{:S(2)}) collective-permute-start(f32[2,64,2,256]{3,2,1,0:T(2,128)S(1)} %get-tuple-element.43), channel_id=1, source_target_pairs={{0,1},{1,2},{2,3},{3,4},{4,5},{5,6},{6,7},{7,8},{8,9},{9,10},{10,1... | collective-permute-start | bytes 786440 | tf_op jit(solution)/shard_map/ppermute | solution.py:19
  41.5 2.1 %collective-permute-start.4 = (f32[2,64,2,256]{3,2,1,0:T(2,128)S(1)}, f32[2,64,2,256]{3,2,1,0:T(2,128)S(1)}, u32[]{:S(2)}, u32[]{:S(2)}) collective-permute-start(f32[2,64,2,256]{3,2,1,0:T(2,128)S(1)} %get-tuple-element.44), channel_id=1, source_target_pairs={{1,0},{2,1},{3,2},{4,3},{5,4},{6,5},{7,6},{8,7},{9,8},{10,9},{11,1... | collective-permute-start | bytes 786440 | tf_op jit(solution)/shard_map/ppermute | solution.py:20
  45.0 5.6 %collective-permute-done.4 = f32[2,64,2,256]{3,2,1,0:T(2,128)S(1)} collective-permute-done((f32[2,64,2,256]{3,2,1,0:T(2,128)S(1)}, f32[2,64,2,256]{3,2,1,0:T(2,128)S(1)}, u32[]{:S(2)}, u32[]{:S(2)}) %collective-permute-start.4) | collective-permute-done | bytes 262176 | tf_op jit(solution)/shard_map/ppermute | solution.py:20
  55.6 1.9 %collective-permute-start.7 = (f32[2,32,4,256]{3,2,1,0:T(4,128)S(1)}, f32[2,32,4,256]{3,2,1,0:T(4,128)S(1)}, u32[]{:S(2)}, u32[]{:S(2)}) collective-permute-start(f32[2,32,4,256]{3,2,1,0:T(4,128)S(1)} %pad_maximum_fusion.33), channel_id=1, source_target_pairs={{0,1},{1,2},{2,3},{3,4},{4,5},{5,6},{6,7},{7,8},{8,9},{9,10},{10,1... | collective-permute-start | bytes 786440 | tf_op jit(solution)/shard_map/ppermute | solution.py:19
  57.7 2.6 %collective-permute-start.6 = (f32[2,32,4,256]{3,2,1,0:T(4,128)S(1)}, f32[2,32,4,256]{3,2,1,0:T(4,128)S(1)}, u32[]{:S(2)}, u32[]{:S(2)}) collective-permute-start(f32[2,32,4,256]{3,2,1,0:T(4,128)S(1)} %pad_maximum_fusion.32), channel_id=1, source_target_pairs={{1,0},{2,1},{3,2},{4,3},{5,4},{6,5},{7,6},{8,7},{9,8},{10,9},{11,1... | collective-permute-start | bytes 786440 | tf_op jit(solution)/shard_map/ppermute | solution.py:20
  61.0 5.2 %collective-permute-done.6 = f32[2,32,4,256]{3,2,1,0:T(4,128)S(1)} collective-permute-done((f32[2,32,4,256]{3,2,1,0:T(4,128)S(1)}, f32[2,32,4,256]{3,2,1,0:T(4,128)S(1)}, u32[]{:S(2)}, u32[]{:S(2)}) %collective-permute-start.6) | collective-permute-done | bytes 262176 | tf_op jit(solution)/shard_map/ppermute | solution.py:20
  70.9 1.5 %add_multiply_fusion.2 = (f32[2,32,8,256]{3,2,1,0:T(8,128)S(1)}, f32[2,32,8,256]{3,2,1,0:T(8,128)S(1)}, f32[2,32,8,256]{3,2,1,0:T(8,128)S(1)}, f32[2,32,8,256]{3,2,1,0:T(8,128)S(1)}, f32[2,32,8,256]{3,2,1,0:T(8,128)S(1)}) fusion(pred[]{:T(512)S(6)} %eq.106, f32[2,32,8,256]{3,2,1,0:T(8,128)S(1)} %get-tuple-element.24, ...), kind=kLoop, calls=%fused_computation.139 | loop fusion | flops 6815744 | bytes 7995484 | tf_op jit(solution)/shard_map/mul | solution.py:232
  74.5 9.3 %multiply_add_fusion.1 = (f32[2,64,8,256]{3,2,1,0:T(8,128)S(1)}, f32[2,64,8,256]{3,2,1,0:T(8,128)S(1)}, f32[2,64,8,256]{3,2,1,0:T(8,128)}, f32[2,64,8,256]{3,2,1,0:T(8,128)S(1)}, f32[2,64,8,256]{3,2,1,0:T(8,128)S(1)}) fusion(f32[2,64,8,256]{3,2,1,0:T(8,128)S(1)} %get-tuple-element.41, f32[2,64,8,256]{3,2,1,0:T(8,128)S(1)} %add.797, ...), kind=kLoop, calls=%fused_computation.44 | loop fusion | flops 27787264 | bytes 12582928 | tf_op jit(solution)/shard_map/add | solution.py:138
  83.9 1.9 %collective-permute-start.8 = (f32[2,64,1,256]{3,2,1,0:T(1,128)S(1)}, f32[2,64,1,256]{3,2,1,0:T(1,128)S(1)}, u32[]{:S(2)}, u32[]{:S(2)}) collective-permute-start(f32[2,64,1,256]{3,2,1,0:T(1,128)S(1)} %get-tuple-element.38), channel_id=1, source_target_pairs={{1,0},{2,1},{3,2},{4,3},{5,4},{6,5},{7,6},{8,7},{9,8},{10,9},{11,1... | collective-permute-start | bytes 393224 | tf_op jit(solution)/shard_map/ppermute | solution.py:20
  85.8 3.6 %collective-permute-start.9 = (f32[2,64,1,256]{3,2,1,0:T(1,128)S(1)}, f32[2,64,1,256]{3,2,1,0:T(1,128)S(1)}, u32[]{:S(2)}, u32[]{:S(2)}) collective-permute-start(f32[2,64,1,256]{3,2,1,0:T(1,128)S(1)} %get-tuple-element.39), channel_id=1, source_target_pairs={{0,1},{1,2},{2,3},{3,4},{4,5},{5,6},{6,7},{7,8},{8,9},{9,10},{10,1... | collective-permute-start | bytes 393224 | tf_op jit(solution)/shard_map/ppermute | solution.py:19
  90.2 2.6 %collective-permute-done.9 = f32[2,64,1,256]{3,2,1,0:T(1,128)S(1)} collective-permute-done((f32[2,64,1,256]{3,2,1,0:T(1,128)S(1)}, f32[2,64,1,256]{3,2,1,0:T(1,128)S(1)}, u32[]{:S(2)}, u32[]{:S(2)}) %collective-permute-start.9) | collective-permute-done | bytes 131104 | tf_op jit(solution)/shard_map/ppermute | solution.py:19
  92.8 1.7 %multiply_add_fusion = (f32[2,64,8,256]{3,2,1,0:T(8,128)S(1)}, f32[2,64,8,256]{3,2,1,0:T(8,128)S(1)}) fusion(f32[2,64,8,256]{3,2,1,0:T(8,128)S(1)} %get-tuple-element.13, f32[2,64,8,256]{3,2,1,0:T(8,128)S(1)} %get-tuple-element.12, f32[2,64,8,256]{3,2,1,0:T(8,128)S(1)} %get-tuple-element.9, f32[2,64,8,256]{3,2,1,0:T(8,128)S(1)} %get-tuple-element.10, ...), kind=kLoop, calls=%fused_computation.40 | loop fusion | flops 8912896 | bytes 8650768 | tf_op jit(solution)/shard_map/add | solution.py:145
  94.8 4.4 %collective-permute-start.11 = (f32[2,64,1,256]{3,2,1,0:T(1,128)S(1)}, f32[2,64,1,256]{3,2,1,0:T(1,128)S(1)}, u32[]{:S(2)}, u32[]{:S(2)}) collective-permute-start(f32[2,64,1,256]{3,2,1,0:T(1,128)S(1)} %get-tuple-element.36), channel_id=1, source_target_pairs={{0,1},{1,2},{2,3},{3,4},{4,5},{5,6},{6,7},{7,8},{8,9},{9,10},{10,1... | collective-permute-start | bytes 393224 | tf_op jit(solution)/shard_map/ppermute | solution.py:19
  99.2 2.6 %collective-permute-start.10 = (f32[2,64,1,256]{3,2,1,0:T(1,128)S(1)}, f32[2,64,1,256]{3,2,1,0:T(1,128)S(1)}, u32[]{:S(2)}, u32[]{:S(2)}) collective-permute-start(f32[2,64,1,256]{3,2,1,0:T(1,128)S(1)} %get-tuple-element.37), channel_id=1, source_target_pairs={{1,0},{2,1},{3,2},{4,3},{5,4},{6,5},{7,6},{8,7},{9,8},{10,9},{11,1... | collective-permute-start | bytes 393224 | tf_op jit(solution)/shard_map/ppermute | solution.py:20
  101.8 3.8 %collective-permute-done.10 = f32[2,64,1,256]{3,2,1,0:T(1,128)S(1)} collective-permute-done((f32[2,64,1,256]{3,2,1,0:T(1,128)S(1)}, f32[2,64,1,256]{3,2,1,0:T(1,128)S(1)}, u32[]{:S(2)}, u32[]{:S(2)}) %collective-permute-start.10) | collective-permute-done | bytes 131104 | tf_op jit(solution)/shard_map/ppermute | solution.py:20
  111.6 14.4 %collective-permute-done.13 = f32[2,32,1,256]{3,2,1,0:T(1,128)S(1)} collective-permute-done((f32[2,32,1,256]{3,2,1,0:T(1,128)S(1)}, f32[2,32,1,256]{3,2,1,0:T(1,128)S(1)}, u32[]{:S(2)}, u32[]{:S(2)}) %collective-permute-start.13) | collective-permute-done | bytes 65568 | tf_op jit(solution)/shard_map/ppermute | solution.py:278
  (142 shorter events, 40.9 us)
Async XLA Ops:
  0.0 1.2 copy-start.1
  1.2 1.2 copy-start.4
  2.8 1.2 copy-start.3
  8.3 6.2 %copy-start.6 = (f32[32,8,256]{2,1,0:T(8,128)}, f32[32,8,256]{2,1,0:T(8,128)S(1)}, u32[]{:S(2)}) copy-start(f32[32,8,256]{2,1,0:T(8,128)S(1)} %get-tuple-element.135) | copy-start | bytes 786436
  8.4 6.2 %copy-start.8 = (f32[32,8,256]{2,1,0:T(8,128)}, f32[32,8,256]{2,1,0:T(8,128)S(1)}, u32[]{:S(2)}) copy-start(f32[32,8,256]{2,1,0:T(8,128)S(1)} %get-tuple-element.136) | copy-start | bytes 786436
  8.4 8.1 %copy-start.15 = (f32[2,2]{1,0:T(2,128)S(1)}, f32[2,2]{1,0:T(2,128)}, u32[]{:S(2)}) copy-start(f32[2,2]{1,0:T(2,128)} %param.11) | copy-start | bytes 52
  9.7 10.1 %collective-permute-start.1 = (f32[2,160,1,256]{3,2,1,0:T(1,128)}, f32[2,160,1,256]{3,2,1,0:T(1,128)}, u32[]{:S(2)}, u32[]{:S(2)}) collective-permute-start(f32[2,160,1,256]{3,2,1,0:T(1,128)} %pad_maximum_fusion.31), channel_id=1, source_target_pairs={{0,1},{1,2},{2,3},{3,4},{4,5},{5,6},{6,7},{7,8},{8,9},{9,10},{10,1... | collective-permute-start | bytes 983048 | tf_op jit(solution)/shard_map/ppermute | solution.py:19
  14.6 8.7 %collective-permute-start = (f32[2,160,1,256]{3,2,1,0:T(1,128)}, f32[2,160,1,256]{3,2,1,0:T(1,128)}, u32[]{:S(2)}, u32[]{:S(2)}) collective-permute-start(f32[2,160,1,256]{3,2,1,0:T(1,128)} %pad_maximum_fusion.30), channel_id=1, source_target_pairs={{1,0},{2,1},{3,2},{4,3},{5,4},{6,5},{7,6},{8,7},{9,8},{10,9},{11,1... | collective-permute-start | bytes 983048 | tf_op jit(solution)/shard_map/ppermute | solution.py:20
  26.3 7.5 %collective-permute-start.2 = (f32[2,64,1,256]{3,2,1,0:T(1,128)S(1)}, f32[2,64,1,256]{3,2,1,0:T(1,128)S(1)}, u32[]{:S(2)}, u32[]{:S(2)}) collective-permute-start(f32[2,64,1,256]{3,2,1,0:T(1,128)S(1)} %get-tuple-element.45), channel_id=1, source_target_pairs={{1,0},{2,1},{3,2},{4,3},{5,4},{6,5},{7,6},{8,7},{9,8},{10,9},{11,1... | collective-permute-start | bytes 393224 | tf_op jit(solution)/shard_map/ppermute | solution.py:20
  28.2 6.9 %collective-permute-start.3 = (f32[2,64,1,256]{3,2,1,0:T(1,128)S(1)}, f32[2,64,1,256]{3,2,1,0:T(1,128)S(1)}, u32[]{:S(2)}, u32[]{:S(2)}) collective-permute-start(f32[2,64,1,256]{3,2,1,0:T(1,128)S(1)} %get-tuple-element.46), channel_id=1, source_target_pairs={{0,1},{1,2},{2,3},{3,4},{4,5},{5,6},{6,7},{7,8},{8,9},{9,10},{10,1... | collective-permute-start | bytes 393224 | tf_op jit(solution)/shard_map/ppermute | solution.py:19
  37.1 7.7 %collective-permute-start.5 = (f32[2,64,2,256]{3,2,1,0:T(2,128)S(1)}, f32[2,64,2,256]{3,2,1,0:T(2,128)S(1)}, u32[]{:S(2)}, u32[]{:S(2)}) collective-permute-start(f32[2,64,2,256]{3,2,1,0:T(2,128)S(1)} %get-tuple-element.43), channel_id=1, source_target_pairs={{0,1},{1,2},{2,3},{3,4},{4,5},{5,6},{6,7},{7,8},{8,9},{9,10},{10,1... | collective-permute-start | bytes 786440 | tf_op jit(solution)/shard_map/ppermute | solution.py:19
  41.5 9.0 %collective-permute-start.4 = (f32[2,64,2,256]{3,2,1,0:T(2,128)S(1)}, f32[2,64,2,256]{3,2,1,0:T(2,128)S(1)}, u32[]{:S(2)}, u32[]{:S(2)}) collective-permute-start(f32[2,64,2,256]{3,2,1,0:T(2,128)S(1)} %get-tuple-element.44), channel_id=1, source_target_pairs={{1,0},{2,1},{3,2},{4,3},{5,4},{6,5},{7,6},{8,7},{9,8},{10,9},{11,1... | collective-permute-start | bytes 786440 | tf_op jit(solution)/shard_map/ppermute | solution.py:20
  52.2 1.2 copy-start.11
  52.2 1.4 %copy-start.14 = (f32[2,32,8,256]{3,2,1,0:T(8,128)S(1)}, f32[2,32,8,256]{3,2,1,0:T(8,128)}, u32[]{:S(2)}) copy-start(f32[2,32,8,256]{3,2,1,0:T(8,128)} %copy-done.13) | copy-start | bytes 1572868
  55.6 5.2 %collective-permute-start.7 = (f32[2,32,4,256]{3,2,1,0:T(4,128)S(1)}, f32[2,32,4,256]{3,2,1,0:T(4,128)S(1)}, u32[]{:S(2)}, u32[]{:S(2)}) collective-permute-start(f32[2,32,4,256]{3,2,1,0:T(4,128)S(1)} %pad_maximum_fusion.33), channel_id=1, source_target_pairs={{0,1},{1,2},{2,3},{3,4},{4,5},{5,6},{6,7},{7,8},{8,9},{9,10},{10,1... | collective-permute-start | bytes 786440 | tf_op jit(solution)/shard_map/ppermute | solution.py:19
  57.7 8.5 %collective-permute-start.6 = (f32[2,32,4,256]{3,2,1,0:T(4,128)S(1)}, f32[2,32,4,256]{3,2,1,0:T(4,128)S(1)}, u32[]{:S(2)}, u32[]{:S(2)}) collective-permute-start(f32[2,32,4,256]{3,2,1,0:T(4,128)S(1)} %pad_maximum_fusion.32), channel_id=1, source_target_pairs={{1,0},{2,1},{3,2},{4,3},{5,4},{6,5},{7,6},{8,7},{9,8},{10,9},{11,1... | collective-permute-start | bytes 786440 | tf_op jit(solution)/shard_map/ppermute | solution.py:20
  83.9 6.3 %collective-permute-start.8 = (f32[2,64,1,256]{3,2,1,0:T(1,128)S(1)}, f32[2,64,1,256]{3,2,1,0:T(1,128)S(1)}, u32[]{:S(2)}, u32[]{:S(2)}) collective-permute-start(f32[2,64,1,256]{3,2,1,0:T(1,128)S(1)} %get-tuple-element.38), channel_id=1, source_target_pairs={{1,0},{2,1},{3,2},{4,3},{5,4},{6,5},{7,6},{8,7},{9,8},{10,9},{11,1... | collective-permute-start | bytes 393224 | tf_op jit(solution)/shard_map/ppermute | solution.py:20
  85.8 6.9 %collective-permute-start.9 = (f32[2,64,1,256]{3,2,1,0:T(1,128)S(1)}, f32[2,64,1,256]{3,2,1,0:T(1,128)S(1)}, u32[]{:S(2)}, u32[]{:S(2)}) collective-permute-start(f32[2,64,1,256]{3,2,1,0:T(1,128)S(1)} %get-tuple-element.39), channel_id=1, source_target_pairs={{0,1},{1,2},{2,3},{3,4},{4,5},{5,6},{6,7},{7,8},{8,9},{9,10},{10,1... | collective-permute-start | bytes 393224 | tf_op jit(solution)/shard_map/ppermute | solution.py:19
  94.8 7.1 %collective-permute-start.11 = (f32[2,64,1,256]{3,2,1,0:T(1,128)S(1)}, f32[2,64,1,256]{3,2,1,0:T(1,128)S(1)}, u32[]{:S(2)}, u32[]{:S(2)}) collective-permute-start(f32[2,64,1,256]{3,2,1,0:T(1,128)S(1)} %get-tuple-element.36), channel_id=1, source_target_pairs={{0,1},{1,2},{2,3},{3,4},{4,5},{5,6},{6,7},{7,8},{8,9},{9,10},{10,1... | collective-permute-start | bytes 393224 | tf_op jit(solution)/shard_map/ppermute | solution.py:19
  99.2 6.4 %copy-start.12 = (f32[2,64,8,256]{3,2,1,0:T(8,128)S(1)}, f32[2,64,8,256]{3,2,1,0:T(8,128)}, u32[]{:S(2)}) copy-start(f32[2,64,8,256]{3,2,1,0:T(8,128)} %get-tuple-element.11) | copy-start | bytes 3145732
  99.2 6.4 %collective-permute-start.10 = (f32[2,64,1,256]{3,2,1,0:T(1,128)S(1)}, f32[2,64,1,256]{3,2,1,0:T(1,128)S(1)}, u32[]{:S(2)}, u32[]{:S(2)}) collective-permute-start(f32[2,64,1,256]{3,2,1,0:T(1,128)S(1)} %get-tuple-element.37), channel_id=1, source_target_pairs={{1,0},{2,1},{3,2},{4,3},{5,4},{6,5},{7,6},{8,7},{9,8},{10,9},{11,1... | collective-permute-start | bytes 393224 | tf_op jit(solution)/shard_map/ppermute | solution.py:20
  107.7 18.7 %collective-permute-start.12 = (f32[2,32,8,256]{3,2,1,0:T(8,128)S(1)}, f32[2,32,8,256]{3,2,1,0:T(8,128)S(1)}, u32[]{:S(2)}, u32[]{:S(2)}) collective-permute-start(f32[2,32,8,256]{3,2,1,0:T(8,128)S(1)} %get-tuple-element.5), channel_id=1, source_target_pairs={{0,16},{1,17},{2,18},{3,19},{4,20},{5,21},{6,22},{7,23},{8,24},{9,... | collective-permute-start | bytes 1572872 | tf_op jit(solution)/shard_map/ppermute | solution.py:277
  109.0 17.1 %collective-permute-start.13 = (f32[2,32,1,256]{3,2,1,0:T(1,128)S(1)}, f32[2,32,1,256]{3,2,1,0:T(1,128)S(1)}, u32[]{:S(2)}, u32[]{:S(2)}) collective-permute-start(f32[2,32,1,256]{3,2,1,0:T(1,128)S(1)} %get-tuple-element.49), channel_id=1, source_target_pairs={{0,17},{1,18},{2,19},{3,20},{4,21},{5,22},{6,23},{7,24},{8,25},{9,... | collective-permute-start | bytes 196616 | tf_op jit(solution)/shard_map/ppermute | solution.py:278
  110.3 15.8 %collective-permute-start.14 = (f32[2,32,1,256]{3,2,1,0:T(1,128)S(1)}, f32[2,32,1,256]{3,2,1,0:T(1,128)S(1)}, u32[]{:S(2)}, u32[]{:S(2)}) collective-permute-start(f32[2,32,1,256]{3,2,1,0:T(1,128)S(1)} %get-tuple-element.50), channel_id=1, source_target_pairs={{1,16},{2,17},{3,18},{4,19},{5,20},{6,21},{7,22},{8,23},{9,24},{10... | collective-permute-start | bytes 196616 | tf_op jit(solution)/shard_map/ppermute | solution.py:279
  (7 other events, 6.9 us)

commit v10 on v9

--- a/solution.py
+++ b/solution.py
@@ -245,14 +245,22 @@
     halo_start = pair_map(lambda a, b: jnp.where(first, a, b), halo_zero, halo_earlier)
     start_rate = pick(rates, slab)
 
-    slope_zero = fine_rate(fixed_zero, halo_f0)
-    slope_one = fine_rate(fixed_one, halo_f1)
-    slope_two = fine_rate(fixed_two, halo_f2)
+    def combined(c0, c1, c2):
+        return lambda u0, u1, u2: c0 * u0 + c1 * u1 + c2 * u2
+
+    to_one = combined(-7.0 / 48.0, 1.0 / 6.0, -1.0 / 48.0)
+    to_two = combined(-1.0 / 48.0, -1.0 / 12.0, 5.0 / 48.0)
+    slopes_one = fine_rate(
+        to_one(fixed_zero, fixed_one, fixed_two), to_one(halo_f0, halo_f1, halo_f2)
+    )
+    slopes_two = fine_rate(
+        to_two(fixed_zero, fixed_one, fixed_two), to_two(halo_f0, halo_f1, halo_f2)
+    )
     node_zero = start
     rate_zero = fine_rate(node_zero, halo_start)
-    node_one = first_node(node_zero, rate_zero, slope_zero, slope_one, slope_two)
+    node_one = node_zero + half_step * rate_zero + slopes_one
     rate_one = fine_rate(node_one, halo_of(node_one))
-    node_two = second_node(node_one, rate_one, slope_zero, slope_one, slope_two)
+    node_two = node_one + half_step * rate_one + slopes_two
     rate_two = fine_rate(node_two, halo_of(node_two))
     coarse_end = shrink(node_two)
     source = shrink(slab_step * (rate_zero + 4.0 * rate_one + rate_two) / 6.0)

time: 130 us -> 125 us (0.962)
  other arithmetic: 36.1 us -> 33.1 us
    add x2 -> x1, other arithmetic: 11 us -> 1.7 us  [first_node(): node_zero + half_step * (rate_zero - s0)]
    add x0 -> x4, other arithmetic: none -> 7.35 us  [the longest x1 2.71 us: body(): node_one = node_zero + half_step * rate_zero + slopes_one]
    div x2, other arithmetic: 2.68 us -> 5.42 us  [body(): source = shrink(slab_step * (rate_zero + 4.0 * rate_one + rate_two) / 6.0)]
    add x5 -> x1, other arithmetic: 3.57 us -> 1.11 us  [add_coarse(): return (paired + jnp.expand_dims(coarse, -3)).reshape(shape)]
    add x2 -> x1, other arithmetic: 3.4 us -> 1.97 us  [second_node(): node_one + half_step * (rate_one - s1)]
    slice x4 -> x1, local copies, waits for them, and re-layouts: 1.54 us -> 0.2 us  [east(): return halo[..., 1:2, :]]
    unnamed x32 -> x30, local copies, waits for them, and re-layouts: 5.85 us -> 5.84 us
where the time goes in v10:
time: 125 us
  starting transfers between devices  38.5 us (31%)
  waiting for transfers between devices  37.1 us (30%)
  other arithmetic  33.1 us (26%)
  local copies, waits for them, and re-layouts  15.1 us (12%)
    ppermute x6, starting transfers between devices, exchange(): before = lax.ppermute(to_right, 'space', shift_pairs(count, 1))  21.7 us
    ppermute x6, waiting for transfers between devices, exchange(): after = lax.ppermute(to_left, 'space', shift_pairs(count, -1))  17.5 us
    ppermute x1, waiting for transfers between devices, body(): passed_b = lax.ppermute(hi(after), ('tm', 'space'), to_east)  14.4 us
    ppermute x6, starting transfers between devices, exchange(): after = lax.ppermute(to_left, 'space', shift_pairs(count, -1))  12.9 us
    unnamed x30, local copies, waits for them, and re-layouts  5.84 us
    div x2, other arithmetic, body(): source = shrink(slab_step * (rate_zero + 4.0 * rate_one + rate_two) / 6.0)  5.42 us
    ppermute x6, waiting for transfers between devices, exchange(): before = lax.ppermute(to_right, 'space', shift_pairs(count, 1))  5.21 us
    add x1, other arithmetic, body(): node_one = node_zero + half_step * rate_zero + slopes_one  2.71 us
  transfers between devices with their start and end apart: 15, of which 10 were waited for; matrix products, arithmetic and copies ran while one was open for 7% of the time, Pallas kernels for 0%

profile of v10, /device:TPU:11, one launch (start us, length us, event | category | flops | bytes accessed | tf_op | source)
XLA Modules:
  0.0 124.6 jit_solution(4691164079835458108)
XLA Ops:
  9.7 3.7 %collective-permute-start.1 = (f32[2,160,1,256]{3,2,1,0:T(1,128)}, f32[2,160,1,256]{3,2,1,0:T(1,128)}, u32[]{:S(2)}, u32[]{:S(2)}) collective-permute-start(f32[2,160,1,256]{3,2,1,0:T(1,128)} %pad_maximum_fusion.29), channel_id=1, source_target_pairs={{0,1},{1,2},{2,3},{3,4},{4,5},{5,6},{6,7},{7,8},{8,9},{9,10},{10,1... | collective-permute-start | bytes 983048 | tf_op jit(solution)/shard_map/ppermute | solution.py:19
  14.6 1.9 %collective-permute-start = (f32[2,160,1,256]{3,2,1,0:T(1,128)}, f32[2,160,1,256]{3,2,1,0:T(1,128)}, u32[]{:S(2)}, u32[]{:S(2)}) collective-permute-start(f32[2,160,1,256]{3,2,1,0:T(1,128)} %pad_maximum_fusion.28), channel_id=1, source_target_pairs={{1,0},{2,1},{3,2},{4,3},{5,4},{6,5},{7,6},{8,7},{9,8},{10,9},{11,1... | collective-permute-start | bytes 983048 | tf_op jit(solution)/shard_map/ppermute | solution.py:20
  17.1 2.5 %broadcast_multiply_fusion.1 = (f32[2]{0:T(128)S(1)}, f32[2]{0:T(128)S(1)}, f32[2]{0:T(128)S(1)}, f32[2]{0:T(128)S(1)}) fusion(f32[]{:T(128)} %bitcast.13, f32[]{:T(128)} %bitcast.12, f32[]{:T(128)} %bitcast.11, f32[]{:T(128)} %bitcast.10), kind=kLoop, calls=%fused_computation.224 | loop fusion | flops 10 | bytes 48 | tf_op jit(solution)/shard_map/mul | solution.py:80
  20.8 2.5 %collective-permute-done = f32[2,160,1,256]{3,2,1,0:T(1,128)} collective-permute-done((f32[2,160,1,256]{3,2,1,0:T(1,128)}, f32[2,160,1,256]{3,2,1,0:T(1,128)}, u32[]{:S(2)}, u32[]{:S(2)}) %collective-permute-start) | collective-permute-done | bytes 327712 | tf_op jit(solution)/shard_map/ppermute | solution.py:20
  24.4 1.7 %multiply_add_fusion.3 = (f32[2,64,8,256]{3,2,1,0:T(8,128)S(1)}, f32[2,64,8,256]{3,2,1,0:T(8,128)S(1)}) fusion(f32[2,64,8,256]{3,2,1,0:T(8,128)S(1)} %copy-done.2, f32[2]{0:T(128)S(1)} %get-tuple-element.24, f32[2]{0:T(128)S(1)} %get-tuple-element.138, f32[64,8,256]{2,1,0:T(8,128)S(1)} %copy-done.3, f32[64,8,256]{2,1,0:T(8,128)S(1)} %copy-done, ...), kind=kLoop, calls=%fused_computation.58 | loop fusion | flops 8912896 | bytes 5505040 | tf_op jit(solution)/shard_map/add | solution.py:138
  26.3 1.9 %collective-permute-start.2 = (f32[2,64,1,256]{3,2,1,0:T(1,128)S(1)}, f32[2,64,1,256]{3,2,1,0:T(1,128)S(1)}, u32[]{:S(2)}, u32[]{:S(2)}) collective-permute-start(f32[2,64,1,256]{3,2,1,0:T(1,128)S(1)} %get-tuple-element.42), channel_id=1, source_target_pairs={{1,0},{2,1},{3,2},{4,3},{5,4},{6,5},{7,6},{8,7},{9,8},{10,9},{11,1... | collective-permute-start | bytes 393224 | tf_op jit(solution)/shard_map/ppermute | solution.py:20
  28.2 3.6 %collective-permute-start.3 = (f32[2,64,1,256]{3,2,1,0:T(1,128)S(1)}, f32[2,64,1,256]{3,2,1,0:T(1,128)S(1)}, u32[]{:S(2)}, u32[]{:S(2)}) collective-permute-start(f32[2,64,1,256]{3,2,1,0:T(1,128)S(1)} %get-tuple-element.43), channel_id=1, source_target_pairs={{0,1},{1,2},{2,3},{3,4},{4,5},{5,6},{6,7},{7,8},{8,9},{9,10},{10,1... | collective-permute-start | bytes 393224 | tf_op jit(solution)/shard_map/ppermute | solution.py:19
  35.1 2.0 %multiply_add_fusion.2 = (f32[2,64,8,256]{3,2,1,0:T(8,128)S(1)}, f32[2,64,8,256]{3,2,1,0:T(8,128)S(1)}) fusion(f32[2,64,8,256]{3,2,1,0:T(8,128)S(1)} %get-tuple-element.28, f32[2,64,8,256]{3,2,1,0:T(8,128)S(1)} %copy-done.2, f32[2,64,8,256]{3,2,1,0:T(8,128)S(1)} %get-tuple-element.27, f32[2]{0:T(128)S(1)} %get-tuple-element.24, f32[2]{0:T(128)S(1)} %get-tuple-element.138, ...), kind=kLoop, calls=%fused_computation.54 | loop fusion | flops 11010048 | bytes 7602192 | tf_op jit(solution)/shard_map/add | solution.py:145
  37.4 4.4 %collective-permute-start.5 = (f32[2,64,2,256]{3,2,1,0:T(2,128)S(1)}, f32[2,64,2,256]{3,2,1,0:T(2,128)S(1)}, u32[]{:S(2)}, u32[]{:S(2)}) collective-permute-start(f32[2,64,2,256]{3,2,1,0:T(2,128)S(1)} %get-tuple-element.40), channel_id=1, source_target_pairs={{0,1},{1,2},{2,3},{3,4},{4,5},{5,6},{6,7},{7,8},{8,9},{9,10},{10,1... | collective-permute-start | bytes 786440 | tf_op jit(solution)/shard_map/ppermute | solution.py:19
  41.8 2.1 %collective-permute-start.4 = (f32[2,64,2,256]{3,2,1,0:T(2,128)S(1)}, f32[2,64,2,256]{3,2,1,0:T(2,128)S(1)}, u32[]{:S(2)}, u32[]{:S(2)}) collective-permute-start(f32[2,64,2,256]{3,2,1,0:T(2,128)S(1)} %get-tuple-element.41), channel_id=1, source_target_pairs={{1,0},{2,1},{3,2},{4,3},{5,4},{6,5},{7,6},{8,7},{9,8},{10,9},{11,1... | collective-permute-start | bytes 786440 | tf_op jit(solution)/shard_map/ppermute | solution.py:20
  45.2 5.6 %collective-permute-done.4 = f32[2,64,2,256]{3,2,1,0:T(2,128)S(1)} collective-permute-done((f32[2,64,2,256]{3,2,1,0:T(2,128)S(1)}, f32[2,64,2,256]{3,2,1,0:T(2,128)S(1)}, u32[]{:S(2)}, u32[]{:S(2)}) %collective-permute-start.4) | collective-permute-done | bytes 262176 | tf_op jit(solution)/shard_map/ppermute | solution.py:20
  55.9 1.9 %collective-permute-start.7 = (f32[2,32,4,256]{3,2,1,0:T(4,128)S(1)}, f32[2,32,4,256]{3,2,1,0:T(4,128)S(1)}, u32[]{:S(2)}, u32[]{:S(2)}) collective-permute-start(f32[2,32,4,256]{3,2,1,0:T(4,128)S(1)} %pad_maximum_fusion.31), channel_id=1, source_target_pairs={{0,1},{1,2},{2,3},{3,4},{4,5},{5,6},{6,7},{7,8},{8,9},{9,10},{10,1... | collective-permute-start | bytes 786440 | tf_op jit(solution)/shard_map/ppermute | solution.py:19
  57.9 2.6 %collective-permute-start.6 = (f32[2,32,4,256]{3,2,1,0:T(4,128)S(1)}, f32[2,32,4,256]{3,2,1,0:T(4,128)S(1)}, u32[]{:S(2)}, u32[]{:S(2)}) collective-permute-start(f32[2,32,4,256]{3,2,1,0:T(4,128)S(1)} %pad_maximum_fusion.30), channel_id=1, source_target_pairs={{1,0},{2,1},{3,2},{4,3},{5,4},{6,5},{7,6},{8,7},{9,8},{10,9},{11,1... | collective-permute-start | bytes 786440 | tf_op jit(solution)/shard_map/ppermute | solution.py:20
  61.2 5.2 %collective-permute-done.6 = f32[2,32,4,256]{3,2,1,0:T(4,128)S(1)} collective-permute-done((f32[2,32,4,256]{3,2,1,0:T(4,128)S(1)}, f32[2,32,4,256]{3,2,1,0:T(4,128)S(1)}, u32[]{:S(2)}, u32[]{:S(2)}) %collective-permute-start.6) | collective-permute-done | bytes 262176 | tf_op jit(solution)/shard_map/ppermute | solution.py:20
  73.3 2.7 %add_add_fusion.2 = f32[2,64,8,256]{3,2,1,0:T(8,128)S(1)} fusion(f32[2,64,8,256]{3,2,1,0:T(8,128)S(1)} %get-tuple-element.31, f32[2,64,1,256]{3,2,1,0:T(1,128)S(1)} %get-tuple-element.83, f32[2,64,1,256]{3,2,1,0:T(1,128)S(1)} %get-tuple-element.82, f32[2,64,8,256]{3,2,1,0:T(8,128)S(1)} %get-tuple-element.33, f32[2]{0:T(128)S(1)} %get-tuple-element.24, ...), kind=kLoop, calls=%fused_computation.43 | loop fusion | flops 13369344 | bytes 5767184 | tf_op jit(solution)/shard_map/add | solution.py:261
  76.2 1.9 %collective-permute-start.8 = (f32[2,64,1,256]{3,2,1,0:T(1,128)S(1)}, f32[2,64,1,256]{3,2,1,0:T(1,128)S(1)}, u32[]{:S(2)}, u32[]{:S(2)}) collective-permute-start(f32[2,64,1,256]{3,2,1,0:T(1,128)S(1)} %get-tuple-element.38), channel_id=1, source_target_pairs={{1,0},{2,1},{3,2},{4,3},{5,4},{6,5},{7,6},{8,7},{9,8},{10,9},{11,1... | collective-permute-start | bytes 393224 | tf_op jit(solution)/shard_map/ppermute | solution.py:20
  78.1 3.6 %collective-permute-start.9 = (f32[2,64,1,256]{3,2,1,0:T(1,128)S(1)}, f32[2,64,1,256]{3,2,1,0:T(1,128)S(1)}, u32[]{:S(2)}, u32[]{:S(2)}) collective-permute-start(f32[2,64,1,256]{3,2,1,0:T(1,128)S(1)} %get-tuple-element.39), channel_id=1, source_target_pairs={{0,1},{1,2},{2,3},{3,4},{4,5},{5,6},{6,7},{7,8},{8,9},{9,10},{10,1... | collective-permute-start | bytes 393224 | tf_op jit(solution)/shard_map/ppermute | solution.py:19
  82.5 2.6 %collective-permute-done.9 = f32[2,64,1,256]{3,2,1,0:T(1,128)S(1)} collective-permute-done((f32[2,64,1,256]{3,2,1,0:T(1,128)S(1)}, f32[2,64,1,256]{3,2,1,0:T(1,128)S(1)}, u32[]{:S(2)}, u32[]{:S(2)}) %collective-permute-start.9) | collective-permute-done | bytes 131104 | tf_op jit(solution)/shard_map/ppermute | solution.py:19
  85.1 2.7 %add_add_fusion = f32[2,64,8,256]{3,2,1,0:T(8,128)S(1)} fusion(f32[2,64,8,256]{3,2,1,0:T(8,128)S(1)} %get-tuple-element.32, f32[2,64,1,256]{3,2,1,0:T(1,128)S(1)} %get-tuple-element.85, f32[2,64,1,256]{3,2,1,0:T(1,128)S(1)} %get-tuple-element.84, f32[2,64,8,256]{3,2,1,0:T(8,128)S(1)} %add_add_fusion.2, f32[2]{0:T(128)S(1)} %get-tuple-element.24, ...), kind=kLoop, calls=%fused_computation.36 | loop fusion | flops 13369344 | bytes 5767184 | tf_op jit(solution)/shard_map/add | solution.py:263
  88.0 4.4 %collective-permute-start.11 = (f32[2,64,1,256]{3,2,1,0:T(1,128)S(1)}, f32[2,64,1,256]{3,2,1,0:T(1,128)S(1)}, u32[]{:S(2)}, u32[]{:S(2)}) collective-permute-start(f32[2,64,1,256]{3,2,1,0:T(1,128)S(1)} %get-tuple-element.36), channel_id=1, source_target_pairs={{0,1},{1,2},{2,3},{3,4},{4,5},{5,6},{6,7},{7,8},{8,9},{9,10},{10,1... | collective-permute-start | bytes 393224 | tf_op jit(solution)/shard_map/ppermute | solution.py:19
  92.4 2.4 %collective-permute-start.10 = (f32[2,64,1,256]{3,2,1,0:T(1,128)S(1)}, f32[2,64,1,256]{3,2,1,0:T(1,128)S(1)}, u32[]{:S(2)}, u32[]{:S(2)}) collective-permute-start(f32[2,64,1,256]{3,2,1,0:T(1,128)S(1)} %get-tuple-element.37), channel_id=1, source_target_pairs={{1,0},{2,1},{3,2},{4,3},{5,4},{6,5},{7,6},{8,7},{9,8},{10,9},{11,1... | collective-permute-start | bytes 393224 | tf_op jit(solution)/shard_map/ppermute | solution.py:20
  94.9 3.8 %collective-permute-done.10 = f32[2,64,1,256]{3,2,1,0:T(1,128)S(1)} collective-permute-done((f32[2,64,1,256]{3,2,1,0:T(1,128)S(1)}, f32[2,64,1,256]{3,2,1,0:T(1,128)S(1)}, u32[]{:S(2)}, u32[]{:S(2)}) %collective-permute-start.10) | collective-permute-done | bytes 131104 | tf_op jit(solution)/shard_map/ppermute | solution.py:20
  98.7 4.1 %add_multiply_fusion = f32[2,64,8,256]{3,2,1,0:T(8,128)S(1)} fusion(f32[2,64,8,256]{3,2,1,0:T(8,128)S(1)} %add_add_fusion, f32[2,64,1,256]{3,2,1,0:T(1,128)S(1)} %collective-permute-done.10, f32[2,64,1,256]{3,2,1,0:T(1,128)S(1)} %collective-permute-done.11, f32[2]{0:T(128)S(1)} %get-tuple-element.24, f32[2]{0:T(128)S(1)} %get-tuple-element.138, ...), kind=kLoop, calls=%fused_computation.33 | loop fusion | flops 19922944 | bytes 7077904 | tf_op jit(solution)/shard_map/div | solution.py:266
  107.5 14.4 %collective-permute-done.13 = f32[2,32,1,256]{3,2,1,0:T(1,128)S(1)} collective-permute-done((f32[2,32,1,256]{3,2,1,0:T(1,128)S(1)}, f32[2,32,1,256]{3,2,1,0:T(1,128)S(1)}, u32[]{:S(2)}, u32[]{:S(2)}) %collective-permute-start.13) | collective-permute-done | bytes 65568 | tf_op jit(solution)/shard_map/ppermute | solution.py:286
  (138 shorter events, 39.6 us)
Async XLA Ops:
  0.0 1.2 copy-start
  1.2 1.2 copy-start.2
  2.8 1.2 copy-start.4
  8.3 6.2 %copy-start.6 = (f32[32,8,256]{2,1,0:T(8,128)}, f32[32,8,256]{2,1,0:T(8,128)S(1)}, u32[]{:S(2)}) copy-start(f32[32,8,256]{2,1,0:T(8,128)S(1)} %get-tuple-element.127) | copy-start | bytes 786436
  8.3 6.2 %copy-start.8 = (f32[32,8,256]{2,1,0:T(8,128)}, f32[32,8,256]{2,1,0:T(8,128)S(1)}, u32[]{:S(2)}) copy-start(f32[32,8,256]{2,1,0:T(8,128)S(1)} %get-tuple-element.128) | copy-start | bytes 786436
  8.4 8.1 %copy-start.14 = (f32[2,2]{1,0:T(2,128)S(1)}, f32[2,2]{1,0:T(2,128)}, u32[]{:S(2)}) copy-start(f32[2,2]{1,0:T(2,128)} %param.11) | copy-start | bytes 52
  9.7 10.0 %collective-permute-start.1 = (f32[2,160,1,256]{3,2,1,0:T(1,128)}, f32[2,160,1,256]{3,2,1,0:T(1,128)}, u32[]{:S(2)}, u32[]{:S(2)}) collective-permute-start(f32[2,160,1,256]{3,2,1,0:T(1,128)} %pad_maximum_fusion.29), channel_id=1, source_target_pairs={{0,1},{1,2},{2,3},{3,4},{4,5},{5,6},{6,7},{7,8},{8,9},{9,10},{10,1... | collective-permute-start | bytes 983048 | tf_op jit(solution)/shard_map/ppermute | solution.py:19
  14.6 8.7 %collective-permute-start = (f32[2,160,1,256]{3,2,1,0:T(1,128)}, f32[2,160,1,256]{3,2,1,0:T(1,128)}, u32[]{:S(2)}, u32[]{:S(2)}) collective-permute-start(f32[2,160,1,256]{3,2,1,0:T(1,128)} %pad_maximum_fusion.28), channel_id=1, source_target_pairs={{1,0},{2,1},{3,2},{4,3},{5,4},{6,5},{7,6},{8,7},{9,8},{10,9},{11,1... | collective-permute-start | bytes 983048 | tf_op jit(solution)/shard_map/ppermute | solution.py:20
  26.3 7.5 %collective-permute-start.2 = (f32[2,64,1,256]{3,2,1,0:T(1,128)S(1)}, f32[2,64,1,256]{3,2,1,0:T(1,128)S(1)}, u32[]{:S(2)}, u32[]{:S(2)}) collective-permute-start(f32[2,64,1,256]{3,2,1,0:T(1,128)S(1)} %get-tuple-element.42), channel_id=1, source_target_pairs={{1,0},{2,1},{3,2},{4,3},{5,4},{6,5},{7,6},{8,7},{9,8},{10,9},{11,1... | collective-permute-start | bytes 393224 | tf_op jit(solution)/shard_map/ppermute | solution.py:20
  28.2 6.9 %collective-permute-start.3 = (f32[2,64,1,256]{3,2,1,0:T(1,128)S(1)}, f32[2,64,1,256]{3,2,1,0:T(1,128)S(1)}, u32[]{:S(2)}, u32[]{:S(2)}) collective-permute-start(f32[2,64,1,256]{3,2,1,0:T(1,128)S(1)} %get-tuple-element.43), channel_id=1, source_target_pairs={{0,1},{1,2},{2,3},{3,4},{4,5},{5,6},{6,7},{7,8},{8,9},{9,10},{10,1... | collective-permute-start | bytes 393224 | tf_op jit(solution)/shard_map/ppermute | solution.py:19
  37.4 7.7 %collective-permute-start.5 = (f32[2,64,2,256]{3,2,1,0:T(2,128)S(1)}, f32[2,64,2,256]{3,2,1,0:T(2,128)S(1)}, u32[]{:S(2)}, u32[]{:S(2)}) collective-permute-start(f32[2,64,2,256]{3,2,1,0:T(2,128)S(1)} %get-tuple-element.40), channel_id=1, source_target_pairs={{0,1},{1,2},{2,3},{3,4},{4,5},{5,6},{6,7},{7,8},{8,9},{9,10},{10,1... | collective-permute-start | bytes 786440 | tf_op jit(solution)/shard_map/ppermute | solution.py:19
  41.8 9.0 %collective-permute-start.4 = (f32[2,64,2,256]{3,2,1,0:T(2,128)S(1)}, f32[2,64,2,256]{3,2,1,0:T(2,128)S(1)}, u32[]{:S(2)}, u32[]{:S(2)}) collective-permute-start(f32[2,64,2,256]{3,2,1,0:T(2,128)S(1)} %get-tuple-element.41), channel_id=1, source_target_pairs={{1,0},{2,1},{3,2},{4,3},{5,4},{6,5},{7,6},{8,7},{9,8},{10,9},{11,1... | collective-permute-start | bytes 786440 | tf_op jit(solution)/shard_map/ppermute | solution.py:20
  52.4 1.2 copy-start.9
  52.5 1.2 copy-start.11
  52.5 1.4 %copy-start.13 = (f32[2,32,8,256]{3,2,1,0:T(8,128)S(1)}, f32[2,32,8,256]{3,2,1,0:T(8,128)}, u32[]{:S(2)}) copy-start(f32[2,32,8,256]{3,2,1,0:T(8,128)} %copy-done.12) | copy-start | bytes 1572868
  55.9 5.2 %collective-permute-start.7 = (f32[2,32,4,256]{3,2,1,0:T(4,128)S(1)}, f32[2,32,4,256]{3,2,1,0:T(4,128)S(1)}, u32[]{:S(2)}, u32[]{:S(2)}) collective-permute-start(f32[2,32,4,256]{3,2,1,0:T(4,128)S(1)} %pad_maximum_fusion.31), channel_id=1, source_target_pairs={{0,1},{1,2},{2,3},{3,4},{4,5},{5,6},{6,7},{7,8},{8,9},{9,10},{10,1... | collective-permute-start | bytes 786440 | tf_op jit(solution)/shard_map/ppermute | solution.py:19
  57.9 8.5 %collective-permute-start.6 = (f32[2,32,4,256]{3,2,1,0:T(4,128)S(1)}, f32[2,32,4,256]{3,2,1,0:T(4,128)S(1)}, u32[]{:S(2)}, u32[]{:S(2)}) collective-permute-start(f32[2,32,4,256]{3,2,1,0:T(4,128)S(1)} %pad_maximum_fusion.30), channel_id=1, source_target_pairs={{1,0},{2,1},{3,2},{4,3},{5,4},{6,5},{7,6},{8,7},{9,8},{10,9},{11,1... | collective-permute-start | bytes 786440 | tf_op jit(solution)/shard_map/ppermute | solution.py:20
  76.2 6.3 %collective-permute-start.8 = (f32[2,64,1,256]{3,2,1,0:T(1,128)S(1)}, f32[2,64,1,256]{3,2,1,0:T(1,128)S(1)}, u32[]{:S(2)}, u32[]{:S(2)}) collective-permute-start(f32[2,64,1,256]{3,2,1,0:T(1,128)S(1)} %get-tuple-element.38), channel_id=1, source_target_pairs={{1,0},{2,1},{3,2},{4,3},{5,4},{6,5},{7,6},{8,7},{9,8},{10,9},{11,1... | collective-permute-start | bytes 393224 | tf_op jit(solution)/shard_map/ppermute | solution.py:20
  78.1 6.9 %collective-permute-start.9 = (f32[2,64,1,256]{3,2,1,0:T(1,128)S(1)}, f32[2,64,1,256]{3,2,1,0:T(1,128)S(1)}, u32[]{:S(2)}, u32[]{:S(2)}) collective-permute-start(f32[2,64,1,256]{3,2,1,0:T(1,128)S(1)} %get-tuple-element.39), channel_id=1, source_target_pairs={{0,1},{1,2},{2,3},{3,4},{4,5},{5,6},{6,7},{7,8},{8,9},{9,10},{10,1... | collective-permute-start | bytes 393224 | tf_op jit(solution)/shard_map/ppermute | solution.py:19
  88.0 6.9 %collective-permute-start.11 = (f32[2,64,1,256]{3,2,1,0:T(1,128)S(1)}, f32[2,64,1,256]{3,2,1,0:T(1,128)S(1)}, u32[]{:S(2)}, u32[]{:S(2)}) collective-permute-start(f32[2,64,1,256]{3,2,1,0:T(1,128)S(1)} %get-tuple-element.36), channel_id=1, source_target_pairs={{0,1},{1,2},{2,3},{3,4},{4,5},{5,6},{6,7},{7,8},{8,9},{9,10},{10,1... | collective-permute-start | bytes 393224 | tf_op jit(solution)/shard_map/ppermute | solution.py:19
  92.4 6.3 %collective-permute-start.10 = (f32[2,64,1,256]{3,2,1,0:T(1,128)S(1)}, f32[2,64,1,256]{3,2,1,0:T(1,128)S(1)}, u32[]{:S(2)}, u32[]{:S(2)}) collective-permute-start(f32[2,64,1,256]{3,2,1,0:T(1,128)S(1)} %get-tuple-element.37), channel_id=1, source_target_pairs={{1,0},{2,1},{3,2},{4,3},{5,4},{6,5},{7,6},{8,7},{9,8},{10,9},{11,1... | collective-permute-start | bytes 393224 | tf_op jit(solution)/shard_map/ppermute | solution.py:20
  103.5 18.7 %collective-permute-start.12 = (f32[2,32,8,256]{3,2,1,0:T(8,128)S(1)}, f32[2,32,8,256]{3,2,1,0:T(8,128)S(1)}, u32[]{:S(2)}, u32[]{:S(2)}) collective-permute-start(f32[2,32,8,256]{3,2,1,0:T(8,128)S(1)} %get-tuple-element.5), channel_id=1, source_target_pairs={{0,16},{1,17},{2,18},{3,19},{4,20},{5,21},{6,22},{7,23},{8,24},{9,... | collective-permute-start | bytes 1572872 | tf_op jit(solution)/shard_map/ppermute | solution.py:285
  104.8 17.1 %collective-permute-start.13 = (f32[2,32,1,256]{3,2,1,0:T(1,128)S(1)}, f32[2,32,1,256]{3,2,1,0:T(1,128)S(1)}, u32[]{:S(2)}, u32[]{:S(2)}) collective-permute-start(f32[2,32,1,256]{3,2,1,0:T(1,128)S(1)} %get-tuple-element.46), channel_id=1, source_target_pairs={{0,17},{1,18},{2,19},{3,20},{4,21},{5,22},{6,23},{7,24},{8,25},{9,... | collective-permute-start | bytes 196616 | tf_op jit(solution)/shard_map/ppermute | solution.py:286
  106.1 15.8 %collective-permute-start.14 = (f32[2,32,1,256]{3,2,1,0:T(1,128)S(1)}, f32[2,32,1,256]{3,2,1,0:T(1,128)S(1)}, u32[]{:S(2)}, u32[]{:S(2)}) collective-permute-start(f32[2,32,1,256]{3,2,1,0:T(1,128)S(1)} %get-tuple-element.47), channel_id=1, source_target_pairs={{1,16},{2,17},{3,18},{4,19},{5,20},{6,21},{7,22},{8,23},{9,24},{10... | collective-permute-start | bytes 196616 | tf_op jit(solution)/shard_map/ppermute | solution.py:287
  (6 other events, 5.7 us)

commit v11 on v10

--- a/solution.py
+++ b/solution.py
@@ -250,20 +250,22 @@
 
     to_one = combined(-7.0 / 48.0, 1.0 / 6.0, -1.0 / 48.0)
     to_two = combined(-1.0 / 48.0, -1.0 / 12.0, 5.0 / 48.0)
-    slopes_one = fine_rate(
-        to_one(fixed_zero, fixed_one, fixed_two), to_one(halo_f0, halo_f1, halo_f2)
-    )
-    slopes_two = fine_rate(
-        to_two(fixed_zero, fixed_one, fixed_two), to_two(halo_f0, halo_f1, halo_f2)
-    )
     node_zero = start
-    rate_zero = fine_rate(node_zero, halo_start)
-    node_one = node_zero + half_step * rate_zero + slopes_one
-    rate_one = fine_rate(node_one, halo_of(node_one))
-    node_two = node_one + half_step * rate_one + slopes_two
-    rate_two = fine_rate(node_two, halo_of(node_two))
+    node_one = node_zero + fine_rate(
+        half_step * node_zero + to_one(fixed_zero, fixed_one, fixed_two),
+        half_step * halo_start + to_one(halo_f0, halo_f1, halo_f2),
+    )
+    halo_one = halo_of(node_one)
+    node_two = node_one + fine_rate(
+        half_step * node_one + to_two(fixed_zero, fixed_one, fixed_two),
+        half_step * halo_one + to_two(halo_f0, halo_f1, halo_f2),
+    )
+    halo_two = halo_of(node_two)
     coarse_end = shrink(node_two)
-    source = shrink(slab_step * (rate_zero + 4.0 * rate_one + rate_two) / 6.0)
+    quadrature = fine_rate(
+        node_zero + 4.0 * node_one + node_two, halo_start + 4.0 * halo_one + halo_two
+    )
+    source = shrink(slab_step * quadrature / 6.0)
     offset = source - slab_step * start_rate
 
     down = shift_pairs(slabs, 1)

time: 125 us -> 121 us (0.968)
  starting transfers between devices: 38.5 us -> 35 us
  other arithmetic: 33.1 us -> 30.1 us
  waiting for transfers between devices: 37.1 us -> 39.3 us
    ppermute x6, waiting for transfers between devices: 17.5 us -> 22.4 us  [exchange(): after = lax.ppermute(to_left, 'space', shift_pairs(count, -1))]
    ppermute x6, starting transfers between devices: 21.7 us -> 17.5 us  [exchange(): before = lax.ppermute(to_right, 'space', shift_pairs(count, 1))]
    div x2 -> x1, other arithmetic: 5.42 us -> 1.34 us  [body(): source = shrink(slab_step * (rate_zero + 4.0 * rate_one + rate_two) / 6.0)]
    ppermute x6, waiting for transfers between devices: 5.21 us -> 2.63 us  [exchange(): before = lax.ppermute(to_right, 'space', shift_pairs(count, 1))]
    div x0 -> x1, other arithmetic: none -> 1.3 us  [body(): source = shrink(slab_step * quadrature / 6.0)]
    add x4 -> x6, other arithmetic: 7.35 us -> 7.26 us  [the longest x1 2.15 us: body(): half_step * node_one + to_two(fixed_zero, fixed_one, fixed_two)]
  transfers between devices with their start and end apart: 15 -> 15, of which waited for: 10 -> 9; matrix products, arithmetic and copies ran while one was open for 7% -> 7% of each run, Pallas kernels for 0% -> 0%
where the time goes in v11:
time: 121 us; the launch traced here: 120 us
  waiting for transfers between devices  39.3 us (32%)
  starting transfers between devices  35 us (29%)
  other arithmetic  30.1 us (25%)
  local copies, waits for them, and re-layouts  15.1 us (12%)
    ppermute x6, waiting for transfers between devices, exchange(): after = lax.ppermute(to_left, 'space', shift_pairs(count, -1))  22.4 us
    ppermute x6, starting transfers between devices, exchange(): before = lax.ppermute(to_right, 'space', shift_pairs(count, 1))  17.5 us
    ppermute x1, waiting for transfers between devices, body(): passed_b = lax.ppermute(hi(after), ('tm', 'space'), to_east)  14.2 us
    ppermute x6, starting transfers between devices, exchange(): after = lax.ppermute(to_left, 'space', shift_pairs(count, -1))  13.6 us
    unnamed x30, local copies, waits for them, and re-layouts  5.83 us
    ppermute x6, waiting for transfers between devices, exchange(): before = lax.ppermute(to_right, 'space', shift_pairs(count, 1))  2.63 us
    mul x1, other arithmetic, stencil(): reaction = own * middle + other * middle[::-1]  2.48 us
  transfers between devices with their start and end apart: 15, of which 9 were waited for; matrix products, arithmetic and copies ran while one was open for 7% of the time, Pallas kernels for 0%

profile of v11, /device:TPU:11, one launch (start us, length us, event | category | flops | bytes accessed | tf_op | source)
XLA Modules:
  0.0 120.3 jit_solution(5472689852787297925)
XLA Ops:
  9.7 3.7 %collective-permute-start.1 = (f32[2,160,1,256]{3,2,1,0:T(1,128)}, f32[2,160,1,256]{3,2,1,0:T(1,128)}, u32[]{:S(2)}, u32[]{:S(2)}) collective-permute-start(f32[2,160,1,256]{3,2,1,0:T(1,128)} %pad_maximum_fusion.25), channel_id=1, source_target_pairs={{0,1},{1,2},{2,3},{3,4},{4,5},{5,6},{6,7},{7,8},{8,9},{9,10},{10,1... | collective-permute-start | bytes 983048 | tf_op jit(solution)/shard_map/ppermute | solution.py:19
  14.6 1.9 %collective-permute-start = (f32[2,160,1,256]{3,2,1,0:T(1,128)}, f32[2,160,1,256]{3,2,1,0:T(1,128)}, u32[]{:S(2)}, u32[]{:S(2)}) collective-permute-start(f32[2,160,1,256]{3,2,1,0:T(1,128)} %pad_maximum_fusion.24), channel_id=1, source_target_pairs={{1,0},{2,1},{3,2},{4,3},{5,4},{6,5},{7,6},{8,7},{9,8},{10,9},{11,1... | collective-permute-start | bytes 983048 | tf_op jit(solution)/shard_map/ppermute | solution.py:20
  17.2 2.5 %broadcast_multiply_fusion.1 = (f32[2]{0:T(128)S(1)}, f32[2]{0:T(128)S(1)}, f32[2]{0:T(128)S(1)}, f32[2]{0:T(128)S(1)}) fusion(f32[]{:T(128)} %bitcast.13, f32[]{:T(128)} %bitcast.12, f32[]{:T(128)} %bitcast.11, f32[]{:T(128)} %bitcast.10), kind=kLoop, calls=%fused_computation.213 | loop fusion | flops 10 | bytes 48 | tf_op jit(solution)/shard_map/mul | solution.py:80
  20.8 2.5 %collective-permute-done = f32[2,160,1,256]{3,2,1,0:T(1,128)} collective-permute-done((f32[2,160,1,256]{3,2,1,0:T(1,128)}, f32[2,160,1,256]{3,2,1,0:T(1,128)}, u32[]{:S(2)}, u32[]{:S(2)}) %collective-permute-start) | collective-permute-done | bytes 327712 | tf_op jit(solution)/shard_map/ppermute | solution.py:20
  24.4 1.7 %multiply_add_fusion.1 = (f32[2,64,8,256]{3,2,1,0:T(8,128)S(1)}, f32[2,64,8,256]{3,2,1,0:T(8,128)S(1)}) fusion(f32[2,64,8,256]{3,2,1,0:T(8,128)S(1)} %copy-done, f32[2]{0:T(128)S(1)} %get-tuple-element.30, f32[2]{0:T(128)S(1)} %get-tuple-element.139, f32[64,8,256]{2,1,0:T(8,128)S(1)} %copy-done.3, f32[64,8,256]{2,1,0:T(8,128)S(1)} %copy-done.2, ...), kind=kLoop, calls=%fused_computation.45 | loop fusion | flops 8912896 | bytes 5505040 | tf_op jit(solution)/shard_map/add | solution.py:138
  26.3 1.9 %collective-permute-start.2 = (f32[2,64,1,256]{3,2,1,0:T(1,128)S(1)}, f32[2,64,1,256]{3,2,1,0:T(1,128)S(1)}, u32[]{:S(2)}, u32[]{:S(2)}) collective-permute-start(f32[2,64,1,256]{3,2,1,0:T(1,128)S(1)} %get-tuple-element.43), channel_id=1, source_target_pairs={{1,0},{2,1},{3,2},{4,3},{5,4},{6,5},{7,6},{8,7},{9,8},{10,9},{11,1... | collective-permute-start | bytes 393224 | tf_op jit(solution)/shard_map/ppermute | solution.py:20
  28.2 3.6 %collective-permute-start.3 = (f32[2,64,1,256]{3,2,1,0:T(1,128)S(1)}, f32[2,64,1,256]{3,2,1,0:T(1,128)S(1)}, u32[]{:S(2)}, u32[]{:S(2)}) collective-permute-start(f32[2,64,1,256]{3,2,1,0:T(1,128)S(1)} %get-tuple-element.44), channel_id=1, source_target_pairs={{0,1},{1,2},{2,3},{3,4},{4,5},{5,6},{6,7},{7,8},{8,9},{9,10},{10,1... | collective-permute-start | bytes 393224 | tf_op jit(solution)/shard_map/ppermute | solution.py:19
  35.1 2.0 %multiply_add_fusion = (f32[2,64,8,256]{3,2,1,0:T(8,128)S(1)}, f32[2,64,8,256]{3,2,1,0:T(8,128)S(1)}) fusion(f32[2,64,8,256]{3,2,1,0:T(8,128)S(1)} %get-tuple-element.34, f32[2,64,8,256]{3,2,1,0:T(8,128)S(1)} %copy-done, f32[2,64,8,256]{3,2,1,0:T(8,128)S(1)} %get-tuple-element.33, f32[2]{0:T(128)S(1)} %get-tuple-element.30, f32[2]{0:T(128)S(1)} %get-tuple-element.139, ...), kind=kLoop, calls=%fused_computation.41 | loop fusion | flops 11010048 | bytes 7602192 | tf_op jit(solution)/shard_map/add | solution.py:145
  37.4 4.4 %collective-permute-start.5 = (f32[2,64,2,256]{3,2,1,0:T(2,128)S(1)}, f32[2,64,2,256]{3,2,1,0:T(2,128)S(1)}, u32[]{:S(2)}, u32[]{:S(2)}) collective-permute-start(f32[2,64,2,256]{3,2,1,0:T(2,128)S(1)} %get-tuple-element.41), channel_id=1, source_target_pairs={{0,1},{1,2},{2,3},{3,4},{4,5},{5,6},{6,7},{7,8},{8,9},{9,10},{10,1... | collective-permute-start | bytes 786440 | tf_op jit(solution)/shard_map/ppermute | solution.py:19
  41.8 2.1 %collective-permute-start.4 = (f32[2,64,2,256]{3,2,1,0:T(2,128)S(1)}, f32[2,64,2,256]{3,2,1,0:T(2,128)S(1)}, u32[]{:S(2)}, u32[]{:S(2)}) collective-permute-start(f32[2,64,2,256]{3,2,1,0:T(2,128)S(1)} %get-tuple-element.42), channel_id=1, source_target_pairs={{1,0},{2,1},{3,2},{4,3},{5,4},{6,5},{7,6},{8,7},{9,8},{10,9},{11,1... | collective-permute-start | bytes 786440 | tf_op jit(solution)/shard_map/ppermute | solution.py:20
  45.2 5.6 %collective-permute-done.4 = f32[2,64,2,256]{3,2,1,0:T(2,128)S(1)} collective-permute-done((f32[2,64,2,256]{3,2,1,0:T(2,128)S(1)}, f32[2,64,2,256]{3,2,1,0:T(2,128)S(1)}, u32[]{:S(2)}, u32[]{:S(2)}) %collective-permute-start.4) | collective-permute-done | bytes 262176 | tf_op jit(solution)/shard_map/ppermute | solution.py:20
  55.9 1.9 %collective-permute-start.7 = (f32[2,32,4,256]{3,2,1,0:T(4,128)S(1)}, f32[2,32,4,256]{3,2,1,0:T(4,128)S(1)}, u32[]{:S(2)}, u32[]{:S(2)}) collective-permute-start(f32[2,32,4,256]{3,2,1,0:T(4,128)S(1)} %pad_maximum_fusion.27), channel_id=1, source_target_pairs={{0,1},{1,2},{2,3},{3,4},{4,5},{5,6},{6,7},{7,8},{8,9},{9,10},{10,1... | collective-permute-start | bytes 786440 | tf_op jit(solution)/shard_map/ppermute | solution.py:19
  58.0 2.6 %collective-permute-start.6 = (f32[2,32,4,256]{3,2,1,0:T(4,128)S(1)}, f32[2,32,4,256]{3,2,1,0:T(4,128)S(1)}, u32[]{:S(2)}, u32[]{:S(2)}) collective-permute-start(f32[2,32,4,256]{3,2,1,0:T(4,128)S(1)} %pad_maximum_fusion.26), channel_id=1, source_target_pairs={{1,0},{2,1},{3,2},{4,3},{5,4},{6,5},{7,6},{8,7},{9,8},{10,9},{11,1... | collective-permute-start | bytes 786440 | tf_op jit(solution)/shard_map/ppermute | solution.py:20
  61.3 5.2 %collective-permute-done.6 = f32[2,32,4,256]{3,2,1,0:T(4,128)S(1)} collective-permute-done((f32[2,32,4,256]{3,2,1,0:T(4,128)S(1)}, f32[2,32,4,256]{3,2,1,0:T(4,128)S(1)}, u32[]{:S(2)}, u32[]{:S(2)}) %collective-permute-start.6) | collective-permute-done | bytes 262176 | tf_op jit(solution)/shard_map/ppermute | solution.py:20
  69.9 1.5 %add_multiply_fusion.2 = (f32[2,32,8,256]{3,2,1,0:T(8,128)S(1)}, f32[2,32,8,256]{3,2,1,0:T(8,128)S(1)}, f32[2,32,8,256]{3,2,1,0:T(8,128)S(1)}, f32[2,32,8,256]{3,2,1,0:T(8,128)S(1)}, f32[2,32,8,256]{3,2,1,0:T(8,128)S(1)}) fusion(pred[]{:T(512)S(6)} %eq.100, f32[2,32,8,256]{3,2,1,0:T(8,128)S(1)} %get-tuple-element.25, ...), kind=kLoop, calls=%fused_computation.119 | loop fusion | flops 6815744 | bytes 7995484 | tf_op jit(solution)/shard_map/mul | solution.py:232
  72.7 2.2 %add_add_fusion.2 = (f32[2,64,8,256]{3,2,1,0:T(8,128)S(1)}, f32[2,64,8,256]{3,2,1,0:T(8,128)S(1)}) fusion(f32[2,64,8,256]{3,2,1,0:T(8,128)S(1)} %get-tuple-element.31, f32[2,64,8,256]{3,2,1,0:T(8,128)S(1)} %bitcast.47, f32[2,64,8,256]{3,2,1,0:T(8,128)S(1)} %bitcast.43, f32[2,64,8,256]{3,2,1,0:T(8,128)S(1)} %copy-done, f32[2,64,8,256]{3,2,1,0:T(8,128)S(1)} %bitcast.45, ...), kind=kLoop, calls=%fused_computation.32 | loop fusion | flops 11796480 | bytes 12845072 | tf_op jit(solution)/shard_map/add | solution.py:260
  75.0 1.9 %collective-permute-start.8 = (f32[2,64,1,256]{3,2,1,0:T(1,128)S(1)}, f32[2,64,1,256]{3,2,1,0:T(1,128)S(1)}, u32[]{:S(2)}, u32[]{:S(2)}) collective-permute-start(f32[2,64,1,256]{3,2,1,0:T(1,128)S(1)} %get-tuple-element.39), channel_id=1, source_target_pairs={{0,1},{1,2},{2,3},{3,4},{4,5},{5,6},{6,7},{7,8},{8,9},{9,10},{10,1... | collective-permute-start | bytes 393224 | tf_op jit(solution)/shard_map/ppermute | solution.py:19
  77.0 2.4 %collective-permute-start.9 = (f32[2,64,1,256]{3,2,1,0:T(1,128)S(1)}, f32[2,64,1,256]{3,2,1,0:T(1,128)S(1)}, u32[]{:S(2)}, u32[]{:S(2)}) collective-permute-start(f32[2,64,1,256]{3,2,1,0:T(1,128)S(1)} %get-tuple-element.40), channel_id=1, source_target_pairs={{1,0},{2,1},{3,2},{4,3},{5,4},{6,5},{7,6},{8,7},{9,8},{10,9},{11,1... | collective-permute-start | bytes 393224 | tf_op jit(solution)/shard_map/ppermute | solution.py:20
  79.4 4.8 %collective-permute-done.9 = f32[2,64,1,256]{3,2,1,0:T(1,128)S(1)} collective-permute-done((f32[2,64,1,256]{3,2,1,0:T(1,128)S(1)}, f32[2,64,1,256]{3,2,1,0:T(1,128)S(1)}, u32[]{:S(2)}, u32[]{:S(2)}) %collective-permute-start.9) | collective-permute-done | bytes 131104 | tf_op jit(solution)/shard_map/ppermute | solution.py:20
  85.5 1.6 %add_add_fusion = (f32[2,64,8,256]{3,2,1,0:T(8,128)S(1)}, f32[2,64,8,256]{3,2,1,0:T(8,128)S(1)}) fusion(f32[2,64,8,256]{3,2,1,0:T(8,128)S(1)} %get-tuple-element.18, f32[2,64,8,256]{3,2,1,0:T(8,128)S(1)} %get-tuple-element.10, f32[2,64,8,256]{3,2,1,0:T(8,128)S(1)} %get-tuple-element.9, f32[2]{0:T(128)S(1)} %get-tuple-element.30, ...), kind=kLoop, calls=%fused_computation.28 | loop fusion | flops 7340032 | bytes 7602192 | tf_op jit(solution)/shard_map/add | solution.py:266
  87.4 1.9 %collective-permute-start.10 = (f32[2,64,1,256]{3,2,1,0:T(1,128)S(1)}, f32[2,64,1,256]{3,2,1,0:T(1,128)S(1)}, u32[]{:S(2)}, u32[]{:S(2)}) collective-permute-start(f32[2,64,1,256]{3,2,1,0:T(1,128)S(1)} %get-tuple-element.37), channel_id=1, source_target_pairs={{0,1},{1,2},{2,3},{3,4},{4,5},{5,6},{6,7},{7,8},{8,9},{9,10},{10,1... | collective-permute-start | bytes 393224 | tf_op jit(solution)/shard_map/ppermute | solution.py:19
  89.3 2.6 %collective-permute-start.11 = (f32[2,64,1,256]{3,2,1,0:T(1,128)S(1)}, f32[2,64,1,256]{3,2,1,0:T(1,128)S(1)}, u32[]{:S(2)}, u32[]{:S(2)}) collective-permute-start(f32[2,64,1,256]{3,2,1,0:T(1,128)S(1)} %get-tuple-element.38), channel_id=1, source_target_pairs={{1,0},{2,1},{3,2},{4,3},{5,4},{6,5},{7,6},{8,7},{9,8},{10,9},{11,1... | collective-permute-start | bytes 393224 | tf_op jit(solution)/shard_map/ppermute | solution.py:20
  92.0 4.5 %collective-permute-done.11 = f32[2,64,1,256]{3,2,1,0:T(1,128)S(1)} collective-permute-done((f32[2,64,1,256]{3,2,1,0:T(1,128)S(1)}, f32[2,64,1,256]{3,2,1,0:T(1,128)S(1)}, u32[]{:S(2)}, u32[]{:S(2)}) %collective-permute-start.11) | collective-permute-done | bytes 131104 | tf_op jit(solution)/shard_map/ppermute | solution.py:20
  103.3 14.2 %collective-permute-done.13 = f32[2,32,1,256]{3,2,1,0:T(1,128)S(1)} collective-permute-done((f32[2,32,1,256]{3,2,1,0:T(1,128)S(1)}, f32[2,32,1,256]{3,2,1,0:T(1,128)S(1)}, u32[]{:S(2)}, u32[]{:S(2)}) %collective-permute-start.13) | collective-permute-done | bytes 65568 | tf_op jit(solution)/shard_map/ppermute | solution.py:288
  (139 shorter events, 40.3 us)
Async XLA Ops:
  0.0 1.2 %copy-start.2 = (f32[64,8,256]{2,1,0:T(8,128)S(1)}, f32[64,8,256]{2,1,0:T(8,128)}, u32[]{:S(2)}) copy-start(f32[64,8,256]{2,1,0:T(8,128)} %param.7) | copy-start | bytes 1572868
  1.2 1.2 %copy-start = (f32[2,64,8,256]{3,2,1,0:T(8,128)S(1)}, f32[2,64,8,256]{3,2,1,0:T(8,128)}, u32[]{:S(2)}) copy-start(f32[2,64,8,256]{3,2,1,0:T(8,128)} %param.6) | copy-start | bytes 3145732
  2.8 1.2 copy-start.4
  8.3 6.2 %copy-start.6 = (f32[32,8,256]{2,1,0:T(8,128)}, f32[32,8,256]{2,1,0:T(8,128)S(1)}, u32[]{:S(2)}) copy-start(f32[32,8,256]{2,1,0:T(8,128)S(1)} %get-tuple-element.128) | copy-start | bytes 786436
  8.3 6.2 %copy-start.8 = (f32[32,8,256]{2,1,0:T(8,128)}, f32[32,8,256]{2,1,0:T(8,128)S(1)}, u32[]{:S(2)}) copy-start(f32[32,8,256]{2,1,0:T(8,128)S(1)} %get-tuple-element.129) | copy-start | bytes 786436
  8.4 8.1 %copy-start.14 = (f32[2,2]{1,0:T(2,128)S(1)}, f32[2,2]{1,0:T(2,128)}, u32[]{:S(2)}) copy-start(f32[2,2]{1,0:T(2,128)} %param.11) | copy-start | bytes 52
  9.7 10.0 %collective-permute-start.1 = (f32[2,160,1,256]{3,2,1,0:T(1,128)}, f32[2,160,1,256]{3,2,1,0:T(1,128)}, u32[]{:S(2)}, u32[]{:S(2)}) collective-permute-start(f32[2,160,1,256]{3,2,1,0:T(1,128)} %pad_maximum_fusion.25), channel_id=1, source_target_pairs={{0,1},{1,2},{2,3},{3,4},{4,5},{5,6},{6,7},{7,8},{8,9},{9,10},{10,1... | collective-permute-start | bytes 983048 | tf_op jit(solution)/shard_map/ppermute | solution.py:19
  14.6 8.7 %collective-permute-start = (f32[2,160,1,256]{3,2,1,0:T(1,128)}, f32[2,160,1,256]{3,2,1,0:T(1,128)}, u32[]{:S(2)}, u32[]{:S(2)}) collective-permute-start(f32[2,160,1,256]{3,2,1,0:T(1,128)} %pad_maximum_fusion.24), channel_id=1, source_target_pairs={{1,0},{2,1},{3,2},{4,3},{5,4},{6,5},{7,6},{8,7},{9,8},{10,9},{11,1... | collective-permute-start | bytes 983048 | tf_op jit(solution)/shard_map/ppermute | solution.py:20
  26.3 7.5 %collective-permute-start.2 = (f32[2,64,1,256]{3,2,1,0:T(1,128)S(1)}, f32[2,64,1,256]{3,2,1,0:T(1,128)S(1)}, u32[]{:S(2)}, u32[]{:S(2)}) collective-permute-start(f32[2,64,1,256]{3,2,1,0:T(1,128)S(1)} %get-tuple-element.43), channel_id=1, source_target_pairs={{1,0},{2,1},{3,2},{4,3},{5,4},{6,5},{7,6},{8,7},{9,8},{10,9},{11,1... | collective-permute-start | bytes 393224 | tf_op jit(solution)/shard_map/ppermute | solution.py:20
  28.2 6.9 %collective-permute-start.3 = (f32[2,64,1,256]{3,2,1,0:T(1,128)S(1)}, f32[2,64,1,256]{3,2,1,0:T(1,128)S(1)}, u32[]{:S(2)}, u32[]{:S(2)}) collective-permute-start(f32[2,64,1,256]{3,2,1,0:T(1,128)S(1)} %get-tuple-element.44), channel_id=1, source_target_pairs={{0,1},{1,2},{2,3},{3,4},{4,5},{5,6},{6,7},{7,8},{8,9},{9,10},{10,1... | collective-permute-start | bytes 393224 | tf_op jit(solution)/shard_map/ppermute | solution.py:19
  37.4 7.7 %collective-permute-start.5 = (f32[2,64,2,256]{3,2,1,0:T(2,128)S(1)}, f32[2,64,2,256]{3,2,1,0:T(2,128)S(1)}, u32[]{:S(2)}, u32[]{:S(2)}) collective-permute-start(f32[2,64,2,256]{3,2,1,0:T(2,128)S(1)} %get-tuple-element.41), channel_id=1, source_target_pairs={{0,1},{1,2},{2,3},{3,4},{4,5},{5,6},{6,7},{7,8},{8,9},{9,10},{10,1... | collective-permute-start | bytes 786440 | tf_op jit(solution)/shard_map/ppermute | solution.py:19
  41.8 9.0 %collective-permute-start.4 = (f32[2,64,2,256]{3,2,1,0:T(2,128)S(1)}, f32[2,64,2,256]{3,2,1,0:T(2,128)S(1)}, u32[]{:S(2)}, u32[]{:S(2)}) collective-permute-start(f32[2,64,2,256]{3,2,1,0:T(2,128)S(1)} %get-tuple-element.42), channel_id=1, source_target_pairs={{1,0},{2,1},{3,2},{4,3},{5,4},{6,5},{7,6},{8,7},{9,8},{10,9},{11,1... | collective-permute-start | bytes 786440 | tf_op jit(solution)/shard_map/ppermute | solution.py:20
  52.5 1.2 copy-start.9
  52.5 1.2 %copy-start.11 = (f32[32,8,256]{2,1,0:T(8,128)S(1)}, f32[32,8,256]{2,1,0:T(8,128)}, u32[]{:S(2)}) copy-start(f32[32,8,256]{2,1,0:T(8,128)} %copy-done.10) | copy-start | bytes 786436
  52.5 1.4 %copy-start.13 = (f32[2,32,8,256]{3,2,1,0:T(8,128)S(1)}, f32[2,32,8,256]{3,2,1,0:T(8,128)}, u32[]{:S(2)}) copy-start(f32[2,32,8,256]{3,2,1,0:T(8,128)} %copy-done.12) | copy-start | bytes 1572868
  55.9 5.2 %collective-permute-start.7 = (f32[2,32,4,256]{3,2,1,0:T(4,128)S(1)}, f32[2,32,4,256]{3,2,1,0:T(4,128)S(1)}, u32[]{:S(2)}, u32[]{:S(2)}) collective-permute-start(f32[2,32,4,256]{3,2,1,0:T(4,128)S(1)} %pad_maximum_fusion.27), channel_id=1, source_target_pairs={{0,1},{1,2},{2,3},{3,4},{4,5},{5,6},{6,7},{7,8},{8,9},{9,10},{10,1... | collective-permute-start | bytes 786440 | tf_op jit(solution)/shard_map/ppermute | solution.py:19
  58.0 8.5 %collective-permute-start.6 = (f32[2,32,4,256]{3,2,1,0:T(4,128)S(1)}, f32[2,32,4,256]{3,2,1,0:T(4,128)S(1)}, u32[]{:S(2)}, u32[]{:S(2)}) collective-permute-start(f32[2,32,4,256]{3,2,1,0:T(4,128)S(1)} %pad_maximum_fusion.26), channel_id=1, source_target_pairs={{1,0},{2,1},{3,2},{4,3},{5,4},{6,5},{7,6},{8,7},{9,8},{10,9},{11,1... | collective-permute-start | bytes 786440 | tf_op jit(solution)/shard_map/ppermute | solution.py:20
  75.0 4.3 %collective-permute-start.8 = (f32[2,64,1,256]{3,2,1,0:T(1,128)S(1)}, f32[2,64,1,256]{3,2,1,0:T(1,128)S(1)}, u32[]{:S(2)}, u32[]{:S(2)}) collective-permute-start(f32[2,64,1,256]{3,2,1,0:T(1,128)S(1)} %get-tuple-element.39), channel_id=1, source_target_pairs={{0,1},{1,2},{2,3},{3,4},{4,5},{5,6},{6,7},{7,8},{8,9},{9,10},{10,1... | collective-permute-start | bytes 393224 | tf_op jit(solution)/shard_map/ppermute | solution.py:19
  77.0 7.2 %collective-permute-start.9 = (f32[2,64,1,256]{3,2,1,0:T(1,128)S(1)}, f32[2,64,1,256]{3,2,1,0:T(1,128)S(1)}, u32[]{:S(2)}, u32[]{:S(2)}) collective-permute-start(f32[2,64,1,256]{3,2,1,0:T(1,128)S(1)} %get-tuple-element.40), channel_id=1, source_target_pairs={{1,0},{2,1},{3,2},{4,3},{5,4},{6,5},{7,6},{8,7},{9,8},{10,9},{11,1... | collective-permute-start | bytes 393224 | tf_op jit(solution)/shard_map/ppermute | solution.py:20
  87.4 4.6 %collective-permute-start.10 = (f32[2,64,1,256]{3,2,1,0:T(1,128)S(1)}, f32[2,64,1,256]{3,2,1,0:T(1,128)S(1)}, u32[]{:S(2)}, u32[]{:S(2)}) collective-permute-start(f32[2,64,1,256]{3,2,1,0:T(1,128)S(1)} %get-tuple-element.37), channel_id=1, source_target_pairs={{0,1},{1,2},{2,3},{3,4},{4,5},{5,6},{6,7},{7,8},{8,9},{9,10},{10,1... | collective-permute-start | bytes 393224 | tf_op jit(solution)/shard_map/ppermute | solution.py:19
  89.3 7.2 %collective-permute-start.11 = (f32[2,64,1,256]{3,2,1,0:T(1,128)S(1)}, f32[2,64,1,256]{3,2,1,0:T(1,128)S(1)}, u32[]{:S(2)}, u32[]{:S(2)}) collective-permute-start(f32[2,64,1,256]{3,2,1,0:T(1,128)S(1)} %get-tuple-element.38), channel_id=1, source_target_pairs={{1,0},{2,1},{3,2},{4,3},{5,4},{6,5},{7,6},{8,7},{9,8},{10,9},{11,1... | collective-permute-start | bytes 393224 | tf_op jit(solution)/shard_map/ppermute | solution.py:20
  99.3 18.5 %collective-permute-start.12 = (f32[2,32,8,256]{3,2,1,0:T(8,128)S(1)}, f32[2,32,8,256]{3,2,1,0:T(8,128)S(1)}, u32[]{:S(2)}, u32[]{:S(2)}) collective-permute-start(f32[2,32,8,256]{3,2,1,0:T(8,128)S(1)} %get-tuple-element.5), channel_id=1, source_target_pairs={{0,16},{1,17},{2,18},{3,19},{4,20},{5,21},{6,22},{7,23},{8,24},{9,... | collective-permute-start | bytes 1572872 | tf_op jit(solution)/shard_map/ppermute | solution.py:287
  100.6 16.9 %collective-permute-start.13 = (f32[2,32,1,256]{3,2,1,0:T(1,128)S(1)}, f32[2,32,1,256]{3,2,1,0:T(1,128)S(1)}, u32[]{:S(2)}, u32[]{:S(2)}) collective-permute-start(f32[2,32,1,256]{3,2,1,0:T(1,128)S(1)} %get-tuple-element.47), channel_id=1, source_target_pairs={{0,17},{1,18},{2,19},{3,20},{4,21},{5,22},{6,23},{7,24},{8,25},{9,... | collective-permute-start | bytes 196616 | tf_op jit(solution)/shard_map/ppermute | solution.py:288
  101.9 15.6 %collective-permute-start.14 = (f32[2,32,1,256]{3,2,1,0:T(1,128)S(1)}, f32[2,32,1,256]{3,2,1,0:T(1,128)S(1)}, u32[]{:S(2)}, u32[]{:S(2)}) collective-permute-start(f32[2,32,1,256]{3,2,1,0:T(1,128)S(1)} %get-tuple-element.48), channel_id=1, source_target_pairs={{1,16},{2,17},{3,18},{4,19},{5,20},{6,21},{7,22},{8,23},{9,24},{10... | collective-permute-start | bytes 196616 | tf_op jit(solution)/shard_map/ppermute | solution.py:289
  (6 other events, 5.7 us)

commit v12 on v11

--- a/solution.py
+++ b/solution.py
@@ -156,28 +156,58 @@
     coarse_coefs = (coarse_x, coarse_y, coarse_h, coarse_v)
     coarse_levels = coarse_first.shape[-3]
 
-    def coef_edge(edge):
-        stacked = jnp.stack([edge(c) for c in coarse_coefs])
+    fine_coefs = (x_velocity, y_velocity, h_diffusion, v_diffusion)
+
+    def coef_edge(edge, coefs):
+        stacked = jnp.stack([edge(c) for c in coefs])
         return stacked.reshape((2, -1) + stacked.shape[-2:])
 
+    def inner_hi(field):
+        return hi(field, 2)[..., 0:1, :]
+
+    def inner_lo(field):
+        return lo(field, 2)[..., 1:2, :]
+
+    sent = [
+        (hi(initial), lo(initial)),
+        (hi(coarse_first), lo(coarse_first)),
+        (coef_edge(hi, coarse_coefs), coef_edge(lo, coarse_coefs)),
+        (inner_hi(initial), inner_lo(initial)),
+        (coef_edge(hi, fine_coefs), coef_edge(lo, fine_coefs)),
+    ]
     before, after = exchange(
-        joined(joined(hi(initial), hi(coarse_first)), coef_edge(hi)),
-        joined(joined(lo(initial), lo(coarse_first)), coef_edge(lo)),
-    )
-    split = (levels, levels + coarse_levels)
-    init_b, first_b = before[..., : split[0], :, :], before[..., split[0] : split[1], :, :]
-    init_a, first_a = after[..., : split[0], :, :], after[..., split[0] : split[1], :, :]
-    edge_coefs = pack(before[..., split[1] :, :, :], after[..., split[1] :, :, :])
-    edge_coefs = edge_coefs.reshape((4, coarse_levels) + edge_coefs.shape[-2:])
-    halo_zero = pack(init_b, init_a)
-    halo_first = pack(first_b, first_a)
+        jnp.concatenate([pair[0] for pair in sent], axis=-3),
+        jnp.concatenate([pair[1] for pair in sent], axis=-3),
+    )
+    bounds = [0]
+    for pair in sent:
+        bounds.append(bounds[-1] + pair[0].shape[-3])
+
+    def piece(k):
+        return pack(
+            before[..., bounds[k] : bounds[k + 1], :, :],
+            after[..., bounds[k] : bounds[k + 1], :, :],
+        )
+
+    halo_zero = piece(0)
+    halo_first = piece(1)
+    edge_coefs = piece(2).reshape((4, coarse_levels) + halo_first.shape[-2:])
+    fine_edge_coefs = piece(4).reshape((4, levels) + halo_zero.shape[-2:])
+    init_inner = piece(3)
     first_rate = fine_rate(initial, halo_zero)
     coarse_first_rate = coarse_rate(coarse_first, halo_first)
 
     node_zero = initial
     rate_zero = first_rate
     node_one = first_node(node_zero, rate_zero, first_rate, first_rate, first_rate)
-    halo_one = halo_of(node_one)
+    edge_rate = stencil(
+        halo_zero,
+        pack(lo(initial), east(init_inner)),
+        pack(west(init_inner), hi(initial)),
+        *(fine_edge_coefs[k] for k in range(4)),
+        coupling, 1.0, 1.0,
+    )
+    halo_one = first_node(halo_zero, edge_rate, edge_rate, edge_rate, edge_rate)
     rate_one = fine_rate(node_one, halo_one)
     node_two = second_node(node_one, rate_one, first_rate, first_rate, first_rate)
     two_b, two_a = exchange(hi(node_two, 2), lo(node_two, 2))

time: 121 us -> 216 us (1.79)
  local copies, waits for them, and re-layouts: 15.1 us -> 107 us
  other arithmetic: 30.1 us -> 46.5 us
  waiting for transfers between devices: 39.3 us -> 29.2 us
  starting transfers between devices: 35 us -> 29.1 us
    add x9 -> x19, local copies, waits for them, and re-layouts: 0.68 us -> 34.1 us  [add_coarse(): return (paired + jnp.expand_dims(coarse, -3)).reshape(shape)]
    slice x4 -> x20, local copies, waits for them, and re-layouts: 4 us -> 31.5 us  [the longest x14 22.9 us: shrink(): levels = field[..., 0::2, :, :] + field[..., 1::2, :, :]]
    unnamed x30 -> x326, local copies, waits for them, and re-layouts: 5.83 us -> 17.4 us
    ppermute x6 -> x5, waiting for transfers between devices: 22.4 us -> 13.2 us  [exchange(): after = lax.ppermute(to_left, 'space', shift_pairs(count, -1))]
    slice x10, local copies, waits for them, and re-layouts: 0.47 us -> 7.13 us  [pair_sum(): jnp.roll(field, 1, axis=-2)]
    add x10, other arithmetic: 1.69 us -> 7.03 us  [shrink(): levels = field[..., 0::2, :, :] + field[..., 1::2, :, :]]
    ppermute x6 -> x5, starting transfers between devices: 17.5 us -> 13.6 us  [exchange(): before = lax.ppermute(to_right, 'space', shift_pairs(count, 1))]
    another operation x4 -> x8, local copies, waits for them, and re-layouts: 0.17 us -> 3.69 us  [coef_edge(): stacked = jnp.stack([edge(c) for c in coefs])]
  transfers between devices with their start and end apart: 15 -> 13, of which waited for: 9 -> 8; matrix products, arithmetic and copies ran while one was open for 7% -> 9% of each run, Pallas kernels for 0% -> 0%
where the time goes in v12:
time: 216 us; the launch traced here: 214 us
  local copies, waits for them, and re-layouts  107 us (50%)
  other arithmetic  46.5 us (22%)
  waiting for transfers between devices  29.2 us (14%)
  starting transfers between devices  29.1 us (13%)
  between operations  2.23 us (1%)
    add x19, local copies, waits for them, and re-layouts, add_coarse(): return (paired + jnp.expand_dims(coarse, -3)).reshape(shape)  34.1 us
    slice x14, local copies, waits for them, and re-layouts, shrink(): levels = field[..., 0::2, :, :] + field[..., 1::2, :, :]  22.9 us
    unnamed x326, local copies, waits for them, and re-layouts  17.4 us
    ppermute x1, waiting for transfers between devices, body(): passed_b = lax.ppermute(hi(after), ('tm', 'space'), to_east)  14.5 us
    ppermute x5, starting transfers between devices, exchange(): before = lax.ppermute(to_right, 'space', shift_pairs(count, 1))  13.6 us
    ppermute x5, waiting for transfers between devices, exchange(): after = lax.ppermute(to_left, 'space', shift_pairs(count, -1))  13.2 us
    ppermute x5, starting transfers between devices, exchange(): after = lax.ppermute(to_left, 'space', shift_pairs(count, -1))  11.6 us
    slice x10, local copies, waits for them, and re-layouts, pair_sum(): jnp.roll(field, 1, axis=-2)  7.13 us
  transfers between devices with their start and end apart: 13, of which 8 were waited for; matrix products, arithmetic and copies ran while one was open for 9% of the time, Pallas kernels for 0%

profile of v12, /device:TPU:11, one launch (start us, length us, event | category | flops | bytes accessed | tf_op | source)
XLA Modules:
  0.0 214.4 jit_solution(2072362952533484000)
XLA Ops:
  23.9 2.6 %collective-permute-start = (f32[2,352,1,256]{3,1,2,0:T(8,128)}, f32[2,352,1,256]{3,1,2,0:T(8,128)}, u32[]{:S(2)}, u32[]{:S(2)}) collective-permute-start(f32[2,352,1,256]{3,1,2,0:T(8,128)} %constant_dynamic-update-slice_fusion), channel_id=1, source_target_pairs={{1,0},{2,1},{3,2},{4,3},{5,4},{6,5},{7,6},{8,7},{9,8},{10,9},{11,1... | collective-permute-start | bytes 2162696 | tf_op jit(solution)/shard_map/ppermute | solution.py:20
  29.4 3.0 %collective-permute-start.1 = (f32[2,352,1,256]{3,1,2,0:T(8,128)}, f32[2,352,1,256]{3,1,2,0:T(8,128)}, u32[]{:S(2)}, u32[]{:S(2)}) collective-permute-start(f32[2,352,1,256]{3,1,2,0:T(8,128)} %constant_dynamic-update-slice_fusion.3), channel_id=1, source_target_pairs={{0,1},{1,2},{2,3},{3,4},{4,5},{5,6},{6,7},{7,8},{8,9},{9,10},{10,1... | collective-permute-start | bytes 2162696 | tf_op jit(solution)/shard_map/ppermute | solution.py:19
  39.9 3.0 %broadcast_multiply_fusion.1 = (f32[2]{0:T(128)}, f32[2]{0:T(128)S(1)}, f32[2]{0:T(128)}, f32[2]{0:T(128)S(1)}) fusion(f32[]{:T(128)} %bitcast.19, f32[]{:T(128)} %bitcast.18, f32[]{:T(128)} %bitcast.17, f32[]{:T(128)} %bitcast.16), kind=kLoop, calls=%fused_computation.303 | loop fusion | flops 10 | bytes 48 | tf_op jit(solution)/shard_map/mul | solution.py:80
  54.1 4.0 %multiply_add_fusion = (f32[2,64,8,256]{3,1,2,0:T(8,128)S(1)}, f32[2,64,8,256]{3,1,2,0:T(8,128)}) fusion(f32[2,64,8,256]{3,1,2,0:T(8,128)S(1)} %get-tuple-element.33, f32[2,64,8,256]{3,2,1,0:T(8,128)S(1)} %copy-done, f32[2,64,8,256]{3,1,2,0:T(8,128)S(1)} %get-tuple-element.32, f32[2]{0:T(128)S(1)} %get-tuple-element.29, f32[2]{0:T(128)S(1)} %get-tuple-element.154, ...), kind=kLoop, calls=%fused_computation.90 | loop fusion | flops 11010048 | bytes 7602192 | tf_op jit(solution)/shard_map/add | solution.py:145
  62.7 3.6 %collective-permute-start.3 = (f32[2,64,2,256]{3,1,2,0:T(8,128)S(1)}, f32[2,64,2,256]{3,1,2,0:T(8,128)S(1)}, u32[]{:S(2)}, u32[]{:S(2)}) collective-permute-start(f32[2,64,2,256]{3,1,2,0:T(8,128)S(1)} %get-tuple-element.40), channel_id=1, source_target_pairs={{0,1},{1,2},{2,3},{3,4},{4,5},{5,6},{6,7},{7,8},{8,9},{9,10},{10,1... | collective-permute-start | bytes 786440 | tf_op jit(solution)/shard_map/ppermute | solution.py:19
  77.6 3.2 %slice.797 = f32[2,32,8,256]{3,1,2,0:T(8,128)} slice(f32[2,64,8,256]{3,1,2,0:T(8,128)} %fusion.19), slice={[0:2:1], [1:64:2], [0:8:1], [0:256:1]} | slice | bytes 1048576 | tf_op jit(solution)/shard_map/slice | solution.py:93
  80.8 3.2 %slice.796 = f32[2,32,8,256]{3,1,2,0:T(8,128)} slice(f32[2,64,8,256]{3,1,2,0:T(8,128)} %fusion.19), slice={[0:2:1], [0:64:2], [0:8:1], [0:256:1]} | slice | bytes 1048576 | tf_op jit(solution)/shard_map/slice | solution.py:93
  100.4 3.0 %collective-permute-start.5 = (f32[2,32,4,256]{3,1,2,0:T(8,128)S(1)}, f32[2,32,4,256]{3,1,2,0:T(8,128)S(1)}, u32[]{:S(2)}, u32[]{:S(2)}) collective-permute-start(f32[2,32,4,256]{3,1,2,0:T(8,128)S(1)} %pad_maximum_fusion.31), channel_id=1, source_target_pairs={{0,1},{1,2},{2,3},{3,4},{4,5},{5,6},{6,7},{7,8},{8,9},{9,10},{10,1... | collective-permute-start | bytes 786440 | tf_op jit(solution)/shard_map/ppermute | solution.py:19
  106.8 4.4 %collective-permute-done.4 = f32[2,32,4,256]{3,1,2,0:T(8,128)S(1)} collective-permute-done((f32[2,32,4,256]{3,1,2,0:T(8,128)S(1)}, f32[2,32,4,256]{3,1,2,0:T(8,128)S(1)}, u32[]{:S(2)}, u32[]{:S(2)}) %collective-permute-start.4) | collective-permute-done | bytes 262176 | tf_op jit(solution)/shard_map/ppermute | solution.py:20
  126.3 2.8 %add_add_fusion.5 = f32[2,64,2,256]{3,1,2,0:T(8,128)S(1)} fusion(f32[2,64,2,256]{3,1,2,0:T(8,128)} %add.778, f32[2,64,2,256]{3,1,2,0:T(8,128)} %add.774, f32[2,64,2,256]{3,1,2,0:T(8,128)} %add.782, f32[2,64,1,256]{3,1,2,0:T(8,128)} %copy-done.58, f32[2,64,1,256]{3,1,2,0:T(8,128)S(1)} %slice.947, f32[2,64,2,256]{3,1,2,0:T(8,128)} %add.771, pred[]{:T(512)S(6)} %eq.97, ...), kind=kLoop, calls=%fused_computation.213 | loop fusion | flops 3014656 | bytes 3145745 | tf_op jit(solution)/shard_map/add | solution.py:286
  129.9 3.8 %add_multiply_fusion = (f32[2,32,8,256]{3,1,2,0:T(8,128)S(1)}, f32[2,32,8,256]{3,1,2,0:T(8,128)}, f32[2,32,8,256]{3,1,2,0:T(8,128)}, f32[2,32,8,256]{3,1,2,0:T(8,128)}, f32[2,32,8,256]{3,1,2,0:T(8,128)}) fusion(pred[]{:T(512)S(6)} %eq.102, f32[2,32,8,256]{3,1,2,0:T(8,128)S(1)} %copy-done.31, f32[2,32,8,256]{3,1,2,0:T(8,128)S(1)} %copy-done.29, ...), kind=kLoop, calls=%fused_computation.165 | loop fusion | flops 6684672 | bytes 7471196 | tf_op jit(solution)/shard_map/mul | solution.py:262
  135.1 2.9 %add.748 = f32[2,64,8,256]{3,1,2,0:T(8,128)} reshape(f32[2,32,2,8,256]{4,2,1,3,0:T(2,128)} %add.747) | data formatting | bytes 2097152 | tf_op jit(solution)/shard_map/add | solution.py:104
  141.3 2.9 %add.740 = f32[2,64,8,256]{3,1,2,0:T(8,128)} reshape(f32[2,32,2,8,256]{4,2,1,3,0:T(2,128)} %add.739) | data formatting | bytes 2097152 | tf_op jit(solution)/shard_map/add | solution.py:104
  144.2 2.4 %add.742 = f32[2,32,2,8,256]{4,2,1,3,0:T(2,128)} broadcast(f32[2,32,8,256]{3,1,2,0:T(8,128)} %get-tuple-element.19), dimensions={0,1,3,4} | broadcast | bytes 1572864 | tf_op jit(solution)/shard_map/add | solution.py:104
  146.6 3.0 %add.743 = f32[2,64,8,256]{3,1,2,0:T(8,128)} reshape(f32[2,32,2,8,256]{4,2,1,3,0:T(2,128)} %add.742) | data formatting | bytes 2097152 | tf_op jit(solution)/shard_map/add | solution.py:104
  149.6 2.4 %add.751 = f32[2,32,2,8,256]{4,2,1,3,0:T(2,128)} broadcast(f32[2,32,8,256]{3,1,2,0:T(8,128)} %get-tuple-element.20), dimensions={0,1,3,4} | broadcast | bytes 1572864 | tf_op jit(solution)/shard_map/add | solution.py:104
  152.0 2.9 %add.752 = f32[2,64,8,256]{3,1,2,0:T(8,128)} reshape(f32[2,32,2,8,256]{4,2,1,3,0:T(2,128)} %add.751) | data formatting | bytes 2097152 | tf_op jit(solution)/shard_map/add | solution.py:104
  154.9 3.5 %add_add_fusion.2 = (f32[2,64,8,256]{3,1,2,0:T(8,128)S(1)}, f32[2,64,8,256]{3,1,2,0:T(8,128)S(1)}) fusion(f32[2,64,8,256]{3,1,2,0:T(8,128)S(1)} %get-tuple-element.30, f32[2,64,8,256]{3,1,2,0:T(8,128)} %add.752, f32[2,64,8,256]{3,1,2,0:T(8,128)} %add.748, f32[2,64,8,256]{3,1,2,0:T(8,128)} %add.743, f32[2,64,8,256]{3,2,1,0:T(8,128)S(1)} %copy-done, ...), kind=kLoop, calls=%fused_computation.86 | loop fusion | flops 5767168 | bytes 9437185 | tf_op jit(solution)/shard_map/add | solution.py:285
  158.7 2.7 %add_add_fusion.1 = (f32[2,64,8,256]{3,1,2,0:T(8,128)S(1)}, f32[2,64,8,256]{3,1,2,0:T(8,128)S(1)}) fusion(f32[2,64,8,256]{3,1,2,0:T(8,128)S(1)} %get-tuple-element.30, f32[2,64,8,256]{3,1,2,0:T(8,128)S(1)} %copy-done.24, f32[2,64,8,256]{3,1,2,0:T(8,128)S(1)} %copy-done.22, f32[2,64,8,256]{3,1,2,0:T(8,128)S(1)} %copy-done.23, ...), kind=kLoop, calls=%fused_computation.83 | loop fusion | flops 11796480 | bytes 12845072 | tf_op jit(solution)/shard_map/add | solution.py:290
  163.5 2.6 %collective-permute-start.7 = (f32[2,64,1,256]{3,1,2,0:T(8,128)S(1)}, f32[2,64,1,256]{3,1,2,0:T(8,128)S(1)}, u32[]{:S(2)}, u32[]{:S(2)}) collective-permute-start(f32[2,64,1,256]{3,1,2,0:T(8,128)S(1)} %get-tuple-element.38), channel_id=1, source_target_pairs={{1,0},{2,1},{3,2},{4,3},{5,4},{6,5},{7,6},{8,7},{9,8},{10,9},{11,1... | collective-permute-start | bytes 393224 | tf_op jit(solution)/shard_map/ppermute | solution.py:20
  166.2 3.6 %collective-permute-done.7 = f32[2,64,1,256]{3,1,2,0:T(8,128)S(1)} collective-permute-done((f32[2,64,1,256]{3,1,2,0:T(8,128)S(1)}, f32[2,64,1,256]{3,1,2,0:T(8,128)S(1)}, u32[]{:S(2)}, u32[]{:S(2)}) %collective-permute-start.7) | collective-permute-done | bytes 131104 | tf_op jit(solution)/shard_map/ppermute | solution.py:20
  176.1 2.4 %collective-permute-start.9 = (f32[2,64,1,256]{3,1,2,0:T(8,128)}, f32[2,64,1,256]{3,1,2,0:T(8,128)S(1)}, u32[]{:S(2)}, u32[]{:S(2)}) collective-permute-start(f32[2,64,1,256]{3,1,2,0:T(8,128)} %get-tuple-element.37), channel_id=1, source_target_pairs={{1,0},{2,1},{3,2},{4,3},{5,4},{6,5},{7,6},{8,7},{9,8},{10,9},{11,1... | collective-permute-start | bytes 393224 | tf_op jit(solution)/shard_map/ppermute | solution.py:20
  180.5 2.7 %collective-permute-done.9 = f32[2,64,1,256]{3,1,2,0:T(8,128)S(1)} collective-permute-done((f32[2,64,1,256]{3,1,2,0:T(8,128)}, f32[2,64,1,256]{3,1,2,0:T(8,128)S(1)}, u32[]{:S(2)}, u32[]{:S(2)}) %collective-permute-start.9) | collective-permute-done | bytes 131104 | tf_op jit(solution)/shard_map/ppermute | solution.py:20
  195.9 14.5 %collective-permute-done.11 = f32[2,32,1,256]{3,1,2,0:T(8,128)S(1)} collective-permute-done((f32[2,32,1,256]{3,1,2,0:T(8,128)S(1)}, f32[2,32,1,256]{3,1,2,0:T(8,128)S(1)}, u32[]{:S(2)}, u32[]{:S(2)}) %collective-permute-start.11) | collective-permute-done | bytes 65568 | tf_op jit(solution)/shard_map/ppermute | solution.py:318
  (472 shorter events, 126.9 us)
Async XLA Ops:
  0.0 20.0 %copy-start.148 = (s32[8]{0:T(128)}, s32[8]{0:T(128)S(1)}, u32[]{:S(2)}) copy-start(s32[8]{0:T(128)S(1)} %get-tuple-element.148) | copy-start | bytes 100
  11.2 16.8 %copy-start.20 = (f32[2,64,8,256]{3,1,2,0:T(8,128)}, f32[2,64,8,256]{3,1,2,0:T(8,128)S(1)}, u32[]{:S(2)}) copy-start(f32[2,64,8,256]{3,1,2,0:T(8,128)S(1)} %copy.55) | copy-start | bytes 3145732
  23.1 27.3 %copy-start.72 = (f32[2,64,1,256]{3,1,2,0:T(8,128)}, f32[2,64,1,256]{3,1,2,0:T(8,128)S(1)}, u32[]{:S(2)}) copy-start(f32[2,64,1,256]{3,1,2,0:T(8,128)S(1)} %get-tuple-element.42) | copy-start | bytes 393220
  23.9 20.7 %collective-permute-start = (f32[2,352,1,256]{3,1,2,0:T(8,128)}, f32[2,352,1,256]{3,1,2,0:T(8,128)}, u32[]{:S(2)}, u32[]{:S(2)}) collective-permute-start(f32[2,352,1,256]{3,1,2,0:T(8,128)} %constant_dynamic-update-slice_fusion), channel_id=1, source_target_pairs={{1,0},{2,1},{3,2},{4,3},{5,4},{6,5},{7,6},{8,7},{9,8},{10,9},{11,1... | collective-permute-start | bytes 2162696 | tf_op jit(solution)/shard_map/ppermute | solution.py:20
  29.4 16.2 %collective-permute-start.1 = (f32[2,352,1,256]{3,1,2,0:T(8,128)}, f32[2,352,1,256]{3,1,2,0:T(8,128)}, u32[]{:S(2)}, u32[]{:S(2)}) collective-permute-start(f32[2,352,1,256]{3,1,2,0:T(8,128)} %constant_dynamic-update-slice_fusion.3), channel_id=1, source_target_pairs={{0,1},{1,2},{2,3},{3,4},{4,5},{5,6},{6,7},{7,8},{8,9},{9,10},{10,1... | collective-permute-start | bytes 2162696 | tf_op jit(solution)/shard_map/ppermute | solution.py:19
  33.4 17.8 %copy-start.1 = (f32[64,8,256]{2,0,1:T(8,128)}, f32[64,8,256]{2,0,1:T(8,128)S(1)}, u32[]{:S(2)}) copy-start(f32[64,8,256]{2,0,1:T(8,128)S(1)} %copy.46) | copy-start | bytes 1572868
  34.8 16.4 %copy-start.5 = (f32[64,8,256]{2,0,1:T(8,128)}, f32[64,8,256]{2,0,1:T(8,128)S(1)}, u32[]{:S(2)}) copy-start(f32[64,8,256]{2,0,1:T(8,128)S(1)} %copy.32) | copy-start | bytes 1572868
  62.7 10.4 %collective-permute-start.3 = (f32[2,64,2,256]{3,1,2,0:T(8,128)S(1)}, f32[2,64,2,256]{3,1,2,0:T(8,128)S(1)}, u32[]{:S(2)}, u32[]{:S(2)}) collective-permute-start(f32[2,64,2,256]{3,1,2,0:T(8,128)S(1)} %get-tuple-element.40), channel_id=1, source_target_pairs={{0,1},{1,2},{2,3},{3,4},{4,5},{5,6},{6,7},{7,8},{8,9},{9,10},{10,1... | collective-permute-start | bytes 786440 | tf_op jit(solution)/shard_map/ppermute | solution.py:19
  66.3 7.7 %collective-permute-start.2 = (f32[2,64,2,256]{3,1,2,0:T(8,128)S(1)}, f32[2,64,2,256]{3,1,2,0:T(8,128)S(1)}, u32[]{:S(2)}, u32[]{:S(2)}) collective-permute-start(f32[2,64,2,256]{3,1,2,0:T(8,128)S(1)} %get-tuple-element.41), channel_id=1, source_target_pairs={{1,0},{2,1},{3,2},{4,3},{5,4},{6,5},{7,6},{8,7},{9,8},{10,9},{11,1... | collective-permute-start | bytes 786440 | tf_op jit(solution)/shard_map/ppermute | solution.py:20
  100.4 6.3 %collective-permute-start.5 = (f32[2,32,4,256]{3,1,2,0:T(8,128)S(1)}, f32[2,32,4,256]{3,1,2,0:T(8,128)S(1)}, u32[]{:S(2)}, u32[]{:S(2)}) collective-permute-start(f32[2,32,4,256]{3,1,2,0:T(8,128)S(1)} %pad_maximum_fusion.31), channel_id=1, source_target_pairs={{0,1},{1,2},{2,3},{3,4},{4,5},{5,6},{6,7},{7,8},{8,9},{9,10},{10,1... | collective-permute-start | bytes 786440 | tf_op jit(solution)/shard_map/ppermute | solution.py:19
  103.5 7.7 %collective-permute-start.4 = (f32[2,32,4,256]{3,1,2,0:T(8,128)S(1)}, f32[2,32,4,256]{3,1,2,0:T(8,128)S(1)}, u32[]{:S(2)}, u32[]{:S(2)}) collective-permute-start(f32[2,32,4,256]{3,1,2,0:T(8,128)S(1)} %pad_maximum_fusion.30), channel_id=1, source_target_pairs={{1,0},{2,1},{3,2},{4,3},{5,4},{6,5},{7,6},{8,7},{9,8},{10,9},{11,1... | collective-permute-start | bytes 786440 | tf_op jit(solution)/shard_map/ppermute | solution.py:20
  161.5 4.7 %collective-permute-start.6 = (f32[2,64,1,256]{3,1,2,0:T(8,128)S(1)}, f32[2,64,1,256]{3,1,2,0:T(8,128)S(1)}, u32[]{:S(2)}, u32[]{:S(2)}) collective-permute-start(f32[2,64,1,256]{3,1,2,0:T(8,128)S(1)} %get-tuple-element.39), channel_id=1, source_target_pairs={{0,1},{1,2},{2,3},{3,4},{4,5},{5,6},{6,7},{7,8},{8,9},{9,10},{10,1... | collective-permute-start | bytes 393224 | tf_op jit(solution)/shard_map/ppermute | solution.py:19
  163.5 6.3 %collective-permute-start.7 = (f32[2,64,1,256]{3,1,2,0:T(8,128)S(1)}, f32[2,64,1,256]{3,1,2,0:T(8,128)S(1)}, u32[]{:S(2)}, u32[]{:S(2)}) collective-permute-start(f32[2,64,1,256]{3,1,2,0:T(8,128)S(1)} %get-tuple-element.38), channel_id=1, source_target_pairs={{1,0},{2,1},{3,2},{4,3},{5,4},{6,5},{7,6},{8,7},{9,8},{10,9},{11,1... | collective-permute-start | bytes 393224 | tf_op jit(solution)/shard_map/ppermute | solution.py:20
  174.2 6.3 %collective-permute-start.8 = (f32[2,64,1,256]{3,1,2,0:T(8,128)}, f32[2,64,1,256]{3,1,2,0:T(8,128)S(1)}, u32[]{:S(2)}, u32[]{:S(2)}) collective-permute-start(f32[2,64,1,256]{3,1,2,0:T(8,128)} %get-tuple-element.36), channel_id=1, source_target_pairs={{0,1},{1,2},{2,3},{3,4},{4,5},{5,6},{6,7},{7,8},{8,9},{9,10},{10,1... | collective-permute-start | bytes 393224 | tf_op jit(solution)/shard_map/ppermute | solution.py:19
  176.1 7.1 %collective-permute-start.9 = (f32[2,64,1,256]{3,1,2,0:T(8,128)}, f32[2,64,1,256]{3,1,2,0:T(8,128)S(1)}, u32[]{:S(2)}, u32[]{:S(2)}) collective-permute-start(f32[2,64,1,256]{3,1,2,0:T(8,128)} %get-tuple-element.37), channel_id=1, source_target_pairs={{1,0},{2,1},{3,2},{4,3},{5,4},{6,5},{7,6},{8,7},{9,8},{10,9},{11,1... | collective-permute-start | bytes 393224 | tf_op jit(solution)/shard_map/ppermute | solution.py:20
  191.6 19.0 %copy-start.92 = (f32[2,32,1,256]{3,1,2,0:T(8,128)S(1)}, f32[2,32,1,256]{3,1,2,0:T(8,128)}, u32[]{:S(2)}) copy-start(f32[2,32,1,256]{3,1,2,0:T(8,128)} %slice.942) | copy-start | bytes 196612
  191.6 19.0 %copy-start.95 = (f32[2,32,1,256]{3,1,2,0:T(8,128)S(1)}, f32[2,32,1,256]{3,1,2,0:T(8,128)}, u32[]{:S(2)}) copy-start(f32[2,32,1,256]{3,1,2,0:T(8,128)} %slice.943) | copy-start | bytes 196612
  191.9 18.7 %collective-permute-start.10 = (f32[2,32,8,256]{3,1,2,0:T(8,128)S(1)}, f32[2,32,8,256]{3,1,2,0:T(8,128)S(1)}, u32[]{:S(2)}, u32[]{:S(2)}) collective-permute-start(f32[2,32,8,256]{3,1,2,0:T(8,128)S(1)} %get-tuple-element.5), channel_id=1, source_target_pairs={{0,16},{1,17},{2,18},{3,19},{4,20},{5,21},{6,22},{7,23},{8,24},{9,... | collective-permute-start | bytes 1572872 | tf_op jit(solution)/shard_map/ppermute | solution.py:317
  193.2 17.2 %collective-permute-start.11 = (f32[2,32,1,256]{3,1,2,0:T(8,128)S(1)}, f32[2,32,1,256]{3,1,2,0:T(8,128)S(1)}, u32[]{:S(2)}, u32[]{:S(2)}) collective-permute-start(f32[2,32,1,256]{3,1,2,0:T(8,128)S(1)} %get-tuple-element.52), channel_id=1, source_target_pairs={{0,17},{1,18},{2,19},{3,20},{4,21},{5,22},{6,23},{7,24},{8,25},{9,... | collective-permute-start | bytes 196616 | tf_op jit(solution)/shard_map/ppermute | solution.py:318
  194.5 16.1 %collective-permute-start.12 = (f32[2,32,1,256]{3,1,2,0:T(8,128)S(1)}, f32[2,32,1,256]{3,1,2,0:T(8,128)S(1)}, u32[]{:S(2)}, u32[]{:S(2)}) collective-permute-start(f32[2,32,1,256]{3,1,2,0:T(8,128)S(1)} %get-tuple-element.53), channel_id=1, source_target_pairs={{1,16},{2,17},{3,18},{4,19},{5,20},{6,21},{7,22},{8,23},{9,24},{10... | collective-permute-start | bytes 196616 | tf_op jit(solution)/shard_map/ppermute | solution.py:319
  195.9 14.9 %copy-start.43 = (f32[32,8,256]{2,0,1:T(8,128)S(1)}, f32[32,8,256]{2,0,1:T(8,128)}, u32[]{:S(2)}) copy-start(f32[32,8,256]{2,0,1:T(8,128)} %copy.52) | copy-start | bytes 786436
  195.9 14.9 %copy-start.46 = (f32[32,8,256]{2,0,1:T(8,128)S(1)}, f32[32,8,256]{2,0,1:T(8,128)}, u32[]{:S(2)}) copy-start(f32[32,8,256]{2,0,1:T(8,128)} %copy.53) | copy-start | bytes 786436
  195.9 14.9 %copy-start.49 = (f32[32,8,256]{2,0,1:T(8,128)S(1)}, f32[32,8,256]{2,0,1:T(8,128)}, u32[]{:S(2)}) copy-start(f32[32,8,256]{2,0,1:T(8,128)} %copy.51) | copy-start | bytes 786436
  195.9 14.9 %copy-start.52 = (f32[32,8,256]{2,0,1:T(8,128)S(1)}, f32[32,8,256]{2,0,1:T(8,128)}, u32[]{:S(2)}) copy-start(f32[32,8,256]{2,0,1:T(8,128)} %copy.54) | copy-start | bytes 786436
  (144 other events, 564.5 us)

commit v13 on v11

--- a/solution.py
+++ b/solution.py
@@ -180,10 +180,12 @@
     halo_one = halo_of(node_one)
     rate_one = fine_rate(node_one, halo_one)
     node_two = second_node(node_one, rate_one, first_rate, first_rate, first_rate)
-    two_b, two_a = exchange(hi(node_two, 2), lo(node_two, 2))
-    halo_two = pack(hi(two_b), lo(two_a))
     coarse_end = shrink(node_two)
-    halo_end = pack(hi(shrink(two_b)), lo(shrink(two_a)))
+    two_b, two_a = exchange(
+        joined(hi(node_two), hi(coarse_end)), joined(lo(node_two), lo(coarse_end))
+    )
+    halo_two = pack(two_b[..., :levels, :, :], two_a[..., :levels, :, :])
+    halo_end = pack(two_b[..., levels:, :, :], two_a[..., levels:, :, :])
     rate_two = fine_rate(node_two, halo_two)
     source = shrink(slab_step * (rate_zero + 4.0 * rate_one + rate_two) / 6.0)
     offset = source - slab_step * coarse_first_rate

time: 121 us -> 127 us (1.050)
  other arithmetic: 30.1 us -> 35.6 us
  waiting for transfers between devices: 39.3 us -> 35.5 us
  starting transfers between devices: 35 us -> 37 us
  local copies, waits for them, and re-layouts: 15.1 us -> 16.6 us
    ppermute x6, waiting for transfers between devices: 22.4 us -> 17.2 us  [exchange(): after = lax.ppermute(to_left, 'space', shift_pairs(count, -1))]
    add x1, other arithmetic: 1.97 us -> 5.53 us  [second_node(): node_one + half_step * (rate_one - s1)]
    ppermute x6, starting transfers between devices: 13.6 us -> 15.6 us  [exchange(): after = lax.ppermute(to_left, 'space', shift_pairs(count, -1))]
    unnamed x30 -> x52, local copies, waits for them, and re-layouts: 5.83 us -> 7.56 us
    ppermute x6, waiting for transfers between devices: 2.63 us -> 4.12 us  [exchange(): before = lax.ppermute(to_right, 'space', shift_pairs(count, 1))]
where the time goes in v13:
time: 127 us; the launch traced here: 126 us
  starting transfers between devices  37 us (29%)
  other arithmetic  35.6 us (28%)
  waiting for transfers between devices  35.5 us (28%)
  local copies, waits for them, and re-layouts  16.6 us (13%)
    ppermute x6, starting transfers between devices, exchange(): before = lax.ppermute(to_right, 'space', shift_pairs(count, 1))  17.5 us
    ppermute x6, waiting for transfers between devices, exchange(): after = lax.ppermute(to_left, 'space', shift_pairs(count, -1))  17.2 us
    ppermute x6, starting transfers between devices, exchange(): after = lax.ppermute(to_left, 'space', shift_pairs(count, -1))  15.6 us
    ppermute x1, waiting for transfers between devices, body(): passed_b = lax.ppermute(hi(after), ('tm', 'space'), to_east)  14.2 us
    unnamed x52, local copies, waits for them, and re-layouts  7.56 us
    add x1, other arithmetic, second_node(): node_one + half_step * (rate_one - s1)  5.53 us
    ppermute x6, waiting for transfers between devices, exchange(): before = lax.ppermute(to_right, 'space', shift_pairs(count, 1))  4.12 us
    mul x1, other arithmetic, stencil(): reaction = own * middle + other * middle[::-1]  3.29 us
  transfers between devices with their start and end apart: 15, of which 9 were waited for; matrix products, arithmetic and copies ran while one was open for 7% of the time, Pallas kernels for 0%

profile of v13, /device:TPU:11, one launch (start us, length us, event | category | flops | bytes accessed | tf_op | source)
XLA Modules:
  0.0 125.7 jit_solution(15566304237932923714)
XLA Ops:
  8.9 3.7 %collective-permute-start.1 = (f32[2,160,1,256]{3,2,1,0:T(1,128)S(1)}, f32[2,160,1,256]{3,2,1,0:T(1,128)S(1)}, u32[]{:S(2)}, u32[]{:S(2)}) collective-permute-start(f32[2,160,1,256]{3,2,1,0:T(1,128)S(1)} %pad_maximum_fusion.25), channel_id=1, source_target_pairs={{0,1},{1,2},{2,3},{3,4},{4,5},{5,6},{6,7},{7,8},{8,9},{9,10},{10,1... | collective-permute-start | bytes 983048 | tf_op jit(solution)/shard_map/ppermute | solution.py:19
  13.1 1.9 %collective-permute-start = (f32[2,160,1,256]{3,2,1,0:T(1,128)S(1)}, f32[2,160,1,256]{3,2,1,0:T(1,128)S(1)}, u32[]{:S(2)}, u32[]{:S(2)}) collective-permute-start(f32[2,160,1,256]{3,2,1,0:T(1,128)S(1)} %pad_maximum_fusion.24), channel_id=1, source_target_pairs={{1,0},{2,1},{3,2},{4,3},{5,4},{6,5},{7,6},{8,7},{9,8},{10,9},{11,1... | collective-permute-start | bytes 983048 | tf_op jit(solution)/shard_map/ppermute | solution.py:20
  15.7 3.3 %broadcast_multiply_fusion.1 = (f32[2]{0:T(128)}, f32[2]{0:T(128)S(1)}, f32[2]{0:T(128)}, f32[2]{0:T(128)S(1)}) fusion(f32[]{:T(128)} %bitcast.13, f32[]{:T(128)} %bitcast.12, f32[]{:T(128)} %bitcast.11, f32[]{:T(128)} %bitcast.10), kind=kLoop, calls=%fused_computation.207 | loop fusion | flops 10 | bytes 48 | tf_op jit(solution)/shard_map/mul | solution.py:80
  19.8 1.9 %collective-permute-done = f32[2,160,1,256]{3,2,1,0:T(1,128)S(1)} collective-permute-done((f32[2,160,1,256]{3,2,1,0:T(1,128)S(1)}, f32[2,160,1,256]{3,2,1,0:T(1,128)S(1)}, u32[]{:S(2)}, u32[]{:S(2)}) %collective-permute-start) | collective-permute-done | bytes 327712 | tf_op jit(solution)/shard_map/ppermute | solution.py:20
  22.6 1.7 %multiply_add_fusion.1 = (f32[2,64,8,256]{3,2,1,0:T(8,128)S(1)}, f32[2,64,8,256]{3,2,1,0:T(8,128)S(1)}) fusion(f32[2,64,8,256]{3,2,1,0:T(8,128)S(1)} %copy-done, f32[2]{0:T(128)S(1)} %get-tuple-element.29, f32[2]{0:T(128)S(1)} %get-tuple-element.136, f32[64,8,256]{2,1,0:T(8,128)S(1)} %copy-done.3, f32[64,8,256]{2,1,0:T(8,128)S(1)} %copy-done.2, ...), kind=kLoop, calls=%fused_computation.45 | loop fusion | flops 8912896 | bytes 5505040 | tf_op jit(solution)/shard_map/add | solution.py:138
  26.1 1.9 %collective-permute-start.2 = (f32[2,64,1,256]{3,2,1,0:T(1,128)}, f32[2,64,1,256]{3,2,1,0:T(1,128)}, u32[]{:S(2)}, u32[]{:S(2)}) collective-permute-start(f32[2,64,1,256]{3,2,1,0:T(1,128)} %get-tuple-element.42), channel_id=1, source_target_pairs={{1,0},{2,1},{3,2},{4,3},{5,4},{6,5},{7,6},{8,7},{9,8},{10,9},{11,1... | collective-permute-start | bytes 393224 | tf_op jit(solution)/shard_map/ppermute | solution.py:20
  28.0 3.6 %collective-permute-start.3 = (f32[2,64,1,256]{3,2,1,0:T(1,128)}, f32[2,64,1,256]{3,2,1,0:T(1,128)}, u32[]{:S(2)}, u32[]{:S(2)}) collective-permute-start(f32[2,64,1,256]{3,2,1,0:T(1,128)} %get-tuple-element.43), channel_id=1, source_target_pairs={{0,1},{1,2},{2,3},{3,4},{4,5},{5,6},{6,7},{7,8},{8,9},{9,10},{10,1... | collective-permute-start | bytes 393224 | tf_op jit(solution)/shard_map/ppermute | solution.py:19
  35.0 5.5 %multiply_add_fusion = (f32[2,64,8,256]{3,2,1,0:T(8,128)S(1)}, f32[2,64,8,256]{3,2,1,0:T(8,128)S(1)}) fusion(f32[2,64,8,256]{3,2,1,0:T(8,128)S(1)} %get-tuple-element.33, f32[2,64,8,256]{3,2,1,0:T(8,128)S(1)} %copy-done, f32[2,64,8,256]{3,2,1,0:T(8,128)} %copy-done.8, f32[2]{0:T(128)S(1)} %get-tuple-element.29, f32[2]{0:T(128)S(1)} %get-tuple-element.136, ...), kind=kLoop, calls=%fused_computation.41 | loop fusion | flops 11010048 | bytes 7602192 | tf_op jit(solution)/shard_map/add | solution.py:145
  42.0 4.6 %collective-permute-start.4 = (f32[2,96,1,256]{3,2,1,0:T(1,128)S(1)}, f32[2,96,1,256]{3,2,1,0:T(1,128)S(1)}, u32[]{:S(2)}, u32[]{:S(2)}) collective-permute-start(f32[2,96,1,256]{3,2,1,0:T(1,128)S(1)} %pad_maximum_fusion.32), channel_id=1, source_target_pairs={{1,0},{2,1},{3,2},{4,3},{5,4},{6,5},{7,6},{8,7},{9,8},{10,9},{11,1... | collective-permute-start | bytes 589832 | tf_op jit(solution)/shard_map/ppermute | solution.py:20
  46.8 1.9 %collective-permute-start.5 = (f32[2,96,1,256]{3,2,1,0:T(1,128)S(1)}, f32[2,96,1,256]{3,2,1,0:T(1,128)S(1)}, u32[]{:S(2)}, u32[]{:S(2)}) collective-permute-start(f32[2,96,1,256]{3,2,1,0:T(1,128)S(1)} %pad_maximum_fusion.33), channel_id=1, source_target_pairs={{0,1},{1,2},{2,3},{3,4},{4,5},{5,6},{6,7},{7,8},{8,9},{9,10},{10,1... | collective-permute-start | bytes 589832 | tf_op jit(solution)/shard_map/ppermute | solution.py:19
  49.8 2.8 %collective-permute-done.5 = f32[2,96,1,256]{3,2,1,0:T(1,128)S(1)} collective-permute-done((f32[2,96,1,256]{3,2,1,0:T(1,128)S(1)}, f32[2,96,1,256]{3,2,1,0:T(1,128)S(1)}, u32[]{:S(2)}, u32[]{:S(2)}) %collective-permute-start.5) | collective-permute-done | bytes 196640 | tf_op jit(solution)/shard_map/ppermute | solution.py:19
  57.2 4.4 %collective-permute-start.7 = (f32[2,32,4,256]{3,2,1,0:T(4,128)S(1)}, f32[2,32,4,256]{3,2,1,0:T(4,128)S(1)}, u32[]{:S(2)}, u32[]{:S(2)}) collective-permute-start(f32[2,32,4,256]{3,2,1,0:T(4,128)S(1)} %pad_maximum_fusion.27), channel_id=1, source_target_pairs={{0,1},{1,2},{2,3},{3,4},{4,5},{5,6},{6,7},{7,8},{8,9},{9,10},{10,1... | collective-permute-start | bytes 786440 | tf_op jit(solution)/shard_map/ppermute | solution.py:19
  61.7 2.1 %collective-permute-start.6 = (f32[2,32,4,256]{3,2,1,0:T(4,128)S(1)}, f32[2,32,4,256]{3,2,1,0:T(4,128)S(1)}, u32[]{:S(2)}, u32[]{:S(2)}) collective-permute-start(f32[2,32,4,256]{3,2,1,0:T(4,128)S(1)} %pad_maximum_fusion.26), channel_id=1, source_target_pairs={{1,0},{2,1},{3,2},{4,3},{5,4},{6,5},{7,6},{8,7},{9,8},{10,9},{11,1... | collective-permute-start | bytes 786440 | tf_op jit(solution)/shard_map/ppermute | solution.py:20
  65.0 5.1 %collective-permute-done.6 = f32[2,32,4,256]{3,2,1,0:T(4,128)S(1)} collective-permute-done((f32[2,32,4,256]{3,2,1,0:T(4,128)S(1)}, f32[2,32,4,256]{3,2,1,0:T(4,128)S(1)}, u32[]{:S(2)}, u32[]{:S(2)}) %collective-permute-start.6) | collective-permute-done | bytes 262176 | tf_op jit(solution)/shard_map/ppermute | solution.py:20
  72.4 2.0 %add_add_fusion.9 = (f32[2,64,2,256]{3,2,1,0:T(2,128)S(1)}, f32[2,64,2,256]{3,2,1,0:T(2,128)S(1)}) fusion(f32[2,64,2,256]{3,2,1,0:T(2,128)S(1)} %bitcast.54, f32[2,64,1,256]{3,2,1,0:T(1,128)S(1)} %copy-done.18, f32[2,64,1,256]{3,2,1,0:T(1,128)S(1)} %get-tuple-element.79, f32[2,64,2,256]{3,2,1,0:T(2,128)S(1)} %bitcast.52, f32[2,64,1,256]{3,2,1,0:T(1,128)S(1)} %slice.808, ...), kind=kLoop, calls=%fused_computation.157 | loop fusion | flops 983040 | bytes 2359297 | tf_op jit(solution)/shard_map/add | solution.py:258
  77.2 2.1 %add_add_fusion.2 = (f32[2,64,8,256]{3,2,1,0:T(8,128)S(1)}, f32[2,64,8,256]{3,2,1,0:T(8,128)S(1)}) fusion(f32[2,64,8,256]{3,2,1,0:T(8,128)S(1)} %get-tuple-element.30, f32[2,64,8,256]{3,2,1,0:T(8,128)S(1)} %bitcast.47, f32[2,64,8,256]{3,2,1,0:T(8,128)S(1)} %bitcast.43, f32[2,64,8,256]{3,2,1,0:T(8,128)S(1)} %copy-done, f32[2,64,8,256]{3,2,1,0:T(8,128)S(1)} %bitcast.45, ...), kind=kLoop, calls=%fused_computation.32 | loop fusion | flops 11796480 | bytes 12845072 | tf_op jit(solution)/shard_map/add | solution.py:262
  79.5 1.9 %collective-permute-start.8 = (f32[2,64,1,256]{3,2,1,0:T(1,128)S(1)}, f32[2,64,1,256]{3,2,1,0:T(1,128)S(1)}, u32[]{:S(2)}, u32[]{:S(2)}) collective-permute-start(f32[2,64,1,256]{3,2,1,0:T(1,128)S(1)} %get-tuple-element.38), channel_id=1, source_target_pairs={{0,1},{1,2},{2,3},{3,4},{4,5},{5,6},{6,7},{7,8},{8,9},{9,10},{10,1... | collective-permute-start | bytes 393224 | tf_op jit(solution)/shard_map/ppermute | solution.py:19
  81.4 2.4 %collective-permute-start.9 = (f32[2,64,1,256]{3,2,1,0:T(1,128)S(1)}, f32[2,64,1,256]{3,2,1,0:T(1,128)S(1)}, u32[]{:S(2)}, u32[]{:S(2)}) collective-permute-start(f32[2,64,1,256]{3,2,1,0:T(1,128)S(1)} %get-tuple-element.39), channel_id=1, source_target_pairs={{1,0},{2,1},{3,2},{4,3},{5,4},{6,5},{7,6},{8,7},{9,8},{10,9},{11,1... | collective-permute-start | bytes 393224 | tf_op jit(solution)/shard_map/ppermute | solution.py:20
  83.9 4.8 %collective-permute-done.9 = f32[2,64,1,256]{3,2,1,0:T(1,128)S(1)} collective-permute-done((f32[2,64,1,256]{3,2,1,0:T(1,128)S(1)}, f32[2,64,1,256]{3,2,1,0:T(1,128)S(1)}, u32[]{:S(2)}, u32[]{:S(2)}) %collective-permute-start.9) | collective-permute-done | bytes 131104 | tf_op jit(solution)/shard_map/ppermute | solution.py:20
  88.7 2.1 %add_add_fusion.8 = f32[2,64,2,256]{3,2,1,0:T(2,128)S(1)} fusion(f32[2,64,1,256]{3,2,1,0:T(1,128)S(1)} %collective-permute-done.9, f32[2,64,1,256]{3,2,1,0:T(1,128)S(1)} %collective-permute-done.8, f32[2,64,2,256]{3,2,1,0:T(2,128)S(1)} %bitcast.55, f32[2,64,1,256]{3,2,1,0:T(1,128)S(1)} %copy-done.18, f32[2,64,1,256]{3,2,1,0:T(1,128)S(1)} %get-tuple-element.79, ...), kind=kLoop, calls=%fused_computation.156 | loop fusion | flops 917504 | bytes 2097152 | tf_op jit(solution)/shard_map/add | solution.py:263
  92.8 1.9 %collective-permute-start.10 = (f32[2,64,1,256]{3,2,1,0:T(1,128)S(1)}, f32[2,64,1,256]{3,2,1,0:T(1,128)S(1)}, u32[]{:S(2)}, u32[]{:S(2)}) collective-permute-start(f32[2,64,1,256]{3,2,1,0:T(1,128)S(1)} %get-tuple-element.36), channel_id=1, source_target_pairs={{0,1},{1,2},{2,3},{3,4},{4,5},{5,6},{6,7},{7,8},{8,9},{9,10},{10,1... | collective-permute-start | bytes 393224 | tf_op jit(solution)/shard_map/ppermute | solution.py:19
  94.8 2.6 %collective-permute-start.11 = (f32[2,64,1,256]{3,2,1,0:T(1,128)S(1)}, f32[2,64,1,256]{3,2,1,0:T(1,128)S(1)}, u32[]{:S(2)}, u32[]{:S(2)}) collective-permute-start(f32[2,64,1,256]{3,2,1,0:T(1,128)S(1)} %get-tuple-element.37), channel_id=1, source_target_pairs={{1,0},{2,1},{3,2},{4,3},{5,4},{6,5},{7,6},{8,7},{9,8},{10,9},{11,1... | collective-permute-start | bytes 393224 | tf_op jit(solution)/shard_map/ppermute | solution.py:20
  97.5 4.5 %collective-permute-done.11 = f32[2,64,1,256]{3,2,1,0:T(1,128)S(1)} collective-permute-done((f32[2,64,1,256]{3,2,1,0:T(1,128)S(1)}, f32[2,64,1,256]{3,2,1,0:T(1,128)S(1)}, u32[]{:S(2)}, u32[]{:S(2)}) %collective-permute-start.11) | collective-permute-done | bytes 131104 | tf_op jit(solution)/shard_map/ppermute | solution.py:20
  108.7 14.2 %collective-permute-done.13 = f32[2,32,1,256]{3,2,1,0:T(1,128)S(1)} collective-permute-done((f32[2,32,1,256]{3,2,1,0:T(1,128)S(1)}, f32[2,32,1,256]{3,2,1,0:T(1,128)S(1)}, u32[]{:S(2)}, u32[]{:S(2)}) %collective-permute-start.13) | collective-permute-done | bytes 65568 | tf_op jit(solution)/shard_map/ppermute | solution.py:290
  (161 shorter events, 41.6 us)
Async XLA Ops:
  0.0 7.9 %copy-start.21 = (s32[8]{0:T(128)}, s32[8]{0:T(128)S(1)}, u32[]{:S(2)}) copy-start(s32[8]{0:T(128)S(1)} %get-tuple-element.132) | copy-start | bytes 100
  8.3 4.7 %copy-start.9 = (f32[32,8,256]{2,1,0:T(8,128)}, f32[32,8,256]{2,1,0:T(8,128)S(1)}, u32[]{:S(2)}) copy-start(f32[32,8,256]{2,1,0:T(8,128)S(1)} %get-tuple-element.125) | copy-start | bytes 786436
  8.3 4.7 %copy-start.11 = (f32[32,8,256]{2,1,0:T(8,128)}, f32[32,8,256]{2,1,0:T(8,128)S(1)}, u32[]{:S(2)}) copy-start(f32[32,8,256]{2,1,0:T(8,128)S(1)} %get-tuple-element.126) | copy-start | bytes 786436
  8.4 6.6 %copy-start.23 = (f32[2,2]{1,0:T(2,128)S(1)}, f32[2,2]{1,0:T(2,128)}, u32[]{:S(2)}) copy-start(f32[2,2]{1,0:T(2,128)} %param.11) | copy-start | bytes 52
  8.9 10.1 %collective-permute-start.1 = (f32[2,160,1,256]{3,2,1,0:T(1,128)S(1)}, f32[2,160,1,256]{3,2,1,0:T(1,128)S(1)}, u32[]{:S(2)}, u32[]{:S(2)}) collective-permute-start(f32[2,160,1,256]{3,2,1,0:T(1,128)S(1)} %pad_maximum_fusion.25), channel_id=1, source_target_pairs={{0,1},{1,2},{2,3},{3,4},{4,5},{5,6},{6,7},{7,8},{8,9},{9,10},{10,1... | collective-permute-start | bytes 983048 | tf_op jit(solution)/shard_map/ppermute | solution.py:19
  13.1 8.6 %collective-permute-start = (f32[2,160,1,256]{3,2,1,0:T(1,128)S(1)}, f32[2,160,1,256]{3,2,1,0:T(1,128)S(1)}, u32[]{:S(2)}, u32[]{:S(2)}) collective-permute-start(f32[2,160,1,256]{3,2,1,0:T(1,128)S(1)} %pad_maximum_fusion.24), channel_id=1, source_target_pairs={{1,0},{2,1},{3,2},{4,3},{5,4},{6,5},{7,6},{8,7},{9,8},{10,9},{11,1... | collective-permute-start | bytes 983048 | tf_op jit(solution)/shard_map/ppermute | solution.py:20
  19.0 3.6 %copy-start.19 = (f32[2,160,1,256]{3,2,1,0:T(1,128)}, f32[2,160,1,256]{3,2,1,0:T(1,128)S(1)}, u32[]{:S(2)}) copy-start(f32[2,160,1,256]{3,2,1,0:T(1,128)S(1)} %collective-permute-done.1) | copy-start | bytes 983044
  22.6 1.7 %copy-start.17 = (f32[2,64,1,256]{3,2,1,0:T(1,128)}, f32[2,64,1,256]{3,2,1,0:T(1,128)S(1)}, u32[]{:S(2)}) copy-start(f32[2,64,1,256]{3,2,1,0:T(1,128)S(1)} %get-tuple-element.81) | copy-start | bytes 393220
  26.1 8.6 %collective-permute-start.2 = (f32[2,64,1,256]{3,2,1,0:T(1,128)}, f32[2,64,1,256]{3,2,1,0:T(1,128)}, u32[]{:S(2)}, u32[]{:S(2)}) collective-permute-start(f32[2,64,1,256]{3,2,1,0:T(1,128)} %get-tuple-element.42), channel_id=1, source_target_pairs={{1,0},{2,1},{3,2},{4,3},{5,4},{6,5},{7,6},{8,7},{9,8},{10,9},{11,1... | collective-permute-start | bytes 393224 | tf_op jit(solution)/shard_map/ppermute | solution.py:20
  28.0 7.0 %collective-permute-start.3 = (f32[2,64,1,256]{3,2,1,0:T(1,128)}, f32[2,64,1,256]{3,2,1,0:T(1,128)}, u32[]{:S(2)}, u32[]{:S(2)}) collective-permute-start(f32[2,64,1,256]{3,2,1,0:T(1,128)} %get-tuple-element.43), channel_id=1, source_target_pairs={{0,1},{1,2},{2,3},{3,4},{4,5},{5,6},{6,7},{7,8},{8,9},{9,10},{10,1... | collective-permute-start | bytes 393224 | tf_op jit(solution)/shard_map/ppermute | solution.py:19
  31.7 3.3 %copy-start.4 = (f32[64,8,256]{2,1,0:T(8,128)S(1)}, f32[64,8,256]{2,1,0:T(8,128)}, u32[]{:S(2)}) copy-start(f32[64,8,256]{2,1,0:T(8,128)} %param.8) | copy-start | bytes 1572868
  41.8 10.9 %copy-start.6 = (f32[64,8,256]{2,1,0:T(8,128)S(1)}, f32[64,8,256]{2,1,0:T(8,128)}, u32[]{:S(2)}) copy-start(f32[64,8,256]{2,1,0:T(8,128)} %param.9) | copy-start | bytes 1572868
  42.0 7.7 %collective-permute-start.4 = (f32[2,96,1,256]{3,2,1,0:T(1,128)S(1)}, f32[2,96,1,256]{3,2,1,0:T(1,128)S(1)}, u32[]{:S(2)}, u32[]{:S(2)}) collective-permute-start(f32[2,96,1,256]{3,2,1,0:T(1,128)S(1)} %pad_maximum_fusion.32), channel_id=1, source_target_pairs={{1,0},{2,1},{3,2},{4,3},{5,4},{6,5},{7,6},{8,7},{9,8},{10,9},{11,1... | collective-permute-start | bytes 589832 | tf_op jit(solution)/shard_map/ppermute | solution.py:20
  46.8 5.8 %collective-permute-start.5 = (f32[2,96,1,256]{3,2,1,0:T(1,128)S(1)}, f32[2,96,1,256]{3,2,1,0:T(1,128)S(1)}, u32[]{:S(2)}, u32[]{:S(2)}) collective-permute-start(f32[2,96,1,256]{3,2,1,0:T(1,128)S(1)} %pad_maximum_fusion.33), channel_id=1, source_target_pairs={{0,1},{1,2},{2,3},{3,4},{4,5},{5,6},{6,7},{7,8},{8,9},{9,10},{10,1... | collective-permute-start | bytes 589832 | tf_op jit(solution)/shard_map/ppermute | solution.py:19
  54.2 1.4 %copy-start.16 = (f32[2,32,8,256]{3,2,1,0:T(8,128)S(1)}, f32[2,32,8,256]{3,2,1,0:T(8,128)}, u32[]{:S(2)}) copy-start(f32[2,32,8,256]{3,2,1,0:T(8,128)} %copy-done.15) | copy-start | bytes 1572868
  57.2 7.7 %collective-permute-start.7 = (f32[2,32,4,256]{3,2,1,0:T(4,128)S(1)}, f32[2,32,4,256]{3,2,1,0:T(4,128)S(1)}, u32[]{:S(2)}, u32[]{:S(2)}) collective-permute-start(f32[2,32,4,256]{3,2,1,0:T(4,128)S(1)} %pad_maximum_fusion.27), channel_id=1, source_target_pairs={{0,1},{1,2},{2,3},{3,4},{4,5},{5,6},{6,7},{7,8},{8,9},{9,10},{10,1... | collective-permute-start | bytes 786440 | tf_op jit(solution)/shard_map/ppermute | solution.py:19
  61.7 8.4 %collective-permute-start.6 = (f32[2,32,4,256]{3,2,1,0:T(4,128)S(1)}, f32[2,32,4,256]{3,2,1,0:T(4,128)S(1)}, u32[]{:S(2)}, u32[]{:S(2)}) collective-permute-start(f32[2,32,4,256]{3,2,1,0:T(4,128)S(1)} %pad_maximum_fusion.26), channel_id=1, source_target_pairs={{1,0},{2,1},{3,2},{4,3},{5,4},{6,5},{7,6},{8,7},{9,8},{10,9},{11,1... | collective-permute-start | bytes 786440 | tf_op jit(solution)/shard_map/ppermute | solution.py:20
  79.5 4.3 %collective-permute-start.8 = (f32[2,64,1,256]{3,2,1,0:T(1,128)S(1)}, f32[2,64,1,256]{3,2,1,0:T(1,128)S(1)}, u32[]{:S(2)}, u32[]{:S(2)}) collective-permute-start(f32[2,64,1,256]{3,2,1,0:T(1,128)S(1)} %get-tuple-element.38), channel_id=1, source_target_pairs={{0,1},{1,2},{2,3},{3,4},{4,5},{5,6},{6,7},{7,8},{8,9},{9,10},{10,1... | collective-permute-start | bytes 393224 | tf_op jit(solution)/shard_map/ppermute | solution.py:19
  81.4 7.2 %collective-permute-start.9 = (f32[2,64,1,256]{3,2,1,0:T(1,128)S(1)}, f32[2,64,1,256]{3,2,1,0:T(1,128)S(1)}, u32[]{:S(2)}, u32[]{:S(2)}) collective-permute-start(f32[2,64,1,256]{3,2,1,0:T(1,128)S(1)} %get-tuple-element.39), channel_id=1, source_target_pairs={{1,0},{2,1},{3,2},{4,3},{5,4},{6,5},{7,6},{8,7},{9,8},{10,9},{11,1... | collective-permute-start | bytes 393224 | tf_op jit(solution)/shard_map/ppermute | solution.py:20
  92.8 4.6 %collective-permute-start.10 = (f32[2,64,1,256]{3,2,1,0:T(1,128)S(1)}, f32[2,64,1,256]{3,2,1,0:T(1,128)S(1)}, u32[]{:S(2)}, u32[]{:S(2)}) collective-permute-start(f32[2,64,1,256]{3,2,1,0:T(1,128)S(1)} %get-tuple-element.36), channel_id=1, source_target_pairs={{0,1},{1,2},{2,3},{3,4},{4,5},{5,6},{6,7},{7,8},{8,9},{9,10},{10,1... | collective-permute-start | bytes 393224 | tf_op jit(solution)/shard_map/ppermute | solution.py:19
  94.8 7.2 %collective-permute-start.11 = (f32[2,64,1,256]{3,2,1,0:T(1,128)S(1)}, f32[2,64,1,256]{3,2,1,0:T(1,128)S(1)}, u32[]{:S(2)}, u32[]{:S(2)}) collective-permute-start(f32[2,64,1,256]{3,2,1,0:T(1,128)S(1)} %get-tuple-element.37), channel_id=1, source_target_pairs={{1,0},{2,1},{3,2},{4,3},{5,4},{6,5},{7,6},{8,7},{9,8},{10,9},{11,1... | collective-permute-start | bytes 393224 | tf_op jit(solution)/shard_map/ppermute | solution.py:20
  104.7 18.5 %collective-permute-start.12 = (f32[2,32,8,256]{3,2,1,0:T(8,128)S(1)}, f32[2,32,8,256]{3,2,1,0:T(8,128)S(1)}, u32[]{:S(2)}, u32[]{:S(2)}) collective-permute-start(f32[2,32,8,256]{3,2,1,0:T(8,128)S(1)} %get-tuple-element.5), channel_id=1, source_target_pairs={{0,16},{1,17},{2,18},{3,19},{4,20},{5,21},{6,22},{7,23},{8,24},{9,... | collective-permute-start | bytes 1572872 | tf_op jit(solution)/shard_map/ppermute | solution.py:289
  106.0 16.9 %collective-permute-start.13 = (f32[2,32,1,256]{3,2,1,0:T(1,128)S(1)}, f32[2,32,1,256]{3,2,1,0:T(1,128)S(1)}, u32[]{:S(2)}, u32[]{:S(2)}) collective-permute-start(f32[2,32,1,256]{3,2,1,0:T(1,128)S(1)} %get-tuple-element.46), channel_id=1, source_target_pairs={{0,17},{1,18},{2,19},{3,20},{4,21},{5,22},{6,23},{7,24},{8,25},{9,... | collective-permute-start | bytes 196616 | tf_op jit(solution)/shard_map/ppermute | solution.py:290
  107.3 15.6 %collective-permute-start.14 = (f32[2,32,1,256]{3,2,1,0:T(1,128)S(1)}, f32[2,32,1,256]{3,2,1,0:T(1,128)S(1)}, u32[]{:S(2)}, u32[]{:S(2)}) collective-permute-start(f32[2,32,1,256]{3,2,1,0:T(1,128)S(1)} %get-tuple-element.47), channel_id=1, source_target_pairs={{1,16},{2,17},{3,18},{4,19},{5,20},{6,21},{7,22},{8,23},{9,24},{10... | collective-permute-start | bytes 196616 | tf_op jit(solution)/shard_map/ppermute | solution.py:291
  (17 other events, 17.9 us)

commit v14 on v11

--- a/solution.py
+++ b/solution.py
@@ -284,7 +284,8 @@
     rate = coarse_first_rate
     for count in range(slabs - 1):
         after = carried + slab_step * rate + offset
-        passed = lax.ppermute(after, "tm", down)
+        rows = after.reshape(after.shape[:-2] + (after.shape[-2] // 2, 2, after.shape[-1]))
+        passed = jnp.repeat(lax.ppermute(rows[..., 0, :], "tm", down), 2, axis=-2)
         passed_b = lax.ppermute(hi(after), ("tm", "space"), to_east)
         passed_a = lax.ppermute(lo(after), ("tm", "space"), to_west)
         carried = jnp.where(first, coarse_first, passed)

time: 121 us -> 121 us (level)
  the two profiles are of different devices: /device:TPU:11 before, /device:TPU:6 now
where the time goes in v14:
time: 121 us
  starting transfers between devices  43 us (36%)
  other arithmetic  33.1 us (27%)
  waiting for transfers between devices  25.2 us (21%)
  local copies, waits for them, and re-layouts  18.2 us (15%)
    ppermute x6, starting transfers between devices, exchange(): before = lax.ppermute(to_right, 'space', shift_pairs(count, 1))  21.9 us
    ppermute x6, starting transfers between devices, exchange(): after = lax.ppermute(to_left, 'space', shift_pairs(count, -1))  17.3 us
    ppermute x6, waiting for transfers between devices, exchange(): after = lax.ppermute(to_left, 'space', shift_pairs(count, -1))  9.09 us
    ppermute x1, waiting for transfers between devices, body(): passed = jnp.repeat(lax.ppermute(rows[..., 0, :], 'tm', down), 2, axis=-2)  6.18 us
    unnamed x47, local copies, waits for them, and re-layouts  6.11 us
    ppermute x6, waiting for transfers between devices, exchange(): before = lax.ppermute(to_right, 'space', shift_pairs(count, 1))  4.99 us
    ppermute x1, waiting for transfers between devices, body(): passed_a = lax.ppermute(lo(after), ('tm', 'space'), to_west)  2.97 us
    mul x1, other arithmetic, stencil(): reaction = own * middle + other * middle[::-1]  2.49 us
  transfers between devices with their start and end apart: 15, of which 10 were waited for; matrix products, arithmetic and copies ran while one was open for 9% of the time, Pallas kernels for 0%

profile of v14, /device:TPU:6, one launch (start us, length us, event | category | flops | bytes accessed | tf_op | source)
XLA Modules:
  0.0 120.5 jit_solution(1375954331208511977)
XLA Ops:
  9.7 1.9 %collective-permute-start.1 = (f32[2,160,1,256]{3,2,1,0:T(1,128)}, f32[2,160,1,256]{3,2,1,0:T(1,128)}, u32[]{:S(2)}, u32[]{:S(2)}) collective-permute-start(f32[2,160,1,256]{3,2,1,0:T(1,128)} %pad_maximum_fusion.25), channel_id=1, source_target_pairs={{0,1},{1,2},{2,3},{3,4},{4,5},{5,6},{6,7},{7,8},{8,9},{9,10},{10,1... | collective-permute-start | bytes 983048 | tf_op jit(solution)/shard_map/ppermute | solution.py:19
  12.8 3.6 %collective-permute-start = (f32[2,160,1,256]{3,2,1,0:T(1,128)}, f32[2,160,1,256]{3,2,1,0:T(1,128)}, u32[]{:S(2)}, u32[]{:S(2)}) collective-permute-start(f32[2,160,1,256]{3,2,1,0:T(1,128)} %pad_maximum_fusion.24), channel_id=1, source_target_pairs={{1,0},{2,1},{3,2},{4,3},{5,4},{6,5},{7,6},{8,7},{9,8},{10,9},{11,1... | collective-permute-start | bytes 983048 | tf_op jit(solution)/shard_map/ppermute | solution.py:20
  17.1 2.5 %broadcast_multiply_fusion.1 = (f32[2]{0:T(128)S(1)}, f32[2]{0:T(128)S(1)}, f32[2]{0:T(128)S(1)}, f32[2]{0:T(128)S(1)}) fusion(f32[]{:T(128)} %bitcast.13, f32[]{:T(128)} %bitcast.12, f32[]{:T(128)} %bitcast.11, f32[]{:T(128)} %bitcast.10), kind=kLoop, calls=%fused_computation.214 | loop fusion | flops 10 | bytes 48 | tf_op jit(solution)/shard_map/mul | solution.py:80
  22.5 1.7 %multiply_add_fusion.1 = (f32[2,64,8,256]{3,2,1,0:T(8,128)S(1)}, f32[2,64,8,256]{3,2,1,0:T(8,128)S(1)}) fusion(f32[2,64,8,256]{3,2,1,0:T(8,128)S(1)} %copy-done, f32[2]{0:T(128)S(1)} %get-tuple-element.30, f32[2]{0:T(128)S(1)} %get-tuple-element.139, f32[64,8,256]{2,1,0:T(8,128)S(1)} %copy-done.3, f32[64,8,256]{2,1,0:T(8,128)S(1)} %copy-done.2, ...), kind=kLoop, calls=%fused_computation.45 | loop fusion | flops 8912896 | bytes 5505040 | tf_op jit(solution)/shard_map/add | solution.py:138
  24.4 3.8 %collective-permute-start.2 = (f32[2,64,1,256]{3,2,1,0:T(1,128)S(1)}, f32[2,64,1,256]{3,2,1,0:T(1,128)S(1)}, u32[]{:S(2)}, u32[]{:S(2)}) collective-permute-start(f32[2,64,1,256]{3,2,1,0:T(1,128)S(1)} %get-tuple-element.43), channel_id=1, source_target_pairs={{1,0},{2,1},{3,2},{4,3},{5,4},{6,5},{7,6},{8,7},{9,8},{10,9},{11,1... | collective-permute-start | bytes 393224 | tf_op jit(solution)/shard_map/ppermute | solution.py:20
  28.2 2.7 %collective-permute-start.3 = (f32[2,64,1,256]{3,2,1,0:T(1,128)S(1)}, f32[2,64,1,256]{3,2,1,0:T(1,128)S(1)}, u32[]{:S(2)}, u32[]{:S(2)}) collective-permute-start(f32[2,64,1,256]{3,2,1,0:T(1,128)S(1)} %get-tuple-element.44), channel_id=1, source_target_pairs={{0,1},{1,2},{2,3},{3,4},{4,5},{5,6},{6,7},{7,8},{8,9},{9,10},{10,1... | collective-permute-start | bytes 393224 | tf_op jit(solution)/shard_map/ppermute | solution.py:19
  32.9 2.9 %collective-permute-done.3 = f32[2,64,1,256]{3,2,1,0:T(1,128)S(1)} collective-permute-done((f32[2,64,1,256]{3,2,1,0:T(1,128)S(1)}, f32[2,64,1,256]{3,2,1,0:T(1,128)S(1)}, u32[]{:S(2)}, u32[]{:S(2)}) %collective-permute-start.3) | collective-permute-done | bytes 131104 | tf_op jit(solution)/shard_map/ppermute | solution.py:19
  35.8 2.0 %multiply_add_fusion = (f32[2,64,8,256]{3,2,1,0:T(8,128)S(1)}, f32[2,64,8,256]{3,2,1,0:T(8,128)S(1)}) fusion(f32[2,64,8,256]{3,2,1,0:T(8,128)S(1)} %get-tuple-element.34, f32[2,64,8,256]{3,2,1,0:T(8,128)S(1)} %copy-done, f32[2,64,8,256]{3,2,1,0:T(8,128)S(1)} %get-tuple-element.33, f32[2]{0:T(128)S(1)} %get-tuple-element.30, f32[2]{0:T(128)S(1)} %get-tuple-element.139, ...), kind=kLoop, calls=%fused_computation.41 | loop fusion | flops 11010048 | bytes 7602192 | tf_op jit(solution)/shard_map/add | solution.py:145
  38.1 1.9 %collective-permute-start.5 = (f32[2,64,2,256]{3,2,1,0:T(2,128)S(1)}, f32[2,64,2,256]{3,2,1,0:T(2,128)S(1)}, u32[]{:S(2)}, u32[]{:S(2)}) collective-permute-start(f32[2,64,2,256]{3,2,1,0:T(2,128)S(1)} %get-tuple-element.41), channel_id=1, source_target_pairs={{0,1},{1,2},{2,3},{3,4},{4,5},{5,6},{6,7},{7,8},{8,9},{9,10},{10,1... | collective-permute-start | bytes 786440 | tf_op jit(solution)/shard_map/ppermute | solution.py:19
  40.1 3.6 %collective-permute-start.4 = (f32[2,64,2,256]{3,2,1,0:T(2,128)S(1)}, f32[2,64,2,256]{3,2,1,0:T(2,128)S(1)}, u32[]{:S(2)}, u32[]{:S(2)}) collective-permute-start(f32[2,64,2,256]{3,2,1,0:T(2,128)S(1)} %get-tuple-element.42), channel_id=1, source_target_pairs={{1,0},{2,1},{3,2},{4,3},{5,4},{6,5},{7,6},{8,7},{9,8},{10,9},{11,1... | collective-permute-start | bytes 786440 | tf_op jit(solution)/shard_map/ppermute | solution.py:20
  43.8 2.0 %collective-permute-done.5 = f32[2,64,2,256]{3,2,1,0:T(2,128)S(1)} collective-permute-done((f32[2,64,2,256]{3,2,1,0:T(2,128)S(1)}, f32[2,64,2,256]{3,2,1,0:T(2,128)S(1)}, u32[]{:S(2)}, u32[]{:S(2)}) %collective-permute-start.5) | collective-permute-done | bytes 262176 | tf_op jit(solution)/shard_map/ppermute | solution.py:19
  52.7 5.9 %collective-permute-start.7 = (f32[2,32,4,256]{3,2,1,0:T(4,128)S(1)}, f32[2,32,4,256]{3,2,1,0:T(4,128)S(1)}, u32[]{:S(2)}, u32[]{:S(2)}) collective-permute-start(f32[2,32,4,256]{3,2,1,0:T(4,128)S(1)} %pad_maximum_fusion.27), channel_id=1, source_target_pairs={{0,1},{1,2},{2,3},{3,4},{4,5},{5,6},{6,7},{7,8},{8,9},{9,10},{10,1... | collective-permute-start | bytes 786440 | tf_op jit(solution)/shard_map/ppermute | solution.py:19
  58.7 2.1 %collective-permute-start.6 = (f32[2,32,4,256]{3,2,1,0:T(4,128)S(1)}, f32[2,32,4,256]{3,2,1,0:T(4,128)S(1)}, u32[]{:S(2)}, u32[]{:S(2)}) collective-permute-start(f32[2,32,4,256]{3,2,1,0:T(4,128)S(1)} %pad_maximum_fusion.26), channel_id=1, source_target_pairs={{1,0},{2,1},{3,2},{4,3},{5,4},{6,5},{7,6},{8,7},{9,8},{10,9},{11,1... | collective-permute-start | bytes 786440 | tf_op jit(solution)/shard_map/ppermute | solution.py:20
  61.3 3.3 %collective-permute-done.6 = f32[2,32,4,256]{3,2,1,0:T(4,128)S(1)} collective-permute-done((f32[2,32,4,256]{3,2,1,0:T(4,128)S(1)}, f32[2,32,4,256]{3,2,1,0:T(4,128)S(1)}, u32[]{:S(2)}, u32[]{:S(2)}) %collective-permute-start.6) | collective-permute-done | bytes 262176 | tf_op jit(solution)/shard_map/ppermute | solution.py:20
  70.9 2.2 %add_add_fusion.2 = (f32[2,64,8,256]{3,2,1,0:T(8,128)S(1)}, f32[2,64,8,256]{3,2,1,0:T(8,128)S(1)}) fusion(f32[2,64,8,256]{3,2,1,0:T(8,128)S(1)} %get-tuple-element.31, f32[2,64,8,256]{3,2,1,0:T(8,128)S(1)} %bitcast.52, f32[2,64,8,256]{3,2,1,0:T(8,128)S(1)} %bitcast.48, f32[2,64,8,256]{3,2,1,0:T(8,128)S(1)} %copy-done, f32[2,64,8,256]{3,2,1,0:T(8,128)S(1)} %bitcast.50, ...), kind=kLoop, calls=%fused_computation.32 | loop fusion | flops 11796480 | bytes 12845072 | tf_op jit(solution)/shard_map/add | solution.py:260
  73.2 4.7 %collective-permute-start.8 = (f32[2,64,1,256]{3,2,1,0:T(1,128)S(1)}, f32[2,64,1,256]{3,2,1,0:T(1,128)S(1)}, u32[]{:S(2)}, u32[]{:S(2)}) collective-permute-start(f32[2,64,1,256]{3,2,1,0:T(1,128)S(1)} %get-tuple-element.39), channel_id=1, source_target_pairs={{0,1},{1,2},{2,3},{3,4},{4,5},{5,6},{6,7},{7,8},{8,9},{9,10},{10,1... | collective-permute-start | bytes 393224 | tf_op jit(solution)/shard_map/ppermute | solution.py:19
  77.9 1.9 %collective-permute-start.9 = (f32[2,64,1,256]{3,2,1,0:T(1,128)S(1)}, f32[2,64,1,256]{3,2,1,0:T(1,128)S(1)}, u32[]{:S(2)}, u32[]{:S(2)}) collective-permute-start(f32[2,64,1,256]{3,2,1,0:T(1,128)S(1)} %get-tuple-element.40), channel_id=1, source_target_pairs={{1,0},{2,1},{3,2},{4,3},{5,4},{6,5},{7,6},{8,7},{9,8},{10,9},{11,1... | collective-permute-start | bytes 393224 | tf_op jit(solution)/shard_map/ppermute | solution.py:20
  79.9 2.5 %collective-permute-done.9 = f32[2,64,1,256]{3,2,1,0:T(1,128)S(1)} collective-permute-done((f32[2,64,1,256]{3,2,1,0:T(1,128)S(1)}, f32[2,64,1,256]{3,2,1,0:T(1,128)S(1)}, u32[]{:S(2)}, u32[]{:S(2)}) %collective-permute-start.9) | collective-permute-done | bytes 131104 | tf_op jit(solution)/shard_map/ppermute | solution.py:20
  85.6 4.7 %collective-permute-start.10 = (f32[2,64,1,256]{3,2,1,0:T(1,128)S(1)}, f32[2,64,1,256]{3,2,1,0:T(1,128)S(1)}, u32[]{:S(2)}, u32[]{:S(2)}) collective-permute-start(f32[2,64,1,256]{3,2,1,0:T(1,128)S(1)} %get-tuple-element.37), channel_id=1, source_target_pairs={{0,1},{1,2},{2,3},{3,4},{4,5},{5,6},{6,7},{7,8},{8,9},{9,10},{10,1... | collective-permute-start | bytes 393224 | tf_op jit(solution)/shard_map/ppermute | solution.py:19
  90.3 2.1 %collective-permute-start.11 = (f32[2,64,1,256]{3,2,1,0:T(1,128)S(1)}, f32[2,64,1,256]{3,2,1,0:T(1,128)S(1)}, u32[]{:S(2)}, u32[]{:S(2)}) collective-permute-start(f32[2,64,1,256]{3,2,1,0:T(1,128)S(1)} %get-tuple-element.38), channel_id=1, source_target_pairs={{1,0},{2,1},{3,2},{4,3},{5,4},{6,5},{7,6},{8,7},{9,8},{10,9},{11,1... | collective-permute-start | bytes 393224 | tf_op jit(solution)/shard_map/ppermute | solution.py:20
  102.0 2.0 %collective-permute-done.13 = f32[2,32,1,256]{3,2,1,0:T(1,128)} collective-permute-done((f32[2,32,1,256]{3,2,1,0:T(1,128)S(1)}, f32[2,32,1,256]{3,2,1,0:T(1,128)}, u32[]{:S(2)}, u32[]{:S(2)}) %collective-permute-start.13) | collective-permute-done | bytes 65568 | tf_op jit(solution)/shard_map/ppermute | solution.py:289
  104.0 3.0 %collective-permute-done.14 = f32[2,32,1,256]{3,2,1,0:T(1,128)} collective-permute-done((f32[2,32,1,256]{3,2,1,0:T(1,128)S(1)}, f32[2,32,1,256]{3,2,1,0:T(1,128)}, u32[]{:S(2)}, u32[]{:S(2)}) %collective-permute-start.14) | collective-permute-done | bytes 65568 | tf_op jit(solution)/shard_map/ppermute | solution.py:290
  108.2 6.2 %collective-permute-done.12 = f32[2,32,4,256]{3,2,1,0:T(4,128)S(1)} collective-permute-done((f32[2,32,4,256]{3,2,1,0:T(4,128)S(1)}, f32[2,32,4,256]{3,2,1,0:T(4,128)S(1)}, u32[]{:S(2)}, u32[]{:S(2)}) %collective-permute-start.12) | collective-permute-done | bytes 262176 | tf_op jit(solution)/shard_map/ppermute | solution.py:288
  117.2 2.1 %fusion.30 = f32[2,32,8,256]{3,2,1,0:T(8,128)S(1)} fusion(f32[2,32,8,256]{3,2,1,0:T(8,128)S(1)} %get-tuple-element.6, f32[2,32,8,256]{3,2,1,0:T(8,128)S(1)} %broadcast_select_fusion, f32[2,32,1,256]{3,2,1,0:T(1,128)S(1)} %get-tuple-element.50, f32[2,32,7,256]{3,2,1,0:T(8,128)} %get-tuple-element.52, f32[2,32,7,256]{3,2,1,0:T(8,128)S(1)} %copy-done.18, ...), kind=kLoop, calls=%fused_computation.85 | loop fusion | flops 5373952 | bytes 4849752 | tf_op jit(solution)/shard_map/sub | solution.py:295
  (160 shorter events, 48.1 us)
Async XLA Ops:
  0.0 8.0 %copy-start.19 = (s32[8]{0:T(128)}, s32[8]{0:T(128)S(1)}, u32[]{:S(2)}) copy-start(s32[8]{0:T(128)S(1)} %get-tuple-element.135) | copy-start | bytes 100
  8.4 4.4 %copy-start.7 = (f32[32,8,256]{2,1,0:T(8,128)}, f32[32,8,256]{2,1,0:T(8,128)S(1)}, u32[]{:S(2)}) copy-start(f32[32,8,256]{2,1,0:T(8,128)S(1)} %get-tuple-element.128) | copy-start | bytes 786436
  8.4 4.4 %copy-start.10 = (f32[32,8,256]{2,1,0:T(8,128)}, f32[32,8,256]{2,1,0:T(8,128)S(1)}, u32[]{:S(2)}) copy-start(f32[32,8,256]{2,1,0:T(8,128)S(1)} %get-tuple-element.129) | copy-start | bytes 786436
  8.4 8.0 %copy-start.22 = (f32[2,2]{1,0:T(2,128)S(1)}, f32[2,2]{1,0:T(2,128)}, u32[]{:S(2)}) copy-start(f32[2,2]{1,0:T(2,128)} %param.11) | copy-start | bytes 52
  9.7 9.9 %collective-permute-start.1 = (f32[2,160,1,256]{3,2,1,0:T(1,128)}, f32[2,160,1,256]{3,2,1,0:T(1,128)}, u32[]{:S(2)}, u32[]{:S(2)}) collective-permute-start(f32[2,160,1,256]{3,2,1,0:T(1,128)} %pad_maximum_fusion.25), channel_id=1, source_target_pairs={{0,1},{1,2},{2,3},{3,4},{4,5},{5,6},{6,7},{7,8},{8,9},{9,10},{10,1... | collective-permute-start | bytes 983048 | tf_op jit(solution)/shard_map/ppermute | solution.py:19
  12.8 8.5 %collective-permute-start = (f32[2,160,1,256]{3,2,1,0:T(1,128)}, f32[2,160,1,256]{3,2,1,0:T(1,128)}, u32[]{:S(2)}, u32[]{:S(2)}) collective-permute-start(f32[2,160,1,256]{3,2,1,0:T(1,128)} %pad_maximum_fusion.24), channel_id=1, source_target_pairs={{1,0},{2,1},{3,2},{4,3},{5,4},{6,5},{7,6},{8,7},{9,8},{10,9},{11,1... | collective-permute-start | bytes 983048 | tf_op jit(solution)/shard_map/ppermute | solution.py:20
  24.4 8.5 %collective-permute-start.2 = (f32[2,64,1,256]{3,2,1,0:T(1,128)S(1)}, f32[2,64,1,256]{3,2,1,0:T(1,128)S(1)}, u32[]{:S(2)}, u32[]{:S(2)}) collective-permute-start(f32[2,64,1,256]{3,2,1,0:T(1,128)S(1)} %get-tuple-element.43), channel_id=1, source_target_pairs={{1,0},{2,1},{3,2},{4,3},{5,4},{6,5},{7,6},{8,7},{9,8},{10,9},{11,1... | collective-permute-start | bytes 393224 | tf_op jit(solution)/shard_map/ppermute | solution.py:20
  28.2 7.6 %collective-permute-start.3 = (f32[2,64,1,256]{3,2,1,0:T(1,128)S(1)}, f32[2,64,1,256]{3,2,1,0:T(1,128)S(1)}, u32[]{:S(2)}, u32[]{:S(2)}) collective-permute-start(f32[2,64,1,256]{3,2,1,0:T(1,128)S(1)} %get-tuple-element.44), channel_id=1, source_target_pairs={{0,1},{1,2},{2,3},{3,4},{4,5},{5,6},{6,7},{7,8},{8,9},{9,10},{10,1... | collective-permute-start | bytes 393224 | tf_op jit(solution)/shard_map/ppermute | solution.py:19
  38.1 7.7 %collective-permute-start.5 = (f32[2,64,2,256]{3,2,1,0:T(2,128)S(1)}, f32[2,64,2,256]{3,2,1,0:T(2,128)S(1)}, u32[]{:S(2)}, u32[]{:S(2)}) collective-permute-start(f32[2,64,2,256]{3,2,1,0:T(2,128)S(1)} %get-tuple-element.41), channel_id=1, source_target_pairs={{0,1},{1,2},{2,3},{3,4},{4,5},{5,6},{6,7},{7,8},{8,9},{9,10},{10,1... | collective-permute-start | bytes 786440 | tf_op jit(solution)/shard_map/ppermute | solution.py:19
  40.1 7.5 %collective-permute-start.4 = (f32[2,64,2,256]{3,2,1,0:T(2,128)S(1)}, f32[2,64,2,256]{3,2,1,0:T(2,128)S(1)}, u32[]{:S(2)}, u32[]{:S(2)}) collective-permute-start(f32[2,64,2,256]{3,2,1,0:T(2,128)S(1)} %get-tuple-element.42), channel_id=1, source_target_pairs={{1,0},{2,1},{3,2},{4,3},{5,4},{6,5},{7,6},{8,7},{9,8},{10,9},{11,1... | collective-permute-start | bytes 786440 | tf_op jit(solution)/shard_map/ppermute | solution.py:20
  49.2 1.4 %copy-start.17 = (f32[2,32,8,256]{3,2,1,0:T(8,128)S(1)}, f32[2,32,8,256]{3,2,1,0:T(8,128)}, u32[]{:S(2)}) copy-start(f32[2,32,8,256]{3,2,1,0:T(8,128)} %copy-done.16) | copy-start | bytes 1572868
  49.2 1.4 %copy-start.20 = (s32[8]{0:T(128)S(1)}, s32[8]{0:T(128)}, u32[]{:S(2)}) copy-start(s32[8]{0:T(128)} %copy-done.19) | copy-start | bytes 100
  52.7 8.5 %collective-permute-start.7 = (f32[2,32,4,256]{3,2,1,0:T(4,128)S(1)}, f32[2,32,4,256]{3,2,1,0:T(4,128)S(1)}, u32[]{:S(2)}, u32[]{:S(2)}) collective-permute-start(f32[2,32,4,256]{3,2,1,0:T(4,128)S(1)} %pad_maximum_fusion.27), channel_id=1, source_target_pairs={{0,1},{1,2},{2,3},{3,4},{4,5},{5,6},{6,7},{7,8},{8,9},{9,10},{10,1... | collective-permute-start | bytes 786440 | tf_op jit(solution)/shard_map/ppermute | solution.py:19
  58.7 5.8 %collective-permute-start.6 = (f32[2,32,4,256]{3,2,1,0:T(4,128)S(1)}, f32[2,32,4,256]{3,2,1,0:T(4,128)S(1)}, u32[]{:S(2)}, u32[]{:S(2)}) collective-permute-start(f32[2,32,4,256]{3,2,1,0:T(4,128)S(1)} %pad_maximum_fusion.26), channel_id=1, source_target_pairs={{1,0},{2,1},{3,2},{4,3},{5,4},{6,5},{7,6},{8,7},{9,8},{10,9},{11,1... | collective-permute-start | bytes 786440 | tf_op jit(solution)/shard_map/ppermute | solution.py:20
  73.2 6.7 %collective-permute-start.8 = (f32[2,64,1,256]{3,2,1,0:T(1,128)S(1)}, f32[2,64,1,256]{3,2,1,0:T(1,128)S(1)}, u32[]{:S(2)}, u32[]{:S(2)}) collective-permute-start(f32[2,64,1,256]{3,2,1,0:T(1,128)S(1)} %get-tuple-element.39), channel_id=1, source_target_pairs={{0,1},{1,2},{2,3},{3,4},{4,5},{5,6},{6,7},{7,8},{8,9},{9,10},{10,1... | collective-permute-start | bytes 393224 | tf_op jit(solution)/shard_map/ppermute | solution.py:19
  77.9 4.4 %collective-permute-start.9 = (f32[2,64,1,256]{3,2,1,0:T(1,128)S(1)}, f32[2,64,1,256]{3,2,1,0:T(1,128)S(1)}, u32[]{:S(2)}, u32[]{:S(2)}) collective-permute-start(f32[2,64,1,256]{3,2,1,0:T(1,128)S(1)} %get-tuple-element.40), channel_id=1, source_target_pairs={{1,0},{2,1},{3,2},{4,3},{5,4},{6,5},{7,6},{8,7},{9,8},{10,9},{11,1... | collective-permute-start | bytes 393224 | tf_op jit(solution)/shard_map/ppermute | solution.py:20
  85.6 7.9 %collective-permute-start.10 = (f32[2,64,1,256]{3,2,1,0:T(1,128)S(1)}, f32[2,64,1,256]{3,2,1,0:T(1,128)S(1)}, u32[]{:S(2)}, u32[]{:S(2)}) collective-permute-start(f32[2,64,1,256]{3,2,1,0:T(1,128)S(1)} %get-tuple-element.37), channel_id=1, source_target_pairs={{0,1},{1,2},{2,3},{3,4},{4,5},{5,6},{6,7},{7,8},{8,9},{9,10},{10,1... | collective-permute-start | bytes 393224 | tf_op jit(solution)/shard_map/ppermute | solution.py:19
  90.3 4.4 %collective-permute-start.11 = (f32[2,64,1,256]{3,2,1,0:T(1,128)S(1)}, f32[2,64,1,256]{3,2,1,0:T(1,128)S(1)}, u32[]{:S(2)}, u32[]{:S(2)}) collective-permute-start(f32[2,64,1,256]{3,2,1,0:T(1,128)S(1)} %get-tuple-element.38), channel_id=1, source_target_pairs={{1,0},{2,1},{3,2},{4,3},{5,4},{6,5},{7,6},{8,7},{9,8},{10,9},{11,1... | collective-permute-start | bytes 393224 | tf_op jit(solution)/shard_map/ppermute | solution.py:20
  97.5 6.6 %collective-permute-start.13 = (f32[2,32,1,256]{3,2,1,0:T(1,128)S(1)}, f32[2,32,1,256]{3,2,1,0:T(1,128)}, u32[]{:S(2)}, u32[]{:S(2)}) collective-permute-start(f32[2,32,1,256]{3,2,1,0:T(1,128)S(1)} %get-tuple-element.47), channel_id=1, source_target_pairs={{0,17},{1,18},{2,19},{3,20},{4,21},{5,22},{6,23},{7,24},{8,25},{9,... | collective-permute-start | bytes 196616 | tf_op jit(solution)/shard_map/ppermute | solution.py:289
  98.8 8.3 %collective-permute-start.14 = (f32[2,32,1,256]{3,2,1,0:T(1,128)S(1)}, f32[2,32,1,256]{3,2,1,0:T(1,128)}, u32[]{:S(2)}, u32[]{:S(2)}) collective-permute-start(f32[2,32,1,256]{3,2,1,0:T(1,128)S(1)} %get-tuple-element.48), channel_id=1, source_target_pairs={{1,16},{2,17},{3,18},{4,19},{5,20},{6,21},{7,22},{8,23},{9,24},{10... | collective-permute-start | bytes 196616 | tf_op jit(solution)/shard_map/ppermute | solution.py:290
  100.7 13.7 %collective-permute-start.12 = (f32[2,32,4,256]{3,2,1,0:T(4,128)S(1)}, f32[2,32,4,256]{3,2,1,0:T(4,128)S(1)}, u32[]{:S(2)}, u32[]{:S(2)}) collective-permute-start(f32[2,32,4,256]{3,2,1,0:T(4,128)S(1)} %bitcast.65), channel_id=1, source_target_pairs={{0,16},{1,17},{2,18},{3,19},{4,20},{5,21},{6,22},{7,23},{8,24},{9,... | collective-permute-start | bytes 786440 | tf_op jit(solution)/shard_map/ppermute | solution.py:288
  108.1 7.7 %copy-start.6 = (f32[2,32,8,256]{3,2,1,0:T(8,128)S(1)}, f32[2,32,8,256]{3,2,1,0:T(8,128)}, u32[]{:S(2)}) copy-start(f32[2,32,8,256]{3,2,1,0:T(8,128)} %get-tuple-element.36) | copy-start | bytes 1572868
  115.8 1.4 %copy-start.18 = (f32[2,32,7,256]{3,2,1,0:T(8,128)S(1)}, f32[2,32,7,256]{3,2,1,0:T(8,128)}, u32[]{:S(2)}) copy-start(f32[2,32,7,256]{3,2,1,0:T(8,128)} %get-tuple-element.51) | copy-start | bytes 1376260
  115.8 1.4 %copy-start.21 = (s32[8]{0:T(128)S(1)}, s32[8]{0:T(128)}, u32[]{:S(2)}) copy-start(s32[8]{0:T(128)} %copy-done.19) | copy-start | bytes 100
  (14 other events, 15.6 us)

commit v15 on v11

--- a/solution.py
+++ b/solution.py
@@ -184,8 +184,10 @@
     halo_two = pack(hi(two_b), lo(two_a))
     coarse_end = shrink(node_two)
     halo_end = pack(hi(shrink(two_b)), lo(shrink(two_a)))
-    rate_two = fine_rate(node_two, halo_two)
-    source = shrink(slab_step * (rate_zero + 4.0 * rate_one + rate_two) / 6.0)
+    quadrature = fine_rate(
+        node_zero + 4.0 * node_one + node_two, halo_zero + 4.0 * halo_one + halo_two
+    )
+    source = shrink(slab_step * quadrature / 6.0)
     offset = source - slab_step * coarse_first_rate
 
     chain = [coarse_first]

time: 121 us -> 123 us (1.017)
    add x1 -> x2, other arithmetic: 1.61 us -> 3.67 us  [body(): node_zero + 4.0 * node_one + node_two]
    div x1 -> x0, other arithmetic: 1.34 us -> none  [body(): source = shrink(slab_step * (rate_zero + 4.0 * rate_one + rate_two) / 6.0)]
    add x1, other arithmetic: 1.97 us -> 0.66 us  [body(): halo_zero + 4.0 * halo_one + halo_two]
    div x1 -> x2, other arithmetic: 1.3 us -> 2.57 us  [body(): source = shrink(slab_step * quadrature / 6.0)]
where the time goes in v15:
time: 123 us; the launch traced here: 122 us
  waiting for transfers between devices  39.4 us (32%)
  starting transfers between devices  35 us (28%)
  other arithmetic  31.2 us (25%)
  local copies, waits for them, and re-layouts  15.3 us (12%)
    ppermute x6, waiting for transfers between devices, exchange(): after = lax.ppermute(to_left, 'space', shift_pairs(count, -1))  22.5 us
    ppermute x6, starting transfers between devices, exchange(): before = lax.ppermute(to_right, 'space', shift_pairs(count, 1))  17.7 us
    ppermute x1, waiting for transfers between devices, body(): passed_b = lax.ppermute(hi(after), ('tm', 'space'), to_east)  14.2 us
    ppermute x6, starting transfers between devices, exchange(): after = lax.ppermute(to_left, 'space', shift_pairs(count, -1))  13.4 us
    unnamed x30, local copies, waits for them, and re-layouts  5.84 us
    add x2, other arithmetic, body(): node_zero + 4.0 * node_one + node_two  3.67 us
    ppermute x6, waiting for transfers between devices, exchange(): before = lax.ppermute(to_right, 'space', shift_pairs(count, 1))  2.63 us
    div x2, other arithmetic, body(): source = shrink(slab_step * quadrature / 6.0)  2.57 us
  transfers between devices with their start and end apart: 15, of which 9 were waited for; matrix products, arithmetic and copies ran while one was open for 7% of the time, Pallas kernels for 0%

profile of v15, /device:TPU:11, one launch (start us, length us, event | category | flops | bytes accessed | tf_op | source)
XLA Modules:
  0.0 121.7 jit_solution(12872772492459407013)
XLA Ops:
  9.7 3.7 %collective-permute-start.1 = (f32[2,160,1,256]{3,2,1,0:T(1,128)}, f32[2,160,1,256]{3,2,1,0:T(1,128)}, u32[]{:S(2)}, u32[]{:S(2)}) collective-permute-start(f32[2,160,1,256]{3,2,1,0:T(1,128)} %pad_maximum_fusion.25), channel_id=1, source_target_pairs={{0,1},{1,2},{2,3},{3,4},{4,5},{5,6},{6,7},{7,8},{8,9},{9,10},{10,1... | collective-permute-start | bytes 983048 | tf_op jit(solution)/shard_map/ppermute | solution.py:19
  14.6 1.9 %collective-permute-start = (f32[2,160,1,256]{3,2,1,0:T(1,128)}, f32[2,160,1,256]{3,2,1,0:T(1,128)}, u32[]{:S(2)}, u32[]{:S(2)}) collective-permute-start(f32[2,160,1,256]{3,2,1,0:T(1,128)} %pad_maximum_fusion.24), channel_id=1, source_target_pairs={{1,0},{2,1},{3,2},{4,3},{5,4},{6,5},{7,6},{8,7},{9,8},{10,9},{11,1... | collective-permute-start | bytes 983048 | tf_op jit(solution)/shard_map/ppermute | solution.py:20
  17.2 2.5 %broadcast_multiply_fusion.1 = (f32[2]{0:T(128)S(1)}, f32[2]{0:T(128)S(1)}, f32[2]{0:T(128)S(1)}, f32[2]{0:T(128)S(1)}) fusion(f32[]{:T(128)} %bitcast.13, f32[]{:T(128)} %bitcast.12, f32[]{:T(128)} %bitcast.11, f32[]{:T(128)} %bitcast.10), kind=kLoop, calls=%fused_computation.213 | loop fusion | flops 10 | bytes 48 | tf_op jit(solution)/shard_map/mul | solution.py:80
  20.9 2.4 %collective-permute-done = f32[2,160,1,256]{3,2,1,0:T(1,128)} collective-permute-done((f32[2,160,1,256]{3,2,1,0:T(1,128)}, f32[2,160,1,256]{3,2,1,0:T(1,128)}, u32[]{:S(2)}, u32[]{:S(2)}) %collective-permute-start) | collective-permute-done | bytes 327712 | tf_op jit(solution)/shard_map/ppermute | solution.py:20
  24.4 1.7 %multiply_add_fusion.1 = (f32[2,64,8,256]{3,2,1,0:T(8,128)S(1)}, f32[2,64,8,256]{3,2,1,0:T(8,128)S(1)}) fusion(f32[2,64,8,256]{3,2,1,0:T(8,128)S(1)} %copy-done, f32[2]{0:T(128)S(1)} %get-tuple-element.29, f32[2]{0:T(128)S(1)} %get-tuple-element.140, f32[64,8,256]{2,1,0:T(8,128)S(1)} %copy-done.3, f32[64,8,256]{2,1,0:T(8,128)S(1)} %copy-done.1, ...), kind=kLoop, calls=%fused_computation.45 | loop fusion | flops 8912896 | bytes 5505040 | tf_op jit(solution)/shard_map/add | solution.py:138
  26.3 1.9 %collective-permute-start.2 = (f32[2,64,1,256]{3,2,1,0:T(1,128)S(1)}, f32[2,64,1,256]{3,2,1,0:T(1,128)S(1)}, u32[]{:S(2)}, u32[]{:S(2)}) collective-permute-start(f32[2,64,1,256]{3,2,1,0:T(1,128)S(1)} %get-tuple-element.42), channel_id=1, source_target_pairs={{1,0},{2,1},{3,2},{4,3},{5,4},{6,5},{7,6},{8,7},{9,8},{10,9},{11,1... | collective-permute-start | bytes 393224 | tf_op jit(solution)/shard_map/ppermute | solution.py:20
  28.3 3.6 %collective-permute-start.3 = (f32[2,64,1,256]{3,2,1,0:T(1,128)S(1)}, f32[2,64,1,256]{3,2,1,0:T(1,128)S(1)}, u32[]{:S(2)}, u32[]{:S(2)}) collective-permute-start(f32[2,64,1,256]{3,2,1,0:T(1,128)S(1)} %get-tuple-element.43), channel_id=1, source_target_pairs={{0,1},{1,2},{2,3},{3,4},{4,5},{5,6},{6,7},{7,8},{8,9},{9,10},{10,1... | collective-permute-start | bytes 393224 | tf_op jit(solution)/shard_map/ppermute | solution.py:19
  35.1 2.0 %add_add_fusion.5 = (f32[2,64,8,256]{3,2,1,0:T(8,128)S(1)}, f32[2,64,8,256]{3,2,1,0:T(8,128)S(1)}) fusion(f32[2,64,8,256]{3,2,1,0:T(8,128)S(1)} %copy-done, f32[2,64,8,256]{3,2,1,0:T(8,128)S(1)} %get-tuple-element.33, f32[2,64,8,256]{3,2,1,0:T(8,128)S(1)} %get-tuple-element.32, f32[2]{0:T(128)S(1)} %get-tuple-element.29, f32[2]{0:T(128)S(1)} %get-tuple-element.140, ...), kind=kLoop, calls=%fused_computation.41 | loop fusion | flops 11796480 | bytes 7602192 | tf_op jit(solution)/shard_map/add | solution.py:188
  37.5 4.4 %collective-permute-start.4 = (f32[2,64,2,256]{3,2,1,0:T(2,128)S(1)}, f32[2,64,2,256]{3,2,1,0:T(2,128)S(1)}, u32[]{:S(2)}, u32[]{:S(2)}) collective-permute-start(f32[2,64,2,256]{3,2,1,0:T(2,128)S(1)} %get-tuple-element.40), channel_id=1, source_target_pairs={{0,1},{1,2},{2,3},{3,4},{4,5},{5,6},{6,7},{7,8},{8,9},{9,10},{10,1... | collective-permute-start | bytes 786440 | tf_op jit(solution)/shard_map/ppermute | solution.py:19
  41.9 2.1 %collective-permute-start.5 = (f32[2,64,2,256]{3,2,1,0:T(2,128)S(1)}, f32[2,64,2,256]{3,2,1,0:T(2,128)S(1)}, u32[]{:S(2)}, u32[]{:S(2)}) collective-permute-start(f32[2,64,2,256]{3,2,1,0:T(2,128)S(1)} %get-tuple-element.41), channel_id=1, source_target_pairs={{1,0},{2,1},{3,2},{4,3},{5,4},{6,5},{7,6},{8,7},{9,8},{10,9},{11,1... | collective-permute-start | bytes 786440 | tf_op jit(solution)/shard_map/ppermute | solution.py:20
  45.4 5.6 %collective-permute-done.5 = f32[2,64,2,256]{3,2,1,0:T(2,128)S(1)} collective-permute-done((f32[2,64,2,256]{3,2,1,0:T(2,128)S(1)}, f32[2,64,2,256]{3,2,1,0:T(2,128)S(1)}, u32[]{:S(2)}, u32[]{:S(2)}) %collective-permute-start.5) | collective-permute-done | bytes 262176 | tf_op jit(solution)/shard_map/ppermute | solution.py:20
  56.8 2.1 %collective-permute-start.7 = (f32[2,32,4,256]{3,2,1,0:T(4,128)S(1)}, f32[2,32,4,256]{3,2,1,0:T(4,128)S(1)}, u32[]{:S(2)}, u32[]{:S(2)}) collective-permute-start(f32[2,32,4,256]{3,2,1,0:T(4,128)S(1)} %pad_maximum_fusion.30), channel_id=1, source_target_pairs={{0,1},{1,2},{2,3},{3,4},{4,5},{5,6},{6,7},{7,8},{8,9},{9,10},{10,1... | collective-permute-start | bytes 786440 | tf_op jit(solution)/shard_map/ppermute | solution.py:19
  59.1 2.4 %collective-permute-start.6 = (f32[2,32,4,256]{3,2,1,0:T(4,128)S(1)}, f32[2,32,4,256]{3,2,1,0:T(4,128)S(1)}, u32[]{:S(2)}, u32[]{:S(2)}) collective-permute-start(f32[2,32,4,256]{3,2,1,0:T(4,128)S(1)} %pad_maximum_fusion.29), channel_id=1, source_target_pairs={{1,0},{2,1},{3,2},{4,3},{5,4},{6,5},{7,6},{8,7},{9,8},{10,9},{11,1... | collective-permute-start | bytes 786440 | tf_op jit(solution)/shard_map/ppermute | solution.py:20
  62.2 5.4 %collective-permute-done.6 = f32[2,32,4,256]{3,2,1,0:T(4,128)S(1)} collective-permute-done((f32[2,32,4,256]{3,2,1,0:T(4,128)S(1)}, f32[2,32,4,256]{3,2,1,0:T(4,128)S(1)}, u32[]{:S(2)}, u32[]{:S(2)}) %collective-permute-start.6) | collective-permute-done | bytes 262176 | tf_op jit(solution)/shard_map/ppermute | solution.py:20
  71.0 1.5 %add_multiply_fusion.2 = (f32[2,32,8,256]{3,2,1,0:T(8,128)S(1)}, f32[2,32,8,256]{3,2,1,0:T(8,128)S(1)}, f32[2,32,8,256]{3,2,1,0:T(8,128)S(1)}, f32[2,32,8,256]{3,2,1,0:T(8,128)S(1)}, f32[2,32,8,256]{3,2,1,0:T(8,128)S(1)}) fusion(pred[]{:T(512)S(6)} %eq.100, f32[2,32,8,256]{3,2,1,0:T(8,128)S(1)} %get-tuple-element.24, ...), kind=kLoop, calls=%fused_computation.119 | loop fusion | flops 6815744 | bytes 7995484 | tf_op jit(solution)/shard_map/mul | solution.py:234
  73.8 2.1 %add_add_fusion.2 = (f32[2,64,8,256]{3,2,1,0:T(8,128)S(1)}, f32[2,64,8,256]{3,2,1,0:T(8,128)S(1)}) fusion(f32[2,64,8,256]{3,2,1,0:T(8,128)S(1)} %get-tuple-element.31, f32[2,64,8,256]{3,2,1,0:T(8,128)S(1)} %bitcast.47, f32[2,64,8,256]{3,2,1,0:T(8,128)S(1)} %bitcast.43, f32[2,64,8,256]{3,2,1,0:T(8,128)S(1)} %copy-done, f32[2,64,8,256]{3,2,1,0:T(8,128)S(1)} %bitcast.45, ...), kind=kLoop, calls=%fused_computation.32 | loop fusion | flops 11796480 | bytes 12845072 | tf_op jit(solution)/shard_map/add | solution.py:262
  76.2 1.9 %collective-permute-start.8 = (f32[2,64,1,256]{3,2,1,0:T(1,128)S(1)}, f32[2,64,1,256]{3,2,1,0:T(1,128)S(1)}, u32[]{:S(2)}, u32[]{:S(2)}) collective-permute-start(f32[2,64,1,256]{3,2,1,0:T(1,128)S(1)} %get-tuple-element.38), channel_id=1, source_target_pairs={{0,1},{1,2},{2,3},{3,4},{4,5},{5,6},{6,7},{7,8},{8,9},{9,10},{10,1... | collective-permute-start | bytes 393224 | tf_op jit(solution)/shard_map/ppermute | solution.py:19
  78.1 2.4 %collective-permute-start.9 = (f32[2,64,1,256]{3,2,1,0:T(1,128)S(1)}, f32[2,64,1,256]{3,2,1,0:T(1,128)S(1)}, u32[]{:S(2)}, u32[]{:S(2)}) collective-permute-start(f32[2,64,1,256]{3,2,1,0:T(1,128)S(1)} %get-tuple-element.39), channel_id=1, source_target_pairs={{1,0},{2,1},{3,2},{4,3},{5,4},{6,5},{7,6},{8,7},{9,8},{10,9},{11,1... | collective-permute-start | bytes 393224 | tf_op jit(solution)/shard_map/ppermute | solution.py:20
  80.5 4.8 %collective-permute-done.9 = f32[2,64,1,256]{3,2,1,0:T(1,128)S(1)} collective-permute-done((f32[2,64,1,256]{3,2,1,0:T(1,128)S(1)}, f32[2,64,1,256]{3,2,1,0:T(1,128)S(1)}, u32[]{:S(2)}, u32[]{:S(2)}) %collective-permute-start.9) | collective-permute-done | bytes 131104 | tf_op jit(solution)/shard_map/ppermute | solution.py:20
  86.6 1.6 %add_add_fusion = (f32[2,64,8,256]{3,2,1,0:T(8,128)S(1)}, f32[2,64,8,256]{3,2,1,0:T(8,128)S(1)}) fusion(f32[2,64,8,256]{3,2,1,0:T(8,128)S(1)} %get-tuple-element.17, f32[2,64,8,256]{3,2,1,0:T(8,128)S(1)} %get-tuple-element.10, f32[2,64,8,256]{3,2,1,0:T(8,128)S(1)} %get-tuple-element.9, f32[2]{0:T(128)S(1)} %get-tuple-element.29, ...), kind=kLoop, calls=%fused_computation.28 | loop fusion | flops 7340032 | bytes 7602192 | tf_op jit(solution)/shard_map/add | solution.py:268
  88.5 1.9 %collective-permute-start.10 = (f32[2,64,1,256]{3,2,1,0:T(1,128)S(1)}, f32[2,64,1,256]{3,2,1,0:T(1,128)S(1)}, u32[]{:S(2)}, u32[]{:S(2)}) collective-permute-start(f32[2,64,1,256]{3,2,1,0:T(1,128)S(1)} %get-tuple-element.36), channel_id=1, source_target_pairs={{0,1},{1,2},{2,3},{3,4},{4,5},{5,6},{6,7},{7,8},{8,9},{9,10},{10,1... | collective-permute-start | bytes 393224 | tf_op jit(solution)/shard_map/ppermute | solution.py:19
  90.4 2.6 %collective-permute-start.11 = (f32[2,64,1,256]{3,2,1,0:T(1,128)S(1)}, f32[2,64,1,256]{3,2,1,0:T(1,128)S(1)}, u32[]{:S(2)}, u32[]{:S(2)}) collective-permute-start(f32[2,64,1,256]{3,2,1,0:T(1,128)S(1)} %get-tuple-element.37), channel_id=1, source_target_pairs={{1,0},{2,1},{3,2},{4,3},{5,4},{6,5},{7,6},{8,7},{9,8},{10,9},{11,1... | collective-permute-start | bytes 393224 | tf_op jit(solution)/shard_map/ppermute | solution.py:20
  93.2 4.5 %collective-permute-done.11 = f32[2,64,1,256]{3,2,1,0:T(1,128)S(1)} collective-permute-done((f32[2,64,1,256]{3,2,1,0:T(1,128)S(1)}, f32[2,64,1,256]{3,2,1,0:T(1,128)S(1)}, u32[]{:S(2)}, u32[]{:S(2)}) %collective-permute-start.11) | collective-permute-done | bytes 131104 | tf_op jit(solution)/shard_map/ppermute | solution.py:20
  104.8 14.2 %collective-permute-done.13 = f32[2,32,1,256]{3,2,1,0:T(1,128)S(1)} collective-permute-done((f32[2,32,1,256]{3,2,1,0:T(1,128)S(1)}, f32[2,32,1,256]{3,2,1,0:T(1,128)S(1)}, u32[]{:S(2)}, u32[]{:S(2)}) %collective-permute-start.13) | collective-permute-done | bytes 65568 | tf_op jit(solution)/shard_map/ppermute | solution.py:290
  (141 shorter events, 41.5 us)
Async XLA Ops:
  0.0 1.2 %copy-start.1 = (f32[64,8,256]{2,1,0:T(8,128)S(1)}, f32[64,8,256]{2,1,0:T(8,128)}, u32[]{:S(2)}) copy-start(f32[64,8,256]{2,1,0:T(8,128)} %param.7) | copy-start | bytes 1572868
  1.2 1.2 %copy-start = (f32[2,64,8,256]{3,2,1,0:T(8,128)S(1)}, f32[2,64,8,256]{3,2,1,0:T(8,128)}, u32[]{:S(2)}) copy-start(f32[2,64,8,256]{3,2,1,0:T(8,128)} %param.6) | copy-start | bytes 3145732
  2.8 1.2 copy-start.4
  8.3 6.2 %copy-start.6 = (f32[32,8,256]{2,1,0:T(8,128)}, f32[32,8,256]{2,1,0:T(8,128)S(1)}, u32[]{:S(2)}) copy-start(f32[32,8,256]{2,1,0:T(8,128)S(1)} %get-tuple-element.129) | copy-start | bytes 786436
  8.3 6.2 %copy-start.8 = (f32[32,8,256]{2,1,0:T(8,128)}, f32[32,8,256]{2,1,0:T(8,128)S(1)}, u32[]{:S(2)}) copy-start(f32[32,8,256]{2,1,0:T(8,128)S(1)} %get-tuple-element.130) | copy-start | bytes 786436
  8.4 8.1 %copy-start.14 = (f32[2,2]{1,0:T(2,128)S(1)}, f32[2,2]{1,0:T(2,128)}, u32[]{:S(2)}) copy-start(f32[2,2]{1,0:T(2,128)} %param.11) | copy-start | bytes 52
  9.7 10.0 %collective-permute-start.1 = (f32[2,160,1,256]{3,2,1,0:T(1,128)}, f32[2,160,1,256]{3,2,1,0:T(1,128)}, u32[]{:S(2)}, u32[]{:S(2)}) collective-permute-start(f32[2,160,1,256]{3,2,1,0:T(1,128)} %pad_maximum_fusion.25), channel_id=1, source_target_pairs={{0,1},{1,2},{2,3},{3,4},{4,5},{5,6},{6,7},{7,8},{8,9},{9,10},{10,1... | collective-permute-start | bytes 983048 | tf_op jit(solution)/shard_map/ppermute | solution.py:19
  14.6 8.7 %collective-permute-start = (f32[2,160,1,256]{3,2,1,0:T(1,128)}, f32[2,160,1,256]{3,2,1,0:T(1,128)}, u32[]{:S(2)}, u32[]{:S(2)}) collective-permute-start(f32[2,160,1,256]{3,2,1,0:T(1,128)} %pad_maximum_fusion.24), channel_id=1, source_target_pairs={{1,0},{2,1},{3,2},{4,3},{5,4},{6,5},{7,6},{8,7},{9,8},{10,9},{11,1... | collective-permute-start | bytes 983048 | tf_op jit(solution)/shard_map/ppermute | solution.py:20
  26.3 7.5 %collective-permute-start.2 = (f32[2,64,1,256]{3,2,1,0:T(1,128)S(1)}, f32[2,64,1,256]{3,2,1,0:T(1,128)S(1)}, u32[]{:S(2)}, u32[]{:S(2)}) collective-permute-start(f32[2,64,1,256]{3,2,1,0:T(1,128)S(1)} %get-tuple-element.42), channel_id=1, source_target_pairs={{1,0},{2,1},{3,2},{4,3},{5,4},{6,5},{7,6},{8,7},{9,8},{10,9},{11,1... | collective-permute-start | bytes 393224 | tf_op jit(solution)/shard_map/ppermute | solution.py:20
  28.3 6.9 %collective-permute-start.3 = (f32[2,64,1,256]{3,2,1,0:T(1,128)S(1)}, f32[2,64,1,256]{3,2,1,0:T(1,128)S(1)}, u32[]{:S(2)}, u32[]{:S(2)}) collective-permute-start(f32[2,64,1,256]{3,2,1,0:T(1,128)S(1)} %get-tuple-element.43), channel_id=1, source_target_pairs={{0,1},{1,2},{2,3},{3,4},{4,5},{5,6},{6,7},{7,8},{8,9},{9,10},{10,1... | collective-permute-start | bytes 393224 | tf_op jit(solution)/shard_map/ppermute | solution.py:19
  37.5 7.7 %collective-permute-start.4 = (f32[2,64,2,256]{3,2,1,0:T(2,128)S(1)}, f32[2,64,2,256]{3,2,1,0:T(2,128)S(1)}, u32[]{:S(2)}, u32[]{:S(2)}) collective-permute-start(f32[2,64,2,256]{3,2,1,0:T(2,128)S(1)} %get-tuple-element.40), channel_id=1, source_target_pairs={{0,1},{1,2},{2,3},{3,4},{4,5},{5,6},{6,7},{7,8},{8,9},{9,10},{10,1... | collective-permute-start | bytes 786440 | tf_op jit(solution)/shard_map/ppermute | solution.py:19
  41.9 9.0 %collective-permute-start.5 = (f32[2,64,2,256]{3,2,1,0:T(2,128)S(1)}, f32[2,64,2,256]{3,2,1,0:T(2,128)S(1)}, u32[]{:S(2)}, u32[]{:S(2)}) collective-permute-start(f32[2,64,2,256]{3,2,1,0:T(2,128)S(1)} %get-tuple-element.41), channel_id=1, source_target_pairs={{1,0},{2,1},{3,2},{4,3},{5,4},{6,5},{7,6},{8,7},{9,8},{10,9},{11,1... | collective-permute-start | bytes 786440 | tf_op jit(solution)/shard_map/ppermute | solution.py:20
  53.4 1.2 copy-start.9
  53.4 1.2 %copy-start.11 = (f32[32,8,256]{2,1,0:T(8,128)S(1)}, f32[32,8,256]{2,1,0:T(8,128)}, u32[]{:S(2)}) copy-start(f32[32,8,256]{2,1,0:T(8,128)} %copy-done.10) | copy-start | bytes 786436
  53.4 1.4 %copy-start.13 = (f32[2,32,8,256]{3,2,1,0:T(8,128)S(1)}, f32[2,32,8,256]{3,2,1,0:T(8,128)}, u32[]{:S(2)}) copy-start(f32[2,32,8,256]{3,2,1,0:T(8,128)} %copy-done.12) | copy-start | bytes 1572868
  56.8 5.2 %collective-permute-start.7 = (f32[2,32,4,256]{3,2,1,0:T(4,128)S(1)}, f32[2,32,4,256]{3,2,1,0:T(4,128)S(1)}, u32[]{:S(2)}, u32[]{:S(2)}) collective-permute-start(f32[2,32,4,256]{3,2,1,0:T(4,128)S(1)} %pad_maximum_fusion.30), channel_id=1, source_target_pairs={{0,1},{1,2},{2,3},{3,4},{4,5},{5,6},{6,7},{7,8},{8,9},{9,10},{10,1... | collective-permute-start | bytes 786440 | tf_op jit(solution)/shard_map/ppermute | solution.py:19
  59.1 8.5 %collective-permute-start.6 = (f32[2,32,4,256]{3,2,1,0:T(4,128)S(1)}, f32[2,32,4,256]{3,2,1,0:T(4,128)S(1)}, u32[]{:S(2)}, u32[]{:S(2)}) collective-permute-start(f32[2,32,4,256]{3,2,1,0:T(4,128)S(1)} %pad_maximum_fusion.29), channel_id=1, source_target_pairs={{1,0},{2,1},{3,2},{4,3},{5,4},{6,5},{7,6},{8,7},{9,8},{10,9},{11,1... | collective-permute-start | bytes 786440 | tf_op jit(solution)/shard_map/ppermute | solution.py:20
  76.2 4.3 %collective-permute-start.8 = (f32[2,64,1,256]{3,2,1,0:T(1,128)S(1)}, f32[2,64,1,256]{3,2,1,0:T(1,128)S(1)}, u32[]{:S(2)}, u32[]{:S(2)}) collective-permute-start(f32[2,64,1,256]{3,2,1,0:T(1,128)S(1)} %get-tuple-element.38), channel_id=1, source_target_pairs={{0,1},{1,2},{2,3},{3,4},{4,5},{5,6},{6,7},{7,8},{8,9},{9,10},{10,1... | collective-permute-start | bytes 393224 | tf_op jit(solution)/shard_map/ppermute | solution.py:19
  78.1 7.2 %collective-permute-start.9 = (f32[2,64,1,256]{3,2,1,0:T(1,128)S(1)}, f32[2,64,1,256]{3,2,1,0:T(1,128)S(1)}, u32[]{:S(2)}, u32[]{:S(2)}) collective-permute-start(f32[2,64,1,256]{3,2,1,0:T(1,128)S(1)} %get-tuple-element.39), channel_id=1, source_target_pairs={{1,0},{2,1},{3,2},{4,3},{5,4},{6,5},{7,6},{8,7},{9,8},{10,9},{11,1... | collective-permute-start | bytes 393224 | tf_op jit(solution)/shard_map/ppermute | solution.py:20
  88.5 4.7 %collective-permute-start.10 = (f32[2,64,1,256]{3,2,1,0:T(1,128)S(1)}, f32[2,64,1,256]{3,2,1,0:T(1,128)S(1)}, u32[]{:S(2)}, u32[]{:S(2)}) collective-permute-start(f32[2,64,1,256]{3,2,1,0:T(1,128)S(1)} %get-tuple-element.36), channel_id=1, source_target_pairs={{0,1},{1,2},{2,3},{3,4},{4,5},{5,6},{6,7},{7,8},{8,9},{9,10},{10,1... | collective-permute-start | bytes 393224 | tf_op jit(solution)/shard_map/ppermute | solution.py:19
  90.4 7.2 %collective-permute-start.11 = (f32[2,64,1,256]{3,2,1,0:T(1,128)S(1)}, f32[2,64,1,256]{3,2,1,0:T(1,128)S(1)}, u32[]{:S(2)}, u32[]{:S(2)}) collective-permute-start(f32[2,64,1,256]{3,2,1,0:T(1,128)S(1)} %get-tuple-element.37), channel_id=1, source_target_pairs={{1,0},{2,1},{3,2},{4,3},{5,4},{6,5},{7,6},{8,7},{9,8},{10,9},{11,1... | collective-permute-start | bytes 393224 | tf_op jit(solution)/shard_map/ppermute | solution.py:20
  100.8 18.5 %collective-permute-start.12 = (f32[2,32,8,256]{3,2,1,0:T(8,128)S(1)}, f32[2,32,8,256]{3,2,1,0:T(8,128)S(1)}, u32[]{:S(2)}, u32[]{:S(2)}) collective-permute-start(f32[2,32,8,256]{3,2,1,0:T(8,128)S(1)} %get-tuple-element.5), channel_id=1, source_target_pairs={{0,16},{1,17},{2,18},{3,19},{4,20},{5,21},{6,22},{7,23},{8,24},{9,... | collective-permute-start | bytes 1572872 | tf_op jit(solution)/shard_map/ppermute | solution.py:289
  102.1 16.9 %collective-permute-start.13 = (f32[2,32,1,256]{3,2,1,0:T(1,128)S(1)}, f32[2,32,1,256]{3,2,1,0:T(1,128)S(1)}, u32[]{:S(2)}, u32[]{:S(2)}) collective-permute-start(f32[2,32,1,256]{3,2,1,0:T(1,128)S(1)} %get-tuple-element.46), channel_id=1, source_target_pairs={{0,17},{1,18},{2,19},{3,20},{4,21},{5,22},{6,23},{7,24},{8,25},{9,... | collective-permute-start | bytes 196616 | tf_op jit(solution)/shard_map/ppermute | solution.py:290
  103.4 15.6 %collective-permute-start.14 = (f32[2,32,1,256]{3,2,1,0:T(1,128)S(1)}, f32[2,32,1,256]{3,2,1,0:T(1,128)S(1)}, u32[]{:S(2)}, u32[]{:S(2)}) collective-permute-start(f32[2,32,1,256]{3,2,1,0:T(1,128)S(1)} %get-tuple-element.47), channel_id=1, source_target_pairs={{1,16},{2,17},{3,18},{4,19},{5,20},{6,21},{7,22},{8,23},{9,24},{10... | collective-permute-start | bytes 196616 | tf_op jit(solution)/shard_map/ppermute | solution.py:291
  (6 other events, 5.7 us)

commit v16 on v11

--- a/solution.py
+++ b/solution.py
@@ -75,9 +75,12 @@
     )
     vertical = v_spread * (upward - 2.0 * middle + downward) / (z_spacing * z_spacing)
     tracer = lax.broadcasted_iota(jnp.int32, (2, 1, 1, 1), 0)
-    own = jnp.where(tracer == 0, coupling[0, 0], coupling[1, 1])
-    other = jnp.where(tracer == 0, coupling[0, 1], coupling[1, 0])
-    reaction = own * middle + other * middle[::-1]
+    swapped = middle[::-1]
+    reaction = jnp.where(
+        tracer == 0,
+        coupling[0, 0] * middle + coupling[0, 1] * swapped,
+        coupling[1, 1] * middle + coupling[1, 0] * swapped,
+    )
     return diffusion + vertical - advection + reaction
 
 

time: 121 us -> 145 us (1.20)
  other arithmetic: 30.1 us -> 51.5 us
  between operations: 0.9 us -> 3.4 us
    mul x1, other arithmetic: 1.22 us -> 4.21 us  [body(): halo_f1 = add_coarse(halo_one, (halo_dz + halo_d1) * 0.5)]
    div x1, other arithmetic: 1.34 us -> 4.17 us  [body(): source = shrink(slab_step * (rate_zero + 4.0 * rate_one + rate_two) / 6.0)]
    div x1, other arithmetic: 1.3 us -> 4.06 us  [body(): source = shrink(slab_step * quadrature / 6.0)]
    add x1, other arithmetic: 1.97 us -> 4.64 us  [second_node(): node_one + half_step * (rate_one - s1)]
    add x1, other arithmetic: 1.7 us -> 4.32 us  [first_node(): node_zero + half_step * (rate_zero - s0)]
    add x1, other arithmetic: 2.15 us -> 4.77 us  [body(): half_step * node_one + to_two(fixed_zero, fixed_one, fixed_two)]
    add x1, other arithmetic: 1.61 us -> 4.16 us  [body(): node_zero + 4.0 * node_one + node_two]
    mul x1, other arithmetic: 1.47 us -> 3.98 us  [body(): fixed_one = add_coarse(node_one, (delta_zero + delta_one) * 0.5)]
  transfers between devices with their start and end apart: 15 -> 15, of which waited for: 9 -> 9; matrix products, arithmetic and copies ran while one was open for 7% -> 4% of each run, Pallas kernels for 0% -> 0%
where the time goes in v16:
time: 145 us; the launch traced here: 144 us
  other arithmetic  51.5 us (36%)
  waiting for transfers between devices  39.2 us (27%)
  starting transfers between devices  35 us (24%)
  local copies, waits for them, and re-layouts  15.1 us (10%)
  between operations  3.4 us (2%)
    ppermute x6, waiting for transfers between devices, exchange(): after = lax.ppermute(to_left, 'space', shift_pairs(count, -1))  22.4 us
    ppermute x6, starting transfers between devices, exchange(): before = lax.ppermute(to_right, 'space', shift_pairs(count, 1))  17.5 us
    ppermute x1, waiting for transfers between devices, body(): passed_b = lax.ppermute(hi(after), ('tm', 'space'), to_east)  14.2 us
    ppermute x6, starting transfers between devices, exchange(): after = lax.ppermute(to_left, 'space', shift_pairs(count, -1))  13.6 us
    unnamed x30, local copies, waits for them, and re-layouts  5.84 us
    add x1, other arithmetic, body(): half_step * node_one + to_two(fixed_zero, fixed_one, fixed_two)  4.77 us
    add x1, other arithmetic, second_node(): node_one + half_step * (rate_one - s1)  4.64 us
    add x1, other arithmetic, first_node(): node_zero + half_step * (rate_zero - s0)  4.32 us
  transfers between devices with their start and end apart: 15, of which 9 were waited for; matrix products, arithmetic and copies ran while one was open for 4% of the time, Pallas kernels for 0%

profile of v16, /device:TPU:11, one launch (start us, length us, event | category | flops | bytes accessed | tf_op | source)
XLA Modules:
  0.0 144.1 jit_solution(15139469054804027849)
XLA Ops:
  9.7 3.7 %collective-permute-start.1 = (f32[2,160,1,256]{3,2,1,0:T(1,128)}, f32[2,160,1,256]{3,2,1,0:T(1,128)}, u32[]{:S(2)}, u32[]{:S(2)}) collective-permute-start(f32[2,160,1,256]{3,2,1,0:T(1,128)} %pad_maximum_fusion.25), channel_id=1, source_target_pairs={{0,1},{1,2},{2,3},{3,4},{4,5},{5,6},{6,7},{7,8},{8,9},{9,10},{10,1... | collective-permute-start | bytes 983048 | tf_op jit(solution)/shard_map/ppermute | solution.py:19
  20.8 2.4 %collective-permute-done = f32[2,160,1,256]{3,2,1,0:T(1,128)} collective-permute-done((f32[2,160,1,256]{3,2,1,0:T(1,128)}, f32[2,160,1,256]{3,2,1,0:T(1,128)}, u32[]{:S(2)}, u32[]{:S(2)}) %collective-permute-start) | collective-permute-done | bytes 327712 | tf_op jit(solution)/shard_map/ppermute | solution.py:20
  24.4 4.3 %multiply_add_fusion.1 = (f32[2,64,8,256]{3,2,1,0:T(8,128)S(1)}, f32[2,64,8,256]{3,2,1,0:T(8,128)S(1)}) fusion(f32[2,64,8,256]{3,2,1,0:T(8,128)S(1)} %copy-done, f32[]{:T(128)} %bitcast.13, f32[]{:T(128)} %bitcast.12, f32[]{:T(128)} %bitcast.11, f32[]{:T(128)} %bitcast.10, pred[2]{0:T(512)(128)(4,1)S(1)} %iota_compare_fusion, ...), kind=kLoop, calls=%fused_computation.45 | loop fusion | flops 9961472 | bytes 5505042 | tf_op jit(solution)/shard_map/add | solution.py:141
  28.9 1.9 %collective-permute-start.2 = (f32[2,64,1,256]{3,2,1,0:T(1,128)S(1)}, f32[2,64,1,256]{3,2,1,0:T(1,128)S(1)}, u32[]{:S(2)}, u32[]{:S(2)}) collective-permute-start(f32[2,64,1,256]{3,2,1,0:T(1,128)S(1)} %get-tuple-element.39), channel_id=1, source_target_pairs={{1,0},{2,1},{3,2},{4,3},{5,4},{6,5},{7,6},{8,7},{9,8},{10,9},{11,1... | collective-permute-start | bytes 393224 | tf_op jit(solution)/shard_map/ppermute | solution.py:20
  30.8 3.6 %collective-permute-start.3 = (f32[2,64,1,256]{3,2,1,0:T(1,128)S(1)}, f32[2,64,1,256]{3,2,1,0:T(1,128)S(1)}, u32[]{:S(2)}, u32[]{:S(2)}) collective-permute-start(f32[2,64,1,256]{3,2,1,0:T(1,128)S(1)} %get-tuple-element.40), channel_id=1, source_target_pairs={{0,1},{1,2},{2,3},{3,4},{4,5},{5,6},{6,7},{7,8},{8,9},{9,10},{10,1... | collective-permute-start | bytes 393224 | tf_op jit(solution)/shard_map/ppermute | solution.py:19
  37.7 4.6 %multiply_add_fusion = (f32[2,64,8,256]{3,2,1,0:T(8,128)S(1)}, f32[2,64,8,256]{3,2,1,0:T(8,128)S(1)}) fusion(f32[2,64,8,256]{3,2,1,0:T(8,128)S(1)} %get-tuple-element.30, f32[2,64,8,256]{3,2,1,0:T(8,128)S(1)} %copy-done, f32[]{:T(128)} %bitcast.13, f32[2,64,8,256]{3,2,1,0:T(8,128)S(1)} %get-tuple-element.29, f32[]{:T(128)} %bitcast.12, f32[]{:T(128)} %bitcast.11, ...), kind=kLoop, calls=%fused_computation.41 | loop fusion | flops 12058624 | bytes 7602194 | tf_op jit(solution)/shard_map/add | solution.py:148
  42.7 4.4 %collective-permute-start.5 = (f32[2,64,2,256]{3,2,1,0:T(2,128)S(1)}, f32[2,64,2,256]{3,2,1,0:T(2,128)S(1)}, u32[]{:S(2)}, u32[]{:S(2)}) collective-permute-start(f32[2,64,2,256]{3,2,1,0:T(2,128)S(1)} %get-tuple-element.37), channel_id=1, source_target_pairs={{0,1},{1,2},{2,3},{3,4},{4,5},{5,6},{6,7},{7,8},{8,9},{9,10},{10,1... | collective-permute-start | bytes 786440 | tf_op jit(solution)/shard_map/ppermute | solution.py:19
  47.1 2.1 %collective-permute-start.4 = (f32[2,64,2,256]{3,2,1,0:T(2,128)S(1)}, f32[2,64,2,256]{3,2,1,0:T(2,128)S(1)}, u32[]{:S(2)}, u32[]{:S(2)}) collective-permute-start(f32[2,64,2,256]{3,2,1,0:T(2,128)S(1)} %get-tuple-element.38), channel_id=1, source_target_pairs={{1,0},{2,1},{3,2},{4,3},{5,4},{6,5},{7,6},{8,7},{9,8},{10,9},{11,1... | collective-permute-start | bytes 786440 | tf_op jit(solution)/shard_map/ppermute | solution.py:20
  50.5 5.6 %collective-permute-done.4 = f32[2,64,2,256]{3,2,1,0:T(2,128)S(1)} collective-permute-done((f32[2,64,2,256]{3,2,1,0:T(2,128)S(1)}, f32[2,64,2,256]{3,2,1,0:T(2,128)S(1)}, u32[]{:S(2)}, u32[]{:S(2)}) %collective-permute-start.4) | collective-permute-done | bytes 262176 | tf_op jit(solution)/shard_map/ppermute | solution.py:20
  56.2 4.2 %add_multiply_fusion.1 = f32[2,64,8,256]{3,2,1,0:T(8,128)S(1)} fusion(f32[2,64,8,256]{3,2,1,0:T(8,128)S(1)} %get-tuple-element.27, f32[2,64,1,256]{3,2,1,0:T(1,128)S(1)} %slice.835, f32[2,64,1,256]{3,2,1,0:T(1,128)S(1)} %slice.837, f32[2,64,8,256]{3,2,1,0:T(8,128)S(1)} %get-tuple-element.30, f32[2,64,8,256]{3,2,1,0:T(8,128)S(1)} %get-tuple-element.28, ...), kind=kLoop, calls=%fused_computation.38 | loop fusion | flops 8388608 | bytes 6553618 | tf_op jit(solution)/shard_map/div | solution.py:191
  64.0 1.9 %collective-permute-start.7 = (f32[2,32,4,256]{3,2,1,0:T(4,128)S(1)}, f32[2,32,4,256]{3,2,1,0:T(4,128)S(1)}, u32[]{:S(2)}, u32[]{:S(2)}) collective-permute-start(f32[2,32,4,256]{3,2,1,0:T(4,128)S(1)} %pad_maximum_fusion.27), channel_id=1, source_target_pairs={{0,1},{1,2},{2,3},{3,4},{4,5},{5,6},{6,7},{7,8},{8,9},{9,10},{10,1... | collective-permute-start | bytes 786440 | tf_op jit(solution)/shard_map/ppermute | solution.py:19
  66.1 2.6 %collective-permute-start.6 = (f32[2,32,4,256]{3,2,1,0:T(4,128)S(1)}, f32[2,32,4,256]{3,2,1,0:T(4,128)S(1)}, u32[]{:S(2)}, u32[]{:S(2)}) collective-permute-start(f32[2,32,4,256]{3,2,1,0:T(4,128)S(1)} %pad_maximum_fusion.26), channel_id=1, source_target_pairs={{1,0},{2,1},{3,2},{4,3},{5,4},{6,5},{7,6},{8,7},{9,8},{10,9},{11,1... | collective-permute-start | bytes 786440 | tf_op jit(solution)/shard_map/ppermute | solution.py:20
  69.4 5.2 %collective-permute-done.6 = f32[2,32,4,256]{3,2,1,0:T(4,128)S(1)} collective-permute-done((f32[2,32,4,256]{3,2,1,0:T(4,128)S(1)}, f32[2,32,4,256]{3,2,1,0:T(4,128)S(1)}, u32[]{:S(2)}, u32[]{:S(2)}) %collective-permute-start.6) | collective-permute-done | bytes 262176 | tf_op jit(solution)/shard_map/ppermute | solution.py:20
  74.8 4.2 %add_multiply_fusion.3 = (f32[2,32,2,256]{3,2,1,0:T(2,128)S(1)}, f32[2,32,2,256]{3,2,1,0:T(2,128)S(1)}, f32[2,32,2,256]{3,2,1,0:T(2,128)S(1)}, f32[2,32,2,256]{3,2,1,0:T(2,128)S(1)}) fusion(f32[2,32,1,256]{3,2,1,0:T(1,128)S(1)} %fusion.65, f32[2,32,1,256]{3,2,1,0:T(1,128)S(1)} %fusion.64, f32[2,32,1,256]{3,2,1,0:T(1,128)S(1)} %slice.832, ...), kind=kLoop, calls=%fused_computation.179 | loop fusion | flops 1507328 | bytes 1703958 | tf_op jit(solution)/shard_map/mul | solution.py:240
  80.9 4.0 %add_multiply_fusion.2 = (f32[2,32,8,256]{3,2,1,0:T(8,128)S(1)}, f32[2,32,8,256]{3,2,1,0:T(8,128)S(1)}, f32[2,32,8,256]{3,2,1,0:T(8,128)S(1)}, f32[2,32,8,256]{3,2,1,0:T(8,128)S(1)}, f32[2,32,8,256]{3,2,1,0:T(8,128)S(1)}) fusion(pred[]{:T(512)S(6)} %eq.103, f32[2,32,8,256]{3,2,1,0:T(8,128)S(1)} %get-tuple-element.25, ...), kind=kLoop, calls=%fused_computation.119 | loop fusion | flops 7340032 | bytes 7995486 | tf_op jit(solution)/shard_map/mul | solution.py:235
  86.2 4.8 %add_add_fusion.2 = (f32[2,64,8,256]{3,2,1,0:T(8,128)S(1)}, f32[2,64,8,256]{3,2,1,0:T(8,128)S(1)}) fusion(f32[2,64,8,256]{3,2,1,0:T(8,128)S(1)} %get-tuple-element.27, f32[2,64,8,256]{3,2,1,0:T(8,128)S(1)} %bitcast.47, f32[2,64,8,256]{3,2,1,0:T(8,128)S(1)} %bitcast.43, f32[2,64,8,256]{3,2,1,0:T(8,128)S(1)} %copy-done, f32[2,64,8,256]{3,2,1,0:T(8,128)S(1)} %bitcast.45, ...), kind=kLoop, calls=%fused_computation.32 | loop fusion | flops 12845056 | bytes 12845074 | tf_op jit(solution)/shard_map/add | solution.py:263
  93.1 2.4 %collective-permute-start.9 = (f32[2,64,1,256]{3,2,1,0:T(1,128)S(1)}, f32[2,64,1,256]{3,2,1,0:T(1,128)S(1)}, u32[]{:S(2)}, u32[]{:S(2)}) collective-permute-start(f32[2,64,1,256]{3,2,1,0:T(1,128)S(1)} %get-tuple-element.36), channel_id=1, source_target_pairs={{1,0},{2,1},{3,2},{4,3},{5,4},{6,5},{7,6},{8,7},{9,8},{10,9},{11,1... | collective-permute-start | bytes 393224 | tf_op jit(solution)/shard_map/ppermute | solution.py:20
  95.5 4.8 %collective-permute-done.9 = f32[2,64,1,256]{3,2,1,0:T(1,128)S(1)} collective-permute-done((f32[2,64,1,256]{3,2,1,0:T(1,128)S(1)}, f32[2,64,1,256]{3,2,1,0:T(1,128)S(1)}, u32[]{:S(2)}, u32[]{:S(2)}) %collective-permute-start.9) | collective-permute-done | bytes 131104 | tf_op jit(solution)/shard_map/ppermute | solution.py:20
  101.6 4.2 %add_add_fusion = (f32[2,64,8,256]{3,2,1,0:T(8,128)S(1)}, f32[2,64,8,256]{3,2,1,0:T(8,128)S(1)}) fusion(f32[2,64,8,256]{3,2,1,0:T(8,128)S(1)} %get-tuple-element.18, f32[2,64,8,256]{3,2,1,0:T(8,128)S(1)} %get-tuple-element.10, f32[]{:T(128)} %bitcast.13, f32[2,64,8,256]{3,2,1,0:T(8,128)S(1)} %get-tuple-element.9, f32[]{:T(128)} %bitcast.12, f32[]{:T(128)} %bitcast.11, ...), kind=kLoop, calls=%fused_computation.28 | loop fusion | flops 8388608 | bytes 7602194 | tf_op jit(solution)/shard_map/add | solution.py:269
  108.0 2.6 %collective-permute-start.11 = (f32[2,64,1,256]{3,2,1,0:T(1,128)S(1)}, f32[2,64,1,256]{3,2,1,0:T(1,128)S(1)}, u32[]{:S(2)}, u32[]{:S(2)}) collective-permute-start(f32[2,64,1,256]{3,2,1,0:T(1,128)S(1)} %get-tuple-element.34), channel_id=1, source_target_pairs={{1,0},{2,1},{3,2},{4,3},{5,4},{6,5},{7,6},{8,7},{9,8},{10,9},{11,1... | collective-permute-start | bytes 393224 | tf_op jit(solution)/shard_map/ppermute | solution.py:20
  110.7 4.5 %collective-permute-done.11 = f32[2,64,1,256]{3,2,1,0:T(1,128)S(1)} collective-permute-done((f32[2,64,1,256]{3,2,1,0:T(1,128)S(1)}, f32[2,64,1,256]{3,2,1,0:T(1,128)S(1)}, u32[]{:S(2)}, u32[]{:S(2)}) %collective-permute-start.11) | collective-permute-done | bytes 131104 | tf_op jit(solution)/shard_map/ppermute | solution.py:20
  115.9 4.1 %add_multiply_fusion = f32[2,64,8,256]{3,2,1,0:T(8,128)S(1)} fusion(f32[2,64,8,256]{3,2,1,0:T(8,128)S(1)} %get-tuple-element.7, f32[2,64,1,256]{3,2,1,0:T(1,128)S(1)} %get-tuple-element.78, f32[2,64,1,256]{3,2,1,0:T(1,128)S(1)} %get-tuple-element.77, f32[]{:T(128)} %bitcast.13, f32[]{:T(128)} %bitcast.12, f32[]{:T(128)} %bitcast.11, f32[]{:T(128)} %bitcast.10, ...), kind=kLoop, calls=%fused_computation.25 | loop fusion | flops 7602176 | bytes 4456466 | tf_op jit(solution)/shard_map/div | solution.py:271
  124.7 14.2 %collective-permute-done.13 = f32[2,32,1,256]{3,2,1,0:T(1,128)S(1)} collective-permute-done((f32[2,32,1,256]{3,2,1,0:T(1,128)S(1)}, f32[2,32,1,256]{3,2,1,0:T(1,128)S(1)}, u32[]{:S(2)}, u32[]{:S(2)}) %collective-permute-start.13) | collective-permute-done | bytes 65568 | tf_op jit(solution)/shard_map/ppermute | solution.py:291
  139.3 3.7 %fusion.30 = f32[2,32,8,256]{3,2,1,0:T(8,128)S(1)} fusion(f32[2,32,8,256]{3,2,1,0:T(8,128)S(1)} %get-tuple-element.6, f32[2,32,8,256]{3,2,1,0:T(8,128)S(1)} %broadcast_select_fusion, f32[2,32,1,256]{3,2,1,0:T(1,128)S(1)} %get-tuple-element.46, f32[2,32,7,256]{3,2,1,0:T(8,128)S(1)} %get-tuple-element.48, f32[2,32,7,256]{3,2,1,0:T(8,128)S(1)} %get-tuple-element.47, ...), kind=kLoop, calls=%fused_computation.85 | loop fusion | flops 5898240 | bytes 4849754 | tf_op jit(solution)/shard_map/sub | solution.py:297
  (139 shorter events, 40.8 us)
Async XLA Ops:
  0.0 1.2 copy-start.2
  1.2 1.2 copy-start
  2.8 1.2 copy-start.4
  8.3 6.2 %copy-start.6 = (f32[32,8,256]{2,1,0:T(8,128)}, f32[32,8,256]{2,1,0:T(8,128)S(1)}, u32[]{:S(2)}) copy-start(f32[32,8,256]{2,1,0:T(8,128)S(1)} %get-tuple-element.124) | copy-start | bytes 786436
  8.3 6.2 %copy-start.8 = (f32[32,8,256]{2,1,0:T(8,128)}, f32[32,8,256]{2,1,0:T(8,128)S(1)}, u32[]{:S(2)}) copy-start(f32[32,8,256]{2,1,0:T(8,128)S(1)} %get-tuple-element.125) | copy-start | bytes 786436
  8.4 8.1 %copy-start.14 = (f32[2,2]{1,0:T(2,128)S(1)}, f32[2,2]{1,0:T(2,128)}, u32[]{:S(2)}) copy-start(f32[2,2]{1,0:T(2,128)} %param.11) | copy-start | bytes 52
  9.7 10.0 %collective-permute-start.1 = (f32[2,160,1,256]{3,2,1,0:T(1,128)}, f32[2,160,1,256]{3,2,1,0:T(1,128)}, u32[]{:S(2)}, u32[]{:S(2)}) collective-permute-start(f32[2,160,1,256]{3,2,1,0:T(1,128)} %pad_maximum_fusion.25), channel_id=1, source_target_pairs={{0,1},{1,2},{2,3},{3,4},{4,5},{5,6},{6,7},{7,8},{8,9},{9,10},{10,1... | collective-permute-start | bytes 983048 | tf_op jit(solution)/shard_map/ppermute | solution.py:19
  14.5 8.7 %collective-permute-start = (f32[2,160,1,256]{3,2,1,0:T(1,128)}, f32[2,160,1,256]{3,2,1,0:T(1,128)}, u32[]{:S(2)}, u32[]{:S(2)}) collective-permute-start(f32[2,160,1,256]{3,2,1,0:T(1,128)} %pad_maximum_fusion.24), channel_id=1, source_target_pairs={{1,0},{2,1},{3,2},{4,3},{5,4},{6,5},{7,6},{8,7},{9,8},{10,9},{11,1... | collective-permute-start | bytes 983048 | tf_op jit(solution)/shard_map/ppermute | solution.py:20
  28.9 7.5 %collective-permute-start.2 = (f32[2,64,1,256]{3,2,1,0:T(1,128)S(1)}, f32[2,64,1,256]{3,2,1,0:T(1,128)S(1)}, u32[]{:S(2)}, u32[]{:S(2)}) collective-permute-start(f32[2,64,1,256]{3,2,1,0:T(1,128)S(1)} %get-tuple-element.39), channel_id=1, source_target_pairs={{1,0},{2,1},{3,2},{4,3},{5,4},{6,5},{7,6},{8,7},{9,8},{10,9},{11,1... | collective-permute-start | bytes 393224 | tf_op jit(solution)/shard_map/ppermute | solution.py:20
  30.8 6.9 %collective-permute-start.3 = (f32[2,64,1,256]{3,2,1,0:T(1,128)S(1)}, f32[2,64,1,256]{3,2,1,0:T(1,128)S(1)}, u32[]{:S(2)}, u32[]{:S(2)}) collective-permute-start(f32[2,64,1,256]{3,2,1,0:T(1,128)S(1)} %get-tuple-element.40), channel_id=1, source_target_pairs={{0,1},{1,2},{2,3},{3,4},{4,5},{5,6},{6,7},{7,8},{8,9},{9,10},{10,1... | collective-permute-start | bytes 393224 | tf_op jit(solution)/shard_map/ppermute | solution.py:19
  42.7 7.7 %collective-permute-start.5 = (f32[2,64,2,256]{3,2,1,0:T(2,128)S(1)}, f32[2,64,2,256]{3,2,1,0:T(2,128)S(1)}, u32[]{:S(2)}, u32[]{:S(2)}) collective-permute-start(f32[2,64,2,256]{3,2,1,0:T(2,128)S(1)} %get-tuple-element.37), channel_id=1, source_target_pairs={{0,1},{1,2},{2,3},{3,4},{4,5},{5,6},{6,7},{7,8},{8,9},{9,10},{10,1... | collective-permute-start | bytes 786440 | tf_op jit(solution)/shard_map/ppermute | solution.py:19
  47.1 9.0 %collective-permute-start.4 = (f32[2,64,2,256]{3,2,1,0:T(2,128)S(1)}, f32[2,64,2,256]{3,2,1,0:T(2,128)S(1)}, u32[]{:S(2)}, u32[]{:S(2)}) collective-permute-start(f32[2,64,2,256]{3,2,1,0:T(2,128)S(1)} %get-tuple-element.38), channel_id=1, source_target_pairs={{1,0},{2,1},{3,2},{4,3},{5,4},{6,5},{7,6},{8,7},{9,8},{10,9},{11,1... | collective-permute-start | bytes 786440 | tf_op jit(solution)/shard_map/ppermute | solution.py:20
  60.6 1.2 copy-start.9
  60.6 1.2 copy-start.11
  60.6 1.4 copy-start.13
  64.0 5.2 %collective-permute-start.7 = (f32[2,32,4,256]{3,2,1,0:T(4,128)S(1)}, f32[2,32,4,256]{3,2,1,0:T(4,128)S(1)}, u32[]{:S(2)}, u32[]{:S(2)}) collective-permute-start(f32[2,32,4,256]{3,2,1,0:T(4,128)S(1)} %pad_maximum_fusion.27), channel_id=1, source_target_pairs={{0,1},{1,2},{2,3},{3,4},{4,5},{5,6},{6,7},{7,8},{8,9},{9,10},{10,1... | collective-permute-start | bytes 786440 | tf_op jit(solution)/shard_map/ppermute | solution.py:19
  66.1 8.5 %collective-permute-start.6 = (f32[2,32,4,256]{3,2,1,0:T(4,128)S(1)}, f32[2,32,4,256]{3,2,1,0:T(4,128)S(1)}, u32[]{:S(2)}, u32[]{:S(2)}) collective-permute-start(f32[2,32,4,256]{3,2,1,0:T(4,128)S(1)} %pad_maximum_fusion.26), channel_id=1, source_target_pairs={{1,0},{2,1},{3,2},{4,3},{5,4},{6,5},{7,6},{8,7},{9,8},{10,9},{11,1... | collective-permute-start | bytes 786440 | tf_op jit(solution)/shard_map/ppermute | solution.py:20
  91.2 4.3 %collective-permute-start.8 = (f32[2,64,1,256]{3,2,1,0:T(1,128)S(1)}, f32[2,64,1,256]{3,2,1,0:T(1,128)S(1)}, u32[]{:S(2)}, u32[]{:S(2)}) collective-permute-start(f32[2,64,1,256]{3,2,1,0:T(1,128)S(1)} %get-tuple-element.35), channel_id=1, source_target_pairs={{0,1},{1,2},{2,3},{3,4},{4,5},{5,6},{6,7},{7,8},{8,9},{9,10},{10,1... | collective-permute-start | bytes 393224 | tf_op jit(solution)/shard_map/ppermute | solution.py:19
  93.1 7.2 %collective-permute-start.9 = (f32[2,64,1,256]{3,2,1,0:T(1,128)S(1)}, f32[2,64,1,256]{3,2,1,0:T(1,128)S(1)}, u32[]{:S(2)}, u32[]{:S(2)}) collective-permute-start(f32[2,64,1,256]{3,2,1,0:T(1,128)S(1)} %get-tuple-element.36), channel_id=1, source_target_pairs={{1,0},{2,1},{3,2},{4,3},{5,4},{6,5},{7,6},{8,7},{9,8},{10,9},{11,1... | collective-permute-start | bytes 393224 | tf_op jit(solution)/shard_map/ppermute | solution.py:20
  106.1 4.7 %collective-permute-start.10 = (f32[2,64,1,256]{3,2,1,0:T(1,128)S(1)}, f32[2,64,1,256]{3,2,1,0:T(1,128)S(1)}, u32[]{:S(2)}, u32[]{:S(2)}) collective-permute-start(f32[2,64,1,256]{3,2,1,0:T(1,128)S(1)} %get-tuple-element.33), channel_id=1, source_target_pairs={{0,1},{1,2},{2,3},{3,4},{4,5},{5,6},{6,7},{7,8},{8,9},{9,10},{10,1... | collective-permute-start | bytes 393224 | tf_op jit(solution)/shard_map/ppermute | solution.py:19
  108.0 7.2 %collective-permute-start.11 = (f32[2,64,1,256]{3,2,1,0:T(1,128)S(1)}, f32[2,64,1,256]{3,2,1,0:T(1,128)S(1)}, u32[]{:S(2)}, u32[]{:S(2)}) collective-permute-start(f32[2,64,1,256]{3,2,1,0:T(1,128)S(1)} %get-tuple-element.34), channel_id=1, source_target_pairs={{1,0},{2,1},{3,2},{4,3},{5,4},{6,5},{7,6},{8,7},{9,8},{10,9},{11,1... | collective-permute-start | bytes 393224 | tf_op jit(solution)/shard_map/ppermute | solution.py:20
  120.7 18.5 %collective-permute-start.12 = (f32[2,32,8,256]{3,2,1,0:T(8,128)S(1)}, f32[2,32,8,256]{3,2,1,0:T(8,128)S(1)}, u32[]{:S(2)}, u32[]{:S(2)}) collective-permute-start(f32[2,32,8,256]{3,2,1,0:T(8,128)S(1)} %get-tuple-element.5), channel_id=1, source_target_pairs={{0,16},{1,17},{2,18},{3,19},{4,20},{5,21},{6,22},{7,23},{8,24},{9,... | collective-permute-start | bytes 1572872 | tf_op jit(solution)/shard_map/ppermute | solution.py:290
  122.0 16.9 %collective-permute-start.13 = (f32[2,32,1,256]{3,2,1,0:T(1,128)S(1)}, f32[2,32,1,256]{3,2,1,0:T(1,128)S(1)}, u32[]{:S(2)}, u32[]{:S(2)}) collective-permute-start(f32[2,32,1,256]{3,2,1,0:T(1,128)S(1)} %get-tuple-element.43), channel_id=1, source_target_pairs={{0,17},{1,18},{2,19},{3,20},{4,21},{5,22},{6,23},{7,24},{8,25},{9,... | collective-permute-start | bytes 196616 | tf_op jit(solution)/shard_map/ppermute | solution.py:291
  123.3 15.6 %collective-permute-start.14 = (f32[2,32,1,256]{3,2,1,0:T(1,128)S(1)}, f32[2,32,1,256]{3,2,1,0:T(1,128)S(1)}, u32[]{:S(2)}, u32[]{:S(2)}) collective-permute-start(f32[2,32,1,256]{3,2,1,0:T(1,128)S(1)} %get-tuple-element.44), channel_id=1, source_target_pairs={{1,16},{2,17},{3,18},{4,19},{5,20},{6,21},{7,22},{8,23},{9,24},{10... | collective-permute-start | bytes 196616 | tf_op jit(solution)/shard_map/ppermute | solution.py:292
  (6 other events, 5.7 us)

commit v17 on v11

--- a/solution.py
+++ b/solution.py
@@ -176,10 +176,10 @@
 
     node_zero = initial
     rate_zero = first_rate
-    node_one = first_node(node_zero, rate_zero, first_rate, first_rate, first_rate)
+    node_one = node_zero + half_step * rate_zero
     halo_one = halo_of(node_one)
     rate_one = fine_rate(node_one, halo_one)
-    node_two = second_node(node_one, rate_one, first_rate, first_rate, first_rate)
+    node_two = node_one + half_step * rate_one
     two_b, two_a = exchange(hi(node_two, 2), lo(node_two, 2))
     halo_two = pack(hi(two_b), lo(two_a))
     coarse_end = shrink(node_two)

time: 121 us -> 120 us (level)
  other arithmetic: 30.1 us -> 28.4 us
where the time goes in v17:
time: 120 us; the launch traced here: 119 us
  waiting for transfers between devices  39.4 us (33%)
  starting transfers between devices  35 us (29%)
  other arithmetic  28.4 us (24%)
  local copies, waits for them, and re-layouts  15.1 us (13%)
    ppermute x6, waiting for transfers between devices, exchange(): after = lax.ppermute(to_left, 'space', shift_pairs(count, -1))  22.6 us
    ppermute x6, starting transfers between devices, exchange(): before = lax.ppermute(to_right, 'space', shift_pairs(count, 1))  17.5 us
    ppermute x1, waiting for transfers between devices, body(): passed_b = lax.ppermute(hi(after), ('tm', 'space'), to_east)  14.2 us
    ppermute x6, starting transfers between devices, exchange(): after = lax.ppermute(to_left, 'space', shift_pairs(count, -1))  13.6 us
    unnamed x30, local copies, waits for them, and re-layouts  5.84 us
    ppermute x6, waiting for transfers between devices, exchange(): before = lax.ppermute(to_right, 'space', shift_pairs(count, 1))  2.63 us
    mul x1, other arithmetic, stencil(): reaction = own * middle + other * middle[::-1]  2.48 us
  transfers between devices with their start and end apart: 15, of which 9 were waited for; matrix products, arithmetic and copies ran while one was open for 7% of the time, Pallas kernels for 0%

profile of v17, /device:TPU:11, one launch (start us, length us, event | category | flops | bytes accessed | tf_op | source)
XLA Modules:
  0.0 118.8 jit_solution(13610075011863955027)
XLA Ops:
  9.7 3.7 %collective-permute-start.1 = (f32[2,160,1,256]{3,2,1,0:T(1,128)}, f32[2,160,1,256]{3,2,1,0:T(1,128)}, u32[]{:S(2)}, u32[]{:S(2)}) collective-permute-start(f32[2,160,1,256]{3,2,1,0:T(1,128)} %pad_maximum_fusion.25), channel_id=1, source_target_pairs={{0,1},{1,2},{2,3},{3,4},{4,5},{5,6},{6,7},{7,8},{8,9},{9,10},{10,1... | collective-permute-start | bytes 983048 | tf_op jit(solution)/shard_map/ppermute | solution.py:19
  14.6 1.9 %collective-permute-start = (f32[2,160,1,256]{3,2,1,0:T(1,128)}, f32[2,160,1,256]{3,2,1,0:T(1,128)}, u32[]{:S(2)}, u32[]{:S(2)}) collective-permute-start(f32[2,160,1,256]{3,2,1,0:T(1,128)} %pad_maximum_fusion.24), channel_id=1, source_target_pairs={{1,0},{2,1},{3,2},{4,3},{5,4},{6,5},{7,6},{8,7},{9,8},{10,9},{11,1... | collective-permute-start | bytes 983048 | tf_op jit(solution)/shard_map/ppermute | solution.py:20
  17.2 2.5 %broadcast_multiply_fusion.1 = (f32[2]{0:T(128)S(1)}, f32[2]{0:T(128)S(1)}, f32[2]{0:T(128)S(1)}, f32[2]{0:T(128)S(1)}) fusion(f32[]{:T(128)} %bitcast.13, f32[]{:T(128)} %bitcast.12, f32[]{:T(128)} %bitcast.11, f32[]{:T(128)} %bitcast.10), kind=kLoop, calls=%fused_computation.213 | loop fusion | flops 10 | bytes 48 | tf_op jit(solution)/shard_map/mul | solution.py:80
  20.8 2.5 %collective-permute-done = f32[2,160,1,256]{3,2,1,0:T(1,128)} collective-permute-done((f32[2,160,1,256]{3,2,1,0:T(1,128)}, f32[2,160,1,256]{3,2,1,0:T(1,128)}, u32[]{:S(2)}, u32[]{:S(2)}) %collective-permute-start) | collective-permute-done | bytes 327712 | tf_op jit(solution)/shard_map/ppermute | solution.py:20
  25.8 1.9 %collective-permute-start.2 = (f32[2,64,1,256]{3,2,1,0:T(1,128)S(1)}, f32[2,64,1,256]{3,2,1,0:T(1,128)S(1)}, u32[]{:S(2)}, u32[]{:S(2)}) collective-permute-start(f32[2,64,1,256]{3,2,1,0:T(1,128)S(1)} %get-tuple-element.43), channel_id=1, source_target_pairs={{1,0},{2,1},{3,2},{4,3},{5,4},{6,5},{7,6},{8,7},{9,8},{10,9},{11,1... | collective-permute-start | bytes 393224 | tf_op jit(solution)/shard_map/ppermute | solution.py:20
  27.8 3.6 %collective-permute-start.3 = (f32[2,64,1,256]{3,2,1,0:T(1,128)S(1)}, f32[2,64,1,256]{3,2,1,0:T(1,128)S(1)}, u32[]{:S(2)}, u32[]{:S(2)}) collective-permute-start(f32[2,64,1,256]{3,2,1,0:T(1,128)S(1)} %get-tuple-element.44), channel_id=1, source_target_pairs={{0,1},{1,2},{2,3},{3,4},{4,5},{5,6},{6,7},{7,8},{8,9},{9,10},{10,1... | collective-permute-start | bytes 393224 | tf_op jit(solution)/shard_map/ppermute | solution.py:19
  36.3 4.4 %collective-permute-start.5 = (f32[2,64,2,256]{3,2,1,0:T(2,128)S(1)}, f32[2,64,2,256]{3,2,1,0:T(2,128)S(1)}, u32[]{:S(2)}, u32[]{:S(2)}) collective-permute-start(f32[2,64,2,256]{3,2,1,0:T(2,128)S(1)} %get-tuple-element.41), channel_id=1, source_target_pairs={{0,1},{1,2},{2,3},{3,4},{4,5},{5,6},{6,7},{7,8},{8,9},{9,10},{10,1... | collective-permute-start | bytes 786440 | tf_op jit(solution)/shard_map/ppermute | solution.py:19
  40.7 2.1 %collective-permute-start.4 = (f32[2,64,2,256]{3,2,1,0:T(2,128)S(1)}, f32[2,64,2,256]{3,2,1,0:T(2,128)S(1)}, u32[]{:S(2)}, u32[]{:S(2)}) collective-permute-start(f32[2,64,2,256]{3,2,1,0:T(2,128)S(1)} %get-tuple-element.42), channel_id=1, source_target_pairs={{1,0},{2,1},{3,2},{4,3},{5,4},{6,5},{7,6},{8,7},{9,8},{10,9},{11,1... | collective-permute-start | bytes 786440 | tf_op jit(solution)/shard_map/ppermute | solution.py:20
  44.1 5.6 %collective-permute-done.4 = f32[2,64,2,256]{3,2,1,0:T(2,128)S(1)} collective-permute-done((f32[2,64,2,256]{3,2,1,0:T(2,128)S(1)}, f32[2,64,2,256]{3,2,1,0:T(2,128)S(1)}, u32[]{:S(2)}, u32[]{:S(2)}) %collective-permute-start.4) | collective-permute-done | bytes 262176 | tf_op jit(solution)/shard_map/ppermute | solution.py:20
  49.8 1.3 %add_multiply_fusion.1 = f32[2,64,8,256]{3,2,1,0:T(8,128)S(1)} fusion(f32[2,64,8,256]{3,2,1,0:T(8,128)S(1)} %get-tuple-element.31, f32[2,64,1,256]{3,2,1,0:T(1,128)S(1)} %slice.835, f32[2,64,1,256]{3,2,1,0:T(1,128)S(1)} %slice.837, f32[2,64,8,256]{3,2,1,0:T(8,128)S(1)} %get-tuple-element.34, f32[2,64,8,256]{3,2,1,0:T(8,128)S(1)} %get-tuple-element.32, ...), kind=kLoop, calls=%fused_computation.38 | loop fusion | flops 7340032 | bytes 6553616 | tf_op jit(solution)/shard_map/div | solution.py:188
  54.8 1.9 %collective-permute-start.7 = (f32[2,32,4,256]{3,2,1,0:T(4,128)S(1)}, f32[2,32,4,256]{3,2,1,0:T(4,128)S(1)}, u32[]{:S(2)}, u32[]{:S(2)}) collective-permute-start(f32[2,32,4,256]{3,2,1,0:T(4,128)S(1)} %pad_maximum_fusion.27), channel_id=1, source_target_pairs={{0,1},{1,2},{2,3},{3,4},{4,5},{5,6},{6,7},{7,8},{8,9},{9,10},{10,1... | collective-permute-start | bytes 786440 | tf_op jit(solution)/shard_map/ppermute | solution.py:19
  56.8 2.6 %collective-permute-start.6 = (f32[2,32,4,256]{3,2,1,0:T(4,128)S(1)}, f32[2,32,4,256]{3,2,1,0:T(4,128)S(1)}, u32[]{:S(2)}, u32[]{:S(2)}) collective-permute-start(f32[2,32,4,256]{3,2,1,0:T(4,128)S(1)} %pad_maximum_fusion.26), channel_id=1, source_target_pairs={{1,0},{2,1},{3,2},{4,3},{5,4},{6,5},{7,6},{8,7},{9,8},{10,9},{11,1... | collective-permute-start | bytes 786440 | tf_op jit(solution)/shard_map/ppermute | solution.py:20
  60.1 5.4 %collective-permute-done.6 = f32[2,32,4,256]{3,2,1,0:T(4,128)S(1)} collective-permute-done((f32[2,32,4,256]{3,2,1,0:T(4,128)S(1)}, f32[2,32,4,256]{3,2,1,0:T(4,128)S(1)}, u32[]{:S(2)}, u32[]{:S(2)}) %collective-permute-start.6) | collective-permute-done | bytes 262176 | tf_op jit(solution)/shard_map/ppermute | solution.py:20
  68.9 1.5 %add_multiply_fusion.2 = (f32[2,32,8,256]{3,2,1,0:T(8,128)S(1)}, f32[2,32,8,256]{3,2,1,0:T(8,128)S(1)}, f32[2,32,8,256]{3,2,1,0:T(8,128)S(1)}, f32[2,32,8,256]{3,2,1,0:T(8,128)S(1)}, f32[2,32,8,256]{3,2,1,0:T(8,128)S(1)}) fusion(pred[]{:T(512)S(6)} %eq.100, f32[2,32,8,256]{3,2,1,0:T(8,128)S(1)} %get-tuple-element.25, ...), kind=kLoop, calls=%fused_computation.119 | loop fusion | flops 6815744 | bytes 7995484 | tf_op jit(solution)/shard_map/mul | solution.py:232
  71.5 1.9 %add_add_fusion.2 = (f32[2,64,8,256]{3,2,1,0:T(8,128)S(1)}, f32[2,64,8,256]{3,2,1,0:T(8,128)S(1)}) fusion(f32[2,64,8,256]{3,2,1,0:T(8,128)S(1)} %bitcast.47, f32[2,64,8,256]{3,2,1,0:T(8,128)S(1)} %get-tuple-element.33, f32[2,64,8,256]{3,2,1,0:T(8,128)S(1)} %bitcast.43, f32[2,64,8,256]{3,2,1,0:T(8,128)S(1)} %copy-done.2, f32[2,64,8,256]{3,2,1,0:T(8,128)S(1)} %bitcast.45, ...), kind=kLoop, calls=%fused_computation.32 | loop fusion | flops 9699328 | bytes 12845072 | tf_op jit(solution)/shard_map/add | solution.py:260
  73.6 1.9 %collective-permute-start.8 = (f32[2,64,1,256]{3,2,1,0:T(1,128)S(1)}, f32[2,64,1,256]{3,2,1,0:T(1,128)S(1)}, u32[]{:S(2)}, u32[]{:S(2)}) collective-permute-start(f32[2,64,1,256]{3,2,1,0:T(1,128)S(1)} %get-tuple-element.39), channel_id=1, source_target_pairs={{0,1},{1,2},{2,3},{3,4},{4,5},{5,6},{6,7},{7,8},{8,9},{9,10},{10,1... | collective-permute-start | bytes 393224 | tf_op jit(solution)/shard_map/ppermute | solution.py:19
  75.5 2.4 %collective-permute-start.9 = (f32[2,64,1,256]{3,2,1,0:T(1,128)S(1)}, f32[2,64,1,256]{3,2,1,0:T(1,128)S(1)}, u32[]{:S(2)}, u32[]{:S(2)}) collective-permute-start(f32[2,64,1,256]{3,2,1,0:T(1,128)S(1)} %get-tuple-element.40), channel_id=1, source_target_pairs={{1,0},{2,1},{3,2},{4,3},{5,4},{6,5},{7,6},{8,7},{9,8},{10,9},{11,1... | collective-permute-start | bytes 393224 | tf_op jit(solution)/shard_map/ppermute | solution.py:20
  77.9 4.8 %collective-permute-done.9 = f32[2,64,1,256]{3,2,1,0:T(1,128)S(1)} collective-permute-done((f32[2,64,1,256]{3,2,1,0:T(1,128)S(1)}, f32[2,64,1,256]{3,2,1,0:T(1,128)S(1)}, u32[]{:S(2)}, u32[]{:S(2)}) %collective-permute-start.9) | collective-permute-done | bytes 131104 | tf_op jit(solution)/shard_map/ppermute | solution.py:20
  84.0 1.6 %add_add_fusion = (f32[2,64,8,256]{3,2,1,0:T(8,128)S(1)}, f32[2,64,8,256]{3,2,1,0:T(8,128)S(1)}) fusion(f32[2,64,8,256]{3,2,1,0:T(8,128)S(1)} %get-tuple-element.18, f32[2,64,8,256]{3,2,1,0:T(8,128)S(1)} %get-tuple-element.10, f32[2,64,8,256]{3,2,1,0:T(8,128)S(1)} %get-tuple-element.9, f32[2]{0:T(128)S(1)} %get-tuple-element.30, ...), kind=kLoop, calls=%fused_computation.28 | loop fusion | flops 7340032 | bytes 7602192 | tf_op jit(solution)/shard_map/add | solution.py:266
  85.9 1.9 %collective-permute-start.10 = (f32[2,64,1,256]{3,2,1,0:T(1,128)S(1)}, f32[2,64,1,256]{3,2,1,0:T(1,128)S(1)}, u32[]{:S(2)}, u32[]{:S(2)}) collective-permute-start(f32[2,64,1,256]{3,2,1,0:T(1,128)S(1)} %get-tuple-element.37), channel_id=1, source_target_pairs={{0,1},{1,2},{2,3},{3,4},{4,5},{5,6},{6,7},{7,8},{8,9},{9,10},{10,1... | collective-permute-start | bytes 393224 | tf_op jit(solution)/shard_map/ppermute | solution.py:19
  87.8 2.6 %collective-permute-start.11 = (f32[2,64,1,256]{3,2,1,0:T(1,128)S(1)}, f32[2,64,1,256]{3,2,1,0:T(1,128)S(1)}, u32[]{:S(2)}, u32[]{:S(2)}) collective-permute-start(f32[2,64,1,256]{3,2,1,0:T(1,128)S(1)} %get-tuple-element.38), channel_id=1, source_target_pairs={{1,0},{2,1},{3,2},{4,3},{5,4},{6,5},{7,6},{8,7},{9,8},{10,9},{11,1... | collective-permute-start | bytes 393224 | tf_op jit(solution)/shard_map/ppermute | solution.py:20
  90.6 4.5 %collective-permute-done.11 = f32[2,64,1,256]{3,2,1,0:T(1,128)S(1)} collective-permute-done((f32[2,64,1,256]{3,2,1,0:T(1,128)S(1)}, f32[2,64,1,256]{3,2,1,0:T(1,128)S(1)}, u32[]{:S(2)}, u32[]{:S(2)}) %collective-permute-start.11) | collective-permute-done | bytes 131104 | tf_op jit(solution)/shard_map/ppermute | solution.py:20
  95.7 1.3 %add_multiply_fusion = f32[2,64,8,256]{3,2,1,0:T(8,128)S(1)} fusion(f32[2,64,8,256]{3,2,1,0:T(8,128)S(1)} %get-tuple-element.7, f32[2,64,1,256]{3,2,1,0:T(1,128)S(1)} %get-tuple-element.82, f32[2,64,1,256]{3,2,1,0:T(1,128)S(1)} %get-tuple-element.81, f32[2]{0:T(128)S(1)} %get-tuple-element.30, f32[2]{0:T(128)S(1)} %get-tuple-element.139, ...), kind=kLoop, calls=%fused_computation.25 | loop fusion | flops 6553600 | bytes 4456464 | tf_op jit(solution)/shard_map/div | solution.py:268
  101.8 14.2 %collective-permute-done.13 = f32[2,32,1,256]{3,2,1,0:T(1,128)S(1)} collective-permute-done((f32[2,32,1,256]{3,2,1,0:T(1,128)S(1)}, f32[2,32,1,256]{3,2,1,0:T(1,128)S(1)}, u32[]{:S(2)}, u32[]{:S(2)}) %collective-permute-start.13) | collective-permute-done | bytes 65568 | tf_op jit(solution)/shard_map/ppermute | solution.py:288
  (139 shorter events, 39.9 us)
Async XLA Ops:
  0.0 1.2 %copy-start.1 = (f32[64,8,256]{2,1,0:T(8,128)S(1)}, f32[64,8,256]{2,1,0:T(8,128)}, u32[]{:S(2)}) copy-start(f32[64,8,256]{2,1,0:T(8,128)} %param.7) | copy-start | bytes 1572868
  1.2 1.2 %copy-start.2 = (f32[2,64,8,256]{3,2,1,0:T(8,128)S(1)}, f32[2,64,8,256]{3,2,1,0:T(8,128)}, u32[]{:S(2)}) copy-start(f32[2,64,8,256]{3,2,1,0:T(8,128)} %param.6) | copy-start | bytes 3145732
  2.8 1.2 %copy-start.4 = (f32[64,8,256]{2,1,0:T(8,128)S(1)}, f32[64,8,256]{2,1,0:T(8,128)}, u32[]{:S(2)}) copy-start(f32[64,8,256]{2,1,0:T(8,128)} %param.9) | copy-start | bytes 1572868
  8.3 6.2 %copy-start.6 = (f32[32,8,256]{2,1,0:T(8,128)}, f32[32,8,256]{2,1,0:T(8,128)S(1)}, u32[]{:S(2)}) copy-start(f32[32,8,256]{2,1,0:T(8,128)S(1)} %get-tuple-element.128) | copy-start | bytes 786436
  8.3 6.2 %copy-start.8 = (f32[32,8,256]{2,1,0:T(8,128)}, f32[32,8,256]{2,1,0:T(8,128)S(1)}, u32[]{:S(2)}) copy-start(f32[32,8,256]{2,1,0:T(8,128)S(1)} %get-tuple-element.129) | copy-start | bytes 786436
  8.4 8.1 %copy-start.14 = (f32[2,2]{1,0:T(2,128)S(1)}, f32[2,2]{1,0:T(2,128)}, u32[]{:S(2)}) copy-start(f32[2,2]{1,0:T(2,128)} %param.11) | copy-start | bytes 52
  9.7 10.0 %collective-permute-start.1 = (f32[2,160,1,256]{3,2,1,0:T(1,128)}, f32[2,160,1,256]{3,2,1,0:T(1,128)}, u32[]{:S(2)}, u32[]{:S(2)}) collective-permute-start(f32[2,160,1,256]{3,2,1,0:T(1,128)} %pad_maximum_fusion.25), channel_id=1, source_target_pairs={{0,1},{1,2},{2,3},{3,4},{4,5},{5,6},{6,7},{7,8},{8,9},{9,10},{10,1... | collective-permute-start | bytes 983048 | tf_op jit(solution)/shard_map/ppermute | solution.py:19
  14.6 8.7 %collective-permute-start = (f32[2,160,1,256]{3,2,1,0:T(1,128)}, f32[2,160,1,256]{3,2,1,0:T(1,128)}, u32[]{:S(2)}, u32[]{:S(2)}) collective-permute-start(f32[2,160,1,256]{3,2,1,0:T(1,128)} %pad_maximum_fusion.24), channel_id=1, source_target_pairs={{1,0},{2,1},{3,2},{4,3},{5,4},{6,5},{7,6},{8,7},{9,8},{10,9},{11,1... | collective-permute-start | bytes 983048 | tf_op jit(solution)/shard_map/ppermute | solution.py:20
  25.8 7.5 %collective-permute-start.2 = (f32[2,64,1,256]{3,2,1,0:T(1,128)S(1)}, f32[2,64,1,256]{3,2,1,0:T(1,128)S(1)}, u32[]{:S(2)}, u32[]{:S(2)}) collective-permute-start(f32[2,64,1,256]{3,2,1,0:T(1,128)S(1)} %get-tuple-element.43), channel_id=1, source_target_pairs={{1,0},{2,1},{3,2},{4,3},{5,4},{6,5},{7,6},{8,7},{9,8},{10,9},{11,1... | collective-permute-start | bytes 393224 | tf_op jit(solution)/shard_map/ppermute | solution.py:20
  27.8 6.9 %collective-permute-start.3 = (f32[2,64,1,256]{3,2,1,0:T(1,128)S(1)}, f32[2,64,1,256]{3,2,1,0:T(1,128)S(1)}, u32[]{:S(2)}, u32[]{:S(2)}) collective-permute-start(f32[2,64,1,256]{3,2,1,0:T(1,128)S(1)} %get-tuple-element.44), channel_id=1, source_target_pairs={{0,1},{1,2},{2,3},{3,4},{4,5},{5,6},{6,7},{7,8},{8,9},{9,10},{10,1... | collective-permute-start | bytes 393224 | tf_op jit(solution)/shard_map/ppermute | solution.py:19
  36.3 7.7 %collective-permute-start.5 = (f32[2,64,2,256]{3,2,1,0:T(2,128)S(1)}, f32[2,64,2,256]{3,2,1,0:T(2,128)S(1)}, u32[]{:S(2)}, u32[]{:S(2)}) collective-permute-start(f32[2,64,2,256]{3,2,1,0:T(2,128)S(1)} %get-tuple-element.41), channel_id=1, source_target_pairs={{0,1},{1,2},{2,3},{3,4},{4,5},{5,6},{6,7},{7,8},{8,9},{9,10},{10,1... | collective-permute-start | bytes 786440 | tf_op jit(solution)/shard_map/ppermute | solution.py:19
  40.7 9.0 %collective-permute-start.4 = (f32[2,64,2,256]{3,2,1,0:T(2,128)S(1)}, f32[2,64,2,256]{3,2,1,0:T(2,128)S(1)}, u32[]{:S(2)}, u32[]{:S(2)}) collective-permute-start(f32[2,64,2,256]{3,2,1,0:T(2,128)S(1)} %get-tuple-element.42), channel_id=1, source_target_pairs={{1,0},{2,1},{3,2},{4,3},{5,4},{6,5},{7,6},{8,7},{9,8},{10,9},{11,1... | collective-permute-start | bytes 786440 | tf_op jit(solution)/shard_map/ppermute | solution.py:20
  51.3 1.2 copy-start.9
  51.3 1.2 %copy-start.11 = (f32[32,8,256]{2,1,0:T(8,128)S(1)}, f32[32,8,256]{2,1,0:T(8,128)}, u32[]{:S(2)}) copy-start(f32[32,8,256]{2,1,0:T(8,128)} %copy-done.10) | copy-start | bytes 786436
  51.3 1.4 %copy-start.13 = (f32[2,32,8,256]{3,2,1,0:T(8,128)S(1)}, f32[2,32,8,256]{3,2,1,0:T(8,128)}, u32[]{:S(2)}) copy-start(f32[2,32,8,256]{3,2,1,0:T(8,128)} %copy-done.12) | copy-start | bytes 1572868
  54.8 5.2 %collective-permute-start.7 = (f32[2,32,4,256]{3,2,1,0:T(4,128)S(1)}, f32[2,32,4,256]{3,2,1,0:T(4,128)S(1)}, u32[]{:S(2)}, u32[]{:S(2)}) collective-permute-start(f32[2,32,4,256]{3,2,1,0:T(4,128)S(1)} %pad_maximum_fusion.27), channel_id=1, source_target_pairs={{0,1},{1,2},{2,3},{3,4},{4,5},{5,6},{6,7},{7,8},{8,9},{9,10},{10,1... | collective-permute-start | bytes 786440 | tf_op jit(solution)/shard_map/ppermute | solution.py:19
  56.8 8.7 %collective-permute-start.6 = (f32[2,32,4,256]{3,2,1,0:T(4,128)S(1)}, f32[2,32,4,256]{3,2,1,0:T(4,128)S(1)}, u32[]{:S(2)}, u32[]{:S(2)}) collective-permute-start(f32[2,32,4,256]{3,2,1,0:T(4,128)S(1)} %pad_maximum_fusion.26), channel_id=1, source_target_pairs={{1,0},{2,1},{3,2},{4,3},{5,4},{6,5},{7,6},{8,7},{9,8},{10,9},{11,1... | collective-permute-start | bytes 786440 | tf_op jit(solution)/shard_map/ppermute | solution.py:20
  73.6 4.3 %collective-permute-start.8 = (f32[2,64,1,256]{3,2,1,0:T(1,128)S(1)}, f32[2,64,1,256]{3,2,1,0:T(1,128)S(1)}, u32[]{:S(2)}, u32[]{:S(2)}) collective-permute-start(f32[2,64,1,256]{3,2,1,0:T(1,128)S(1)} %get-tuple-element.39), channel_id=1, source_target_pairs={{0,1},{1,2},{2,3},{3,4},{4,5},{5,6},{6,7},{7,8},{8,9},{9,10},{10,1... | collective-permute-start | bytes 393224 | tf_op jit(solution)/shard_map/ppermute | solution.py:19
  75.5 7.2 %collective-permute-start.9 = (f32[2,64,1,256]{3,2,1,0:T(1,128)S(1)}, f32[2,64,1,256]{3,2,1,0:T(1,128)S(1)}, u32[]{:S(2)}, u32[]{:S(2)}) collective-permute-start(f32[2,64,1,256]{3,2,1,0:T(1,128)S(1)} %get-tuple-element.40), channel_id=1, source_target_pairs={{1,0},{2,1},{3,2},{4,3},{5,4},{6,5},{7,6},{8,7},{9,8},{10,9},{11,1... | collective-permute-start | bytes 393224 | tf_op jit(solution)/shard_map/ppermute | solution.py:20
  85.9 4.7 %collective-permute-start.10 = (f32[2,64,1,256]{3,2,1,0:T(1,128)S(1)}, f32[2,64,1,256]{3,2,1,0:T(1,128)S(1)}, u32[]{:S(2)}, u32[]{:S(2)}) collective-permute-start(f32[2,64,1,256]{3,2,1,0:T(1,128)S(1)} %get-tuple-element.37), channel_id=1, source_target_pairs={{0,1},{1,2},{2,3},{3,4},{4,5},{5,6},{6,7},{7,8},{8,9},{9,10},{10,1... | collective-permute-start | bytes 393224 | tf_op jit(solution)/shard_map/ppermute | solution.py:19
  87.8 7.2 %collective-permute-start.11 = (f32[2,64,1,256]{3,2,1,0:T(1,128)S(1)}, f32[2,64,1,256]{3,2,1,0:T(1,128)S(1)}, u32[]{:S(2)}, u32[]{:S(2)}) collective-permute-start(f32[2,64,1,256]{3,2,1,0:T(1,128)S(1)} %get-tuple-element.38), channel_id=1, source_target_pairs={{1,0},{2,1},{3,2},{4,3},{5,4},{6,5},{7,6},{8,7},{9,8},{10,9},{11,1... | collective-permute-start | bytes 393224 | tf_op jit(solution)/shard_map/ppermute | solution.py:20
  97.8 18.5 %collective-permute-start.12 = (f32[2,32,8,256]{3,2,1,0:T(8,128)S(1)}, f32[2,32,8,256]{3,2,1,0:T(8,128)S(1)}, u32[]{:S(2)}, u32[]{:S(2)}) collective-permute-start(f32[2,32,8,256]{3,2,1,0:T(8,128)S(1)} %get-tuple-element.5), channel_id=1, source_target_pairs={{0,16},{1,17},{2,18},{3,19},{4,20},{5,21},{6,22},{7,23},{8,24},{9,... | collective-permute-start | bytes 1572872 | tf_op jit(solution)/shard_map/ppermute | solution.py:287
  99.1 16.9 %collective-permute-start.13 = (f32[2,32,1,256]{3,2,1,0:T(1,128)S(1)}, f32[2,32,1,256]{3,2,1,0:T(1,128)S(1)}, u32[]{:S(2)}, u32[]{:S(2)}) collective-permute-start(f32[2,32,1,256]{3,2,1,0:T(1,128)S(1)} %get-tuple-element.47), channel_id=1, source_target_pairs={{0,17},{1,18},{2,19},{3,20},{4,21},{5,22},{6,23},{7,24},{8,25},{9,... | collective-permute-start | bytes 196616 | tf_op jit(solution)/shard_map/ppermute | solution.py:288
  100.4 15.6 %collective-permute-start.14 = (f32[2,32,1,256]{3,2,1,0:T(1,128)S(1)}, f32[2,32,1,256]{3,2,1,0:T(1,128)S(1)}, u32[]{:S(2)}, u32[]{:S(2)}) collective-permute-start(f32[2,32,1,256]{3,2,1,0:T(1,128)S(1)} %get-tuple-element.48), channel_id=1, source_target_pairs={{1,16},{2,17},{3,18},{4,19},{5,20},{6,21},{7,22},{8,23},{9,24},{10... | collective-permute-start | bytes 196616 | tf_op jit(solution)/shard_map/ppermute | solution.py:289
  (6 other events, 5.7 us)
